TPU v7x, 32 devices: a whole 2x2x4 slice. The times are simulated.
32 devices in a mesh: section: 2 (over x), seq: 16 (over z, y, core).
Axes of the slice: x: 2, y: 2, z: 4, core: 2. Of those that a mesh axis runs over, the one named last changes fastest.
Arguments:
- clips: bfloat16 [2, 16, 512, 384], P(None, 'seq'), may hold values from -6 to 6
- cotangent: bfloat16 [2, 16, 512, 384], P(None, 'seq'), may hold values from -6 to 6
- spatial_taps: float32 [2, 9, 384], P('section'), may hold values from -1 to 1
- modulation: float32 [2, 2, 2, 384], P('section'), may hold values from -1 to 1
- norm_gain: float32 [2, 384], P('section'), may hold values from 0.5 to 1.5
- w_in: bfloat16 [2, 384, 768], P('section'), may hold values from -0.3125 to 0.3125
- w_out: bfloat16 [2, 768, 384], P('section'), may hold values from -0.21875 to 0.21875
- band_taps: float32 [2, 9, 384], P('section'), may hold values from -0.8 to 0.8
Outputs:
- activations: bfloat16 [2, 2, 16, 512, 384], P('section', None, 'seq')
- input_grads: bfloat16 [2, 2, 16, 512, 384], P('section', None, 'seq')
All inputs are finite; a program needn't handle non-finite values.
Results may differ from a plain program's by a relative error of at most 0.017.
Values may be sent and summed in bfloat16 or wider, within the bound.
No kernel may reach another device: no remote copies, remote signals or barrier semaphores. Data moves between devices by JAX's collectives and lax.ppermute only.
A program may use at most 64 MiB of HBM per device.

v0:
```python
import jax
import jax.numpy as jnp
from jax import lax
from jax.sharding import PartitionSpec as P

H = 32
W = 16
BAND = 9


EPSILON = 1e-06


def spatial_block(values, stencil_taps, modulate, norm_gain, w_in, w_out):
    frame_count, pixel_count, channels = values.shape
    volume = values.astype(jnp.float32).reshape(frame_count, H, W, channels)
    padded = jnp.pad(volume, ((0, 0), (1, 1), (1, 1), (0, 0)))
    stencil_sum = jnp.zeros_like(volume)
    for down_step in range(3):
        for across in range(3):
            stencil_sum = (
                stencil_sum
                + stencil_taps[3 * down_step + across]
                * padded[:, down_step : down_step + H, across : across + W]
            )
    stencil_sum = stencil_sum.reshape(frame_count * pixel_count, channels)
    modulated = stencil_sum * (1.0 + modulate[0]) + modulate[1]
    scaled = (
        modulated
        * lax.rsqrt(jnp.mean(modulated * modulated, axis=-1, keepdims=True) + EPSILON)
        * norm_gain
    )
    normed = scaled.astype(jnp.bfloat16)
    hidden = jax.nn.silu(jnp.dot(normed, w_in, preferred_element_type=jnp.float32)).astype(
        jnp.bfloat16
    )
    update = jnp.dot(hidden, w_out, preferred_element_type=jnp.float32)
    return (values.astype(jnp.float32) + update.reshape(frame_count, pixel_count, channels)).astype(
        jnp.bfloat16
    )


def band_frames(values, tap_table):
    frame_count = values.shape[0]
    reach = BAND // 2
    volume = values.astype(jnp.float32)
    padded = jnp.pad(volume, ((reach, reach), (0, 0), (0, 0)))
    total = volume
    for offset in range(BAND):
        total = total + tap_table[offset] * padded[offset : offset + frame_count]
    return total.astype(jnp.bfloat16)


def temporal(values, tap_table):
    pixel_view = lax.all_to_all(values, "seq", split_axis=1, concat_axis=0, tiled=True)
    banded = band_frames(pixel_view, tap_table)
    return lax.all_to_all(banded, "seq", split_axis=0, concat_axis=1, tiled=True)


def on_device(clips, cotangent, spatial_taps, modulation, norm_gain, w_in, w_out, band_taps):
    clip_total = clips.shape[0]
    per_device = clip_total // lax.axis_size("section")
    first_clip = lax.axis_index("section") * per_device
    all_taps, all_mod, all_gain, all_band = (
        lax.all_gather(spatial_taps.astype(jnp.bfloat16), "section", axis=0, tiled=True).astype(
            spatial_taps.dtype
        ),
        lax.all_gather(modulation.astype(jnp.bfloat16), "section", axis=0, tiled=True).astype(
            modulation.dtype
        ),
        lax.all_gather(norm_gain.astype(jnp.bfloat16), "section", axis=0, tiled=True).astype(
            norm_gain.dtype
        ),
        lax.all_gather(band_taps.astype(jnp.bfloat16), "section", axis=0, tiled=True).astype(
            band_taps.dtype
        ),
    )
    all_in, all_out = (
        lax.all_gather(w_in, "section", axis=0, tiled=True),
        lax.all_gather(w_out, "section", axis=0, tiled=True),
    )

    def section_spatial(values, which, clip_id):
        modulate = lax.dynamic_index_in_dim(all_mod[which], clip_id, 0, keepdims=False)
        return spatial_block(
            values, all_taps[which], modulate, all_gain[which], all_in[which], all_out[which]
        )

    first_acts, second_acts, first_grads, second_grads = ([], [], [], [])
    clip_id = first_clip + 0
    start_values = lax.dynamic_index_in_dim(clips, clip_id, 0, keepdims=False)
    seed = lax.dynamic_index_in_dim(cotangent, clip_id, 0, keepdims=False)
    first_mixed, first_pull = jax.vjp(
        lambda values: section_spatial(values, 0, clip_id), start_values
    )
    first_result = temporal(first_mixed, all_band[0])
    second_mixed, second_pull = jax.vjp(
        lambda values: section_spatial(values, 1, clip_id), first_result
    )
    second_result = temporal(second_mixed, all_band[1])
    second_grad = second_pull(temporal(seed, all_band[1][::-1]))[0]
    first_grad = first_pull(temporal(second_grad, all_band[0][::-1]))[0]
    first_acts.append(first_result)
    second_acts.append(second_result)
    first_grads.append(first_grad)
    second_grads.append(second_grad)
    local_acts = jnp.stack([jnp.stack(first_acts), jnp.stack(second_acts)])
    local_grads = jnp.stack([jnp.stack(first_grads), jnp.stack(second_grads)])
    activations, input_grads = (
        lax.all_to_all(local_acts, "section", split_axis=0, concat_axis=1, tiled=True),
        lax.all_to_all(local_grads, "section", split_axis=0, concat_axis=1, tiled=True),
    )
    return (activations, input_grads)


def solution(mesh):
    placed = (
        P(None, "seq", None, None),
        P(None, "seq", None, None),
        P("section", None, None),
        P("section", None, None, None),
        P("section", None),
        P("section", None, None),
        P("section", None, None),
        P("section", None, None),
    )
    return jax.shard_map(
        on_device,
        mesh=mesh,
        in_specs=placed,
        out_specs=(P("section", None, "seq", None, None), P("section", None, "seq", None, None)),
        check_vma=False,
    )
```

profile of v0, /device:TPU:0, one launch (start us, length us, event | category | flops | bytes accessed | tf_op | source)
XLA Modules:
  0.0 253.1 jit_solution(4353219714056885673)
XLA Ops:
  9.4 5.2 %all-gather = bf16[2,1,384]{2,1,0:T(2,128)(2,1)S(1)} all-gather(bf16[1,1,384]{2,1,0:T(2,128)(2,1)S(1)} %convert_bitcast_fusion), channel_id=1, replica_groups=mesh['section'=2,'seq'=16] {'section'}, dimensions={0}, use_global_device_ids=true | all-gather | bytes 2304 | tf_op jit(solution)/shard_map/all_gather | solution.py:71
  15.3 4.3 %all_gather.19 = bf16[2,2,2,384]{3,2,1,0:T(2,128)(2,1)S(1)} all-gather(bf16[1,2,2,384]{3,2,1,0:T(2,128)(2,1)S(1)} %convert_element_type.221), channel_id=1, replica_groups=mesh['section'=2,'seq'=16] {'section'}, dimensions={0}, use_global_device_ids=true | all-gather | bytes 9216 | tf_op jit(solution)/shard_map/all_gather | solution.py:68
  20.9 4.6 %all_gather.18 = bf16[2,9,384]{2,1,0:T(8,128)(2,1)S(1)} all-gather(bf16[1,9,384]{2,1,0:T(8,128)(2,1)S(1)} %copy.31), channel_id=1, replica_groups=mesh['section'=2,'seq'=16] {'section'}, dimensions={0}, use_global_device_ids=true | all-gather | bytes 20736 | tf_op jit(solution)/shard_map/all_gather | solution.py:65
  28.0 7.2 %all-gather.4.cloned.1.call-done = bf16[2,384,768]{2,1,0:T(8,128)(2,1)} async-done(((bf16[1,384,768]{2,1,0:T(8,128)(2,1)}), bf16[2,384,768]{2,1,0:T(8,128)(2,1)}) %all-gather.4.cloned.1.call-update) | async-done | bytes 1179664 | tf_op jit(solution)/shard_map/all_gather | solution.py:79
  36.9 22.8 %all-gather.6.cloned.1.call-done = bf16[2,768,384]{2,1,0:T(8,128)(2,1)} async-done(((bf16[1,768,384]{2,1,0:T(8,128)(2,1)}), bf16[2,768,384]{2,1,0:T(8,128)(2,1)}) %all-gather.6.cloned.1.call-update) | async-done | bytes 1179664 | tf_op jit(solution)/shard_map/all_gather | solution.py:80
  66.6 5.6 %all-to-all-start = ((bf16[16,2,6144]{2,1,0:T(2,128)(2,1)}), bf16[16,2,6144]{2,1,0:T(2,128)(2,1)S(1)}, u32[]{:S(2)}, u32[]{:S(2)}) async-start(bf16[16,2,6144]{2,1,0:T(2,128)(2,1)} %reshape.801), calls=%async_computation | async-start | bytes 786432 | tf_op jit(solution)/shard_map/all_to_all | solution.py:55
  72.2 4.4 %all_gather.23 = bf16[2,9,384]{2,1,0:T(8,128)(2,1)S(1)} all-gather(bf16[1,9,384]{2,1,0:T(8,128)(2,1)S(1)} %copy.30), channel_id=1, replica_groups=mesh['section'=2,'seq'=16] {'section'}, dimensions={0}, use_global_device_ids=true | all-gather | bytes 20736 | tf_op jit(solution)/shard_map/all_gather | solution.py:74
  77.3 7.1 %all-to-all-done = bf16[16,2,6144]{2,1,0:T(2,128)(2,1)S(1)} async-done(((bf16[16,2,6144]{2,1,0:T(2,128)(2,1)}), bf16[16,2,6144]{2,1,0:T(2,128)(2,1)S(1)}, u32[]{:S(2)}, u32[]{:S(2)}) %all-to-all-start) | async-done | bytes 393248 | tf_op jit(solution)/shard_map/all_to_all | solution.py:55
  86.1 3.6 %all-to-all-start.1 = ((bf16[16,32,384]{2,1,0:T(8,128)(2,1)}), bf16[16,32,384]{2,1,0:T(8,128)(2,1)S(1)}, u32[]{:S(2)}, u32[]{:S(2)}) async-start(bf16[16,32,384]{2,1,0:T(8,128)(2,1)} %fusion.44), calls=%async_computation.1 | async-start | bytes 786432 | tf_op jit(solution)/shard_map/all_to_all | solution.py:57
  94.4 7.4 %all-to-all-done.1 = bf16[16,32,384]{2,1,0:T(8,128)(2,1)S(1)} async-done(((bf16[16,32,384]{2,1,0:T(8,128)(2,1)}), bf16[16,32,384]{2,1,0:T(8,128)(2,1)S(1)}, u32[]{:S(2)}, u32[]{:S(2)}) %all-to-all-start.1) | async-done | bytes 393248 | tf_op jit(solution)/shard_map/all_to_all | solution.py:57
  101.8 4.4 %all-to-all-start.5 = ((bf16[16,2,6144]{2,1,0:T(2,128)(2,1)}), bf16[16,2,6144]{2,1,0:T(2,128)(2,1)}, u32[]{:S(2)}, u32[]{:S(2)}) async-start(bf16[16,2,6144]{2,1,0:T(2,128)(2,1)} %reshape.805), calls=%async_computation.5 | async-start | bytes 786432 | tf_op jit(solution)/shard_map/all_to_all | solution.py:55
  111.0 3.8 %reduce.88 = bf16[512,384]{1,0:T(8,128)(2,1)} reduce(bf16[512,1,384]{2,1,0:T(2,128)(2,1)S(1)} %bitcast.120, bf16[]{:T(256)} %broadcast.419), dimensions={1}, to_apply=%bitcast.99.reduce_sub_computation | reduce | bytes 786434
  118.3 4.2 %all-to-all-start.2 = ((bf16[16,2,6144]{2,1,0:T(2,128)(2,1)}), bf16[16,2,6144]{2,1,0:T(2,128)(2,1)}, u32[]{:S(2)}, u32[]{:S(2)}) async-start(bf16[16,2,6144]{2,1,0:T(2,128)(2,1)} %reshape.803), calls=%async_computation.2 | async-start | bytes 786432 | tf_op jit(solution)/shard_map/all_to_all | solution.py:55
  126.2 8.5 %all-to-all-done.2 = bf16[16,2,6144]{2,1,0:T(2,128)(2,1)} async-done(((bf16[16,2,6144]{2,1,0:T(2,128)(2,1)}), bf16[16,2,6144]{2,1,0:T(2,128)(2,1)}, u32[]{:S(2)}, u32[]{:S(2)}) %all-to-all-start.2) | async-done | bytes 393248 | tf_op jit(solution)/shard_map/all_to_all | solution.py:55
  140.5 3.8 %all-to-all-start.6 = ((bf16[16,32,384]{2,1,0:T(8,128)(2,1)}), bf16[16,32,384]{2,1,0:T(8,128)(2,1)S(1)}, u32[]{:S(2)}, u32[]{:S(2)}) async-start(bf16[16,32,384]{2,1,0:T(8,128)(2,1)} %get-tuple-element.70), calls=%async_computation.6 | async-start | bytes 786432 | tf_op jit(solution)/shard_map/all_to_all | solution.py:57
  144.4 11.8 %all-to-all-done.6 = bf16[16,32,384]{2,1,0:T(8,128)(2,1)S(1)} async-done(((bf16[16,32,384]{2,1,0:T(8,128)(2,1)}), bf16[16,32,384]{2,1,0:T(8,128)(2,1)S(1)}, u32[]{:S(2)}, u32[]{:S(2)}) %all-to-all-start.6) | async-done | bytes 393248 | tf_op jit(solution)/shard_map/all_to_all | solution.py:57
  156.2 3.7 %multiply_reduce_fusion.1 = (f32[512]{0:T(512)S(1)}, f32[512,384]{1,0:T(8,128)}) fusion(f32[1,32,16,384]{3,2,1,0:T(8,128)S(1)} %get-tuple-element.49, f32[384]{0:T(512)S(1)} %copy-done.15, f32[384]{0:T(512)S(1)} %copy-done.13, f32[384]{0:T(512)S(1)} %copy-done.75, bf16[2,384,768]{2,1,0:T(8,128)(2,1)} %all-gather.4.cloned.1.call-done, ...), kind=kOutput, calls=%fused_computation.208 | convolution fusion | flops 609680896 | bytes 4725248 | tf_op jit(solution)/shard_map/transpose(jvp())/dot_general | solution.py:34
  164.5 4.0 %reduce.89 = bf16[512,384]{1,0:T(8,128)(2,1)S(1)} reduce(bf16[512,1,384]{2,1,0:T(2,128)(2,1)} %bitcast.116, bf16[]{:T(256)} %broadcast.419), dimensions={1}, to_apply=%bitcast.97.reduce_sub_computation | reduce | bytes 786434
  168.6 15.6 %all_to_all.105 = bf16[16,2,6144]{2,1,0:T(2,128)(2,1)} all-to-all(bf16[16,2,6144]{2,1,0:T(2,128)(2,1)S(1)} %reshape.807), channel_id=1, replica_groups=mesh['section'=2,'seq'=16] {'seq'}, dimensions={0} | all-to-all | bytes 786432 | tf_op jit(solution)/shard_map/all_to_all | solution.py:55
  184.2 3.6 %all-to-all-start.3 = ((bf16[16,32,384]{2,1,0:T(8,128)(2,1)}), bf16[16,32,384]{2,1,0:T(8,128)(2,1)S(1)}, u32[]{:S(2)}, u32[]{:S(2)}) async-start(bf16[16,32,384]{2,1,0:T(8,128)(2,1)} %get-tuple-element.71), calls=%async_computation.3 | async-start | bytes 786432 | tf_op jit(solution)/shard_map/all_to_all | solution.py:57
  193.8 6.1 %all-to-all-done.3 = bf16[16,32,384]{2,1,0:T(8,128)(2,1)S(1)} async-done(((bf16[16,32,384]{2,1,0:T(8,128)(2,1)}), bf16[16,32,384]{2,1,0:T(8,128)(2,1)S(1)}, u32[]{:S(2)}, u32[]{:S(2)}) %all-to-all-start.3) | async-done | bytes 393248 | tf_op jit(solution)/shard_map/all_to_all | solution.py:57
  206.0 9.7 %all-to-all-done.8 = bf16[16,32,384]{2,1,0:T(8,128)(2,1)S(1)} async-done(((bf16[16,32,384]{2,1,0:T(8,128)(2,1)}), bf16[16,32,384]{2,1,0:T(8,128)(2,1)S(1)}, u32[]{:S(2)}, u32[]{:S(2)}) %all-to-all-start.8) | async-done | bytes 393248 | tf_op jit(solution)/shard_map/all_to_all | solution.py:57
  226.8 3.7 %all-to-all-done.4 = bf16[2,1,1,512,384]{4,3,2,1,0:T(8,128)(2,1)S(1)} async-done(((bf16[2,1,1,512,384]{4,3,2,1,0:T(8,128)(2,1)}), bf16[2,1,1,512,384]{4,3,2,1,0:T(8,128)(2,1)S(1)}, u32[]{:S(2)}, u32[]{:S(2)}) %all-to-all-start.4) | async-done | bytes 786464 | tf_op jit(solution)/shard_map/all_to_all | solution.py:110
  234.1 10.5 %all-to-all-done.9 = bf16[2,1,1,512,384]{4,3,2,1,0:T(8,128)(2,1)S(1)} async-done(((bf16[2,1,1,512,384]{4,3,2,1,0:T(8,128)(2,1)}), bf16[2,1,1,512,384]{4,3,2,1,0:T(8,128)(2,1)S(1)}, u32[]{:S(2)}, u32[]{:S(2)}) %all-to-all-start.9) | async-done | bytes 786464 | tf_op jit(solution)/shard_map/all_to_all | solution.py:111
  (250 shorter events, 72.0 us)
Async XLA Ops:
  7.2 82.5 %copy-start = (bf16[2,1,512,384]{3,2,1,0:T(8,128)(2,1)S(1)}, bf16[2,1,512,384]{3,2,1,0:T(8,128)(2,1)}, u32[]{:S(2)}) copy-start(bf16[2,1,512,384]{3,2,1,0:T(8,128)(2,1)} %param.9) | copy-start | bytes 2359300
  7.2 19.7 %copy-start.6 = (bf16[2,1,512,384]{3,2,1,0:T(8,128)(2,1)S(1)}, bf16[2,1,512,384]{3,2,1,0:T(8,128)(2,1)}, u32[]{:S(2)}) copy-start(bf16[2,1,512,384]{3,2,1,0:T(8,128)(2,1)} %param.8) | copy-start | bytes 2359300
  7.2 28.0 %all-gather.4.cloned.1.call-start = ((), (), s32[]{:S(2)}) async-start(), calls=%async_computation.10 | async-start | bytes 1769472 | tf_op jit(solution)/shard_map/all_gather | solution.py:79
  7.9 51.8 %all-gather.6.cloned.1.call-start = ((), (), s32[]{:S(2)}) async-start(), calls=%async_computation.11 | async-start | bytes 1769472 | tf_op jit(solution)/shard_map/all_gather | solution.py:80
  36.8 22.9 %copy-start.2 = (f32[512,768]{1,0:T(8,128)}, f32[512,768]{1,0:T(8,128)S(1)}, u32[]{:S(2)}) copy-start(f32[512,768]{1,0:T(8,128)S(1)} %fusion.144) | copy-start | bytes 4718596
  66.6 17.8 %all-to-all-start = ((bf16[16,2,6144]{2,1,0:T(2,128)(2,1)}), bf16[16,2,6144]{2,1,0:T(2,128)(2,1)S(1)}, u32[]{:S(2)}, u32[]{:S(2)}) async-start(bf16[16,2,6144]{2,1,0:T(2,128)(2,1)} %reshape.801), calls=%async_computation | async-start | bytes 786432 | tf_op jit(solution)/shard_map/all_to_all | solution.py:55
  86.1 15.7 %all-to-all-start.1 = ((bf16[16,32,384]{2,1,0:T(8,128)(2,1)}), bf16[16,32,384]{2,1,0:T(8,128)(2,1)S(1)}, u32[]{:S(2)}, u32[]{:S(2)}) async-start(bf16[16,32,384]{2,1,0:T(8,128)(2,1)} %fusion.44), calls=%async_computation.1 | async-start | bytes 786432 | tf_op jit(solution)/shard_map/all_to_all | solution.py:57
  93.4 12.9 %copy-start.34 = (f32[384]{0:T(512)S(1)}, f32[384]{0:T(512)}, u32[]{:S(2)}) copy-start(f32[384]{0:T(512)} %get-tuple-element.24) | copy-start | bytes 4612
  93.4 12.9 %copy-start.36 = (f32[384]{0:T(512)S(1)}, f32[384]{0:T(512)}, u32[]{:S(2)}) copy-start(f32[384]{0:T(512)} %get-tuple-element.25) | copy-start | bytes 4612
  94.4 13.5 %copy-start.12 = (f32[384]{0:T(512)}, f32[384]{0:T(512)S(1)}, u32[]{:S(2)}) copy-start(f32[384]{0:T(512)S(1)} %get-tuple-element.42) | copy-start | bytes 4612
  94.4 13.5 %copy-start.14 = (f32[384]{0:T(512)}, f32[384]{0:T(512)S(1)}, u32[]{:S(2)}) copy-start(f32[384]{0:T(512)S(1)} %get-tuple-element.43) | copy-start | bytes 4612
  101.8 16.4 %all-to-all-start.5 = ((bf16[16,2,6144]{2,1,0:T(2,128)(2,1)}), bf16[16,2,6144]{2,1,0:T(2,128)(2,1)}, u32[]{:S(2)}, u32[]{:S(2)}) async-start(bf16[16,2,6144]{2,1,0:T(2,128)(2,1)} %reshape.805), calls=%async_computation.5 | async-start | bytes 786432 | tf_op jit(solution)/shard_map/all_to_all | solution.py:55
  118.3 16.4 %all-to-all-start.2 = ((bf16[16,2,6144]{2,1,0:T(2,128)(2,1)}), bf16[16,2,6144]{2,1,0:T(2,128)(2,1)}, u32[]{:S(2)}, u32[]{:S(2)}) async-start(bf16[16,2,6144]{2,1,0:T(2,128)(2,1)} %reshape.803), calls=%async_computation.2 | async-start | bytes 786432 | tf_op jit(solution)/shard_map/all_to_all | solution.py:55
  138.6 17.6 %copy-start.13 = (f32[384]{0:T(512)S(1)}, f32[384]{0:T(512)}, u32[]{:S(2)}) copy-start(f32[384]{0:T(512)} %copy-done.12) | copy-start | bytes 4612
  138.6 17.6 %copy-start.15 = (f32[384]{0:T(512)S(1)}, f32[384]{0:T(512)}, u32[]{:S(2)}) copy-start(f32[384]{0:T(512)} %copy-done.14) | copy-start | bytes 4612
  138.7 17.6 %copy-start.75 = (f32[384]{0:T(512)S(1)}, f32[384]{0:T(512)}, u32[]{:S(2)}) copy-start(f32[384]{0:T(512)} %get-tuple-element.46) | copy-start | bytes 4612
  140.5 15.7 %all-to-all-start.6 = ((bf16[16,32,384]{2,1,0:T(8,128)(2,1)}), bf16[16,32,384]{2,1,0:T(8,128)(2,1)S(1)}, u32[]{:S(2)}, u32[]{:S(2)}) async-start(bf16[16,32,384]{2,1,0:T(8,128)(2,1)} %get-tuple-element.70), calls=%async_computation.6 | async-start | bytes 786432 | tf_op jit(solution)/shard_map/all_to_all | solution.py:57
  184.2 15.7 %all-to-all-start.3 = ((bf16[16,32,384]{2,1,0:T(8,128)(2,1)}), bf16[16,32,384]{2,1,0:T(8,128)(2,1)S(1)}, u32[]{:S(2)}, u32[]{:S(2)}) async-start(bf16[16,32,384]{2,1,0:T(8,128)(2,1)} %get-tuple-element.71), calls=%async_computation.3 | async-start | bytes 786432 | tf_op jit(solution)/shard_map/all_to_all | solution.py:57
  199.9 15.7 %all-to-all-start.8 = ((bf16[16,32,384]{2,1,0:T(8,128)(2,1)}), bf16[16,32,384]{2,1,0:T(8,128)(2,1)S(1)}, u32[]{:S(2)}, u32[]{:S(2)}) async-start(bf16[16,32,384]{2,1,0:T(8,128)(2,1)} %fusion.98), calls=%async_computation.8 | async-start | bytes 786432 | tf_op jit(solution)/shard_map/all_to_all | solution.py:57
  205.0 14.2 %copy-start.9 = (f32[384]{0:T(512)S(1)}, f32[384]{0:T(512)}, u32[]{:S(2)}) copy-start(f32[384]{0:T(512)} %copy-done.8) | copy-start | bytes 4612
  205.0 14.2 %copy-start.11 = (f32[384]{0:T(512)S(1)}, f32[384]{0:T(512)}, u32[]{:S(2)}) copy-start(f32[384]{0:T(512)} %copy-done.10) | copy-start | bytes 4612
  205.0 14.2 %copy-start.73 = (f32[384]{0:T(512)S(1)}, f32[384]{0:T(512)}, u32[]{:S(2)}) copy-start(f32[384]{0:T(512)} %copy-done.72) | copy-start | bytes 4612
  215.6 14.9 %all-to-all-start.4 = ((bf16[2,1,1,512,384]{4,3,2,1,0:T(8,128)(2,1)}), bf16[2,1,1,512,384]{4,3,2,1,0:T(8,128)(2,1)S(1)}, u32[]{:S(2)}, u32[]{:S(2)}) async-start(bf16[2,1,1,512,384]{4,3,2,1,0:T(8,128)(2,1)} %pad_maximum_fusion), calls=%async_computation.4 | async-start | bytes 1572864 | tf_op jit(solution)/shard_map/all_to_all | solution.py:110
  230.5 14.0 %all-to-all-start.9 = ((bf16[2,1,1,512,384]{4,3,2,1,0:T(8,128)(2,1)}), bf16[2,1,1,512,384]{4,3,2,1,0:T(8,128)(2,1)S(1)}, u32[]{:S(2)}, u32[]{:S(2)}) async-start(bf16[2,1,1,512,384]{4,3,2,1,0:T(8,128)(2,1)} %pad_maximum_fusion.1), calls=%async_computation.9 | async-start | bytes 1572864 | tf_op jit(solution)/shard_map/all_to_all | solution.py:111
  (74 other events, 295.3 us)
Sparse Core Ops, SparseCore 0:
  9.6 25.5 all-gather.3
  36.7 22.9 all-gather.5
where the time goes:
time: 255 us; the launch traced here: 253 us
  waiting for transfers between devices  98 us (38%)
  starting transfers between devices  35.8 us (14%)
  blocking collectives  34.2 us (13%)
  other arithmetic  30.2 us (12%)
  local copies, waits for them, and re-layouts  27.7 us (11%)
  between operations  15.4 us (6%)
  matrix products  11.8 us (5%)
    all_to_all x4, waiting for transfers between devices, temporal(): lax.all_to_all(banded, 'seq', split_axis=0, concat_axis=1, tiled=True)  35.1 us
    all_gather x1, waiting for transfers between devices, on_device(): lax.all_gather(w_out, 'section', axis=0, tiled=True)  22.8 us
    unnamed x191, local copies, waits for them, and re-layouts  21.1 us
    all_to_all x3, waiting for transfers between devices, temporal(): lax.all_to_all(values, 'seq', split_axis=1, concat_axis=0, tiled=True)  17.3 us
    all_to_all x1, blocking collectives, temporal(): lax.all_to_all(values, 'seq', split_axis=1, concat_axis=0, tiled=True)  15.6 us
    unnamed x5, other arithmetic  14.5 us
    all_to_all x4, starting transfers between devices, temporal(): lax.all_to_all(banded, 'seq', split_axis=0, concat_axis=1, tiled=True)  14.4 us
    all_to_all x3, starting transfers between devices, temporal(): lax.all_to_all(values, 'seq', split_axis=1, concat_axis=0, tiled=True)  14.2 us
  transfers between devices with their start and end apart: 11, of which 11 were waited for; matrix products, arithmetic and copies ran while one was open for 16% of the time, Pallas kernels for 0%

commit v1 on v0

v1 whole, which is shorter than its diff:
```python
import jax
import jax.numpy as jnp
from jax import lax
from jax.sharding import PartitionSpec as P

H = 32
W = 16
BAND = 9


EPSILON = 1e-06


def spatial_block(values, stencil_taps, modulate, norm_gain, w_in, w_out):
    clip_count, frame_count, pixel_count, channels = values.shape
    volume = values.astype(jnp.float32).reshape(clip_count, frame_count, H, W, channels)
    padded = jnp.pad(volume, ((0, 0), (0, 0), (1, 1), (1, 1), (0, 0)))
    stencil_sum = jnp.zeros_like(volume)
    for down_step in range(3):
        for across in range(3):
            stencil_sum = (
                stencil_sum
                + stencil_taps[3 * down_step + across]
                * padded[:, :, down_step : down_step + H, across : across + W]
            )
    stencil_sum = stencil_sum.reshape(clip_count, frame_count, pixel_count, channels)
    scale = (1.0 + modulate[:, 0])[:, None, None, :]
    shift = modulate[:, 1][:, None, None, :]
    modulated = stencil_sum * scale + shift
    scaled = (
        modulated
        * lax.rsqrt(jnp.mean(modulated * modulated, axis=-1, keepdims=True) + EPSILON)
        * norm_gain
    )
    normed = scaled.astype(jnp.bfloat16).reshape(-1, channels)
    hidden = jax.nn.silu(jnp.dot(normed, w_in, preferred_element_type=jnp.float32)).astype(
        jnp.bfloat16
    )
    update = jnp.dot(hidden, w_out, preferred_element_type=jnp.float32)
    return (values.astype(jnp.float32) + update.reshape(values.shape)).astype(jnp.bfloat16)


def band_frames(values, tap_table):
    frame_count = values.shape[1]
    reach = BAND // 2
    volume = values.astype(jnp.float32)
    padded = jnp.pad(volume, ((0, 0), (reach, reach), (0, 0), (0, 0)))
    total = volume
    for offset in range(BAND):
        total = total + tap_table[offset] * padded[:, offset : offset + frame_count]
    return total.astype(jnp.bfloat16)


def temporal(values, tap_table):
    clip_count, frame_count, pixel_count, channels = values.shape
    groups = lax.axis_size("seq")
    grouped = values.reshape(clip_count, frame_count, groups, pixel_count // groups, channels)
    pixel_view = lax.all_to_all(grouped, "seq", split_axis=2, concat_axis=1, tiled=True)
    pixel_view = pixel_view.reshape(clip_count, groups * frame_count, pixel_count // groups, channels)
    banded = band_frames(pixel_view, tap_table)
    banded = banded.reshape(clip_count, groups * frame_count, 1, pixel_count // groups, channels)
    back = lax.all_to_all(banded, "seq", split_axis=1, concat_axis=2, tiled=True)
    return back.reshape(values.shape)


def on_device(clips, cotangent, spatial_taps, modulation, norm_gain, w_in, w_out, band_taps):
    first = lax.axis_index("section") == 0
    taps, mod, gain = spatial_taps[0], modulation[0], norm_gain[0]
    weight_in, weight_out, band = w_in[0], w_out[0], band_taps[0]

    def spatial(values):
        return spatial_block(values, taps, mod, gain, weight_in, weight_out)

    first_mixed, first_pull = jax.vjp(spatial, clips)
    lead_in = jnp.where(first, first_mixed, cotangent)
    lead_taps = jnp.where(first, band, band[::-1])
    lead_out = temporal(lead_in, lead_taps)

    first_acts = lax.ppermute(lead_out, "section", perm=[(0, 1)])
    second_mixed, second_pull = jax.vjp(spatial, first_acts)
    second_grad = second_pull(lead_out)[0]

    arrived_grad = lax.ppermute(second_grad, "section", perm=[(1, 0)])
    tail_in = jnp.where(first, arrived_grad, second_mixed)
    tail_taps = jnp.where(first, band[::-1], band)
    tail_out = temporal(tail_in, tail_taps)
    first_grad = first_pull(tail_out)[0]

    activations = jnp.where(first, lead_out, tail_out)
    input_grads = jnp.where(first, first_grad, second_grad)
    return (activations[None], input_grads[None])


def solution(mesh):
    placed = (
        P(None, "seq", None, None),
        P(None, "seq", None, None),
        P("section", None, None),
        P("section", None, None, None),
        P("section", None),
        P("section", None, None),
        P("section", None, None),
        P("section", None, None),
    )
    return jax.shard_map(
        on_device,
        mesh=mesh,
        in_specs=placed,
        out_specs=(P("section", None, "seq", None, None), P("section", None, "seq", None, None)),
        check_vma=False,
    )
```

time: 255 us -> 193 us (0.76)
  waiting for transfers between devices: 98 us -> 74.7 us
  local copies, waits for them, and re-layouts: 27.7 us -> 5.79 us
  starting transfers between devices: 35.8 us -> 16.7 us
  blocking collectives: 34.2 us -> 51 us
  between operations: 15.4 us -> 1.01 us
  matrix products: 11.8 us -> 18.2 us
  other arithmetic: 30.2 us -> 24.7 us
    ppermute x0 -> x2, waiting for transfers between devices: none -> 37.6 us  [the longest x1 20.1 us: on_device(): arrived_grad = lax.ppermute(second_grad, 'section', perm=[(1, 0)])]
    all_to_all x1 -> x2, blocking collectives: 15.6 us -> 51 us  [temporal(): lax.all_to_all(banded, 'seq', split_axis=1, concat_axis=2, tiled=True)]
    all_gather x2 -> x0, waiting for transfers between devices: 30.1 us -> none  [the longest x1 22.8 us: on_device(): lax.all_gather(w_out, 'section', axis=0, tiled=True)]
    all_to_all x9 -> x2, waiting for transfers between devices: 66.6 us -> 37.2 us  [temporal(): lax.all_to_all(grouped, 'seq', split_axis=2, concat_axis=1, tiled=True)]
    all_to_all x9 -> x2, starting transfers between devices: 35.7 us -> 11.7 us  [temporal(): lax.all_to_all(grouped, 'seq', split_axis=2, concat_axis=1, tiled=True)]
    unnamed x191 -> x34, local copies, waits for them, and re-layouts: 21.1 us -> 1.47 us
    all_gather x4 -> x0, blocking collectives: 18.5 us -> none  [the longest x1 5.21 us: on_device(): lax.all_gather(norm_gain.astype(jnp.bfloat16), 'section', axis=0, tiled=T...]
    unnamed x5 -> x1, other arithmetic: 14.5 us -> 0.02 us
  transfers between devices with their start and end apart: 11 -> 4, of which waited for: 11 -> 4; matrix products, arithmetic and copies ran while one was open for 16% -> 0% of each run, Pallas kernels for 0% -> 0%
where the time goes in v1:
time: 193 us; the launch traced here: 192 us
  waiting for transfers between devices  74.7 us (39%)
  blocking collectives  51 us (26%)
  other arithmetic  24.7 us (13%)
  matrix products  18.2 us (9%)
  starting transfers between devices  16.7 us (9%)
  local copies, waits for them, and re-layouts  5.79 us (3%)
    all_to_all x2, blocking collectives, temporal(): lax.all_to_all(banded, 'seq', split_axis=1, concat_axis=2, tiled=True)  51 us
    all_to_all x2, waiting for transfers between devices, temporal(): lax.all_to_all(grouped, 'seq', split_axis=2, concat_axis=1, tiled=True)  37.2 us
    ppermute x1, waiting for transfers between devices, on_device(): arrived_grad = lax.ppermute(second_grad, 'section', perm=[(1, 0)])  20.1 us
    ppermute x1, waiting for transfers between devices, on_device(): first_acts = lax.ppermute(lead_out, 'section', perm=[(0, 1)])  17.5 us
    dot_general x4, matrix products, spatial_block(): jnp.dot(normed, w_in, preferred_element_type=jnp.float32)  16.1 us
    all_to_all x2, starting transfers between devices, temporal(): lax.all_to_all(grouped, 'seq', split_axis=2, concat_axis=1, tiled=True)  11.7 us
    reduce_sum x2, other arithmetic, spatial_block(): jnp.mean(modulated * modulated, axis=-1, keepdims=True) + EPSILON  4.73 us
  transfers between devices with their start and end apart: 4, of which 4 were waited for; matrix products, arithmetic and copies ran while one was open for 0% of the time, Pallas kernels for 0%

profile of v1, /device:TPU:0, one launch (start us, length us, event | category | flops | bytes accessed | tf_op | source)
XLA Modules:
  0.0 192.1 jit_solution(2414029886634623730)
XLA Ops:
  2.3 1.2 bitcast_convert_fusion.2
  3.6 1.9 %multiply_reduce_fusion.1 = (f32[2,32,16]{2,1,0:T(8,128)S(1)}, f32[2,1,32,16,384]{4,3,2,0,1:T(8,128)S(1)}) fusion(f32[2,384]{1,0:T(2,128)S(1)} %get-tuple-element.65, f32[2,384]{1,0:T(2,128)S(1)} %get-tuple-element.66, f32[384]{0:T(512)S(1)} %get-tuple-element.29, f32[384]{0:T(512)S(1)} %get-tuple-element.30, f32[384]{0:T(512)S(1)} %get-tuple-element.23, ...), kind=kLoop, calls=%fused_computation.163 | loop fusion | flops 8256512 | bytes 3169792 | tf_op jit(solution)/shard_map/jvp()/reduce_sum | solution.py:32
  6.0 2.8 %multiply_convert_fusion.1 = (bf16[1024,768]{1,0:T(8,128)(2,1)S(1)}, f32[1024,768]{1,0:T(8,128)}) fusion(bf16[1024,384]{1,0:T(8,128)(2,1)S(1)} %bitcast.145, bf16[1,384,768]{2,1,0:T(8,128)(2,1)S(1)} %copy-done), kind=kOutput, calls=%fused_computation.46 | convolution fusion | flops 607911936 | bytes 6094848 | tf_op jit(solution)/shard_map/jvp()/dot_general | solution.py:36
  10.8 7.4 %all-to-all-start = ((bf16[2,1,16,32,384]{4,3,0,1,2:T(8,128)(2,1)}), bf16[2,1,16,32,384]{4,3,0,1,2:T(8,128)(2,1)S(1)}, u32[]{:S(2)}, u32[]{:S(2)}) async-start(bf16[2,1,16,32,384]{4,3,0,1,2:T(8,128)(2,1)} %copy.23), calls=%async_computation | async-start | bytes 1572864 | tf_op jit(solution)/shard_map/all_to_all | solution.py:58
  18.4 18.5 %all-to-all-done = bf16[2,1,16,32,384]{4,3,0,1,2:T(8,128)(2,1)S(1)} async-done(((bf16[2,1,16,32,384]{4,3,0,1,2:T(8,128)(2,1)}), bf16[2,1,16,32,384]{4,3,0,1,2:T(8,128)(2,1)S(1)}, u32[]{:S(2)}, u32[]{:S(2)}) %all-to-all-start) | async-done | bytes 786464 | tf_op jit(solution)/shard_map/all_to_all | solution.py:58
  38.1 25.5 %all_to_all.16 = bf16[2,16,1,32,384]{4,3,0,2,1:T(8,128)(2,1)S(1)} all-to-all(bf16[2,16,1,32,384]{4,3,0,2,1:T(8,128)(2,1)S(1)} %fusion.110), channel_id=1, replica_groups=mesh['section'=2,'seq'=16] {'seq'}, dimensions={1} | all-to-all | bytes 1572864 | tf_op jit(solution)/shard_map/all_to_all | solution.py:62
  63.7 3.6 %collective-permute-start = (bf16[2,1,512,384]{3,2,0,1:T(8,128)(2,1)S(1)}, bf16[2,1,512,384]{3,2,0,1:T(8,128)(2,1)S(1)}, u32[]{:S(2)}, u32[]{:S(2)}) collective-permute-start(bf16[2,1,512,384]{3,2,0,1:T(8,128)(2,1)S(1)} %bitcast.135), channel_id=1, source_target_pairs={{0,16},{1,17},{2,18},{3,19},{4,20},{5,21},{6,22},{7,23},{8,24},{9,... | collective-permute-start | bytes 2359304 | tf_op jit(solution)/shard_map/ppermute | solution.py:79
  67.3 17.5 %collective-permute-done = bf16[2,1,512,384]{3,2,0,1:T(8,128)(2,1)S(1)} collective-permute-done((bf16[2,1,512,384]{3,2,0,1:T(8,128)(2,1)S(1)}, bf16[2,1,512,384]{3,2,0,1:T(8,128)(2,1)S(1)}, u32[]{:S(2)}, u32[]{:S(2)}) %collective-permute-start) | collective-permute-done | bytes 786464 | tf_op jit(solution)/shard_map/ppermute | solution.py:79
  85.8 2.8 %multiply_reduce_fusion = (f32[2,32,16]{2,1,0:T(8,128)S(1)}, f32[2,1,32,16,384]{4,3,2,0,1:T(8,128)}) fusion(f32[2,384]{1,0:T(2,128)S(1)} %get-tuple-element.65, f32[2,384]{1,0:T(2,128)S(1)} %get-tuple-element.66, f32[384]{0:T(512)S(1)} %get-tuple-element.29, f32[384]{0:T(512)S(1)} %get-tuple-element.30, f32[384]{0:T(512)S(1)} %get-tuple-element.23, ...), kind=kLoop, calls=%fused_computation.159 | loop fusion | flops 8256512 | bytes 3169792 | tf_op jit(solution)/shard_map/jvp()/reduce_sum | solution.py:32
  88.7 1.7 fusion.92
  90.4 3.4 %multiply_convert_fusion = (bf16[1024,768]{1,0:T(8,128)(2,1)}, f32[1024,768]{1,0:T(8,128)}) fusion(bf16[1024,384]{1,0:T(8,128)(2,1)S(1)} %bitcast.146, bf16[1,384,768]{2,1,0:T(8,128)(2,1)S(1)} %copy-done), kind=kOutput, calls=%fused_computation.44 | convolution fusion | flops 607911936 | bytes 6094848 | tf_op jit(solution)/shard_map/jvp()/dot_general | solution.py:36
  93.9 4.8 %fusion.103 = bf16[1024,384]{1,0:T(8,128)(2,1)} fusion(f32[1024,768]{1,0:T(8,128)} %get-tuple-element.64, bf16[1024,384]{1,0:T(8,128)(2,1)S(1)} %bitcast.136, bf16[1,768,384]{2,1,0:T(8,128)(2,1)} %param.14, bf16[1,384,768]{2,1,0:T(8,128)(2,1)S(1)} %copy-done), kind=kOutput, calls=%fused_computation.166 | convolution fusion | flops 1217003520 | bytes 5898240 | tf_op jit(solution)/shard_map/transpose(jvp())/dot_general | solution.py:36
  98.7 2.2 %fusion.87 = f32[2,32,16]{2,1,0:T(8,128)S(1)} fusion(bf16[2,1,32,16,384]{4,3,2,0,1:T(8,128)(2,1)} %bitcast.140, f32[2,1,32,16,384]{4,3,2,0,1:T(8,128)} %get-tuple-element.36, f32[384]{0:T(512)S(1)} %reduce.17, f32[2,384]{1,0:T(2,128)S(1)} %get-tuple-element.65, f32[2,384]{1,0:T(2,128)S(1)} %get-tuple-element.66), kind=kLoop, calls=%fused_computation.144 | loop fusion | flops 2358272 | bytes 2371072 | tf_op jit(solution)/shard_map/transpose(jvp())/reduce_sum | solution.py:31
  101.6 1.3 broadcast_multiply_fusion.3
  104.6 1.4 collective-permute-start.1
  106.0 20.1 %collective-permute-done.1 = bf16[2,1,512,384]{3,2,0,1:T(8,128)(2,1)S(1)} collective-permute-done((bf16[2,1,512,384]{3,2,0,1:T(8,128)(2,1)S(1)}, bf16[2,1,512,384]{3,2,0,1:T(8,128)(2,1)S(1)}, u32[]{:S(2)}, u32[]{:S(2)}) %collective-permute-start.1) | collective-permute-done | bytes 786464 | tf_op jit(solution)/shard_map/ppermute | solution.py:83
  128.2 4.3 %all-to-all-start.2 = ((bf16[2,1,16,32,384]{4,3,0,1,2:T(8,128)(2,1)}), bf16[2,1,16,32,384]{4,3,0,1,2:T(8,128)(2,1)}, u32[]{:S(2)}, u32[]{:S(2)}) async-start(bf16[2,1,16,32,384]{4,3,0,1,2:T(8,128)(2,1)} %copy.28), calls=%async_computation.2 | async-start | bytes 1572864 | tf_op jit(solution)/shard_map/all_to_all | solution.py:58
  132.5 18.7 %all-to-all-done.2 = bf16[2,1,16,32,384]{4,3,0,1,2:T(8,128)(2,1)} async-done(((bf16[2,1,16,32,384]{4,3,0,1,2:T(8,128)(2,1)}), bf16[2,1,16,32,384]{4,3,0,1,2:T(8,128)(2,1)}, u32[]{:S(2)}, u32[]{:S(2)}) %all-to-all-start.2) | async-done | bytes 786464 | tf_op jit(solution)/shard_map/all_to_all | solution.py:58
  151.2 1.3 bitcast_convert_fusion
  153.5 25.5 %all_to_all.17 = bf16[2,16,1,32,384]{4,3,0,2,1:T(8,128)(2,1)S(1)} all-to-all(bf16[2,16,1,32,384]{4,3,0,2,1:T(8,128)(2,1)S(1)} %fusion.109), channel_id=1, replica_groups=mesh['section'=2,'seq'=16] {'seq'}, dimensions={1} | all-to-all | bytes 1572864 | tf_op jit(solution)/shard_map/all_to_all | solution.py:62
  179.9 5.1 %fusion.100 = bf16[1024,384]{1,0:T(8,128)(2,1)} fusion(f32[1024,768]{1,0:T(8,128)} %get-tuple-element.62, bf16[1024,384]{1,0:T(8,128)(2,1)} %bitcast.138, bf16[1,768,384]{2,1,0:T(8,128)(2,1)} %param.14, bf16[1,384,768]{2,1,0:T(8,128)(2,1)S(1)} %copy-done), kind=kOutput, calls=%fused_computation.165 | convolution fusion | flops 1217003520 | bytes 5898240 | tf_op jit(solution)/shard_map/transpose(jvp())/dot_general | solution.py:36
  185.0 1.6 fusion.84
  187.2 1.2 broadcast_multiply_fusion.2
  190.4 1.6 fusion.108
  (65 shorter events, 15.5 us)
Async XLA Ops:
  0.6 5.3 %copy-start = (bf16[1,384,768]{2,1,0:T(8,128)(2,1)S(1)}, bf16[1,384,768]{2,1,0:T(8,128)(2,1)}, u32[]{:S(2)}) copy-start(bf16[1,384,768]{2,1,0:T(8,128)(2,1)} %param.13) | copy-start | bytes 1769476
  3.5 2.1 %copy-start.11 = (f32[1,384]{1,0:T(1,128)S(1)}, f32[1,384]{1,0:T(1,128)}, u32[]{:S(2)}) copy-start(f32[1,384]{1,0:T(1,128)} %param.12) | copy-start | bytes 4612
  5.9 2.9 %copy-start.7 = (bf16[2,1,512,384]{3,2,1,0:T(8,128)(2,1)S(1)}, bf16[2,1,512,384]{3,2,1,0:T(8,128)(2,1)}, u32[]{:S(2)}) copy-start(bf16[2,1,512,384]{3,2,1,0:T(8,128)(2,1)} %param.8) | copy-start | bytes 2359300
  5.9 2.9 %copy-start.12 = (bf16[2,1,512,384]{3,2,1,0:T(8,128)(2,1)S(1)}, bf16[2,1,512,384]{3,2,1,0:T(8,128)(2,1)}, u32[]{:S(2)}) copy-start(bf16[2,1,512,384]{3,2,1,0:T(8,128)(2,1)} %param.9) | copy-start | bytes 2359300
  5.9 2.8 %copy-start.13 = (bf16[1,768,384]{2,1,0:T(8,128)(2,1)S(1)}, bf16[1,768,384]{2,1,0:T(8,128)(2,1)}, u32[]{:S(2)}) copy-start(bf16[1,768,384]{2,1,0:T(8,128)(2,1)} %param.14) | copy-start | bytes 1769476
  9.8 8.4 %copy-start.10 = (f32[1,9,384]{2,0,1:T(1,128)S(1)}, f32[1,9,384]{2,0,1:T(1,128)}, u32[]{:S(2)}) copy-start(f32[1,9,384]{2,0,1:T(1,128)} %param.15) | copy-start | bytes 41476
  10.8 26.1 %all-to-all-start = ((bf16[2,1,16,32,384]{4,3,0,1,2:T(8,128)(2,1)}), bf16[2,1,16,32,384]{4,3,0,1,2:T(8,128)(2,1)S(1)}, u32[]{:S(2)}, u32[]{:S(2)}) async-start(bf16[2,1,16,32,384]{4,3,0,1,2:T(8,128)(2,1)} %copy.23), calls=%async_computation | async-start | bytes 1572864 | tf_op jit(solution)/shard_map/all_to_all | solution.py:58
  63.7 21.1 %collective-permute-start = (bf16[2,1,512,384]{3,2,0,1:T(8,128)(2,1)S(1)}, bf16[2,1,512,384]{3,2,0,1:T(8,128)(2,1)S(1)}, u32[]{:S(2)}, u32[]{:S(2)}) collective-permute-start(bf16[2,1,512,384]{3,2,0,1:T(8,128)(2,1)S(1)} %bitcast.135), channel_id=1, source_target_pairs={{0,16},{1,17},{2,18},{3,19},{4,20},{5,21},{6,22},{7,23},{8,24},{9,... | collective-permute-start | bytes 2359304 | tf_op jit(solution)/shard_map/ppermute | solution.py:79
  84.8 0.9 copy-start.8
  98.7 2.2 %copy-start.1 = (f32[2,1,32,16,384]{4,3,2,0,1:T(8,128)S(1)}, f32[2,1,32,16,384]{4,3,2,0,1:T(8,128)}, u32[]{:S(2)}) copy-start(f32[2,1,32,16,384]{4,3,2,0,1:T(8,128)} %get-tuple-element.36) | copy-start | bytes 4718596
  98.7 2.3 %copy-start.6 = (bf16[1024,384]{1,0:T(8,128)(2,1)S(1)}, bf16[1024,384]{1,0:T(8,128)(2,1)}, u32[]{:S(2)}) copy-start(bf16[1024,384]{1,0:T(8,128)(2,1)} %fusion.103) | copy-start | bytes 2359300
  103.4 22.7 %copy-start.15 = (bf16[1024,768]{1,0:T(8,128)(2,1)S(1)}, bf16[1024,768]{1,0:T(8,128)(2,1)}, u32[]{:S(2)}) copy-start(bf16[1024,768]{1,0:T(8,128)(2,1)} %get-tuple-element.63) | copy-start | bytes 4718596
  104.3 22.8 %copy-start.2 = (bf16[2,1,32,16,384]{4,3,2,0,1:T(8,128)(2,1)}, bf16[2,1,32,16,384]{4,3,2,0,1:T(8,128)(2,1)S(1)}, u32[]{:S(2)}) copy-start(bf16[2,1,32,16,384]{4,3,2,0,1:T(8,128)(2,1)S(1)} %fusion.81) | copy-start | bytes 2359300
  104.3 21.8 %copy-start.9 = (bf16[2,1,512,384]{3,2,0,1:T(8,128)(2,1)S(1)}, bf16[2,1,512,384]{3,2,0,1:T(8,128)(2,1)}, u32[]{:S(2)}) copy-start(bf16[2,1,512,384]{3,2,0,1:T(8,128)(2,1)} %copy-done.8) | copy-start | bytes 2359300
  104.4 21.8 %copy-start.14 = (bf16[1,768,384]{2,1,0:T(8,128)(2,1)S(1)}, bf16[1,768,384]{2,1,0:T(8,128)(2,1)}, u32[]{:S(2)}) copy-start(bf16[1,768,384]{2,1,0:T(8,128)(2,1)} %param.14) | copy-start | bytes 1769476
  104.6 21.5 %collective-permute-start.1 = (bf16[2,1,512,384]{3,2,0,1:T(8,128)(2,1)S(1)}, bf16[2,1,512,384]{3,2,0,1:T(8,128)(2,1)S(1)}, u32[]{:S(2)}, u32[]{:S(2)}) collective-permute-start(bf16[2,1,512,384]{3,2,0,1:T(8,128)(2,1)S(1)} %bitcast_add_fusion.4), channel_id=1, source_target_pairs={{16,0},{17,1},{18,2},{19,3},{20,4},{21,5},{22,6},{23,7},{24,8},{25... | collective-permute-start | bytes 2359304 | tf_op jit(solution)/shard_map/ppermute | solution.py:83
  128.2 23.0 %all-to-all-start.2 = ((bf16[2,1,16,32,384]{4,3,0,1,2:T(8,128)(2,1)}), bf16[2,1,16,32,384]{4,3,0,1,2:T(8,128)(2,1)}, u32[]{:S(2)}, u32[]{:S(2)}) async-start(bf16[2,1,16,32,384]{4,3,0,1,2:T(8,128)(2,1)} %copy.28), calls=%async_computation.2 | async-start | bytes 1572864 | tf_op jit(solution)/shard_map/all_to_all | solution.py:58
  185.0 1.6 copy-start.5
  189.1 1.1 copy-start.3
  189.1 1.4 copy-start.4

commit v2 on v1

--- a/solution.py
+++ b/solution.py
@@ -67,28 +67,30 @@
     first = lax.axis_index("section") == 0
     taps, mod, gain = spatial_taps[0], modulation[0], norm_gain[0]
     weight_in, weight_out, band = w_in[0], w_out[0], band_taps[0]
+    lead_taps = jnp.where(first, band, band[::-1])
+    tail_taps = jnp.where(first, band[::-1], band)
 
-    def spatial(values):
-        return spatial_block(values, taps, mod, gain, weight_in, weight_out)
+    def spatial(values, clip):
+        return spatial_block(values, taps, mod[clip : clip + 1], gain, weight_in, weight_out)
 
-    first_mixed, first_pull = jax.vjp(spatial, clips)
-    lead_in = jnp.where(first, first_mixed, cotangent)
-    lead_taps = jnp.where(first, band, band[::-1])
-    lead_out = temporal(lead_in, lead_taps)
+    acts, grads = [], []
+    for clip in range(clips.shape[0]):
+        first_mixed, first_pull = jax.vjp(lambda v: spatial(v, clip), clips[clip : clip + 1])
+        lead_in = jnp.where(first, first_mixed, cotangent[clip : clip + 1])
+        lead_out = temporal(lead_in, lead_taps)
 
-    first_acts = lax.ppermute(lead_out, "section", perm=[(0, 1)])
-    second_mixed, second_pull = jax.vjp(spatial, first_acts)
-    second_grad = second_pull(lead_out)[0]
+        first_acts = lax.ppermute(lead_out, "section", perm=[(0, 1)])
+        second_mixed, second_pull = jax.vjp(lambda v: spatial(v, clip), first_acts)
+        second_grad = second_pull(lead_out)[0]
 
-    arrived_grad = lax.ppermute(second_grad, "section", perm=[(1, 0)])
-    tail_in = jnp.where(first, arrived_grad, second_mixed)
-    tail_taps = jnp.where(first, band[::-1], band)
-    tail_out = temporal(tail_in, tail_taps)
-    first_grad = first_pull(tail_out)[0]
+        arrived_grad = lax.ppermute(second_grad, "section", perm=[(1, 0)])
+        tail_in = jnp.where(first, arrived_grad, second_mixed)
+        tail_out = temporal(tail_in, tail_taps)
+        first_grad = first_pull(tail_out)[0]
 
-    activations = jnp.where(first, lead_out, tail_out)
-    input_grads = jnp.where(first, first_grad, second_grad)
-    return (activations[None], input_grads[None])
+        acts.append(jnp.where(first, lead_out, tail_out))
+        grads.append(jnp.where(first, first_grad, second_grad))
+    return (jnp.concatenate(acts)[None], jnp.concatenate(grads)[None])
 
 
 def solution(mesh):

time: 193 us -> 216 us (1.12)
  starting transfers between devices: 16.7 us -> 39.2 us
  blocking collectives: 51 us -> 31.2 us
  other arithmetic: 24.7 us -> 33.8 us
  matrix products: 18.2 us -> 26.6 us
    all_to_all x2 -> x1, blocking collectives: 51 us -> 15.5 us  [temporal(): lax.all_to_all(banded, 'seq', split_axis=1, concat_axis=2, tiled=True)]
    all_to_all x0 -> x3, waiting for transfers between devices: none -> 22.5 us  [temporal(): lax.all_to_all(banded, 'seq', split_axis=1, concat_axis=2, tiled=True)]
    all_to_all x0 -> x1, blocking collectives: none -> 15.6 us  [temporal(): lax.all_to_all(grouped, 'seq', split_axis=2, concat_axis=1, tiled=True)]
    all_to_all x0 -> x3, starting transfers between devices: none -> 12.4 us  [temporal(): lax.all_to_all(banded, 'seq', split_axis=1, concat_axis=2, tiled=True)]
    all_to_all x2 -> x3, waiting for transfers between devices: 37.2 us -> 26.6 us  [temporal(): lax.all_to_all(grouped, 'seq', split_axis=2, concat_axis=1, tiled=True)]
    ppermute x1 -> x2, waiting for transfers between devices: 17.5 us -> 8.61 us  [on_device(): first_acts = lax.ppermute(lead_out, 'section', perm=[(0, 1)])]
    mul x0 -> x4, other arithmetic: none -> 6.42 us  [spatial_block(): modulated = stencil_sum * scale + shift]
    ppermute x1 -> x2, starting transfers between devices: 3.62 us -> 9.47 us  [on_device(): first_acts = lax.ppermute(lead_out, 'section', perm=[(0, 1)])]
  transfers between devices with their start and end apart: 4 -> 10, of which waited for: 4 -> 9; matrix products, arithmetic and copies ran while one was open for 0% -> 10% of each run, Pallas kernels for 0% -> 0%
where the time goes in v2:
time: 216 us; the launch traced here: 214 us
  waiting for transfers between devices  74.8 us (35%)
  starting transfers between devices  39.2 us (18%)
  other arithmetic  33.8 us (16%)
  blocking collectives  31.2 us (14%)
  matrix products  26.6 us (12%)
  local copies, waits for them, and re-layouts  7.36 us (3%)
    all_to_all x3, waiting for transfers between devices, temporal(): lax.all_to_all(grouped, 'seq', split_axis=2, concat_axis=1, tiled=True)  26.6 us
    all_to_all x3, waiting for transfers between devices, temporal(): lax.all_to_all(banded, 'seq', split_axis=1, concat_axis=2, tiled=True)  22.5 us
    dot_general x8, matrix products, spatial_block(): jnp.dot(normed, w_in, preferred_element_type=jnp.float32)  19.1 us
    ppermute x2, waiting for transfers between devices, on_device(): arrived_grad = lax.ppermute(second_grad, 'section', perm=[(1, 0)])  17.1 us
    all_to_all x1, blocking collectives, temporal(): lax.all_to_all(grouped, 'seq', split_axis=2, concat_axis=1, tiled=True)  15.6 us
    all_to_all x1, blocking collectives, temporal(): lax.all_to_all(banded, 'seq', split_axis=1, concat_axis=2, tiled=True)  15.5 us
    all_to_all x3, starting transfers between devices, temporal(): lax.all_to_all(grouped, 'seq', split_axis=2, concat_axis=1, tiled=True)  14.6 us
    all_to_all x3, starting transfers between devices, temporal(): lax.all_to_all(banded, 'seq', split_axis=1, concat_axis=2, tiled=True)  12.4 us
  transfers between devices with their start and end apart: 10, of which 9 were waited for; matrix products, arithmetic and copies ran while one was open for 10% of the time, Pallas kernels for 0%

profile of v2, /device:TPU:0, one launch (start us, length us, event | category | flops | bytes accessed | tf_op | source)
XLA Modules:
  0.0 214.1 jit_solution(4047377876818105085)
XLA Ops:
  7.4 7.4 %all-to-all-start = ((bf16[1,1,16,32,384]{4,3,1,0,2:T(8,128)(2,1)}), bf16[1,1,16,32,384]{4,3,1,0,2:T(8,128)(2,1)S(1)}, u32[]{:S(2)}, u32[]{:S(2)}) async-start(bf16[1,1,16,32,384]{4,3,1,0,2:T(8,128)(2,1)} %bitcast.7), calls=%async_computation | async-start | bytes 786432 | tf_op jit(solution)/shard_map/all_to_all | solution.py:58
  15.0 12.0 %all-to-all-done = bf16[1,1,16,32,384]{4,3,1,0,2:T(8,128)(2,1)S(1)} async-done(((bf16[1,1,16,32,384]{4,3,1,0,2:T(8,128)(2,1)}), bf16[1,1,16,32,384]{4,3,1,0,2:T(8,128)(2,1)S(1)}, u32[]{:S(2)}, u32[]{:S(2)}) %all-to-all-start) | async-done | bytes 393248 | tf_op jit(solution)/shard_map/all_to_all | solution.py:58
  27.6 15.5 %all_to_all.32 = bf16[1,16,1,32,384]{4,3,2,0,1:T(8,128)(2,1)S(1)} all-to-all(bf16[1,16,1,32,384]{4,3,2,0,1:T(8,128)(2,1)S(1)} %fusion.249), channel_id=1, replica_groups=mesh['section'=2,'seq'=16] {'seq'}, dimensions={1} | all-to-all | bytes 786432 | tf_op jit(solution)/shard_map/all_to_all | solution.py:62
  43.1 3.4 %collective-permute-start = (bf16[1,1,512,384]{3,2,1,0:T(8,128)(2,1)S(1)}, bf16[1,1,512,384]{3,2,1,0:T(8,128)(2,1)S(1)}, u32[]{:S(2)}, u32[]{:S(2)}) collective-permute-start(bf16[1,1,512,384]{3,2,1,0:T(8,128)(2,1)S(1)} %bitcast.226), channel_id=1, source_target_pairs={{0,16},{1,17},{2,18},{3,19},{4,20},{5,21},{6,22},{7,23},{8,24},{9,... | collective-permute-start | bytes 1179656 | tf_op jit(solution)/shard_map/ppermute | solution.py:82
  46.5 8.6 %collective-permute-done = bf16[1,1,512,384]{3,2,1,0:T(8,128)(2,1)S(1)} collective-permute-done((bf16[1,1,512,384]{3,2,1,0:T(8,128)(2,1)S(1)}, bf16[1,1,512,384]{3,2,1,0:T(8,128)(2,1)S(1)}, u32[]{:S(2)}, u32[]{:S(2)}) %collective-permute-start) | collective-permute-done | bytes 393248 | tf_op jit(solution)/shard_map/ppermute | solution.py:82
  58.7 3.6 %multiply_reduce_fusion.5 = (f32[512]{0:T(512)S(1)}, f32[512,384]{1,0:T(8,128)}) fusion(f32[1,1,32,16,384]{4,3,2,1,0:T(8,128)S(1)} %get-tuple-element.40, f32[384]{0:T(512)S(1)} %get-tuple-element.128, f32[384]{0:T(512)S(1)} %get-tuple-element.129, f32[384]{0:T(512)S(1)} %reduce.27, bf16[1,384,768]{2,1,0:T(8,128)(2,1)S(1)} %copy-done, ...), kind=kOutput, calls=%fused_computation.319 | convolution fusion | flops 609680896 | bytes 4725248 | tf_op jit(solution)/shard_map/transpose(jvp())/dot_general | solution.py:36
  70.3 3.7 %all-to-all-start.4 = ((bf16[1,1,16,32,384]{4,3,1,0,2:T(8,128)(2,1)}), bf16[1,1,16,32,384]{4,3,1,0,2:T(8,128)(2,1)S(1)}, u32[]{:S(2)}, u32[]{:S(2)}) async-start(bf16[1,1,16,32,384]{4,3,1,0,2:T(8,128)(2,1)} %bitcast.244), calls=%async_computation.4 | async-start | bytes 786432 | tf_op jit(solution)/shard_map/all_to_all | solution.py:58
  74.0 4.4 %collective-permute-done.1 = bf16[1,1,512,384]{3,2,1,0:T(8,128)(2,1)} collective-permute-done((bf16[1,1,512,384]{3,2,1,0:T(8,128)(2,1)S(1)}, bf16[1,1,512,384]{3,2,1,0:T(8,128)(2,1)}, u32[]{:S(2)}, u32[]{:S(2)}) %collective-permute-start.1) | collective-permute-done | bytes 393248 | tf_op jit(solution)/shard_map/ppermute | solution.py:86
  81.5 4.7 %all-to-all-done.4 = bf16[1,1,16,32,384]{4,3,1,0,2:T(8,128)(2,1)S(1)} async-done(((bf16[1,1,16,32,384]{4,3,1,0,2:T(8,128)(2,1)}), bf16[1,1,16,32,384]{4,3,1,0,2:T(8,128)(2,1)S(1)}, u32[]{:S(2)}, u32[]{:S(2)}) %all-to-all-start.4) | async-done | bytes 393248 | tf_op jit(solution)/shard_map/all_to_all | solution.py:58
  87.0 3.6 %all-to-all-start.2 = ((bf16[1,1,16,32,384]{4,3,1,0,2:T(8,128)(2,1)}), bf16[1,1,16,32,384]{4,3,1,0,2:T(8,128)(2,1)S(1)}, u32[]{:S(2)}, u32[]{:S(2)}) async-start(bf16[1,1,16,32,384]{4,3,1,0,2:T(8,128)(2,1)} %bitcast.243), calls=%async_computation.2 | async-start | bytes 786432 | tf_op jit(solution)/shard_map/all_to_all | solution.py:58
  92.8 9.9 %all-to-all-done.2 = bf16[1,1,16,32,384]{4,3,1,0,2:T(8,128)(2,1)S(1)} async-done(((bf16[1,1,16,32,384]{4,3,1,0,2:T(8,128)(2,1)}), bf16[1,1,16,32,384]{4,3,1,0,2:T(8,128)(2,1)S(1)}, u32[]{:S(2)}, u32[]{:S(2)}) %all-to-all-start.2) | async-done | bytes 393248 | tf_op jit(solution)/shard_map/all_to_all | solution.py:58
  103.4 3.7 %all-to-all-start.5 = ((bf16[1,16,1,32,384]{4,3,2,0,1:T(8,128)(2,1)}), bf16[1,16,1,32,384]{4,3,2,0,1:T(8,128)(2,1)S(1)}, u32[]{:S(2)}, u32[]{:S(2)}) async-start(bf16[1,16,1,32,384]{4,3,2,0,1:T(8,128)(2,1)} %fusion.247), calls=%async_computation.5 | async-start | bytes 786432 | tf_op jit(solution)/shard_map/all_to_all | solution.py:62
  109.5 9.8 %all-to-all-done.5 = bf16[1,16,1,32,384]{4,3,2,0,1:T(8,128)(2,1)S(1)} async-done(((bf16[1,16,1,32,384]{4,3,2,0,1:T(8,128)(2,1)}), bf16[1,16,1,32,384]{4,3,2,0,1:T(8,128)(2,1)S(1)}, u32[]{:S(2)}, u32[]{:S(2)}) %all-to-all-start.5) | async-done | bytes 393248 | tf_op jit(solution)/shard_map/all_to_all | solution.py:62
  119.3 4.2 %all-to-all-start.3 = ((bf16[1,16,1,32,384]{4,3,2,0,1:T(8,128)(2,1)}), bf16[1,16,1,32,384]{4,3,2,0,1:T(8,128)(2,1)}, u32[]{:S(2)}, u32[]{:S(2)}) async-start(bf16[1,16,1,32,384]{4,3,2,0,1:T(8,128)(2,1)} %fusion.248), calls=%async_computation.3 | async-start | bytes 786432 | tf_op jit(solution)/shard_map/all_to_all | solution.py:62
  123.6 6.1 %collective-permute-start.2 = (bf16[1,1,512,384]{3,2,1,0:T(8,128)(2,1)S(1)}, bf16[1,1,512,384]{3,2,1,0:T(8,128)(2,1)}, u32[]{:S(2)}, u32[]{:S(2)}) collective-permute-start(bf16[1,1,512,384]{3,2,1,0:T(8,128)(2,1)S(1)} %bitcast.230), channel_id=1, source_target_pairs={{0,16},{1,17},{2,18},{3,19},{4,20},{5,21},{6,22},{7,23},{8,24},{9,... | collective-permute-start | bytes 1179656 | tf_op jit(solution)/shard_map/ppermute | solution.py:82
  129.7 6.1 %all-to-all-done.3 = bf16[1,16,1,32,384]{4,3,2,0,1:T(8,128)(2,1)} async-done(((bf16[1,16,1,32,384]{4,3,2,0,1:T(8,128)(2,1)}), bf16[1,16,1,32,384]{4,3,2,0,1:T(8,128)(2,1)}, u32[]{:S(2)}, u32[]{:S(2)}) %all-to-all-start.3) | async-done | bytes 393248 | tf_op jit(solution)/shard_map/all_to_all | solution.py:62
  135.8 3.7 %multiply_reduce_fusion.1 = (f32[512]{0:T(512)S(1)}, f32[512,384]{1,0:T(8,128)}) fusion(f32[1,1,32,16,384]{4,3,2,1,0:T(8,128)S(1)} %get-tuple-element.42, f32[384]{0:T(512)S(1)} %get-tuple-element.128, f32[384]{0:T(512)S(1)} %get-tuple-element.129, f32[384]{0:T(512)S(1)} %reduce.27, bf16[1,384,768]{2,1,0:T(8,128)(2,1)S(1)} %copy-done, ...), kind=kOutput, calls=%fused_computation.311 | convolution fusion | flops 609680896 | bytes 4725248 | tf_op jit(solution)/shard_map/transpose(jvp())/dot_general | solution.py:36
  145.6 3.6 %multiply_reduce_fusion.2 = (f32[512]{0:T(512)S(1)}, f32[512,384]{1,0:T(8,128)}) fusion(f32[1,1,32,16,384]{4,3,2,1,0:T(8,128)S(1)} %get-tuple-element.44, f32[384]{0:T(512)S(1)} %get-tuple-element.38, f32[384]{0:T(512)S(1)} %get-tuple-element.37, f32[384]{0:T(512)S(1)} %reduce.27, bf16[1,384,768]{2,1,0:T(8,128)(2,1)S(1)} %copy-done, ...), kind=kOutput, calls=%fused_computation.312 | convolution fusion | flops 609680896 | bytes 4725248 | tf_op jit(solution)/shard_map/transpose(jvp())/dot_general | solution.py:36
  150.7 3.3 %broadcast_multiply_fusion.2 = (f32[1,1,32,16,384]{4,3,2,1,0:T(8,128)S(1)}, f32[1,1,32,16,384]{4,3,2,1,0:T(8,128)S(1)}, f32[1,1,32,16,384]{4,3,2,1,0:T(8,128)S(1...) fusion(f32[1,1,32,16,384]{4,3,2,1,0:T(8,128)S(1)} %bitcast.235,, ...), kind=kLoop, calls=%fused_computation.363 | loop fusion | flops 3538944 | bytes 15742464 | tf_op jit(solution)/shard_map/transpose(jvp())/mul | solution.py:23
  156.2 12.8 %collective-permute-done.3 = bf16[1,1,512,384]{3,2,1,0:T(8,128)(2,1)S(1)} collective-permute-done((bf16[1,1,512,384]{3,2,1,0:T(8,128)(2,1)S(1)}, bf16[1,1,512,384]{3,2,1,0:T(8,128)(2,1)S(1)}, u32[]{:S(2)}, u32[]{:S(2)}) %collective-permute-start.3) | collective-permute-done | bytes 393248 | tf_op jit(solution)/shard_map/ppermute | solution.py:86
  170.6 15.6 %all_to_all.33 = bf16[1,1,16,32,384]{4,3,1,0,2:T(8,128)(2,1)S(1)} all-to-all(bf16[1,1,16,32,384]{4,3,1,0,2:T(8,128)(2,1)S(1)} %bitcast.245), channel_id=1, replica_groups=mesh['section'=2,'seq'=16] {'seq'}, dimensions={2} | all-to-all | bytes 786432 | tf_op jit(solution)/shard_map/all_to_all | solution.py:58
  187.6 4.4 %all-to-all-start.7 = ((bf16[1,16,1,32,384]{4,3,2,0,1:T(8,128)(2,1)}), bf16[1,16,1,32,384]{4,3,2,0,1:T(8,128)(2,1)}, u32[]{:S(2)}, u32[]{:S(2)}) async-start(bf16[1,16,1,32,384]{4,3,2,0,1:T(8,128)(2,1)} %fusion.246), calls=%async_computation.7 | async-start | bytes 786432 | tf_op jit(solution)/shard_map/all_to_all | solution.py:62
  197.4 6.6 %all-to-all-done.7 = bf16[1,16,1,32,384]{4,3,2,0,1:T(8,128)(2,1)} async-done(((bf16[1,16,1,32,384]{4,3,2,0,1:T(8,128)(2,1)}), bf16[1,16,1,32,384]{4,3,2,0,1:T(8,128)(2,1)}, u32[]{:S(2)}, u32[]{:S(2)}) %all-to-all-start.7) | async-done | bytes 393248 | tf_op jit(solution)/shard_map/all_to_all | solution.py:62
  204.0 3.6 %multiply_reduce_fusion = (f32[512]{0:T(512)S(1)}, f32[512,384]{1,0:T(8,128)}) fusion(f32[1,1,32,16,384]{4,3,2,1,0:T(8,128)S(1)} %get-tuple-element.101, f32[384]{0:T(512)S(1)} %get-tuple-element.38, f32[384]{0:T(512)S(1)} %get-tuple-element.37, f32[384]{0:T(512)S(1)} %reduce.27, bf16[1,384,768]{2,1,0:T(8,128)(2,1)S(1)} %copy-done, ...), kind=kOutput, calls=%fused_computation.310 | convolution fusion | flops 609680896 | bytes 4725248 | tf_op jit(solution)/shard_map/transpose(jvp())/dot_general | solution.py:36
  (122 shorter events, 52.6 us)
Async XLA Ops:
  0.6 3.9 %copy-start = (bf16[1,384,768]{2,1,0:T(8,128)(2,1)S(1)}, bf16[1,384,768]{2,1,0:T(8,128)(2,1)}, u32[]{:S(2)}) copy-start(bf16[1,384,768]{2,1,0:T(8,128)(2,1)} %param.13) | copy-start | bytes 1769476
  2.3 2.1 copy-start.19
  4.6 1.5 copy-start.22
  6.1 8.8 %copy-start.18 = (f32[1,9,384]{2,0,1:T(1,128)S(1)}, f32[1,9,384]{2,0,1:T(1,128)}, u32[]{:S(2)}) copy-start(f32[1,9,384]{2,0,1:T(1,128)} %param.15) | copy-start | bytes 41476
  7.4 19.6 %all-to-all-start = ((bf16[1,1,16,32,384]{4,3,1,0,2:T(8,128)(2,1)}), bf16[1,1,16,32,384]{4,3,1,0,2:T(8,128)(2,1)S(1)}, u32[]{:S(2)}, u32[]{:S(2)}) async-start(bf16[1,1,16,32,384]{4,3,1,0,2:T(8,128)(2,1)} %bitcast.7), calls=%async_computation | async-start | bytes 786432 | tf_op jit(solution)/shard_map/all_to_all | solution.py:58
  43.1 12.0 %collective-permute-start = (bf16[1,1,512,384]{3,2,1,0:T(8,128)(2,1)S(1)}, bf16[1,1,512,384]{3,2,1,0:T(8,128)(2,1)S(1)}, u32[]{:S(2)}, u32[]{:S(2)}) collective-permute-start(bf16[1,1,512,384]{3,2,1,0:T(8,128)(2,1)S(1)} %bitcast.226), channel_id=1, source_target_pairs={{0,16},{1,17},{2,18},{3,19},{4,20},{5,21},{6,22},{7,23},{8,24},{9,... | collective-permute-start | bytes 1179656 | tf_op jit(solution)/shard_map/ppermute | solution.py:82
  66.0 12.4 %collective-permute-start.1 = (bf16[1,1,512,384]{3,2,1,0:T(8,128)(2,1)S(1)}, bf16[1,1,512,384]{3,2,1,0:T(8,128)(2,1)}, u32[]{:S(2)}, u32[]{:S(2)}) collective-permute-start(bf16[1,1,512,384]{3,2,1,0:T(8,128)(2,1)S(1)} %bitcast_add_fusion.3), channel_id=1, source_target_pairs={{16,0},{17,1},{18,2},{19,3},{20,4},{21,5},{22,6},{23,7},{24,8},{25... | collective-permute-start | bytes 1179656 | tf_op jit(solution)/shard_map/ppermute | solution.py:86
  70.3 15.9 %all-to-all-start.4 = ((bf16[1,1,16,32,384]{4,3,1,0,2:T(8,128)(2,1)}), bf16[1,1,16,32,384]{4,3,1,0,2:T(8,128)(2,1)S(1)}, u32[]{:S(2)}, u32[]{:S(2)}) async-start(bf16[1,1,16,32,384]{4,3,1,0,2:T(8,128)(2,1)} %bitcast.244), calls=%async_computation.4 | async-start | bytes 786432 | tf_op jit(solution)/shard_map/all_to_all | solution.py:58
  87.0 15.7 %all-to-all-start.2 = ((bf16[1,1,16,32,384]{4,3,1,0,2:T(8,128)(2,1)}), bf16[1,1,16,32,384]{4,3,1,0,2:T(8,128)(2,1)S(1)}, u32[]{:S(2)}, u32[]{:S(2)}) async-start(bf16[1,1,16,32,384]{4,3,1,0,2:T(8,128)(2,1)} %bitcast.243), calls=%async_computation.2 | async-start | bytes 786432 | tf_op jit(solution)/shard_map/all_to_all | solution.py:58
  103.4 15.9 %all-to-all-start.5 = ((bf16[1,16,1,32,384]{4,3,2,0,1:T(8,128)(2,1)}), bf16[1,16,1,32,384]{4,3,2,0,1:T(8,128)(2,1)S(1)}, u32[]{:S(2)}, u32[]{:S(2)}) async-start(bf16[1,16,1,32,384]{4,3,2,0,1:T(8,128)(2,1)} %fusion.247), calls=%async_computation.5 | async-start | bytes 786432 | tf_op jit(solution)/shard_map/all_to_all | solution.py:62
  119.3 16.4 %all-to-all-start.3 = ((bf16[1,16,1,32,384]{4,3,2,0,1:T(8,128)(2,1)}), bf16[1,16,1,32,384]{4,3,2,0,1:T(8,128)(2,1)}, u32[]{:S(2)}, u32[]{:S(2)}) async-start(bf16[1,16,1,32,384]{4,3,2,0,1:T(8,128)(2,1)} %fusion.248), calls=%async_computation.3 | async-start | bytes 786432 | tf_op jit(solution)/shard_map/all_to_all | solution.py:62
  123.6 18.1 %collective-permute-start.2 = (bf16[1,1,512,384]{3,2,1,0:T(8,128)(2,1)S(1)}, bf16[1,1,512,384]{3,2,1,0:T(8,128)(2,1)}, u32[]{:S(2)}, u32[]{:S(2)}) collective-permute-start(bf16[1,1,512,384]{3,2,1,0:T(8,128)(2,1)S(1)} %bitcast.230), channel_id=1, source_target_pairs={{0,16},{1,17},{2,18},{3,19},{4,20},{5,21},{6,22},{7,23},{8,24},{9,... | collective-permute-start | bytes 1179656 | tf_op jit(solution)/shard_map/ppermute | solution.py:82
  154.3 14.7 %copy-start.8 = (f32[512,768]{1,0:T(8,128)S(1)}, f32[512,768]{1,0:T(8,128)}, u32[]{:S(2)}) copy-start(f32[512,768]{1,0:T(8,128)} %fusion.235) | copy-start | bytes 4718596
  154.3 14.7 %copy-start.24 = (bf16[1,768,384]{2,1,0:T(8,128)(2,1)S(1)}, bf16[1,768,384]{2,1,0:T(8,128)(2,1)}, u32[]{:S(2)}) copy-start(bf16[1,768,384]{2,1,0:T(8,128)(2,1)} %param.14) | copy-start | bytes 1769476
  154.8 15.8 %copy-start.9 = (bf16[1,1,512,384]{3,2,1,0:T(8,128)(2,1)}, bf16[1,1,512,384]{3,2,1,0:T(8,128)(2,1)S(1)}, u32[]{:S(2)}) copy-start(bf16[1,1,512,384]{3,2,1,0:T(8,128)(2,1)S(1)} %bitcast_add_fusion.2) | copy-start | bytes 1179652
  154.8 14.2 %collective-permute-start.3 = (bf16[1,1,512,384]{3,2,1,0:T(8,128)(2,1)S(1)}, bf16[1,1,512,384]{3,2,1,0:T(8,128)(2,1)S(1)}, u32[]{:S(2)}, u32[]{:S(2)}) collective-permute-start(bf16[1,1,512,384]{3,2,1,0:T(8,128)(2,1)S(1)} %bitcast_add_fusion.2), channel_id=1, source_target_pairs={{16,0},{17,1},{18,2},{19,3},{20,4},{21,5},{22,6},{23,7},{24,8},{25... | collective-permute-start | bytes 1179656 | tf_op jit(solution)/shard_map/ppermute | solution.py:86
  187.6 16.4 %all-to-all-start.7 = ((bf16[1,16,1,32,384]{4,3,2,0,1:T(8,128)(2,1)}), bf16[1,16,1,32,384]{4,3,2,0,1:T(8,128)(2,1)}, u32[]{:S(2)}, u32[]{:S(2)}) async-start(bf16[1,16,1,32,384]{4,3,2,0,1:T(8,128)(2,1)} %fusion.246), calls=%async_computation.7 | async-start | bytes 786432 | tf_op jit(solution)/shard_map/all_to_all | solution.py:62
  192.1 2.4 %copy-start.1 = (f32[1,1,32,16,384]{4,3,2,1,0:T(8,128)S(1)}, f32[1,1,32,16,384]{4,3,2,1,0:T(8,128)}, u32[]{:S(2)}) copy-start(f32[1,1,32,16,384]{4,3,2,1,0:T(8,128)} %get-tuple-element.95) | copy-start | bytes 2359300
  192.1 2.4 %copy-start.2 = (f32[1,1,32,16,384]{4,3,2,1,0:T(8,128)S(1)}, f32[1,1,32,16,384]{4,3,2,1,0:T(8,128)}, u32[]{:S(2)}) copy-start(f32[1,1,32,16,384]{4,3,2,1,0:T(8,128)} %get-tuple-element.96) | copy-start | bytes 2359300
  192.1 2.5 %copy-start.3 = (f32[1,1,32,16,384]{4,3,2,1,0:T(8,128)S(1)}, f32[1,1,32,16,384]{4,3,2,1,0:T(8,128)}, u32[]{:S(2)}) copy-start(f32[1,1,32,16,384]{4,3,2,1,0:T(8,128)} %get-tuple-element.97) | copy-start | bytes 2359300
  192.1 2.8 %copy-start.4 = (f32[1,1,32,16,384]{4,3,2,1,0:T(8,128)S(1)}, f32[1,1,32,16,384]{4,3,2,1,0:T(8,128)}, u32[]{:S(2)}) copy-start(f32[1,1,32,16,384]{4,3,2,1,0:T(8,128)} %get-tuple-element.98) | copy-start | bytes 2359300
  195.4 8.7 %copy-start.25 = (bf16[1,768,384]{2,1,0:T(8,128)(2,1)S(1)}, bf16[1,768,384]{2,1,0:T(8,128)(2,1)}, u32[]{:S(2)}) copy-start(bf16[1,768,384]{2,1,0:T(8,128)(2,1)} %param.14) | copy-start | bytes 1769476
  210.4 1.8 copy-start.12
  211.0 2.1 copy-start.11
  (12 other events, 13.9 us)

commit v3 on v1

--- a/solution.py
+++ b/solution.py
@@ -47,7 +47,7 @@
     padded = jnp.pad(volume, ((0, 0), (reach, reach), (0, 0), (0, 0)))
     total = volume
     for offset in range(BAND):
-        total = total + tap_table[offset] * padded[:, offset : offset + frame_count]
+        total = total + tap_table[:, offset, None, None, :] * padded[:, offset : offset + frame_count]
     return total.astype(jnp.bfloat16)
 
 
@@ -64,30 +64,69 @@
 
 
 def on_device(clips, cotangent, spatial_taps, modulation, norm_gain, w_in, w_out, band_taps):
-    first = lax.axis_index("section") == 0
-    taps, mod, gain = spatial_taps[0], modulation[0], norm_gain[0]
-    weight_in, weight_out, band = w_in[0], w_out[0], band_taps[0]
+    plane = lax.axis_index("section")
+    first = plane == 0
+    clip_total, channels = clips.shape[0], clips.shape[-1]
+    tap_count = spatial_taps.shape[1]
+    small = jnp.concatenate(
+        [
+            spatial_taps[0],
+            modulation[0].reshape(-1, channels),
+            norm_gain,
+            band_taps[0],
+        ]
+    )
+    small_all = lax.all_gather(small, "section", axis=0, tiled=False)
+    in_all = lax.all_gather(w_in[0], "section", axis=0, tiled=False)
+    out_all = lax.all_gather(w_out[0], "section", axis=0, tiled=False)
 
-    def spatial(values):
-        return spatial_block(values, taps, mod, gain, weight_in, weight_out)
+    def params(segment):
+        table = small_all[segment]
+        taps = table[:tap_count]
+        mods = table[tap_count : tap_count + 2 * clip_total].reshape(clip_total, 2, channels)
+        gain = table[tap_count + 2 * clip_total]
+        band = table[tap_count + 2 * clip_total + 1 :]
+        mod = lax.dynamic_index_in_dim(mods, plane, 0, keepdims=True)
+        return taps, mod, gain, band
 
-    first_mixed, first_pull = jax.vjp(spatial, clips)
-    lead_in = jnp.where(first, first_mixed, cotangent)
-    lead_taps = jnp.where(first, band, band[::-1])
-    lead_out = temporal(lead_in, lead_taps)
+    taps0, mod0, gain0, band0 = params(0)
+    taps1, mod1, gain1, band1 = params(1)
 
-    first_acts = lax.ppermute(lead_out, "section", perm=[(0, 1)])
-    second_mixed, second_pull = jax.vjp(spatial, first_acts)
-    second_grad = second_pull(lead_out)[0]
+    def spatial0(values):
+        return spatial_block(values, taps0, mod0, gain0, in_all[0], out_all[0])
 
-    arrived_grad = lax.ppermute(second_grad, "section", perm=[(1, 0)])
-    tail_in = jnp.where(first, arrived_grad, second_mixed)
-    tail_taps = jnp.where(first, band[::-1], band)
-    tail_out = temporal(tail_in, tail_taps)
-    first_grad = first_pull(tail_out)[0]
+    def spatial1(values):
+        return spatial_block(values, taps1, mod1, gain1, in_all[1], out_all[1])
 
-    activations = jnp.where(first, lead_out, tail_out)
-    input_grads = jnp.where(first, first_grad, second_grad)
+    start = lax.dynamic_index_in_dim(clips, plane, 0, keepdims=True)
+    seed = lax.dynamic_index_in_dim(cotangent, plane, 0, keepdims=True)
+    second_seed = temporal(seed, band1[::-1][None])
+
+    first_mixed, first_pull = jax.vjp(spatial0, start)
+    first_act = temporal(first_mixed, band0[None])
+    second_mixed, second_pull = jax.vjp(spatial1, first_act)
+    second_grad = second_pull(second_seed)[0]
+
+    tail = temporal(
+        jnp.concatenate([second_grad, second_mixed]), jnp.stack([band0[::-1], band1])
+    )
+    first_seed, second_act = tail[:1], tail[1:]
+
+    swap = [(0, 1), (1, 0)]
+    other_act = lax.ppermute(jnp.where(first, second_act, first_act), "section", perm=swap)
+    first_grad = first_pull(first_seed)[0]
+    other_grad = lax.ppermute(jnp.where(first, second_grad, first_grad), "section", perm=swap)
+
+    activations = jnp.where(
+        first,
+        jnp.concatenate([first_act, other_act]),
+        jnp.concatenate([other_act, second_act]),
+    )
+    input_grads = jnp.where(
+        first,
+        jnp.concatenate([first_grad, other_grad]),
+        jnp.concatenate([other_grad, second_grad]),
+    )
     return (activations[None], input_grads[None])
 
 

time: 193 us -> 218 us (1.13)
  blocking collectives: 51 us -> 5.53 us
  waiting for transfers between devices: 74.7 us -> 117 us
  between operations: 1.01 us -> 14.8 us
  local copies, waits for them, and re-layouts: 5.79 us -> 16.9 us
  starting transfers between devices: 16.7 us -> 27.7 us
  other arithmetic: 24.7 us -> 20.2 us
  matrix products: 18.2 us -> 14 us
    all_to_all x2 -> x0, blocking collectives: 51 us -> none  [temporal(): lax.all_to_all(banded, 'seq', split_axis=1, concat_axis=2, tiled=True)]
    all_gather x0 -> x2, waiting for transfers between devices: none -> 39.4 us  [the longest x1 22.7 us: on_device(): out_all = lax.all_gather(w_out[0], 'section', axis=0, tiled=False)]
    all_to_all x0 -> x3, waiting for transfers between devices: none -> 35.4 us  [temporal(): lax.all_to_all(banded, 'seq', split_axis=1, concat_axis=2, tiled=True)]
    ppermute x2, waiting for transfers between devices: 37.6 us -> 8.71 us  [the longest x1 5.52 us: on_device(): lax.ppermute(jnp.where(first, second_grad, first_grad), 'section', perm=s...]
    all_to_all x0 -> x3, starting transfers between devices: none -> 12.6 us  [temporal(): lax.all_to_all(banded, 'seq', split_axis=1, concat_axis=2, tiled=True)]
    unnamed x34 -> x98, local copies, waits for them, and re-layouts: 1.47 us -> 10.1 us
    all_gather x0 -> x1, blocking collectives: none -> 5.53 us  [on_device(): small_all = lax.all_gather(small, 'section', axis=0, tiled=False)]
    dot_general x4, matrix products: 16.1 us -> 10.9 us  [spatial_block(): jnp.dot(normed, w_in, preferred_element_type=jnp.float32)]
  transfers between devices with their start and end apart: 4 -> 10, of which waited for: 4 -> 10; matrix products, arithmetic and copies ran while one was open for 0% -> 14% of each run, Pallas kernels for 0% -> 0%
where the time goes in v3:
time: 218 us; the launch traced here: 216 us
  waiting for transfers between devices  117 us (54%)
  starting transfers between devices  27.7 us (13%)
  other arithmetic  20.2 us (9%)
  local copies, waits for them, and re-layouts  16.9 us (8%)
  between operations  14.8 us (7%)
  matrix products  14 us (6%)
  blocking collectives  5.53 us (3%)
    all_to_all x3, waiting for transfers between devices, temporal(): lax.all_to_all(banded, 'seq', split_axis=1, concat_axis=2, tiled=True)  35.4 us
    all_to_all x3, waiting for transfers between devices, temporal(): lax.all_to_all(grouped, 'seq', split_axis=2, concat_axis=1, tiled=True)  32.2 us
    all_gather x1, waiting for transfers between devices, on_device(): out_all = lax.all_gather(w_out[0], 'section', axis=0, tiled=False)  22.7 us
    all_gather x1, waiting for transfers between devices, on_device(): in_all = lax.all_gather(w_in[0], 'section', axis=0, tiled=False)  16.7 us
    all_to_all x3, starting transfers between devices, temporal(): lax.all_to_all(grouped, 'seq', split_axis=2, concat_axis=1, tiled=True)  12.9 us
    all_to_all x3, starting transfers between devices, temporal(): lax.all_to_all(banded, 'seq', split_axis=1, concat_axis=2, tiled=True)  12.6 us
    dot_general x4, matrix products, spatial_block(): jnp.dot(normed, w_in, preferred_element_type=jnp.float32)  10.9 us
    unnamed x98, local copies, waits for them, and re-layouts  10.1 us
  transfers between devices with their start and end apart: 10, of which 10 were waited for; matrix products, arithmetic and copies ran while one was open for 14% of the time, Pallas kernels for 0%

profile of v3, /device:TPU:0, one launch (start us, length us, event | category | flops | bytes accessed | tf_op | source)
XLA Modules:
  0.0 216.2 jit_solution(1114418649229370256)
XLA Ops:
  10.8 5.5 %all-gather.1 = f32[2,23,384]{2,1,0:T(8,128)S(1)} all-gather(f32[1,23,384]{2,1,0:T(8,128)S(1)} %maximum_bitcast_fusion), channel_id=2, replica_groups=mesh['section'=2,'seq'=16] {'section'}, dimensions={0}, use_global_device_ids=true | all-gather | bytes 105984 | tf_op jit(solution)/shard_map/all_gather | solution.py:79
  18.3 16.7 %all-gather.5.cloned.1.call-done = bf16[2,384,768]{2,1,0:T(8,128)(2,1)} async-done(((bf16[1,384,768]{2,1,0:T(8,128)(2,1)}), bf16[2,384,768]{2,1,0:T(8,128)(2,1)}) %all-gather.5.cloned.1.call-update) | async-done | bytes 1179664 | tf_op jit(solution)/shard_map/all_gather | solution.py:80
  36.7 22.7 %all-gather.7.cloned.1.call-done = bf16[2,768,384]{2,1,0:T(8,128)(2,1)} async-done(((bf16[1,768,384]{2,1,0:T(8,128)(2,1)}), bf16[2,768,384]{2,1,0:T(8,128)(2,1)}) %all-gather.7.cloned.1.call-update) | async-done | bytes 1179664 | tf_op jit(solution)/shard_map/all_gather | solution.py:81
  59.4 2.5 %fusion.29 = bf16[1,1,512,384]{3,2,1,0:T(8,128)(2,1)} fusion(f32[512,768]{1,0:T(8,128)S(1)} %fusion.126, bf16[2,768,384]{2,1,0:T(8,128)(2,1)} %all-gather.7.cloned.1.call-done, bf16[2,1,512,384]{3,2,1,0:T(8,128)(2,1)} %param.8, s32[]{:T(128)S(6)} %select_n.72), kind=kOutput, calls=%fused_computation.81 | convolution fusion | flops 304545792 | bytes 2949124 | tf_op jit(solution)/shard_map/jvp()/dot_general | solution.py:39
  62.0 5.8 %all-to-all-start = ((bf16[1,1,16,32,384]{4,3,1,0,2:T(8,128)(2,1)}), bf16[1,1,16,32,384]{4,3,1,0,2:T(8,128)(2,1)S(1)}, u32[]{:S(2)}, u32[]{:S(2)}) async-start(bf16[1,1,16,32,384]{4,3,1,0,2:T(8,128)(2,1)} %bitcast.172), calls=%async_computation | async-start | bytes 786432 | tf_op jit(solution)/shard_map/all_to_all | solution.py:58
  68.5 11.4 %all-to-all-done = bf16[1,1,16,32,384]{4,3,1,0,2:T(8,128)(2,1)S(1)} async-done(((bf16[1,1,16,32,384]{4,3,1,0,2:T(8,128)(2,1)}), bf16[1,1,16,32,384]{4,3,1,0,2:T(8,128)(2,1)S(1)}, u32[]{:S(2)}, u32[]{:S(2)}) %all-to-all-start) | async-done | bytes 393248 | tf_op jit(solution)/shard_map/all_to_all | solution.py:58
  79.9 3.6 %all-to-all-start.2 = ((bf16[1,1,16,32,384]{4,3,1,0,2:T(8,128)(2,1)}), bf16[1,1,16,32,384]{4,3,1,0,2:T(8,128)(2,1)S(1)}, u32[]{:S(2)}, u32[]{:S(2)}) async-start(bf16[1,1,16,32,384]{4,3,1,0,2:T(8,128)(2,1)} %bitcast.13), calls=%async_computation.2 | async-start | bytes 786432 | tf_op jit(solution)/shard_map/all_to_all | solution.py:58
  84.9 10.7 %all-to-all-done.2 = bf16[1,1,16,32,384]{4,3,1,0,2:T(8,128)(2,1)S(1)} async-done(((bf16[1,1,16,32,384]{4,3,1,0,2:T(8,128)(2,1)}), bf16[1,1,16,32,384]{4,3,1,0,2:T(8,128)(2,1)S(1)}, u32[]{:S(2)}, u32[]{:S(2)}) %all-to-all-start.2) | async-done | bytes 393248 | tf_op jit(solution)/shard_map/all_to_all | solution.py:58
  95.6 3.6 %all-to-all-start.1 = ((bf16[1,16,1,32,384]{4,3,2,0,1:T(8,128)(2,1)}), bf16[1,16,1,32,384]{4,3,2,0,1:T(8,128)(2,1)S(1)}, u32[]{:S(2)}, u32[]{:S(2)}) async-start(bf16[1,16,1,32,384]{4,3,2,0,1:T(8,128)(2,1)} %fusion.130), calls=%async_computation.1 | async-start | bytes 786432 | tf_op jit(solution)/shard_map/all_to_all | solution.py:62
  101.3 10.0 %all-to-all-done.1 = bf16[1,16,1,32,384]{4,3,2,0,1:T(8,128)(2,1)S(1)} async-done(((bf16[1,16,1,32,384]{4,3,2,0,1:T(8,128)(2,1)}), bf16[1,16,1,32,384]{4,3,2,0,1:T(8,128)(2,1)S(1)}, u32[]{:S(2)}, u32[]{:S(2)}) %all-to-all-start.1) | async-done | bytes 393248 | tf_op jit(solution)/shard_map/all_to_all | solution.py:62
  111.4 3.6 %all-to-all-start.3 = ((bf16[1,16,1,32,384]{4,3,2,0,1:T(8,128)(2,1)}), bf16[1,16,1,32,384]{4,3,2,0,1:T(8,128)(2,1)S(1)}, u32[]{:S(2)}, u32[]{:S(2)}) async-start(bf16[1,16,1,32,384]{4,3,2,0,1:T(8,128)(2,1)} %fusion.129), calls=%async_computation.3 | async-start | bytes 786432 | tf_op jit(solution)/shard_map/all_to_all | solution.py:62
  119.8 7.3 %all-to-all-done.3 = bf16[1,16,1,32,384]{4,3,2,0,1:T(8,128)(2,1)S(1)} async-done(((bf16[1,16,1,32,384]{4,3,2,0,1:T(8,128)(2,1)}), bf16[1,16,1,32,384]{4,3,2,0,1:T(8,128)(2,1)S(1)}, u32[]{:S(2)}, u32[]{:S(2)}) %all-to-all-start.3) | async-done | bytes 393248 | tf_op jit(solution)/shard_map/all_to_all | solution.py:62
  127.1 3.7 %multiply_reduce_fusion.1 = (f32[512]{0:T(512)S(1)}, f32[512,384]{1,0:T(8,128)}) fusion(f32[1,1,32,16,384]{4,3,2,1,0:T(8,128)S(1)} %get-tuple-element.45, f32[384]{0:T(512)S(1)} %get-tuple-element.41, f32[384]{0:T(512)S(1)} %get-tuple-element.40, f32[384]{0:T(512)S(1)} %get-tuple-element.2, bf16[2,384,768]{2,1,0:T(8,128)(2,1)} %all-gather.5.cloned.1.call-done, ...), kind=kOutput, calls=%fused_computation.184 | convolution fusion | flops 609680896 | bytes 4725248 | tf_op jit(solution)/shard_map/transpose(jvp())/dot_general | solution.py:36
  136.9 3.6 %all-to-all-start.4 = ((bf16[2,1,16,32,384]{4,3,0,1,2:T(8,128)(2,1)}), bf16[2,1,16,32,384]{4,3,0,1,2:T(8,128)(2,1)S(1)}, u32[]{:S(2)}, u32[]{:S(2)}) async-start(bf16[2,1,16,32,384]{4,3,0,1,2:T(8,128)(2,1)} %copy.15), calls=%async_computation.4 | async-start | bytes 1572864 | tf_op jit(solution)/shard_map/all_to_all | solution.py:58
  140.5 2.0 rev.7
  149.0 10.1 %all-to-all-done.4 = bf16[2,1,16,32,384]{4,3,0,1,2:T(8,128)(2,1)S(1)} async-done(((bf16[2,1,16,32,384]{4,3,0,1,2:T(8,128)(2,1)}), bf16[2,1,16,32,384]{4,3,0,1,2:T(8,128)(2,1)S(1)}, u32[]{:S(2)}, u32[]{:S(2)}) %all-to-all-start.4) | async-done | bytes 786464 | tf_op jit(solution)/shard_map/all_to_all | solution.py:58
  159.9 2.4 %fusion.125 = bf16[2,16,1,32,384]{4,3,2,0,1:T(8,128)(2,1)} fusion(f32[2,16,32,384]{3,2,0,1:T(8,128)S(1)} %bitcast_convert_fusion, f32[2,384]{1,0:T(2,128)S(1)} %bitcast.184, f32[2,384]{1,0:T(2,128)S(1)} %bitcast.185, f32[2,384]{1,0:T(2,128)S(1)} %bitcast.178, f32[2,384]{1,0:T(2,128)S(1)} %bitcast.179, f32[2,384]{1,0:T(2,128)S(1)} %bitcast.180, ...), kind=kLoop, calls=%fused_computation.193 | loop fusion | flops 7471104 | bytes 2386944 | tf_op jit(solution)/shard_map/reshape | solution.py:61
  162.2 5.5 %all-to-all-start.5 = ((bf16[2,16,1,32,384]{4,3,2,0,1:T(8,128)(2,1)}), bf16[2,16,1,32,384]{4,3,2,0,1:T(8,128)(2,1)}, u32[]{:S(2)}, u32[]{:S(2)}) async-start(bf16[2,16,1,32,384]{4,3,2,0,1:T(8,128)(2,1)} %fusion.125), calls=%async_computation.5 | async-start | bytes 1572864 | tf_op jit(solution)/shard_map/all_to_all | solution.py:62
  168.4 18.1 %all-to-all-done.5 = bf16[2,16,1,32,384]{4,3,2,0,1:T(8,128)(2,1)} async-done(((bf16[2,16,1,32,384]{4,3,2,0,1:T(8,128)(2,1)}), bf16[2,16,1,32,384]{4,3,2,0,1:T(8,128)(2,1)}, u32[]{:S(2)}, u32[]{:S(2)}) %all-to-all-start.5) | async-done | bytes 786464 | tf_op jit(solution)/shard_map/all_to_all | solution.py:62
  186.5 2.0 fusion.141
  189.0 3.8 %multiply_reduce_fusion = (f32[512]{0:T(512)S(1)}, f32[512,384]{1,0:T(8,128)}) fusion(f32[1,1,32,16,384]{4,3,2,1,0:T(8,128)S(1)} %get-tuple-element.47, f32[384]{0:T(512)} %copy-done.11, f32[384]{0:T(512)} %copy-done.9, f32[384]{0:T(512)} %copy-done.41, bf16[2,384,768]{2,1,0:T(8,128)(2,1)} %all-gather.5.cloned.1.call-done, f32[512,768]{1,0:T(8,128)} %copy-done.3, ...), kind=kOutput, calls=%fused_computation.183 | convolution fusion | flops 609680896 | bytes 4726784 | tf_op jit(solution)/shard_map/transpose(jvp())/dot_general | solution.py:36
  197.5 3.2 %collective-permute-done = bf16[1,1,512,384]{3,2,1,0:T(8,128)(2,1)} collective-permute-done((bf16[1,1,512,384]{3,2,1,0:T(8,128)(2,1)}, bf16[1,1,512,384]{3,2,1,0:T(8,128)(2,1)}, u32[]{:S(2)}, u32[]{:S(2)}) %collective-permute-start) | collective-permute-done | bytes 393248 | tf_op jit(solution)/shard_map/ppermute | solution.py:116
  200.7 2.1 maximum_select_fusion
  202.9 5.5 %collective-permute-done.1 = bf16[1,1,512,384]{3,2,1,0:T(8,128)(2,1)S(1)} collective-permute-done((bf16[1,1,512,384]{3,2,1,0:T(8,128)(2,1)S(1)}, bf16[1,1,512,384]{3,2,1,0:T(8,128)(2,1)S(1)}, u32[]{:S(2)}, u32[]{:S(2)}) %collective-permute-start.1) | collective-permute-done | bytes 393248 | tf_op jit(solution)/shard_map/ppermute | solution.py:118
  (153 shorter events, 36.1 us)
Async XLA Ops:
  7.2 60.6 %copy-start = (bf16[2,1,512,384]{3,2,1,0:T(8,128)(2,1)S(1)}, bf16[2,1,512,384]{3,2,1,0:T(8,128)(2,1)}, u32[]{:S(2)}) copy-start(bf16[2,1,512,384]{3,2,1,0:T(8,128)(2,1)} %param.9) | copy-start | bytes 2359300
  7.2 10.0 %copy-start.8 = (bf16[2,1,512,384]{3,2,1,0:T(8,128)(2,1)S(1)}, bf16[2,1,512,384]{3,2,1,0:T(8,128)(2,1)}, u32[]{:S(2)}) copy-start(bf16[2,1,512,384]{3,2,1,0:T(8,128)(2,1)} %param.8) | copy-start | bytes 2359300
  7.2 27.9 %all-gather.5.cloned.1.call-start = ((), (), s32[]{:S(2)}) async-start(), calls=%async_computation.6 | async-start | bytes 1769472 | tf_op jit(solution)/shard_map/all_gather | solution.py:80
  7.9 51.5 %all-gather.7.cloned.1.call-start = ((), (), s32[]{:S(2)}) async-start(), calls=%async_computation.7 | async-start | bytes 1769472 | tf_op jit(solution)/shard_map/all_gather | solution.py:81
  36.7 25.2 %copy-start.3 = (f32[512,768]{1,0:T(8,128)}, f32[512,768]{1,0:T(8,128)S(1)}, u32[]{:S(2)}) copy-start(f32[512,768]{1,0:T(8,128)S(1)} %fusion.126) | copy-start | bytes 4718596
  62.0 21.5 %copy-start.7 = (f32[2,23,384]{2,1,0:T(8,128)S(1)}, f32[2,23,384]{2,1,0:T(8,128)}, u32[]{:S(2)}) copy-start(f32[2,23,384]{2,1,0:T(8,128)} %copy-done.6) | copy-start | bytes 211972
  62.0 18.0 %all-to-all-start = ((bf16[1,1,16,32,384]{4,3,1,0,2:T(8,128)(2,1)}), bf16[1,1,16,32,384]{4,3,1,0,2:T(8,128)(2,1)S(1)}, u32[]{:S(2)}, u32[]{:S(2)}) async-start(bf16[1,1,16,32,384]{4,3,1,0,2:T(8,128)(2,1)} %bitcast.172), calls=%async_computation | async-start | bytes 786432 | tf_op jit(solution)/shard_map/all_to_all | solution.py:58
  79.9 15.7 %all-to-all-start.2 = ((bf16[1,1,16,32,384]{4,3,1,0,2:T(8,128)(2,1)}), bf16[1,1,16,32,384]{4,3,1,0,2:T(8,128)(2,1)S(1)}, u32[]{:S(2)}, u32[]{:S(2)}) async-start(bf16[1,1,16,32,384]{4,3,1,0,2:T(8,128)(2,1)} %bitcast.13), calls=%async_computation.2 | async-start | bytes 786432 | tf_op jit(solution)/shard_map/all_to_all | solution.py:58
  83.6 16.2 %copy-start.13 = (f32[1,4,384]{2,1,0:T(4,128)S(1)}, f32[1,4,384]{2,1,0:T(4,128)}, u32[]{:S(2)}) copy-start(f32[1,4,384]{2,1,0:T(4,128)} %get-tuple-element.72) | copy-start | bytes 18436
  95.6 15.7 %all-to-all-start.1 = ((bf16[1,16,1,32,384]{4,3,2,0,1:T(8,128)(2,1)}), bf16[1,16,1,32,384]{4,3,2,0,1:T(8,128)(2,1)S(1)}, u32[]{:S(2)}, u32[]{:S(2)}) async-start(bf16[1,16,1,32,384]{4,3,2,0,1:T(8,128)(2,1)} %fusion.130), calls=%async_computation.1 | async-start | bytes 786432 | tf_op jit(solution)/shard_map/all_to_all | solution.py:62
  111.4 15.7 %all-to-all-start.3 = ((bf16[1,16,1,32,384]{4,3,2,0,1:T(8,128)(2,1)}), bf16[1,16,1,32,384]{4,3,2,0,1:T(8,128)(2,1)S(1)}, u32[]{:S(2)}, u32[]{:S(2)}) async-start(bf16[1,16,1,32,384]{4,3,2,0,1:T(8,128)(2,1)} %fusion.129), calls=%async_computation.3 | async-start | bytes 786432 | tf_op jit(solution)/shard_map/all_to_all | solution.py:62
  133.1 1.6 copy-start.4
  133.1 2.0 copy-start.43
  136.9 22.3 %all-to-all-start.4 = ((bf16[2,1,16,32,384]{4,3,0,1,2:T(8,128)(2,1)}), bf16[2,1,16,32,384]{4,3,0,1,2:T(8,128)(2,1)S(1)}, u32[]{:S(2)}, u32[]{:S(2)}) async-start(bf16[2,1,16,32,384]{4,3,0,1,2:T(8,128)(2,1)} %copy.15), calls=%async_computation.4 | async-start | bytes 1572864 | tf_op jit(solution)/shard_map/all_to_all | solution.py:58
  162.2 24.2 %all-to-all-start.5 = ((bf16[2,16,1,32,384]{4,3,2,0,1:T(8,128)(2,1)}), bf16[2,16,1,32,384]{4,3,2,0,1:T(8,128)(2,1)}, u32[]{:S(2)}, u32[]{:S(2)}) async-start(bf16[2,16,1,32,384]{4,3,2,0,1:T(8,128)(2,1)} %fusion.125), calls=%async_computation.5 | async-start | bytes 1572864 | tf_op jit(solution)/shard_map/all_to_all | solution.py:62
  188.5 12.3 %collective-permute-start = (bf16[1,1,512,384]{3,2,1,0:T(8,128)(2,1)}, bf16[1,1,512,384]{3,2,1,0:T(8,128)(2,1)}, u32[]{:S(2)}, u32[]{:S(2)}) collective-permute-start(bf16[1,1,512,384]{3,2,1,0:T(8,128)(2,1)} %bitcast.37), channel_id=1, source_target_pairs={{0,16},{16,0},{1,17},{17,1},{2,18},{18,2},{3,19},{19,3},{4,20},{20... | collective-permute-start | bytes 1179656 | tf_op jit(solution)/shard_map/ppermute | solution.py:116
  189.0 3.8 %copy-start.42 = (f32[512]{0:T(512)S(1)}, f32[512]{0:T(512)}, u32[]{:S(2)}) copy-start(f32[512]{0:T(512)} %add.356) | copy-start | bytes 6148
  189.0 3.9 %copy-start.10 = (f32[384]{0:T(512)S(1)}, f32[384]{0:T(512)}, u32[]{:S(2)}) copy-start(f32[384]{0:T(512)} %copy-done.9) | copy-start | bytes 4612
  189.0 3.9 %copy-start.12 = (f32[384]{0:T(512)S(1)}, f32[384]{0:T(512)}, u32[]{:S(2)}) copy-start(f32[384]{0:T(512)} %copy-done.11) | copy-start | bytes 4612
  192.8 1.5 copy-start.21
  192.8 1.5 copy-start.23
  192.8 1.5 copy-start.25
  192.8 1.5 copy-start.27
  195.8 12.6 %collective-permute-start.1 = (bf16[1,1,512,384]{3,2,1,0:T(8,128)(2,1)S(1)}, bf16[1,1,512,384]{3,2,1,0:T(8,128)(2,1)S(1)}, u32[]{:S(2)}, u32[]{:S(2)}) collective-permute-start(bf16[1,1,512,384]{3,2,1,0:T(8,128)(2,1)S(1)} %fusion.128), channel_id=1, source_target_pairs={{0,16},{16,0},{1,17},{17,1},{2,18},{18,2},{3,19},{19,3},{4,20},{20... | collective-permute-start | bytes 1179656 | tf_op jit(solution)/shard_map/ppermute | solution.py:118
  (30 other events, 31.6 us)
Sparse Core Ops, SparseCore 0:
  9.6 25.4 all-gather.4
  36.6 22.7 all-gather.6

commit v4 on v1

--- a/solution.py
+++ b/solution.py
@@ -47,7 +47,7 @@
     padded = jnp.pad(volume, ((0, 0), (reach, reach), (0, 0), (0, 0)))
     total = volume
     for offset in range(BAND):
-        total = total + tap_table[offset] * padded[:, offset : offset + frame_count]
+        total = total + tap_table[:, offset, None, None, :] * padded[:, offset : offset + frame_count]
     return total.astype(jnp.bfloat16)
 
 
@@ -68,22 +68,34 @@
     taps, mod, gain = spatial_taps[0], modulation[0], norm_gain[0]
     weight_in, weight_out, band = w_in[0], w_out[0], band_taps[0]
 
+    to_first = [(1, 0)]
+    second_taps, second_mod, second_gain, second_in, second_out = [
+        jnp.where(first, lax.ppermute(p, "section", perm=to_first), p)
+        for p in (taps, mod, gain, weight_in, weight_out)
+    ]
+
     def spatial(values):
         return spatial_block(values, taps, mod, gain, weight_in, weight_out)
+
+    def second_spatial(values):
+        return spatial_block(
+            values, second_taps, second_mod, second_gain, second_in, second_out
+        )
 
     first_mixed, first_pull = jax.vjp(spatial, clips)
     lead_in = jnp.where(first, first_mixed, cotangent)
     lead_taps = jnp.where(first, band, band[::-1])
-    lead_out = temporal(lead_in, lead_taps)
+    lead_out = temporal(lead_in, lead_taps[None])
 
-    first_acts = lax.ppermute(lead_out, "section", perm=[(0, 1)])
-    second_mixed, second_pull = jax.vjp(spatial, first_acts)
-    second_grad = second_pull(lead_out)[0]
+    swapped = lax.ppermute(lead_out, "section", perm=[(0, 1), (1, 0)])
+    first_acts = jnp.where(first, lead_out, swapped)
+    second_seed = jnp.where(first, swapped, lead_out)
+    second_mixed, second_pull = jax.vjp(second_spatial, first_acts)
+    second_grad = second_pull(second_seed)[0]
 
-    arrived_grad = lax.ppermute(second_grad, "section", perm=[(1, 0)])
-    tail_in = jnp.where(first, arrived_grad, second_mixed)
+    tail_in = jnp.where(first, second_grad, second_mixed)
     tail_taps = jnp.where(first, band[::-1], band)
-    tail_out = temporal(tail_in, tail_taps)
+    tail_out = temporal(tail_in, tail_taps[None])
     first_grad = first_pull(tail_out)[0]
 
     activations = jnp.where(first, lead_out, tail_out)

time: 193 us -> 187 us (0.969)
  blocking collectives: 51 us -> 25.5 us
  starting transfers between devices: 16.7 us -> 26.8 us
  waiting for transfers between devices: 74.7 us -> 79.9 us
  matrix products: 18.2 us -> 23.1 us
    all_to_all x2 -> x1, blocking collectives: 51 us -> 25.5 us  [temporal(): lax.all_to_all(banded, 'seq', split_axis=1, concat_axis=2, tiled=True)]
    all_to_all x0 -> x1, waiting for transfers between devices: none -> 11.9 us  [temporal(): lax.all_to_all(banded, 'seq', split_axis=1, concat_axis=2, tiled=True)]
    ppermute x2 -> x6, waiting for transfers between devices: 37.6 us -> 30.8 us  [the longest x1 30.7 us: on_device(): swapped = lax.ppermute(lead_out, 'section', perm=[(0, 1), (1, 0)])]
    all_to_all x0 -> x1, starting transfers between devices: none -> 5.47 us  [temporal(): lax.all_to_all(banded, 'seq', split_axis=1, concat_axis=2, tiled=True)]
    ppermute x2 -> x6, starting transfers between devices: 5.05 us -> 8.2 us  [the longest x5 6.64 us: on_device(): lax.ppermute(p, 'section', perm=to_first)]
    dot_general x4, matrix products: 16.1 us -> 18.7 us  [spatial_block(): jnp.dot(normed, w_in, preferred_element_type=jnp.float32)]
    dot_general x2, matrix products: 2.01 us -> 4.47 us  [spatial_block(): update = jnp.dot(hidden, w_out, preferred_element_type=jnp.float32)]
  transfers between devices with their start and end apart: 4 -> 9, of which waited for: 4 -> 5; matrix products, arithmetic and copies ran while one was open for 0% -> 4% of each run, Pallas kernels for 0% -> 0%
where the time goes in v4:
time: 187 us; the launch traced here: 186 us
  waiting for transfers between devices  79.9 us (43%)
  starting transfers between devices  26.8 us (14%)
  blocking collectives  25.5 us (14%)
  other arithmetic  25.1 us (13%)
  matrix products  23.1 us (12%)
  local copies, waits for them, and re-layouts  4.61 us (2%)
    all_to_all x2, waiting for transfers between devices, temporal(): lax.all_to_all(grouped, 'seq', split_axis=2, concat_axis=1, tiled=True)  37.2 us
    ppermute x1, waiting for transfers between devices, on_device(): swapped = lax.ppermute(lead_out, 'section', perm=[(0, 1), (1, 0)])  30.7 us
    all_to_all x1, blocking collectives, temporal(): lax.all_to_all(banded, 'seq', split_axis=1, concat_axis=2, tiled=True)  25.5 us
    dot_general x4, matrix products, spatial_block(): jnp.dot(normed, w_in, preferred_element_type=jnp.float32)  18.7 us
    all_to_all x2, starting transfers between devices, temporal(): lax.all_to_all(grouped, 'seq', split_axis=2, concat_axis=1, tiled=True)  13.1 us
    all_to_all x1, waiting for transfers between devices, temporal(): lax.all_to_all(banded, 'seq', split_axis=1, concat_axis=2, tiled=True)  11.9 us
    ppermute x5, starting transfers between devices, on_device(): lax.ppermute(p, 'section', perm=to_first)  6.64 us
    all_to_all x1, starting transfers between devices, temporal(): lax.all_to_all(banded, 'seq', split_axis=1, concat_axis=2, tiled=True)  5.47 us
  transfers between devices with their start and end apart: 9, of which 5 were waited for; matrix products, arithmetic and copies ran while one was open for 4% of the time, Pallas kernels for 0%

profile of v4, /device:TPU:0, one launch (start us, length us, event | category | flops | bytes accessed | tf_op | source)
XLA Modules:
  0.0 186.2 jit_solution(825775731859058858)
XLA Ops:
  3.5 1.9 %multiply_reduce_fusion.1 = (f32[2,32,16]{2,1,0:T(8,128)S(1)}, f32[2,1,32,16,384]{4,3,2,0,1:T(8,128)S(1)}) fusion(f32[2,384]{1,0:T(2,128)S(1)} %get-tuple-element.84, f32[2,384]{1,0:T(2,128)S(1)} %get-tuple-element.85, f32[384]{0:T(512)S(1)} %get-tuple-element.45, f32[384]{0:T(512)S(1)} %get-tuple-element.38, f32[384]{0:T(512)S(1)} %get-tuple-element.39, ...), kind=kLoop, calls=%fused_computation.161 | loop fusion | flops 8256512 | bytes 3169792 | tf_op jit(solution)/shard_map/jvp()/reduce_sum | solution.py:32
  5.9 4.0 %multiply_convert_fusion.1 = (bf16[1024,768]{1,0:T(8,128)(2,1)S(1)}, f32[1024,768]{1,0:T(8,128)}) fusion(bf16[1024,384]{1,0:T(8,128)(2,1)S(1)} %bitcast.163, bf16[1,384,768]{2,1,0:T(8,128)(2,1)} %param.13), kind=kOutput, calls=%fused_computation.46 | convolution fusion | flops 607911936 | bytes 6094848 | tf_op jit(solution)/shard_map/jvp()/dot_general | solution.py:36
  9.9 2.1 %fusion.105 = bf16[2,1,512,384]{3,2,0,1:T(8,128)(2,1)S(1)} fusion(bf16[2,512,768]{2,1,0:T(8,128)(2,1)S(1)} %bitcast.169, bf16[2,1,512,384]{3,2,1,0:T(8,128)(2,1)S(1)} %copy-done.16, pred[]{:T(512)S(6)} %eq.3, bf16[1,768,384]{2,1,0:T(8,128)(2,1)} %param.14, bf16[2,1,512,384]{3,2,1,0:T(8,128)(2,1)S(1)} %copy-done.11), kind=kOutput, calls=%fused_computation.166 | convolution fusion | flops 605552640 | bytes 4521985 | tf_op jit(solution)/shard_map/jvp()/dot_general | solution.py:39
  13.0 7.4 %all-to-all-start = ((bf16[2,1,16,32,384]{4,3,0,1,2:T(8,128)(2,1)}), bf16[2,1,16,32,384]{4,3,0,1,2:T(8,128)(2,1)S(1)}, u32[]{:S(2)}, u32[]{:S(2)}) async-start(bf16[2,1,16,32,384]{4,3,0,1,2:T(8,128)(2,1)} %copy.27), calls=%async_computation | async-start | bytes 1572864 | tf_op jit(solution)/shard_map/all_to_all | solution.py:58
  20.6 18.5 %all-to-all-done = bf16[2,1,16,32,384]{4,3,0,1,2:T(8,128)(2,1)S(1)} async-done(((bf16[2,1,16,32,384]{4,3,0,1,2:T(8,128)(2,1)}), bf16[2,1,16,32,384]{4,3,0,1,2:T(8,128)(2,1)S(1)}, u32[]{:S(2)}, u32[]{:S(2)}) %all-to-all-start) | async-done | bytes 786464 | tf_op jit(solution)/shard_map/all_to_all | solution.py:58
  39.3 1.8 fusion.109
  41.2 5.5 %all-to-all-start.1 = ((bf16[2,16,1,32,384]{4,3,0,2,1:T(8,128)(2,1)}), bf16[2,16,1,32,384]{4,3,0,2,1:T(8,128)(2,1)S(1)}, u32[]{:S(2)}, u32[]{:S(2)}) async-start(bf16[2,16,1,32,384]{4,3,0,2,1:T(8,128)(2,1)} %fusion.109), calls=%async_computation.1 | async-start | bytes 1572864 | tf_op jit(solution)/shard_map/all_to_all | solution.py:62
  49.3 1.3 collective-permute-start.1
  51.9 1.5 collective-permute-start.5
  53.5 11.9 %all-to-all-done.1 = bf16[2,16,1,32,384]{4,3,0,2,1:T(8,128)(2,1)S(1)} async-done(((bf16[2,16,1,32,384]{4,3,0,2,1:T(8,128)(2,1)}), bf16[2,16,1,32,384]{4,3,0,2,1:T(8,128)(2,1)S(1)}, u32[]{:S(2)}, u32[]{:S(2)}) %all-to-all-start.1) | async-done | bytes 786464 | tf_op jit(solution)/shard_map/all_to_all | solution.py:62
  65.4 1.6 collective-permute-start
  67.1 30.7 %collective-permute-done = bf16[2,1,512,384]{3,2,0,1:T(8,128)(2,1)S(1)} collective-permute-done((bf16[2,1,512,384]{3,2,0,1:T(8,128)(2,1)S(1)}, bf16[2,1,512,384]{3,2,0,1:T(8,128)(2,1)S(1)}, u32[]{:S(2)}, u32[]{:S(2)}) %collective-permute-start) | collective-permute-done | bytes 786464 | tf_op jit(solution)/shard_map/ppermute | solution.py:90
  99.0 1.9 %multiply_reduce_fusion = (f32[2,32,16]{2,1,0:T(8,128)S(1)}, f32[2,1,32,16,384]{4,3,2,0,1:T(8,128)S(1)}) fusion(f32[2,384]{1,0:T(2,128)S(1)} %get-tuple-element.82, f32[2,384]{1,0:T(2,128)S(1)} %get-tuple-element.83, f32[384]{0:T(512)S(1)} %get-tuple-element.19, f32[384]{0:T(512)S(1)} %get-tuple-element.20, f32[384]{0:T(512)S(1)} %get-tuple-element.21, ...), kind=kLoop, calls=%fused_computation.157 | loop fusion | flops 8256512 | bytes 3169792 | tf_op jit(solution)/shard_map/jvp()/reduce_sum | solution.py:32
  101.3 3.9 %fusion.111 = f32[1024,768]{1,0:T(8,128)} fusion(bf16[1024,384]{1,0:T(8,128)(2,1)S(1)} %fusion.90, bf16[384,768]{1,0:T(8,128)(2,1)} %collective-permute-done.5, pred[]{:T(512)S(6)} %eq.3, bf16[1,384,768]{2,1,0:T(8,128)(2,1)} %param.13), kind=kOutput, calls=%fused_computation.200 | convolution fusion | flops 604274688 | bytes 5111809 | tf_op jit(solution)/shard_map/jvp()/dot_general | solution.py:36
  105.2 5.5 %fusion.102 = bf16[1024,384]{1,0:T(8,128)(2,1)} fusion(f32[1024,768]{1,0:T(8,128)} %fusion.111, bf16[1024,384]{1,0:T(8,128)(2,1)} %bitcast.152, bf16[768,384]{1,0:T(8,128)(2,1)} %collective-permute-done.2, pred[]{:T(512)S(6)} %eq.3, bf16[384,768]{1,0:T(8,128)(2,1)} %collective-permute-done.5, bf16[1,768,384]{2,1,0:T(8,128)(2,1)} %param.14, ...), kind=kOutput, calls=%fused_computation.165 | convolution fusion | flops 1217593344 | bytes 7077889 | tf_op jit(solution)/shard_map/transpose(jvp())/dot_general | solution.py:36
  110.8 1.6 fusion.87
  113.0 1.3 broadcast_multiply_fusion
  116.9 2.4 %fusion.98 = f32[1024,384]{1,0:T(8,128)S(1)} fusion(f32[1024,768]{1,0:T(8,128)S(1)} %copy-done, bf16[768,384]{1,0:T(8,128)(2,1)} %collective-permute-done.2, pred[]{:T(512)S(6)} %eq.3, bf16[1,768,384]{2,1,0:T(8,128)(2,1)} %param.14), kind=kOutput, calls=%fused_computation.163 | convolution fusion | flops 608206848 | bytes 5898241 | tf_op jit(solution)/shard_map/jvp()/dot_general | solution.py:39
  120.9 5.7 %all-to-all-start.2 = ((bf16[2,1,16,32,384]{4,3,0,1,2:T(8,128)(2,1)}), bf16[2,1,16,32,384]{4,3,0,1,2:T(8,128)(2,1)}, u32[]{:S(2)}, u32[]{:S(2)}) async-start(bf16[2,1,16,32,384]{4,3,0,1,2:T(8,128)(2,1)} %copy.30), calls=%async_computation.2 | async-start | bytes 1572864 | tf_op jit(solution)/shard_map/all_to_all | solution.py:58
  126.7 18.7 %all-to-all-done.2 = bf16[2,1,16,32,384]{4,3,0,1,2:T(8,128)(2,1)} async-done(((bf16[2,1,16,32,384]{4,3,0,1,2:T(8,128)(2,1)}), bf16[2,1,16,32,384]{4,3,0,1,2:T(8,128)(2,1)}, u32[]{:S(2)}, u32[]{:S(2)}) %all-to-all-start.2) | async-done | bytes 786464 | tf_op jit(solution)/shard_map/all_to_all | solution.py:58
  145.4 1.3 bitcast_convert_fusion
  147.7 25.5 %all_to_all.16 = bf16[2,16,1,32,384]{4,3,0,2,1:T(8,128)(2,1)S(1)} all-to-all(bf16[2,16,1,32,384]{4,3,0,2,1:T(8,128)(2,1)S(1)} %fusion.108), channel_id=1, replica_groups=mesh['section'=2,'seq'=16] {'seq'}, dimensions={1} | all-to-all | bytes 1572864 | tf_op jit(solution)/shard_map/all_to_all | solution.py:62
  174.5 5.2 %fusion.99 = bf16[1024,384]{1,0:T(8,128)(2,1)} fusion(f32[1024,768]{1,0:T(8,128)} %get-tuple-element.81, bf16[1024,384]{1,0:T(8,128)(2,1)} %bitcast.159, bf16[1,768,384]{2,1,0:T(8,128)(2,1)} %param.14, bf16[1,384,768]{2,1,0:T(8,128)(2,1)} %param.13), kind=kOutput, calls=%fused_computation.164 | convolution fusion | flops 1217003520 | bytes 5898240 | tf_op jit(solution)/shard_map/transpose(jvp())/dot_general | solution.py:36
  179.7 1.6 fusion.84
  (83 shorter events, 22.2 us)
Async XLA Ops:
  3.5 2.1 %copy-start.15 = (f32[1,384]{1,0:T(1,128)S(1)}, f32[1,384]{1,0:T(1,128)}, u32[]{:S(2)}) copy-start(f32[1,384]{1,0:T(1,128)} %param.12) | copy-start | bytes 4612
  5.9 4.0 %copy-start.11 = (bf16[2,1,512,384]{3,2,1,0:T(8,128)(2,1)S(1)}, bf16[2,1,512,384]{3,2,1,0:T(8,128)(2,1)}, u32[]{:S(2)}) copy-start(bf16[2,1,512,384]{3,2,1,0:T(8,128)(2,1)} %param.8) | copy-start | bytes 2359300
  5.9 4.0 %copy-start.16 = (bf16[2,1,512,384]{3,2,1,0:T(8,128)(2,1)S(1)}, bf16[2,1,512,384]{3,2,1,0:T(8,128)(2,1)}, u32[]{:S(2)}) copy-start(bf16[2,1,512,384]{3,2,1,0:T(8,128)(2,1)} %param.9) | copy-start | bytes 2359300
  12.0 8.4 %copy-start.13 = (f32[1,9,384]{2,0,1:T(1,128)S(1)}, f32[1,9,384]{2,0,1:T(1,128)}, u32[]{:S(2)}) copy-start(f32[1,9,384]{2,0,1:T(1,128)} %param.15) | copy-start | bytes 41476
  13.0 26.1 %all-to-all-start = ((bf16[2,1,16,32,384]{4,3,0,1,2:T(8,128)(2,1)}), bf16[2,1,16,32,384]{4,3,0,1,2:T(8,128)(2,1)S(1)}, u32[]{:S(2)}, u32[]{:S(2)}) async-start(bf16[2,1,16,32,384]{4,3,0,1,2:T(8,128)(2,1)} %copy.27), calls=%async_computation | async-start | bytes 1572864 | tf_op jit(solution)/shard_map/all_to_all | solution.py:58
  39.3 8.6 %copy-start.14 = (f32[1,2,2,384]{3,2,1,0:T(2,128)S(1)}, f32[1,2,2,384]{3,2,1,0:T(2,128)}, u32[]{:S(2)}) copy-start(f32[1,2,2,384]{3,2,1,0:T(2,128)} %param.11) | copy-start | bytes 18436
  39.3 9.9 %copy-start.12 = (f32[1,9,384]{2,0,1:T(1,128)S(1)}, f32[1,9,384]{2,0,1:T(1,128)}, u32[]{:S(2)}) copy-start(f32[1,9,384]{2,0,1:T(1,128)} %param.10) | copy-start | bytes 41476
  41.2 24.2 %all-to-all-start.1 = ((bf16[2,16,1,32,384]{4,3,0,2,1:T(8,128)(2,1)}), bf16[2,16,1,32,384]{4,3,0,2,1:T(8,128)(2,1)S(1)}, u32[]{:S(2)}, u32[]{:S(2)}) async-start(bf16[2,16,1,32,384]{4,3,0,2,1:T(8,128)(2,1)} %fusion.109), calls=%async_computation.1 | async-start | bytes 1572864 | tf_op jit(solution)/shard_map/all_to_all | solution.py:62
  46.6 6.7 %collective-permute-start.4 = (f32[384]{0:T(512)S(1)}, f32[384]{0:T(512)S(1)}, u32[]{:S(2)}, u32[]{:S(2)}) collective-permute-start(f32[384]{0:T(512)S(1)} %reduce.17), channel_id=1, source_target_pairs={{16,0},{17,1},{18,2},{19,3},{20,4},{21,5},{22,6},{23,7},{24,8},{25... | collective-permute-start | bytes 4616 | tf_op jit(solution)/shard_map/ppermute | solution.py:73
  47.9 5.5 %collective-permute-start.3 = (f32[2,2,384]{2,1,0:T(2,128)S(1)}, f32[2,2,384]{2,1,0:T(2,128)S(1)}, u32[]{:S(2)}, u32[]{:S(2)}) collective-permute-start(f32[2,2,384]{2,1,0:T(2,128)S(1)} %bitcast.168), channel_id=1, source_target_pairs={{16,0},{17,1},{18,2},{19,3},{20,4},{21,5},{22,6},{23,7},{24,8},{25... | collective-permute-start | bytes 18440 | tf_op jit(solution)/shard_map/ppermute | solution.py:73
  49.3 17.7 %collective-permute-start.1 = (f32[9,384]{1,0:T(8,128)S(1)}, f32[9,384]{1,0:T(8,128)S(1)}, u32[]{:S(2)}, u32[]{:S(2)}) collective-permute-start(f32[9,384]{1,0:T(8,128)S(1)} %bitcast.166), channel_id=1, source_target_pairs={{16,0},{17,1},{18,2},{19,3},{20,4},{21,5},{22,6},{23,7},{24,8},{25... | collective-permute-start | bytes 41480 | tf_op jit(solution)/shard_map/ppermute | solution.py:73
  50.6 54.7 %collective-permute-start.2 = (bf16[768,384]{1,0:T(8,128)(2,1)}, bf16[768,384]{1,0:T(8,128)(2,1)}, u32[]{:S(2)}, u32[]{:S(2)}) collective-permute-start(bf16[768,384]{1,0:T(8,128)(2,1)} %bitcast.7), channel_id=1, source_target_pairs={{16,0},{17,1},{18,2},{19,3},{20,4},{21,5},{22,6},{23,7},{24,8},{25... | collective-permute-start | bytes 1769480 | tf_op jit(solution)/shard_map/ppermute | solution.py:73
  51.9 49.4 %collective-permute-start.5 = (bf16[384,768]{1,0:T(8,128)(2,1)}, bf16[384,768]{1,0:T(8,128)(2,1)}, u32[]{:S(2)}, u32[]{:S(2)}) collective-permute-start(bf16[384,768]{1,0:T(8,128)(2,1)} %bitcast.5), channel_id=1, source_target_pairs={{16,0},{17,1},{18,2},{19,3},{20,4},{21,5},{22,6},{23,7},{24,8},{25... | collective-permute-start | bytes 1769480 | tf_op jit(solution)/shard_map/ppermute | solution.py:73
  65.3 33.6 %copy-start.1 = (bf16[2,16,1,32,384]{4,3,0,2,1:T(8,128)(2,1)}, bf16[2,16,1,32,384]{4,3,0,2,1:T(8,128)(2,1)S(1)}, u32[]{:S(2)}) copy-start(bf16[2,16,1,32,384]{4,3,0,2,1:T(8,128)(2,1)S(1)} %all-to-all-done.1) | copy-start | bytes 2359300
  65.4 33.5 %copy-start.4 = (bf16[2,16,1,32,384]{4,3,1,0,2:T(8,128)(2,1)}, bf16[2,16,1,32,384]{4,3,1,0,2:T(8,128)(2,1)S(1)}, u32[]{:S(2)}) copy-start(bf16[2,16,1,32,384]{4,3,1,0,2:T(8,128)(2,1)S(1)} %copy.32) | copy-start | bytes 2359300
  65.4 32.4 %collective-permute-start = (bf16[2,1,512,384]{3,2,0,1:T(8,128)(2,1)S(1)}, bf16[2,1,512,384]{3,2,0,1:T(8,128)(2,1)S(1)}, u32[]{:S(2)}, u32[]{:S(2)}) collective-permute-start(bf16[2,1,512,384]{3,2,0,1:T(8,128)(2,1)S(1)} %bitcast.153), channel_id=1, source_target_pairs={{0,16},{16,0},{1,17},{17,1},{2,18},{18,2},{3,19},{19,3},{4,20},{20... | collective-permute-start | bytes 2359304 | tf_op jit(solution)/shard_map/ppermute | solution.py:90
  110.8 1.6 copy-start.6
  115.0 1.9 %copy-start = (f32[1024,768]{1,0:T(8,128)S(1)}, f32[1024,768]{1,0:T(8,128)}, u32[]{:S(2)}) copy-start(f32[1024,768]{1,0:T(8,128)} %fusion.111) | copy-start | bytes 9437188
  116.9 2.4 %copy-start.3 = (bf16[2,1,512,384]{3,2,0,1:T(8,128)(2,1)S(1)}, bf16[2,1,512,384]{3,2,0,1:T(8,128)(2,1)}, u32[]{:S(2)}) copy-start(bf16[2,1,512,384]{3,2,0,1:T(8,128)(2,1)} %get-tuple-element.70) | copy-start | bytes 2359300
  116.9 2.4 %copy-start.5 = (bf16[2,16,1,32,384]{4,3,1,0,2:T(8,128)(2,1)S(1)}, bf16[2,16,1,32,384]{4,3,1,0,2:T(8,128)(2,1)}, u32[]{:S(2)}) copy-start(bf16[2,16,1,32,384]{4,3,1,0,2:T(8,128)(2,1)} %copy-done.4) | copy-start | bytes 2359300
  116.9 2.4 %copy-start.9 = (bf16[2,1,512,384]{3,2,0,1:T(8,128)(2,1)S(1)}, bf16[2,1,512,384]{3,2,0,1:T(8,128)(2,1)}, u32[]{:S(2)}) copy-start(bf16[2,1,512,384]{3,2,0,1:T(8,128)(2,1)} %copy-done.8) | copy-start | bytes 2359300
  120.9 24.5 %all-to-all-start.2 = ((bf16[2,1,16,32,384]{4,3,0,1,2:T(8,128)(2,1)}), bf16[2,1,16,32,384]{4,3,0,1,2:T(8,128)(2,1)}, u32[]{:S(2)}, u32[]{:S(2)}) async-start(bf16[2,1,16,32,384]{4,3,0,1,2:T(8,128)(2,1)} %copy.30), calls=%async_computation.2 | async-start | bytes 1572864 | tf_op jit(solution)/shard_map/all_to_all | solution.py:58
  146.7 26.5 %copy-start.2 = (bf16[2,16,1,32,384]{4,3,0,2,1:T(8,128)(2,1)S(1)}, bf16[2,16,1,32,384]{4,3,0,2,1:T(8,128)(2,1)}, u32[]{:S(2)}) copy-start(bf16[2,16,1,32,384]{4,3,0,2,1:T(8,128)(2,1)} %copy-done.1) | copy-start | bytes 2359300
  179.7 1.6 copy-start.7
  (2 other events, 2.3 us)

commit v5 on v4

--- a/solution.py
+++ b/solution.py
@@ -69,9 +69,22 @@
     weight_in, weight_out, band = w_in[0], w_out[0], band_taps[0]
 
     to_first = [(1, 0)]
-    second_taps, second_mod, second_gain, second_in, second_out = [
+    core = lax.axis_index("seq") % 2
+    siblings = [(q, q ^ 1) for q in range(lax.axis_size("seq"))]
+
+    def fetch_halves(p):
+        half = p.shape[0] // 2
+        mine = lax.dynamic_slice_in_dim(p, core * half, half, 0)
+        got = lax.ppermute(mine, "section", perm=to_first)
+        other = lax.ppermute(got, "seq", perm=siblings)
+        return jnp.where(core == 0, jnp.concatenate([got, other]), jnp.concatenate([other, got]))
+
+    second_taps, second_mod, second_gain = [
         jnp.where(first, lax.ppermute(p, "section", perm=to_first), p)
-        for p in (taps, mod, gain, weight_in, weight_out)
+        for p in (taps, mod, gain)
+    ]
+    second_in, second_out = [
+        jnp.where(first, fetch_halves(p), p) for p in (weight_in, weight_out)
     ]
 
     def spatial(values):

time: 187 us -> 172 us (0.920)
  waiting for transfers between devices: 79.9 us -> 66.1 us
  local copies, waits for them, and re-layouts: 4.61 us -> 7.71 us
  other arithmetic: 25.1 us -> 22.3 us
  matrix products: 23.1 us -> 21 us
    ppermute x1, waiting for transfers between devices: 30.7 us -> 16.9 us  [on_device(): swapped = lax.ppermute(lead_out, 'section', perm=[(0, 1), (1, 0)])]
    ppermute x0 -> x4, starting transfers between devices: none -> 2.84 us  [the longest x2 2.76 us: fetch_halves(): got = lax.ppermute(mine, 'section', perm=to_first)]
    ppermute x5 -> x3, starting transfers between devices: 6.64 us -> 3.88 us  [on_device(): lax.ppermute(p, 'section', perm=to_first)]
    unnamed x38 -> x40, local copies, waits for them, and re-layouts: 1.23 us -> 3.29 us
  transfers between devices with their start and end apart: 9 -> 11, of which waited for: 5 -> 5; matrix products, arithmetic and copies ran while one was open for 4% -> 6% of each run, Pallas kernels for 0% -> 0%
where the time goes in v5:
time: 172 us; the launch traced here: 170 us
  waiting for transfers between devices  66.1 us (38%)
  starting transfers between devices  26.7 us (16%)
  blocking collectives  25.5 us (15%)
  other arithmetic  22.3 us (13%)
  matrix products  21 us (12%)
  local copies, waits for them, and re-layouts  7.71 us (4%)
    all_to_all x2, waiting for transfers between devices, temporal(): lax.all_to_all(grouped, 'seq', split_axis=2, concat_axis=1, tiled=True)  37.2 us
    all_to_all x1, blocking collectives, temporal(): lax.all_to_all(banded, 'seq', split_axis=1, concat_axis=2, tiled=True)  25.5 us
    dot_general x4, matrix products, spatial_block(): jnp.dot(normed, w_in, preferred_element_type=jnp.float32)  17.7 us
    ppermute x1, waiting for transfers between devices, on_device(): swapped = lax.ppermute(lead_out, 'section', perm=[(0, 1), (1, 0)])  16.9 us
    all_to_all x2, starting transfers between devices, temporal(): lax.all_to_all(grouped, 'seq', split_axis=2, concat_axis=1, tiled=True)  12.9 us
    all_to_all x1, waiting for transfers between devices, temporal(): lax.all_to_all(banded, 'seq', split_axis=1, concat_axis=2, tiled=True)  10.9 us
    all_to_all x1, starting transfers between devices, temporal(): lax.all_to_all(banded, 'seq', split_axis=1, concat_axis=2, tiled=True)  5.47 us
    ppermute x3, starting transfers between devices, on_device(): lax.ppermute(p, 'section', perm=to_first)  3.88 us
  transfers between devices with their start and end apart: 11, of which 5 were waited for; matrix products, arithmetic and copies ran while one was open for 6% of the time, Pallas kernels for 0%

profile of v5, /device:TPU:0, one launch (start us, length us, event | category | flops | bytes accessed | tf_op | source)
XLA Modules:
  0.0 170.5 jit_solution(15138330302096489122)
XLA Ops:
  3.5 1.9 %multiply_reduce_fusion.1 = (f32[2,32,16]{2,1,0:T(8,128)S(1)}, f32[2,1,32,16,384]{4,3,2,0,1:T(8,128)S(1)}) fusion(f32[2,384]{1,0:T(2,128)S(1)} %get-tuple-element.84, f32[2,384]{1,0:T(2,128)S(1)} %get-tuple-element.85, f32[384]{0:T(512)S(1)} %get-tuple-element.45, f32[384]{0:T(512)S(1)} %get-tuple-element.38, f32[384]{0:T(512)S(1)} %get-tuple-element.39, ...), kind=kLoop, calls=%fused_computation.162 | loop fusion | flops 8256512 | bytes 3169792 | tf_op jit(solution)/shard_map/jvp()/reduce_sum | solution.py:32
  6.6 2.8 %multiply_convert_fusion.1 = (bf16[1024,768]{1,0:T(8,128)(2,1)S(1)}, f32[1024,768]{1,0:T(8,128)}) fusion(bf16[1024,384]{1,0:T(8,128)(2,1)S(1)} %bitcast.167, bf16[1,384,768]{2,1,0:T(8,128)(2,1)S(1)} %copy-done.8), kind=kOutput, calls=%fused_computation.46 | convolution fusion | flops 607911936 | bytes 6094848 | tf_op jit(solution)/shard_map/jvp()/dot_general | solution.py:36
  11.4 7.4 %all-to-all-start = ((bf16[2,1,16,32,384]{4,3,0,1,2:T(8,128)(2,1)}), bf16[2,1,16,32,384]{4,3,0,1,2:T(8,128)(2,1)S(1)}, u32[]{:S(2)}, u32[]{:S(2)}) async-start(bf16[2,1,16,32,384]{4,3,0,1,2:T(8,128)(2,1)} %copy.27), calls=%async_computation | async-start | bytes 1572864 | tf_op jit(solution)/shard_map/all_to_all | solution.py:58
  19.0 18.5 %all-to-all-done = bf16[2,1,16,32,384]{4,3,0,1,2:T(8,128)(2,1)S(1)} async-done(((bf16[2,1,16,32,384]{4,3,0,1,2:T(8,128)(2,1)}), bf16[2,1,16,32,384]{4,3,0,1,2:T(8,128)(2,1)S(1)}, u32[]{:S(2)}, u32[]{:S(2)}) %all-to-all-start) | async-done | bytes 786464 | tf_op jit(solution)/shard_map/all_to_all | solution.py:58
  37.7 1.8 %fusion.110 = bf16[2,16,1,32,384]{4,3,0,2,1:T(8,128)(2,1)} fusion(f32[2,16,32,384]{3,2,0,1:T(8,128)S(1)} %bitcast_convert_fusion.1, f32[384]{0:T(512)S(1)} %get-tuple-element.29, f32[384]{0:T(512)S(1)} %get-tuple-element.30, f32[384]{0:T(512)S(1)} %get-tuple-element.31, f32[384]{0:T(512)S(1)} %get-tuple-element.32, f32[384]{0:T(512)S(1)} %get-tuple-element.33, ...), kind=kLoop, calls=%fused_computation.196 | loop fusion | flops 7471104 | bytes 2373120 | tf_op jit(solution)/shard_map/reshape | solution.py:61
  39.6 5.5 %all-to-all-start.1 = ((bf16[2,16,1,32,384]{4,3,0,2,1:T(8,128)(2,1)}), bf16[2,16,1,32,384]{4,3,0,2,1:T(8,128)(2,1)S(1)}, u32[]{:S(2)}, u32[]{:S(2)}) async-start(bf16[2,16,1,32,384]{4,3,0,2,1:T(8,128)(2,1)} %fusion.110), calls=%async_computation.1 | async-start | bytes 1572864 | tf_op jit(solution)/shard_map/all_to_all | solution.py:62
  45.1 1.3 collective-permute-start.5
  46.4 1.3 collective-permute-start.4
  47.7 1.3 collective-permute-start.1
  49.0 1.3 collective-permute-start.2
  51.3 1.5 collective-permute-start.6
  52.9 10.9 %all-to-all-done.1 = bf16[2,16,1,32,384]{4,3,0,2,1:T(8,128)(2,1)S(1)} async-done(((bf16[2,16,1,32,384]{4,3,0,2,1:T(8,128)(2,1)}), bf16[2,16,1,32,384]{4,3,0,2,1:T(8,128)(2,1)S(1)}, u32[]{:S(2)}, u32[]{:S(2)}) %all-to-all-start.1) | async-done | bytes 786464 | tf_op jit(solution)/shard_map/all_to_all | solution.py:62
  63.8 1.6 collective-permute-start
  66.7 16.9 %collective-permute-done = bf16[2,1,512,384]{3,2,0,1:T(8,128)(2,1)S(1)} collective-permute-done((bf16[2,1,512,384]{3,2,0,1:T(8,128)(2,1)S(1)}, bf16[2,1,512,384]{3,2,0,1:T(8,128)(2,1)S(1)}, u32[]{:S(2)}, u32[]{:S(2)}) %collective-permute-start) | collective-permute-done | bytes 786464 | tf_op jit(solution)/shard_map/ppermute | solution.py:103
  84.8 1.9 %multiply_reduce_fusion = (f32[2,32,16]{2,1,0:T(8,128)S(1)}, f32[2,1,32,16,384]{4,3,2,0,1:T(8,128)S(1)}) fusion(f32[2,384]{1,0:T(2,128)S(1)} %get-tuple-element.86, f32[2,384]{1,0:T(2,128)S(1)} %get-tuple-element.87, f32[384]{0:T(512)S(1)} %get-tuple-element.19, f32[384]{0:T(512)S(1)} %get-tuple-element.20, f32[384]{0:T(512)S(1)} %get-tuple-element.21, ...), kind=kLoop, calls=%fused_computation.158 | loop fusion | flops 8256512 | bytes 3169792 | tf_op jit(solution)/shard_map/jvp()/reduce_sum | solution.py:32
  87.9 4.8 %multiply_convert_fusion = (bf16[1024,768]{1,0:T(8,128)(2,1)}, f32[1024,768]{1,0:T(8,128)}) fusion(bf16[1024,384]{1,0:T(8,128)(2,1)S(1)} %bitcast.166, bf16[1,384,768]{2,1,0:T(8,128)(2,1)S(1)} %copy-done.9, bf16[1,192,768]{2,1,0:T(8,128)(2,1)} %bitcast.28, bf16[1,192,768]{2,1,0:T(8,128)(2,1)} %bitcast.27, pred[]{:T(512)S(6)} %eq.10, pred[]{:T(512)S(6)} %eq.9), kind=kOutput, calls=%fused_computation.44 | convolution fusion | flops 610861056 | bytes 6684674 | tf_op jit(solution)/shard_map/jvp()/dot_general | solution.py:36
  92.6 5.8 %fusion.103 = bf16[1024,384]{1,0:T(8,128)(2,1)} fusion(f32[1024,768]{1,0:T(8,128)} %get-tuple-element.83, bf16[1024,384]{1,0:T(8,128)(2,1)} %bitcast.162, bf16[192,768]{1,0:T(8,128)(2,1)} %collective-permute-done.7, bf16[192,768]{1,0:T(8,128)(2,1)} %collective-permute-done.6, bf16[1,384,768]{2,1,0:T(8,128)(2,1)} %param.13, pred[]{:T(512)S(6)} %eq.10, ...), kind=kOutput, calls=%fused_computation.165 | convolution fusion | flops 1222901760 | bytes 7077890 | tf_op jit(solution)/shard_map/transpose(jvp())/dot_general | solution.py:36
  98.5 1.6 fusion.87
  100.7 1.3 broadcast_multiply_fusion
  105.4 2.3 %fusion.107 = bf16[2,1,512,384]{3,2,0,1:T(8,128)(2,1)S(1)} fusion(bf16[2,1,512,384]{3,2,0,1:T(8,128)(2,1)S(1)} %bitcast_add_fusion.3, f32[2,1,512,384]{3,2,0,1:T(8,128)S(1)} %copy-done.3, bf16[2,512,768]{2,1,0:T(8,128)(2,1)S(1)} %bitcast.174, pred[]{:T(512)S(6)} %eq.9, bf16[1,768,384]{2,1,0:T(8,128)(2,1)S(1)} %copy-done.11, ...), kind=kOutput, calls=%fused_computation.167 | convolution fusion | flops 608108544 | bytes 5898242 | tf_op jit(solution)/shard_map/jvp()/dot_general | solution.py:39
  108.8 5.6 %all-to-all-start.2 = ((bf16[2,1,16,32,384]{4,3,0,1,2:T(8,128)(2,1)}), bf16[2,1,16,32,384]{4,3,0,1,2:T(8,128)(2,1)S(1)}, u32[]{:S(2)}, u32[]{:S(2)}) async-start(bf16[2,1,16,32,384]{4,3,0,1,2:T(8,128)(2,1)} %copy.30), calls=%async_computation.2 | async-start | bytes 1572864 | tf_op jit(solution)/shard_map/all_to_all | solution.py:58
  114.4 18.7 %all-to-all-done.2 = bf16[2,1,16,32,384]{4,3,0,1,2:T(8,128)(2,1)S(1)} async-done(((bf16[2,1,16,32,384]{4,3,0,1,2:T(8,128)(2,1)}), bf16[2,1,16,32,384]{4,3,0,1,2:T(8,128)(2,1)S(1)}, u32[]{:S(2)}, u32[]{:S(2)}) %all-to-all-start.2) | async-done | bytes 786464 | tf_op jit(solution)/shard_map/all_to_all | solution.py:58
  134.2 25.5 %all_to_all.16 = bf16[2,16,1,32,384]{4,3,0,2,1:T(8,128)(2,1)S(1)} all-to-all(bf16[2,16,1,32,384]{4,3,0,2,1:T(8,128)(2,1)S(1)} %fusion.109), channel_id=1, replica_groups=mesh['section'=2,'seq'=16] {'seq'}, dimensions={1} | all-to-all | bytes 1572864 | tf_op jit(solution)/shard_map/all_to_all | solution.py:62
  161.0 4.3 %fusion.100 = bf16[1024,384]{1,0:T(8,128)(2,1)S(1)} fusion(f32[1024,768]{1,0:T(8,128)} %get-tuple-element.81, bf16[1024,384]{1,0:T(8,128)(2,1)} %bitcast.163, bf16[1,768,384]{2,1,0:T(8,128)(2,1)} %param.14, bf16[1,384,768]{2,1,0:T(8,128)(2,1)} %param.13), kind=kOutput, calls=%fused_computation.164 | convolution fusion | flops 1217003520 | bytes 5898240 | tf_op jit(solution)/shard_map/transpose(jvp())/dot_general | solution.py:36
  (91 shorter events, 23.7 us)
Async XLA Ops:
  3.5 2.1 %copy-start.15 = (f32[1,384]{1,0:T(1,128)S(1)}, f32[1,384]{1,0:T(1,128)}, u32[]{:S(2)}) copy-start(f32[1,384]{1,0:T(1,128)} %param.12) | copy-start | bytes 4612
  6.5 2.8 %copy-start.7 = (bf16[2,1,512,384]{3,2,1,0:T(8,128)(2,1)S(1)}, bf16[2,1,512,384]{3,2,1,0:T(8,128)(2,1)}, u32[]{:S(2)}) copy-start(bf16[2,1,512,384]{3,2,1,0:T(8,128)(2,1)} %param.8) | copy-start | bytes 2359300
  6.5 2.8 %copy-start.10 = (bf16[1,768,384]{2,1,0:T(8,128)(2,1)S(1)}, bf16[1,768,384]{2,1,0:T(8,128)(2,1)}, u32[]{:S(2)}) copy-start(bf16[1,768,384]{2,1,0:T(8,128)(2,1)} %param.14) | copy-start | bytes 1769476
  6.5 2.8 %copy-start.16 = (bf16[2,1,512,384]{3,2,1,0:T(8,128)(2,1)S(1)}, bf16[2,1,512,384]{3,2,1,0:T(8,128)(2,1)}, u32[]{:S(2)}) copy-start(bf16[2,1,512,384]{3,2,1,0:T(8,128)(2,1)} %param.9) | copy-start | bytes 2359300
  10.4 8.4 %copy-start.13 = (f32[1,9,384]{2,0,1:T(1,128)S(1)}, f32[1,9,384]{2,0,1:T(1,128)}, u32[]{:S(2)}) copy-start(f32[1,9,384]{2,0,1:T(1,128)} %param.15) | copy-start | bytes 41476
  11.4 26.1 %all-to-all-start = ((bf16[2,1,16,32,384]{4,3,0,1,2:T(8,128)(2,1)}), bf16[2,1,16,32,384]{4,3,0,1,2:T(8,128)(2,1)S(1)}, u32[]{:S(2)}, u32[]{:S(2)}) async-start(bf16[2,1,16,32,384]{4,3,0,1,2:T(8,128)(2,1)} %copy.27), calls=%async_computation | async-start | bytes 1572864 | tf_op jit(solution)/shard_map/all_to_all | solution.py:58
  37.7 8.6 %copy-start.14 = (f32[1,2,2,384]{3,2,1,0:T(2,128)S(1)}, f32[1,2,2,384]{3,2,1,0:T(2,128)}, u32[]{:S(2)}) copy-start(f32[1,2,2,384]{3,2,1,0:T(2,128)} %param.11) | copy-start | bytes 18436
  37.7 9.9 %copy-start.12 = (f32[1,9,384]{2,0,1:T(1,128)S(1)}, f32[1,9,384]{2,0,1:T(1,128)}, u32[]{:S(2)}) copy-start(f32[1,9,384]{2,0,1:T(1,128)} %param.10) | copy-start | bytes 41476
  39.6 24.2 %all-to-all-start.1 = ((bf16[2,16,1,32,384]{4,3,0,2,1:T(8,128)(2,1)}), bf16[2,16,1,32,384]{4,3,0,2,1:T(8,128)(2,1)S(1)}, u32[]{:S(2)}, u32[]{:S(2)}) async-start(bf16[2,16,1,32,384]{4,3,0,2,1:T(8,128)(2,1)} %fusion.110), calls=%async_computation.1 | async-start | bytes 1572864 | tf_op jit(solution)/shard_map/all_to_all | solution.py:62
  45.1 7.8 %collective-permute-start.5 = (f32[384]{0:T(512)S(1)}, f32[384]{0:T(512)S(1)}, u32[]{:S(2)}, u32[]{:S(2)}) collective-permute-start(f32[384]{0:T(512)S(1)} %reduce.17), channel_id=1, source_target_pairs={{16,0},{17,1},{18,2},{19,3},{20,4},{21,5},{22,6},{23,7},{24,8},{25... | collective-permute-start | bytes 4616 | tf_op jit(solution)/shard_map/ppermute | solution.py:83
  46.4 6.5 %collective-permute-start.4 = (f32[2,2,384]{2,1,0:T(2,128)S(1)}, f32[2,2,384]{2,1,0:T(2,128)S(1)}, u32[]{:S(2)}, u32[]{:S(2)}) collective-permute-start(f32[2,2,384]{2,1,0:T(2,128)S(1)} %bitcast.173), channel_id=1, source_target_pairs={{16,0},{17,1},{18,2},{19,3},{20,4},{21,5},{22,6},{23,7},{24,8},{25... | collective-permute-start | bytes 18440 | tf_op jit(solution)/shard_map/ppermute | solution.py:83
  47.7 17.7 %collective-permute-start.1 = (f32[9,384]{1,0:T(8,128)S(1)}, f32[9,384]{1,0:T(8,128)S(1)}, u32[]{:S(2)}, u32[]{:S(2)}) collective-permute-start(f32[9,384]{1,0:T(8,128)S(1)} %bitcast.171), channel_id=1, source_target_pairs={{16,0},{17,1},{18,2},{19,3},{20,4},{21,5},{22,6},{23,7},{24,8},{25... | collective-permute-start | bytes 41480 | tf_op jit(solution)/shard_map/ppermute | solution.py:83
  49.0 16.5 %collective-permute-start.2 = (bf16[384,384]{1,0:T(8,128)(2,1)S(1)}, bf16[384,384]{1,0:T(8,128)(2,1)}, u32[]{:S(2)}, u32[]{:S(2)}) collective-permute-start(bf16[384,384]{1,0:T(8,128)(2,1)S(1)} %dynamic-slice_bitcast_fusion.1), channel_id=1, source_target_pairs={{16,0},{17,1},{18,2},{19,3},{20,4},{21,5},{22,6},{23,7},{24,8},{25... | collective-permute-start | bytes 884744 | tf_op jit(solution)/shard_map/ppermute | solution.py:78
  51.3 15.4 %collective-permute-start.6 = (bf16[192,768]{1,0:T(8,128)(2,1)S(1)}, bf16[192,768]{1,0:T(8,128)(2,1)}, u32[]{:S(2)}, u32[]{:S(2)}) collective-permute-start(bf16[192,768]{1,0:T(8,128)(2,1)S(1)} %dynamic-slice_bitcast_fusion), channel_id=1, source_target_pairs={{16,0},{17,1},{18,2},{19,3},{20,4},{21,5},{22,6},{23,7},{24,8},{25... | collective-permute-start | bytes 884744 | tf_op jit(solution)/shard_map/ppermute | solution.py:78
  63.8 21.0 %copy-start = (bf16[2,16,1,32,384]{4,3,0,2,1:T(8,128)(2,1)}, bf16[2,16,1,32,384]{4,3,0,2,1:T(8,128)(2,1)S(1)}, u32[]{:S(2)}) copy-start(bf16[2,16,1,32,384]{4,3,0,2,1:T(8,128)(2,1)S(1)} %all-to-all-done.1) | copy-start | bytes 2359300
  63.8 19.8 %collective-permute-start = (bf16[2,1,512,384]{3,2,0,1:T(8,128)(2,1)S(1)}, bf16[2,1,512,384]{3,2,0,1:T(8,128)(2,1)S(1)}, u32[]{:S(2)}, u32[]{:S(2)}) collective-permute-start(bf16[2,1,512,384]{3,2,0,1:T(8,128)(2,1)S(1)} %bitcast.161), channel_id=1, source_target_pairs={{0,16},{16,0},{1,17},{17,1},{2,18},{18,2},{3,19},{19,3},{4,20},{20... | collective-permute-start | bytes 2359304 | tf_op jit(solution)/shard_map/ppermute | solution.py:103
  65.5 27.1 %collective-permute-start.3 = (bf16[384,384]{1,0:T(8,128)(2,1)}, bf16[384,384]{1,0:T(8,128)(2,1)}, u32[]{:S(2)}, u32[]{:S(2)}) collective-permute-start(bf16[384,384]{1,0:T(8,128)(2,1)} %collective-permute-done.2), channel_id=1, source_target_pairs={{0,1},{1,0},{2,3},{3,2},{4,5},{5,4},{6,7},{7,6},{8,9},{9,8},{10,11... | collective-permute-start | bytes 884744 | tf_op jit(solution)/shard_map/ppermute | solution.py:79
  66.7 20.4 %collective-permute-start.7 = (bf16[192,768]{1,0:T(8,128)(2,1)}, bf16[192,768]{1,0:T(8,128)(2,1)}, u32[]{:S(2)}, u32[]{:S(2)}) collective-permute-start(bf16[192,768]{1,0:T(8,128)(2,1)} %collective-permute-done.6), channel_id=1, source_target_pairs={{0,1},{1,0},{2,3},{3,2},{4,5},{5,4},{6,7},{7,6},{8,9},{9,8},{10,11... | collective-permute-start | bytes 884744 | tf_op jit(solution)/shard_map/ppermute | solution.py:79
  84.8 1.9 %copy-start.2 = (f32[2,1,512,384]{3,2,0,1:T(8,128)}, f32[2,1,512,384]{3,2,0,1:T(8,128)S(1)}, u32[]{:S(2)}) copy-start(f32[2,1,512,384]{3,2,0,1:T(8,128)S(1)} %get-tuple-element.70) | copy-start | bytes 4718596
  98.5 1.6 copy-start.4
  102.7 1.6 copy-start.17
  103.8 1.7 copy-start.11
  108.8 24.3 %all-to-all-start.2 = ((bf16[2,1,16,32,384]{4,3,0,1,2:T(8,128)(2,1)}), bf16[2,1,16,32,384]{4,3,0,1,2:T(8,128)(2,1)S(1)}, u32[]{:S(2)}, u32[]{:S(2)}) async-start(bf16[2,1,16,32,384]{4,3,0,1,2:T(8,128)(2,1)} %copy.30), calls=%async_computation.2 | async-start | bytes 1572864 | tf_op jit(solution)/shard_map/all_to_all | solution.py:58
  133.3 26.5 %copy-start.1 = (bf16[2,16,1,32,384]{4,3,0,2,1:T(8,128)(2,1)S(1)}, bf16[2,16,1,32,384]{4,3,0,2,1:T(8,128)(2,1)}, u32[]{:S(2)}) copy-start(bf16[2,16,1,32,384]{4,3,0,2,1:T(8,128)(2,1)} %copy-done) | copy-start | bytes 2359300
  (5 other events, 5.9 us)

commit v6 on v5

--- a/solution.py
+++ b/solution.py
@@ -63,6 +63,22 @@
     return back.reshape(values.shape)
 
 
+def temporal_shared(values, tap_table):
+    clip_count, frame_count, pixel_count, channels = values.shape
+    groups = lax.axis_size("seq")
+    planes = lax.axis_size("section")
+    grouped = values.reshape(clip_count, frame_count, groups, pixel_count // groups, channels)
+    pixel_view = lax.all_to_all(grouped, "seq", split_axis=2, concat_axis=1, tiled=True)
+    pixel_view = pixel_view.reshape(clip_count, groups * frame_count, pixel_count // groups, channels)
+    banded = band_frames(pixel_view, tap_table)
+    banded = jnp.broadcast_to(
+        banded[:, None], (clip_count, planes) + banded.shape[1:]
+    ).reshape(clip_count, planes * groups * frame_count, 1, pixel_count // groups, channels)
+    back = lax.all_to_all(banded, ("section", "seq"), split_axis=1, concat_axis=2, tiled=True)
+    back = back.reshape(clip_count, frame_count, planes, pixel_count, channels)
+    return jnp.moveaxis(back, 2, 0)
+
+
 def on_device(clips, cotangent, spatial_taps, modulation, norm_gain, w_in, w_out, band_taps):
     first = lax.axis_index("section") == 0
     taps, mod, gain = spatial_taps[0], modulation[0], norm_gain[0]
@@ -83,9 +99,9 @@
         jnp.where(first, lax.ppermute(p, "section", perm=to_first), p)
         for p in (taps, mod, gain)
     ]
-    second_in, second_out = [
-        jnp.where(first, fetch_halves(p), p) for p in (weight_in, weight_out)
-    ]
+    second_in, second_out = lax.optimization_barrier(
+        [jnp.where(first, fetch_halves(p), p) for p in (weight_in, weight_out)]
+    )
 
     def spatial(values):
         return spatial_block(values, taps, mod, gain, weight_in, weight_out)
@@ -98,11 +114,7 @@
     first_mixed, first_pull = jax.vjp(spatial, clips)
     lead_in = jnp.where(first, first_mixed, cotangent)
     lead_taps = jnp.where(first, band, band[::-1])
-    lead_out = temporal(lead_in, lead_taps[None])
-
-    swapped = lax.ppermute(lead_out, "section", perm=[(0, 1), (1, 0)])
-    first_acts = jnp.where(first, lead_out, swapped)
-    second_seed = jnp.where(first, swapped, lead_out)
+    first_acts, second_seed = temporal_shared(lead_in, lead_taps[None])
     second_mixed, second_pull = jax.vjp(second_spatial, first_acts)
     second_grad = second_pull(second_seed)[0]
 
@@ -111,7 +123,7 @@
     tail_out = temporal(tail_in, tail_taps[None])
     first_grad = first_pull(tail_out)[0]
 
-    activations = jnp.where(first, lead_out, tail_out)
+    activations = jnp.where(first, first_acts, tail_out)
     input_grads = jnp.where(first, first_grad, second_grad)
     return (activations[None], input_grads[None])
 

time: 172 us -> 167 us (0.971)
  waiting for transfers between devices: 66.1 us -> 59.4 us
  local copies, waits for them, and re-layouts: 7.71 us -> 13.2 us
  matrix products: 21 us -> 16.5 us
  other arithmetic: 22.3 us -> 26.6 us
  starting transfers between devices: 26.7 us -> 23.5 us
    all_to_all x2 -> x1, waiting for transfers between devices: 37.2 us -> 18.6 us  [temporal(): lax.all_to_all(grouped, 'seq', split_axis=2, concat_axis=1, tiled=True)]
    ppermute x2, waiting for transfers between devices: 1.13 us -> 18.2 us  [fetch_halves(): got = lax.ppermute(mine, 'section', perm=to_first)]
    ppermute x1 -> x0, waiting for transfers between devices: 16.9 us -> none  [on_device(): swapped = lax.ppermute(lead_out, 'section', perm=[(0, 1), (1, 0)])]
    all_to_all x1 -> x2, waiting for transfers between devices: 10.9 us -> 21.7 us  [the longest x1 17.9 us: temporal_shared(): lax.all_to_all(grouped, 'seq', split_axis=2, concat_axis=1, tiled=True)]
    all_to_all x2 -> x1, starting transfers between devices: 12.9 us -> 4.1 us  [temporal(): lax.all_to_all(grouped, 'seq', split_axis=2, concat_axis=1, tiled=True)]
    all_to_all x1 -> x2, starting transfers between devices: 5.47 us -> 12.8 us  [the longest x1 7.39 us: temporal_shared(): lax.all_to_all(grouped, 'seq', split_axis=2, concat_axis=1, tiled=True)]
    dot_general x4, matrix products: 17.7 us -> 13.2 us  [spatial_block(): jnp.dot(normed, w_in, preferred_element_type=jnp.float32)]
    select_n x1 -> x3, other arithmetic: 1.16 us -> 4.62 us  [the longest x2 4.4 us: on_device(): jnp.where(first, fetch_halves(p), p)]
  transfers between devices with their start and end apart: 11 -> 10, of which waited for: 5 -> 6; matrix products, arithmetic and copies ran while one was open for 6% -> 6% of each run, Pallas kernels for 0% -> 0%
where the time goes in v6:
time: 167 us; the launch traced here: 166 us
  waiting for transfers between devices  59.4 us (36%)
  other arithmetic  26.6 us (16%)
  blocking collectives  25.5 us (15%)
  starting transfers between devices  23.5 us (14%)
  matrix products  16.5 us (10%)
  local copies, waits for them, and re-layouts  13.2 us (8%)
    all_to_all x1, blocking collectives, temporal(): lax.all_to_all(banded, 'seq', split_axis=1, concat_axis=2, tiled=True)  25.5 us
    all_to_all x1, waiting for transfers between devices, temporal(): lax.all_to_all(grouped, 'seq', split_axis=2, concat_axis=1, tiled=True)  18.6 us
    ppermute x2, waiting for transfers between devices, fetch_halves(): got = lax.ppermute(mine, 'section', perm=to_first)  18.2 us
    all_to_all x1, waiting for transfers between devices, temporal_shared(): lax.all_to_all(grouped, 'seq', split_axis=2, concat_axis=1, tiled=True)  17.9 us
    dot_general x4, matrix products, spatial_block(): jnp.dot(normed, w_in, preferred_element_type=jnp.float32)  13.2 us
    all_to_all x1, starting transfers between devices, temporal_shared(): lax.all_to_all(grouped, 'seq', split_axis=2, concat_axis=1, tiled=True)  7.39 us
    all_to_all x1, starting transfers between devices, temporal_shared(): lax.all_to_all(banded, ('section', 'seq'), split_axis=1, concat_axis=2, t...  5.39 us
    unnamed x88, local copies, waits for them, and re-layouts  4.65 us
  transfers between devices with their start and end apart: 10, of which 6 were waited for; matrix products, arithmetic and copies ran while one was open for 6% of the time, Pallas kernels for 0%

profile of v6, /device:TPU:0, one launch (start us, length us, event | category | flops | bytes accessed | tf_op | source)
XLA Modules:
  0.0 166.1 jit_solution(166186382292164111)
XLA Ops:
  3.6 1.9 %multiply_reduce_fusion.1 = (f32[2,32,16]{2,1,0:T(8,128)S(1)}, f32[2,1,32,16,384]{4,3,2,0,1:T(8,128)S(1)}) fusion(f32[2,384]{1,0:T(2,128)S(1)} %get-tuple-element.86, f32[2,384]{1,0:T(2,128)S(1)} %get-tuple-element.87, f32[384]{0:T(512)S(1)} %get-tuple-element.47, f32[384]{0:T(512)S(1)} %get-tuple-element.40, f32[384]{0:T(512)S(1)} %get-tuple-element.41, ...), kind=kLoop, calls=%fused_computation.162 | loop fusion | flops 8256512 | bytes 3169792 | tf_op jit(solution)/shard_map/jvp()/reduce_sum | solution.py:32
  6.7 2.8 %multiply_convert_fusion.1 = (bf16[1024,768]{1,0:T(8,128)(2,1)S(1)}, f32[1024,768]{1,0:T(8,128)}) fusion(bf16[1024,384]{1,0:T(8,128)(2,1)S(1)} %bitcast.152, bf16[1,384,768]{2,1,0:T(8,128)(2,1)S(1)} %copy-done.10), kind=kOutput, calls=%fused_computation.46 | convolution fusion | flops 607911936 | bytes 6094848 | tf_op jit(solution)/shard_map/jvp()/dot_general | solution.py:36
  11.6 7.4 %all-to-all-start = ((bf16[2,1,16,32,384]{4,3,0,1,2:T(8,128)(2,1)}), bf16[2,1,16,32,384]{4,3,0,1,2:T(8,128)(2,1)S(1)}, u32[]{:S(2)}, u32[]{:S(2)}) async-start(bf16[2,1,16,32,384]{4,3,0,1,2:T(8,128)(2,1)} %copy.29), calls=%async_computation | async-start | bytes 1572864 | tf_op jit(solution)/shard_map/all_to_all | solution.py:71
  19.8 17.9 %all-to-all-done = bf16[2,1,16,32,384]{4,3,0,1,2:T(8,128)(2,1)S(1)} async-done(((bf16[2,1,16,32,384]{4,3,0,1,2:T(8,128)(2,1)}), bf16[2,1,16,32,384]{4,3,0,1,2:T(8,128)(2,1)S(1)}, u32[]{:S(2)}, u32[]{:S(2)}) %all-to-all-start) | async-done | bytes 786464 | tf_op jit(solution)/shard_map/all_to_all | solution.py:71
  38.9 1.4 broadcast_in_dim.11
  40.3 5.4 %all-to-all-start.1 = ((bf16[2,32,1,32,384]{4,3,0,2,1:T(8,128)(2,1)}), bf16[2,32,1,32,384]{4,3,0,2,1:T(8,128)(2,1)S(1)}, u32[]{:S(2)}, u32[]{:S(2)}) async-start(bf16[2,32,1,32,384]{4,3,0,2,1:T(8,128)(2,1)} %bitcast.141), calls=%async_computation.1 | async-start | bytes 3145728 | tf_op jit(solution)/shard_map/all_to_all | solution.py:77
  45.7 1.3 collective-permute-start.6
  52.5 1.7 %dynamic-slice_bitcast_fusion.1 = bf16[192,768]{1,0:T(8,128)(2,1)} fusion(bf16[1,384,768]{2,1,0:T(8,128)(2,1)} %param.13, s32[]{:T(128)S(6)} %select_n.122), kind=kLoop, calls=%fused_computation.205 | loop fusion | bytes 589828 | tf_op jit(solution)/shard_map/dynamic_slice | solution.py:93
  54.2 1.5 collective-permute-start.1
  57.2 11.4 %collective-permute-done.3 = bf16[384,384]{1,0:T(8,128)(2,1)} collective-permute-done((bf16[384,384]{1,0:T(8,128)(2,1)S(1)}, bf16[384,384]{1,0:T(8,128)(2,1)}, u32[]{:S(2)}, u32[]{:S(2)}) %collective-permute-start.3) | collective-permute-done | bytes 294944 | tf_op jit(solution)/shard_map/ppermute | solution.py:94
  69.4 6.8 %collective-permute-done.1 = bf16[192,768]{1,0:T(8,128)(2,1)} collective-permute-done((bf16[192,768]{1,0:T(8,128)(2,1)}, bf16[192,768]{1,0:T(8,128)(2,1)}, u32[]{:S(2)}, u32[]{:S(2)}) %collective-permute-start.1) | collective-permute-done | bytes 294944 | tf_op jit(solution)/shard_map/ppermute | solution.py:94
  76.2 2.3 %fusion.109 = bf16[768,384]{1,0:T(8,128)(2,1)} fusion(bf16[384,384]{1,0:T(8,128)(2,1)S(1)} %collective-permute-done.4, bf16[384,384]{1,0:T(8,128)(2,1)} %collective-permute-done.3, bf16[1,768,384]{2,1,0:T(8,128)(2,1)} %param.14, pred[]{:T(512)S(6)} %eq.10, pred[]{:T(512)S(6)} %eq.9), kind=kLoop, calls=%fused_computation.198 | loop fusion | flops 2949120 | bytes 1769474 | tf_op jit(solution)/shard_map/jit(_where)/select_n | solution.py:103
  78.6 2.1 %fusion.108 = bf16[384,768]{1,0:T(8,128)(2,1)} fusion(bf16[192,768]{1,0:T(8,128)(2,1)S(1)} %collective-permute-done.2, bf16[192,768]{1,0:T(8,128)(2,1)} %collective-permute-done.1, bf16[1,384,768]{2,1,0:T(8,128)(2,1)S(1)} %copy-done.11, pred[]{:T(512)S(6)} %eq.10, pred[]{:T(512)S(6)} %eq.9), kind=kLoop, calls=%fused_computation.196 | loop fusion | flops 2949120 | bytes 1769474 | tf_op jit(solution)/shard_map/jit(_where)/select_n | solution.py:103
  80.6 3.8 %all-to-all-done.1 = bf16[2,32,1,32,384]{4,3,0,2,1:T(8,128)(2,1)S(1)} async-done(((bf16[2,32,1,32,384]{4,3,0,2,1:T(8,128)(2,1)}), bf16[2,32,1,32,384]{4,3,0,2,1:T(8,128)(2,1)S(1)}, u32[]{:S(2)}, u32[]{:S(2)}) %all-to-all-start.1) | async-done | bytes 1572896 | tf_op jit(solution)/shard_map/all_to_all | solution.py:77
  86.0 1.9 %multiply_reduce_fusion = (f32[2,32,16]{2,1,0:T(8,128)S(1)}, f32[2,1,32,16,384]{4,3,2,0,1:T(8,128)S(1)}) fusion(f32[2,384]{1,0:T(2,128)S(1)} %get-tuple-element.84, f32[2,384]{1,0:T(2,128)S(1)} %get-tuple-element.85, f32[384]{0:T(512)S(1)} %get-tuple-element.21, f32[384]{0:T(512)S(1)} %get-tuple-element.22, f32[384]{0:T(512)S(1)} %get-tuple-element.23, ...), kind=kLoop, calls=%fused_computation.158 | loop fusion | flops 8256512 | bytes 3169792 | tf_op jit(solution)/shard_map/jvp()/reduce_sum | solution.py:32
  90.2 2.2 %fusion.98 = f32[1024,384]{1,0:T(8,128)} fusion(bf16[768,384]{1,0:T(8,128)(2,1)S(1)} %copy-done.14, f32[1024,768]{1,0:T(8,128)S(1)} %fusion.126), kind=kOutput, calls=%fused_computation.164 | convolution fusion | flops 607911936 | bytes 5308416 | tf_op jit(solution)/shard_map/jvp()/dot_general | solution.py:39
  92.4 5.2 %fusion.102 = bf16[1024,384]{1,0:T(8,128)(2,1)} fusion(bf16[384,768]{1,0:T(8,128)(2,1)} %fusion.108, f32[1024,768]{1,0:T(8,128)} %copy-done.4, bf16[1024,384]{1,0:T(8,128)(2,1)} %bitcast.148, bf16[768,384]{1,0:T(8,128)(2,1)} %fusion.109), kind=kOutput, calls=%fused_computation.166 | convolution fusion | flops 1217003520 | bytes 5898240 | tf_op jit(solution)/shard_map/transpose(jvp())/dot_general | solution.py:36
  97.6 1.6 fusion.87
  99.8 1.3 broadcast_multiply_fusion
  105.0 4.1 %all-to-all-start.2 = ((bf16[2,1,16,32,384]{4,3,0,1,2:T(8,128)(2,1)}), bf16[2,1,16,32,384]{4,3,0,1,2:T(8,128)(2,1)S(1)}, u32[]{:S(2)}, u32[]{:S(2)}) async-start(bf16[2,1,16,32,384]{4,3,0,1,2:T(8,128)(2,1)} %copy.31), calls=%async_computation.2 | async-start | bytes 1572864 | tf_op jit(solution)/shard_map/all_to_all | solution.py:58
  109.2 18.6 %all-to-all-done.2 = bf16[2,1,16,32,384]{4,3,0,1,2:T(8,128)(2,1)S(1)} async-done(((bf16[2,1,16,32,384]{4,3,0,1,2:T(8,128)(2,1)}), bf16[2,1,16,32,384]{4,3,0,1,2:T(8,128)(2,1)S(1)}, u32[]{:S(2)}, u32[]{:S(2)}) %all-to-all-start.2) | async-done | bytes 786464 | tf_op jit(solution)/shard_map/all_to_all | solution.py:58
  129.0 25.5 %all_to_all.16 = bf16[2,16,1,32,384]{4,3,0,2,1:T(8,128)(2,1)S(1)} all-to-all(bf16[2,16,1,32,384]{4,3,0,2,1:T(8,128)(2,1)S(1)} %fusion.107), channel_id=1, replica_groups=mesh['section'=2,'seq'=16] {'seq'}, dimensions={1} | all-to-all | bytes 1572864 | tf_op jit(solution)/shard_map/all_to_all | solution.py:62
  155.5 4.3 %fusion.99 = bf16[1024,384]{1,0:T(8,128)(2,1)S(1)} fusion(f32[1024,768]{1,0:T(8,128)} %get-tuple-element.83, bf16[1024,384]{1,0:T(8,128)(2,1)} %bitcast.146, bf16[1,768,384]{2,1,0:T(8,128)(2,1)} %param.14, bf16[1,384,768]{2,1,0:T(8,128)(2,1)} %param.13), kind=kOutput, calls=%fused_computation.165 | convolution fusion | flops 1217003520 | bytes 5898240 | tf_op jit(solution)/shard_map/transpose(jvp())/dot_general | solution.py:36
  164.7 1.4 select_bitcast_fusion
  (140 shorter events, 30.9 us)
Async XLA Ops:
  2.3 3.3 %copy-start.22 = (f32[384]{0:T(512)}, f32[384]{0:T(512)S(1)}, u32[]{:S(2)}) copy-start(f32[384]{0:T(512)S(1)} %get-tuple-element.47) | copy-start | bytes 4612
  2.3 3.3 %copy-start.24 = (f32[384]{0:T(512)}, f32[384]{0:T(512)S(1)}, u32[]{:S(2)}) copy-start(f32[384]{0:T(512)S(1)} %get-tuple-element.39) | copy-start | bytes 4612
  2.3 3.3 %copy-start.26 = (f32[384]{0:T(512)}, f32[384]{0:T(512)S(1)}, u32[]{:S(2)}) copy-start(f32[384]{0:T(512)S(1)} %get-tuple-element.40) | copy-start | bytes 4612
  2.3 3.3 %copy-start.28 = (f32[384]{0:T(512)}, f32[384]{0:T(512)S(1)}, u32[]{:S(2)}) copy-start(f32[384]{0:T(512)S(1)} %get-tuple-element.41) | copy-start | bytes 4612
  2.3 3.3 %copy-start.30 = (f32[384]{0:T(512)}, f32[384]{0:T(512)S(1)}, u32[]{:S(2)}) copy-start(f32[384]{0:T(512)S(1)} %get-tuple-element.42) | copy-start | bytes 4612
  2.3 3.3 %copy-start.32 = (f32[384]{0:T(512)}, f32[384]{0:T(512)S(1)}, u32[]{:S(2)}) copy-start(f32[384]{0:T(512)S(1)} %get-tuple-element.43) | copy-start | bytes 4612
  2.3 3.3 %copy-start.34 = (f32[384]{0:T(512)}, f32[384]{0:T(512)S(1)}, u32[]{:S(2)}) copy-start(f32[384]{0:T(512)S(1)} %get-tuple-element.44) | copy-start | bytes 4612
  5.8 50.8 %copy-start.18 = (f32[384]{0:T(512)}, f32[384]{0:T(512)S(1)}, u32[]{:S(2)}) copy-start(f32[384]{0:T(512)S(1)} %reduce.17) | copy-start | bytes 4612
  10.6 8.4 %copy-start.17 = (f32[1,9,384]{2,0,1:T(1,128)S(1)}, f32[1,9,384]{2,0,1:T(1,128)}, u32[]{:S(2)}) copy-start(f32[1,9,384]{2,0,1:T(1,128)} %param.15) | copy-start | bytes 41476
  11.6 26.1 %all-to-all-start = ((bf16[2,1,16,32,384]{4,3,0,1,2:T(8,128)(2,1)}), bf16[2,1,16,32,384]{4,3,0,1,2:T(8,128)(2,1)S(1)}, u32[]{:S(2)}, u32[]{:S(2)}) async-start(bf16[2,1,16,32,384]{4,3,0,1,2:T(8,128)(2,1)} %copy.29), calls=%async_computation | async-start | bytes 1572864 | tf_op jit(solution)/shard_map/all_to_all | solution.py:71
  40.3 6.7 %copy-start.21 = (f32[1,2,2,384]{3,2,1,0:T(2,128)S(1)}, f32[1,2,2,384]{3,2,1,0:T(2,128)}, u32[]{:S(2)}) copy-start(f32[1,2,2,384]{3,2,1,0:T(2,128)} %param.11) | copy-start | bytes 18436
  40.3 8.0 %copy-start.15 = (f32[1,9,384]{2,0,1:T(1,128)S(1)}, f32[1,9,384]{2,0,1:T(1,128)}, u32[]{:S(2)}) copy-start(f32[1,9,384]{2,0,1:T(1,128)} %param.10) | copy-start | bytes 41476
  40.3 44.1 %all-to-all-start.1 = ((bf16[2,32,1,32,384]{4,3,0,2,1:T(8,128)(2,1)}), bf16[2,32,1,32,384]{4,3,0,2,1:T(8,128)(2,1)S(1)}, u32[]{:S(2)}, u32[]{:S(2)}) async-start(bf16[2,32,1,32,384]{4,3,0,2,1:T(8,128)(2,1)} %bitcast.141), calls=%async_computation.1 | async-start | bytes 3145728 | tf_op jit(solution)/shard_map/all_to_all | solution.py:77
  45.7 11.0 %collective-permute-start.6 = (f32[384]{0:T(512)S(1)}, f32[384]{0:T(512)S(1)}, u32[]{:S(2)}, u32[]{:S(2)}) collective-permute-start(f32[384]{0:T(512)S(1)} %reduce.17), channel_id=1, source_target_pairs={{16,0},{17,1},{18,2},{19,3},{20,4},{21,5},{22,6},{23,7},{24,8},{25... | collective-permute-start | bytes 4616 | tf_op jit(solution)/shard_map/ppermute | solution.py:99
  47.0 10.2 %collective-permute-start.5 = (f32[2,2,384]{2,1,0:T(2,128)S(1)}, f32[2,2,384]{2,1,0:T(2,128)S(1)}, u32[]{:S(2)}, u32[]{:S(2)}) collective-permute-start(f32[2,2,384]{2,1,0:T(2,128)S(1)} %bitcast.155), channel_id=1, source_target_pairs={{16,0},{17,1},{18,2},{19,3},{20,4},{21,5},{22,6},{23,7},{24,8},{25... | collective-permute-start | bytes 18440 | tf_op jit(solution)/shard_map/ppermute | solution.py:99
  48.9 19.7 %collective-permute-start = (f32[9,384]{1,0:T(8,128)}, f32[9,384]{1,0:T(8,128)}, u32[]{:S(2)}, u32[]{:S(2)}) collective-permute-start(f32[9,384]{1,0:T(8,128)} %bitcast.132), channel_id=1, source_target_pairs={{16,0},{17,1},{18,2},{19,3},{20,4},{21,5},{22,6},{23,7},{24,8},{25... | collective-permute-start | bytes 41480 | tf_op jit(solution)/shard_map/ppermute | solution.py:99
  51.2 17.4 %collective-permute-start.3 = (bf16[384,384]{1,0:T(8,128)(2,1)S(1)}, bf16[384,384]{1,0:T(8,128)(2,1)}, u32[]{:S(2)}, u32[]{:S(2)}) collective-permute-start(bf16[384,384]{1,0:T(8,128)(2,1)S(1)} %dynamic-slice_bitcast_fusion), channel_id=1, source_target_pairs={{16,0},{17,1},{18,2},{19,3},{20,4},{21,5},{22,6},{23,7},{24,8},{25... | collective-permute-start | bytes 884744 | tf_op jit(solution)/shard_map/ppermute | solution.py:94
  54.2 22.0 %collective-permute-start.1 = (bf16[192,768]{1,0:T(8,128)(2,1)}, bf16[192,768]{1,0:T(8,128)(2,1)}, u32[]{:S(2)}, u32[]{:S(2)}) collective-permute-start(bf16[192,768]{1,0:T(8,128)(2,1)} %dynamic-slice_bitcast_fusion.1), channel_id=1, source_target_pairs={{16,0},{17,1},{18,2},{19,3},{20,4},{21,5},{22,6},{23,7},{24,8},{25... | collective-permute-start | bytes 884744 | tf_op jit(solution)/shard_map/ppermute | solution.py:94
  55.7 22.9 %copy-start.11 = (bf16[1,384,768]{2,1,0:T(8,128)(2,1)S(1)}, bf16[1,384,768]{2,1,0:T(8,128)(2,1)}, u32[]{:S(2)}) copy-start(bf16[1,384,768]{2,1,0:T(8,128)(2,1)} %param.13) | copy-start | bytes 1769476
  68.6 7.6 %collective-permute-start.4 = (bf16[384,384]{1,0:T(8,128)(2,1)}, bf16[384,384]{1,0:T(8,128)(2,1)S(1)}, u32[]{:S(2)}, u32[]{:S(2)}) collective-permute-start(bf16[384,384]{1,0:T(8,128)(2,1)} %collective-permute-done.3), channel_id=1, source_target_pairs={{0,1},{1,0},{2,3},{3,2},{4,5},{5,4},{6,7},{7,6},{8,9},{9,8},{10,11... | collective-permute-start | bytes 884744 | tf_op jit(solution)/shard_map/ppermute | solution.py:95
  76.2 2.4 %collective-permute-start.2 = (bf16[192,768]{1,0:T(8,128)(2,1)}, bf16[192,768]{1,0:T(8,128)(2,1)S(1)}, u32[]{:S(2)}, u32[]{:S(2)}) collective-permute-start(bf16[192,768]{1,0:T(8,128)(2,1)} %collective-permute-done.1), channel_id=1, source_target_pairs={{0,1},{1,0},{2,3},{3,2},{4,5},{5,4},{6,7},{7,6},{8,9},{9,8},{10,11... | collective-permute-start | bytes 884744 | tf_op jit(solution)/shard_map/ppermute | solution.py:95
  104.0 5.1 %copy-start.16 = (f32[1,9,384]{2,1,0:T(8,128)S(1)}, f32[1,9,384]{2,1,0:T(8,128)}, u32[]{:S(2)}) copy-start(f32[1,9,384]{2,1,0:T(8,128)} %get-tuple-element.76) | copy-start | bytes 41476
  105.0 22.8 %all-to-all-start.2 = ((bf16[2,1,16,32,384]{4,3,0,1,2:T(8,128)(2,1)}), bf16[2,1,16,32,384]{4,3,0,1,2:T(8,128)(2,1)S(1)}, u32[]{:S(2)}, u32[]{:S(2)}) async-start(bf16[2,1,16,32,384]{4,3,0,1,2:T(8,128)(2,1)} %copy.31), calls=%async_computation.2 | async-start | bytes 1572864 | tf_op jit(solution)/shard_map/all_to_all | solution.py:58
  155.5 4.3 %copy-start.19 = (f32[384]{0:T(512)S(1)}, f32[384]{0:T(512)}, u32[]{:S(2)}) copy-start(f32[384]{0:T(512)} %copy-done.18) | copy-start | bytes 4612
  (28 other events, 44.0 us)

commit v7 on v6

--- a/solution.py
+++ b/solution.py
@@ -63,12 +63,13 @@
     return back.reshape(values.shape)
 
 
-def temporal_shared(values, tap_table):
+def temporal_shared(values, tap_table, carried):
     clip_count, frame_count, pixel_count, channels = values.shape
     groups = lax.axis_size("seq")
     planes = lax.axis_size("section")
     grouped = values.reshape(clip_count, frame_count, groups, pixel_count // groups, channels)
     pixel_view = lax.all_to_all(grouped, "seq", split_axis=2, concat_axis=1, tiled=True)
+    pixel_view, carried = lax.optimization_barrier((pixel_view, carried))
     pixel_view = pixel_view.reshape(clip_count, groups * frame_count, pixel_count // groups, channels)
     banded = band_frames(pixel_view, tap_table)
     banded = jnp.broadcast_to(
@@ -76,7 +77,7 @@
     ).reshape(clip_count, planes * groups * frame_count, 1, pixel_count // groups, channels)
     back = lax.all_to_all(banded, ("section", "seq"), split_axis=1, concat_axis=2, tiled=True)
     back = back.reshape(clip_count, frame_count, planes, pixel_count, channels)
-    return jnp.moveaxis(back, 2, 0)
+    return jnp.moveaxis(back, 2, 0), carried
 
 
 def on_device(clips, cotangent, spatial_taps, modulation, norm_gain, w_in, w_out, band_taps):
@@ -99,22 +100,23 @@
         jnp.where(first, lax.ppermute(p, "section", perm=to_first), p)
         for p in (taps, mod, gain)
     ]
-    second_in, second_out = lax.optimization_barrier(
-        [jnp.where(first, fetch_halves(p), p) for p in (weight_in, weight_out)]
+    second_in, second_out = [
+        jnp.where(first, fetch_halves(p), p) for p in (weight_in, weight_out)
+    ]
+
+    def spatial_first(values):
+        return spatial_block(values, taps, mod, gain, weight_in, weight_out)
+
+    first_mixed, first_pull = jax.vjp(spatial_first, clips)
+    lead_in = jnp.where(first, first_mixed, cotangent)
+    lead_taps = jnp.where(first, band, band[::-1])
+    (first_acts, second_seed), second_params = temporal_shared(
+        lead_in, lead_taps[None], (second_taps, second_mod, second_gain, second_in, second_out)
     )
 
-    def spatial(values):
-        return spatial_block(values, taps, mod, gain, weight_in, weight_out)
+    def second_spatial(values):
+        return spatial_block(values, *second_params)
 
-    def second_spatial(values):
-        return spatial_block(
-            values, second_taps, second_mod, second_gain, second_in, second_out
-        )
-
-    first_mixed, first_pull = jax.vjp(spatial, clips)
-    lead_in = jnp.where(first, first_mixed, cotangent)
-    lead_taps = jnp.where(first, band, band[::-1])
-    first_acts, second_seed = temporal_shared(lead_in, lead_taps[None])
     second_mixed, second_pull = jax.vjp(second_spatial, first_acts)
     second_grad = second_pull(second_seed)[0]
 

time: 167 us -> 185 us (1.11)
  other arithmetic: 26.6 us -> 32 us
  local copies, waits for them, and re-layouts: 13.2 us -> 18 us
  starting transfers between devices: 23.5 us -> 27.8 us
  waiting for transfers between devices: 59.4 us -> 61.7 us
    all_to_all x1, waiting for transfers between devices: 3.75 us -> 38.3 us  [temporal_shared(): lax.all_to_all(banded, ('section', 'seq'), split_axis=1, concat_axis=2, t...]
    ppermute x2, waiting for transfers between devices: 18.2 us -> 0.01 us  [fetch_halves(): got = lax.ppermute(mine, 'section', perm=to_first)]
    all_to_all x1, waiting for transfers between devices: 17.9 us -> 4.71 us  [temporal_shared(): lax.all_to_all(grouped, 'seq', split_axis=2, concat_axis=1, tiled=True)]
    all_to_all x1, starting transfers between devices: 5.39 us -> 9.86 us  [temporal_shared(): lax.all_to_all(banded, ('section', 'seq'), split_axis=1, concat_axis=2, t...]
    select_n x3, other arithmetic: 1.34 us -> 3.91 us  [on_device(): jnp.where(first, lax.ppermute(p, 'section', perm=to_first), p)]
    rev x1, local copies, waits for them, and re-layouts: 0.1 us -> 2 us  [on_device(): lead_taps = jnp.where(first, band, band[::-1])]
    unnamed x88 -> x117, local copies, waits for them, and re-layouts: 4.65 us -> 6.3 us
  transfers between devices with their start and end apart: 10 -> 10, of which waited for: 6 -> 3; matrix products, arithmetic and copies ran while one was open for 6% -> 15% of each run, Pallas kernels for 0% -> 0%
where the time goes in v7:
time: 185 us; the launch traced here: 183 us
  waiting for transfers between devices  61.7 us (33%)
  other arithmetic  32 us (17%)
  starting transfers between devices  27.8 us (15%)
  blocking collectives  25.5 us (14%)
  local copies, waits for them, and re-layouts  18 us (10%)
  matrix products  16.5 us (9%)
    all_to_all x1, waiting for transfers between devices, temporal_shared(): lax.all_to_all(banded, ('section', 'seq'), split_axis=1, concat_axis=2, t...  38.3 us
    all_to_all x1, blocking collectives, temporal(): lax.all_to_all(banded, 'seq', split_axis=1, concat_axis=2, tiled=True)  25.5 us
    all_to_all x1, waiting for transfers between devices, temporal(): lax.all_to_all(grouped, 'seq', split_axis=2, concat_axis=1, tiled=True)  18.6 us
    dot_general x4, matrix products, spatial_block(): jnp.dot(normed, w_in, preferred_element_type=jnp.float32)  13.2 us
    all_to_all x1, starting transfers between devices, temporal_shared(): lax.all_to_all(banded, ('section', 'seq'), split_axis=1, concat_axis=2, t...  9.86 us
    all_to_all x1, starting transfers between devices, temporal_shared(): lax.all_to_all(grouped, 'seq', split_axis=2, concat_axis=1, tiled=True)  7.38 us
    unnamed x117, local copies, waits for them, and re-layouts  6.3 us
    all_to_all x1, waiting for transfers between devices, temporal_shared(): lax.all_to_all(grouped, 'seq', split_axis=2, concat_axis=1, tiled=True)  4.71 us
  transfers between devices with their start and end apart: 10, of which 3 were waited for; matrix products, arithmetic and copies ran while one was open for 15% of the time, Pallas kernels for 0%

profile of v7, /device:TPU:0, one launch (start us, length us, event | category | flops | bytes accessed | tf_op | source)
XLA Modules:
  0.0 183.1 jit_solution(7821196938935582806)
XLA Ops:
  0.6 1.4 reduce.17
  7.2 1.7 dynamic-slice_bitcast_fusion
  10.2 1.7 dynamic-slice_bitcast_fusion.1
  15.1 1.9 %multiply_reduce_fusion.1 = (f32[2,32,16]{2,1,0:T(8,128)S(1)}, f32[2,1,32,16,384]{4,3,2,0,1:T(8,128)S(1)}) fusion(f32[2,384]{1,0:T(2,128)S(1)} %get-tuple-element.92, f32[2,384]{1,0:T(2,128)S(1)} %get-tuple-element.93, f32[384]{0:T(512)S(1)} %get-tuple-element.55, f32[384]{0:T(512)S(1)} %get-tuple-element.48, f32[384]{0:T(512)S(1)} %get-tuple-element.49, ...), kind=kLoop, calls=%fused_computation.162 | loop fusion | flops 8256512 | bytes 3169792 | tf_op jit(solution)/shard_map/jvp()/reduce_sum | solution.py:32
  18.8 2.8 %multiply_convert_fusion.1 = (bf16[1024,768]{1,0:T(8,128)(2,1)S(1)}, f32[1024,768]{1,0:T(8,128)}) fusion(bf16[1024,384]{1,0:T(8,128)(2,1)S(1)} %bitcast.156, bf16[1,384,768]{2,1,0:T(8,128)(2,1)S(1)} %copy-done.10), kind=kOutput, calls=%fused_computation.46 | convolution fusion | flops 607911936 | bytes 6094848 | tf_op jit(solution)/shard_map/jvp()/dot_general | solution.py:36
  23.7 7.4 %all-to-all-start = ((bf16[2,1,16,32,384]{4,3,0,1,2:T(8,128)(2,1)}), bf16[2,1,16,32,384]{4,3,0,1,2:T(8,128)(2,1)S(1)}, u32[]{:S(2)}, u32[]{:S(2)}) async-start(bf16[2,1,16,32,384]{4,3,0,1,2:T(8,128)(2,1)} %copy.29), calls=%async_computation | async-start | bytes 1572864 | tf_op jit(solution)/shard_map/all_to_all | solution.py:71
  32.4 2.0 %rev.4 = f32[9,384]{1,0:T(8,128)} reverse(f32[9,384]{1,0:T(8,128)} %bitcast.157), dimensions={0} | reverse | bytes 27648 | tf_op jit(solution)/shard_map/rev | solution.py:112
  34.4 1.3 select_bitcast_fusion.2
  39.4 1.4 broadcast_select_fusion
  40.8 2.1 %fusion.109 = bf16[768,384]{1,0:T(8,128)(2,1)} fusion(bf16[384,384]{1,0:T(8,128)(2,1)S(1)} %collective-permute-done.6, bf16[384,384]{1,0:T(8,128)(2,1)} %collective-permute-done.5, bf16[1,768,384]{2,1,0:T(8,128)(2,1)S(1)} %copy-done.11, pred[]{:T(512)S(6)} %eq.10, pred[]{:T(512)S(6)} %eq.9), kind=kLoop, calls=%fused_computation.198 | loop fusion | flops 2949120 | bytes 1769474 | tf_op jit(solution)/shard_map/jit(_where)/select_n | solution.py:104
  42.9 2.1 %fusion.108 = bf16[384,768]{1,0:T(8,128)(2,1)} fusion(bf16[192,768]{1,0:T(8,128)(2,1)S(1)} %collective-permute-done.4, bf16[192,768]{1,0:T(8,128)(2,1)} %collective-permute-done.3, bf16[1,384,768]{2,1,0:T(8,128)(2,1)S(1)} %copy-done.10, pred[]{:T(512)S(6)} %eq.10, pred[]{:T(512)S(6)} %eq.9), kind=kLoop, calls=%fused_computation.196 | loop fusion | flops 2949120 | bytes 1769474 | tf_op jit(solution)/shard_map/jit(_where)/select_n | solution.py:104
  45.0 4.7 %all-to-all-done = bf16[2,1,16,32,384]{4,3,0,1,2:T(8,128)(2,1)S(1)} async-done(((bf16[2,1,16,32,384]{4,3,0,1,2:T(8,128)(2,1)}), bf16[2,1,16,32,384]{4,3,0,1,2:T(8,128)(2,1)S(1)}, u32[]{:S(2)}, u32[]{:S(2)}) %all-to-all-start) | async-done | bytes 786464 | tf_op jit(solution)/shard_map/all_to_all | solution.py:71
  51.0 1.4 broadcast_in_dim.11
  52.4 9.9 %all-to-all-start.1 = ((bf16[2,32,1,32,384]{4,3,0,2,1:T(8,128)(2,1)}), bf16[2,32,1,32,384]{4,3,0,2,1:T(8,128)(2,1)S(1)}, u32[]{:S(2)}, u32[]{:S(2)}) async-start(bf16[2,32,1,32,384]{4,3,0,2,1:T(8,128)(2,1)} %bitcast.144), calls=%async_computation.1 | async-start | bytes 3145728 | tf_op jit(solution)/shard_map/all_to_all | solution.py:78
  62.4 38.3 %all-to-all-done.1 = bf16[2,32,1,32,384]{4,3,0,2,1:T(8,128)(2,1)S(1)} async-done(((bf16[2,32,1,32,384]{4,3,0,2,1:T(8,128)(2,1)}), bf16[2,32,1,32,384]{4,3,0,2,1:T(8,128)(2,1)S(1)}, u32[]{:S(2)}, u32[]{:S(2)}) %all-to-all-start.1) | async-done | bytes 1572896 | tf_op jit(solution)/shard_map/all_to_all | solution.py:78
  102.3 1.9 %multiply_reduce_fusion = (f32[2,32,16]{2,1,0:T(8,128)S(1)}, f32[2,1,32,16,384]{4,3,2,0,1:T(8,128)S(1)}) fusion(f32[2,384]{1,0:T(2,128)S(1)} %bitcast.162, f32[2,384]{1,0:T(2,128)S(1)} %bitcast.158, f32[384]{0:T(512)S(1)} %get-tuple-element.29, f32[384]{0:T(512)S(1)} %get-tuple-element.30, f32[384]{0:T(512)S(1)} %get-tuple-element.31, ...), kind=kLoop, calls=%fused_computation.158 | loop fusion | flops 8256512 | bytes 3169792 | tf_op jit(solution)/shard_map/jvp()/reduce_sum | solution.py:32
  106.5 2.2 %fusion.98 = f32[1024,384]{1,0:T(8,128)} fusion(bf16[768,384]{1,0:T(8,128)(2,1)S(1)} %copy-done.14, f32[1024,768]{1,0:T(8,128)S(1)} %fusion.126), kind=kOutput, calls=%fused_computation.164 | convolution fusion | flops 607911936 | bytes 5308416 | tf_op jit(solution)/shard_map/jvp()/dot_general | solution.py:39
  108.7 5.2 %fusion.102 = bf16[1024,384]{1,0:T(8,128)(2,1)} fusion(bf16[384,768]{1,0:T(8,128)(2,1)} %fusion.108, f32[1024,768]{1,0:T(8,128)} %copy-done.4, bf16[1024,384]{1,0:T(8,128)(2,1)} %bitcast.152, bf16[768,384]{1,0:T(8,128)(2,1)} %fusion.109), kind=kOutput, calls=%fused_computation.166 | convolution fusion | flops 1217003520 | bytes 5898240 | tf_op jit(solution)/shard_map/transpose(jvp())/dot_general | solution.py:36
  113.9 1.6 fusion.87
  121.3 3.6 %all-to-all-start.2 = ((bf16[2,1,16,32,384]{4,3,0,1,2:T(8,128)(2,1)}), bf16[2,1,16,32,384]{4,3,0,1,2:T(8,128)(2,1)S(1)}, u32[]{:S(2)}, u32[]{:S(2)}) async-start(bf16[2,1,16,32,384]{4,3,0,1,2:T(8,128)(2,1)} %copy.31), calls=%async_computation.2 | async-start | bytes 1572864 | tf_op jit(solution)/shard_map/all_to_all | solution.py:58
  125.0 18.6 %all-to-all-done.2 = bf16[2,1,16,32,384]{4,3,0,1,2:T(8,128)(2,1)S(1)} async-done(((bf16[2,1,16,32,384]{4,3,0,1,2:T(8,128)(2,1)}), bf16[2,1,16,32,384]{4,3,0,1,2:T(8,128)(2,1)S(1)}, u32[]{:S(2)}, u32[]{:S(2)}) %all-to-all-start.2) | async-done | bytes 786464 | tf_op jit(solution)/shard_map/all_to_all | solution.py:58
  144.7 25.5 %all_to_all.19 = bf16[2,16,1,32,384]{4,3,0,2,1:T(8,128)(2,1)S(1)} all-to-all(bf16[2,16,1,32,384]{4,3,0,2,1:T(8,128)(2,1)S(1)} %fusion.107), channel_id=1, replica_groups=mesh['section'=2,'seq'=16] {'seq'}, dimensions={1} | all-to-all | bytes 1572864 | tf_op jit(solution)/shard_map/all_to_all | solution.py:62
  171.2 4.3 %fusion.99 = bf16[1024,384]{1,0:T(8,128)(2,1)S(1)} fusion(f32[1024,768]{1,0:T(8,128)} %get-tuple-element.91, bf16[1024,384]{1,0:T(8,128)(2,1)} %bitcast.150, bf16[1,768,384]{2,1,0:T(8,128)(2,1)} %param.14, bf16[1,384,768]{2,1,0:T(8,128)(2,1)} %param.13), kind=kOutput, calls=%fused_computation.165 | convolution fusion | flops 1217003520 | bytes 5898240 | tf_op jit(solution)/shard_map/transpose(jvp())/dot_general | solution.py:36
  181.7 1.4 select_bitcast_fusion
  (169 shorter events, 37.1 us)
Async XLA Ops:
  0.6 14.3 %copy-start.12 = (bf16[2,1,512,384]{3,2,1,0:T(8,128)(2,1)S(1)}, bf16[2,1,512,384]{3,2,1,0:T(8,128)(2,1)}, u32[]{:S(2)}) copy-start(bf16[2,1,512,384]{3,2,1,0:T(8,128)(2,1)} %param.8) | copy-start | bytes 2359300
  2.0 34.3 %collective-permute-start.2 = (f32[384]{0:T(512)}, f32[384]{0:T(512)}, u32[]{:S(2)}, u32[]{:S(2)}) collective-permute-start(f32[384]{0:T(512)} %reduce.17), channel_id=1, source_target_pairs={{16,0},{17,1},{18,2},{19,3},{20,4},{21,5},{22,6},{23,7},{24,8},{25... | collective-permute-start | bytes 4616 | tf_op jit(solution)/shard_map/ppermute | solution.py:100
  3.3 34.7 %collective-permute-start.1 = (f32[2,2,384]{2,1,0:T(2,128)}, f32[2,2,384]{2,1,0:T(2,128)}, u32[]{:S(2)}, u32[]{:S(2)}) collective-permute-start(f32[2,2,384]{2,1,0:T(2,128)} %bitcast.166), channel_id=1, source_target_pairs={{16,0},{17,1},{18,2},{19,3},{20,4},{21,5},{22,6},{23,7},{24,8},{25... | collective-permute-start | bytes 18440 | tf_op jit(solution)/shard_map/ppermute | solution.py:100
  5.9 33.5 %collective-permute-start = (f32[9,384]{1,0:T(8,128)}, f32[9,384]{1,0:T(8,128)}, u32[]{:S(2)}, u32[]{:S(2)}) collective-permute-start(f32[9,384]{1,0:T(8,128)} %bitcast.134), channel_id=1, source_target_pairs={{16,0},{17,1},{18,2},{19,3},{20,4},{21,5},{22,6},{23,7},{24,8},{25... | collective-permute-start | bytes 41480 | tf_op jit(solution)/shard_map/ppermute | solution.py:100
  8.9 28.7 %collective-permute-start.5 = (bf16[384,384]{1,0:T(8,128)(2,1)}, bf16[384,384]{1,0:T(8,128)(2,1)}, u32[]{:S(2)}, u32[]{:S(2)}) collective-permute-start(bf16[384,384]{1,0:T(8,128)(2,1)} %dynamic-slice_bitcast_fusion), channel_id=1, source_target_pairs={{16,0},{17,1},{18,2},{19,3},{20,4},{21,5},{22,6},{23,7},{24,8},{25... | collective-permute-start | bytes 884744 | tf_op jit(solution)/shard_map/ppermute | solution.py:95
  11.9 27.4 %collective-permute-start.3 = (bf16[192,768]{1,0:T(8,128)(2,1)}, bf16[192,768]{1,0:T(8,128)(2,1)}, u32[]{:S(2)}, u32[]{:S(2)}) collective-permute-start(bf16[192,768]{1,0:T(8,128)(2,1)} %dynamic-slice_bitcast_fusion.1), channel_id=1, source_target_pairs={{16,0},{17,1},{18,2},{19,3},{20,4},{21,5},{22,6},{23,7},{24,8},{25... | collective-permute-start | bytes 884744 | tf_op jit(solution)/shard_map/ppermute | solution.py:95
  22.6 16.8 %copy-start.19 = (f32[1,9,384]{2,0,1:T(1,128)S(1)}, f32[1,9,384]{2,0,1:T(1,128)}, u32[]{:S(2)}) copy-start(f32[1,9,384]{2,0,1:T(1,128)} %param.10) | copy-start | bytes 41476
  23.7 26.1 %all-to-all-start = ((bf16[2,1,16,32,384]{4,3,0,1,2:T(8,128)(2,1)}), bf16[2,1,16,32,384]{4,3,0,1,2:T(8,128)(2,1)S(1)}, u32[]{:S(2)}, u32[]{:S(2)}) async-start(bf16[2,1,16,32,384]{4,3,0,1,2:T(8,128)(2,1)} %copy.29), calls=%async_computation | async-start | bytes 1572864 | tf_op jit(solution)/shard_map/all_to_all | solution.py:71
  37.6 3.2 %collective-permute-start.6 = (bf16[384,384]{1,0:T(8,128)(2,1)}, bf16[384,384]{1,0:T(8,128)(2,1)S(1)}, u32[]{:S(2)}, u32[]{:S(2)}) collective-permute-start(bf16[384,384]{1,0:T(8,128)(2,1)} %collective-permute-done.5), channel_id=1, source_target_pairs={{0,1},{1,0},{2,3},{3,2},{4,5},{5,4},{6,7},{7,6},{8,9},{9,8},{10,11... | collective-permute-start | bytes 884744 | tf_op jit(solution)/shard_map/ppermute | solution.py:96
  39.3 3.6 %collective-permute-start.4 = (bf16[192,768]{1,0:T(8,128)(2,1)}, bf16[192,768]{1,0:T(8,128)(2,1)S(1)}, u32[]{:S(2)}, u32[]{:S(2)}) collective-permute-start(bf16[192,768]{1,0:T(8,128)(2,1)} %collective-permute-done.3), channel_id=1, source_target_pairs={{0,1},{1,0},{2,3},{3,2},{4,5},{5,4},{6,7},{7,6},{8,9},{9,8},{10,11... | collective-permute-start | bytes 884744 | tf_op jit(solution)/shard_map/ppermute | solution.py:96
  45.0 5.0 %copy-start.46 = (f32[384]{0:T(512)S(1)}, f32[384]{0:T(512)}, u32[]{:S(2)}) copy-start(f32[384]{0:T(512)} %get-tuple-element.38) | copy-start | bytes 4612
  45.0 5.0 %copy-start.47 = (f32[384]{0:T(512)S(1)}, f32[384]{0:T(512)}, u32[]{:S(2)}) copy-start(f32[384]{0:T(512)} %get-tuple-element.39) | copy-start | bytes 4612
  45.0 5.0 %copy-start.48 = (f32[384]{0:T(512)S(1)}, f32[384]{0:T(512)}, u32[]{:S(2)}) copy-start(f32[384]{0:T(512)} %get-tuple-element.40) | copy-start | bytes 4612
  45.0 5.0 %copy-start.49 = (f32[384]{0:T(512)S(1)}, f32[384]{0:T(512)}, u32[]{:S(2)}) copy-start(f32[384]{0:T(512)} %get-tuple-element.41) | copy-start | bytes 4612
  45.0 5.0 %copy-start.50 = (f32[384]{0:T(512)S(1)}, f32[384]{0:T(512)}, u32[]{:S(2)}) copy-start(f32[384]{0:T(512)} %get-tuple-element.42) | copy-start | bytes 4612
  45.0 5.0 %copy-start.51 = (f32[384]{0:T(512)S(1)}, f32[384]{0:T(512)}, u32[]{:S(2)}) copy-start(f32[384]{0:T(512)} %get-tuple-element.43) | copy-start | bytes 4612
  45.0 5.0 %copy-start.52 = (f32[384]{0:T(512)S(1)}, f32[384]{0:T(512)}, u32[]{:S(2)}) copy-start(f32[384]{0:T(512)} %get-tuple-element.44) | copy-start | bytes 4612
  45.0 5.0 %copy-start.53 = (f32[384]{0:T(512)S(1)}, f32[384]{0:T(512)}, u32[]{:S(2)}) copy-start(f32[384]{0:T(512)} %get-tuple-element.45) | copy-start | bytes 4612
  45.0 5.0 %copy-start.54 = (f32[384]{0:T(512)S(1)}, f32[384]{0:T(512)}, u32[]{:S(2)}) copy-start(f32[384]{0:T(512)} %get-tuple-element.46) | copy-start | bytes 4612
  52.4 9.9 %copy-start.27 = (f32[2,2,384]{2,1,0:T(2,128)S(1)}, f32[2,2,384]{2,1,0:T(2,128)}, u32[]{:S(2)}) copy-start(f32[2,2,384]{2,1,0:T(2,128)} %broadcast_select_fusion.1) | copy-start | bytes 18436
  52.4 9.9 %copy-start.25 = (f32[9,384]{1,0:T(8,128)S(1)}, f32[9,384]{1,0:T(8,128)}, u32[]{:S(2)}) copy-start(f32[9,384]{1,0:T(8,128)} %broadcast_select_fusion) | copy-start | bytes 41476
  52.4 48.3 %all-to-all-start.1 = ((bf16[2,32,1,32,384]{4,3,0,2,1:T(8,128)(2,1)}), bf16[2,32,1,32,384]{4,3,0,2,1:T(8,128)(2,1)S(1)}, u32[]{:S(2)}, u32[]{:S(2)}) async-start(bf16[2,32,1,32,384]{4,3,0,2,1:T(8,128)(2,1)} %bitcast.144), calls=%async_computation.1 | async-start | bytes 3145728 | tf_op jit(solution)/shard_map/all_to_all | solution.py:78
  120.3 4.7 %copy-start.24 = (f32[1,9,384]{2,1,0:T(8,128)S(1)}, f32[1,9,384]{2,1,0:T(8,128)}, u32[]{:S(2)}) copy-start(f32[1,9,384]{2,1,0:T(8,128)} %get-tuple-element.84) | copy-start | bytes 41476
  121.3 22.3 %all-to-all-start.2 = ((bf16[2,1,16,32,384]{4,3,0,1,2:T(8,128)(2,1)}), bf16[2,1,16,32,384]{4,3,0,1,2:T(8,128)(2,1)S(1)}, u32[]{:S(2)}, u32[]{:S(2)}) async-start(bf16[2,1,16,32,384]{4,3,0,1,2:T(8,128)(2,1)} %copy.31), calls=%async_computation.2 | async-start | bytes 1572864 | tf_op jit(solution)/shard_map/all_to_all | solution.py:58
  (42 other events, 78.9 us)

commit v8 on v6

--- a/solution.py
+++ b/solution.py
@@ -11,33 +11,50 @@
 EPSILON = 1e-06
 
 
-def spatial_block(values, stencil_taps, modulate, norm_gain, w_in, w_out):
+def stencil(volume, stencil_taps):
+    padded = jnp.pad(volume, ((0, 0), (0, 0), (1, 1), (1, 1), (0, 0)))
+    total = jnp.zeros_like(volume)
+    for down_step in range(3):
+        for across in range(3):
+            total = total + stencil_taps[3 * down_step + across] * padded[
+                :, :, down_step : down_step + H, across : across + W
+            ]
+    return total
+
+
+def spatial_forward(values, stencil_taps, modulate, norm_gain, w_in, w_out):
     clip_count, frame_count, pixel_count, channels = values.shape
     volume = values.astype(jnp.float32).reshape(clip_count, frame_count, H, W, channels)
-    padded = jnp.pad(volume, ((0, 0), (0, 0), (1, 1), (1, 1), (0, 0)))
-    stencil_sum = jnp.zeros_like(volume)
-    for down_step in range(3):
-        for across in range(3):
-            stencil_sum = (
-                stencil_sum
-                + stencil_taps[3 * down_step + across]
-                * padded[:, :, down_step : down_step + H, across : across + W]
-            )
-    stencil_sum = stencil_sum.reshape(clip_count, frame_count, pixel_count, channels)
+    stencil_sum = stencil(volume, stencil_taps).reshape(values.shape)
     scale = (1.0 + modulate[:, 0])[:, None, None, :]
     shift = modulate[:, 1][:, None, None, :]
     modulated = stencil_sum * scale + shift
-    scaled = (
-        modulated
-        * lax.rsqrt(jnp.mean(modulated * modulated, axis=-1, keepdims=True) + EPSILON)
-        * norm_gain
-    )
-    normed = scaled.astype(jnp.bfloat16).reshape(-1, channels)
-    hidden = jax.nn.silu(jnp.dot(normed, w_in, preferred_element_type=jnp.float32)).astype(
-        jnp.bfloat16
-    )
+    inv_rms = lax.rsqrt(jnp.mean(modulated * modulated, axis=-1, keepdims=True) + EPSILON)
+    normed = (modulated * inv_rms * norm_gain).astype(jnp.bfloat16).reshape(-1, channels)
+    pre = jnp.dot(normed, w_in, preferred_element_type=jnp.float32)
+    hidden = jax.nn.silu(pre).astype(jnp.bfloat16)
     update = jnp.dot(hidden, w_out, preferred_element_type=jnp.float32)
-    return (values.astype(jnp.float32) + update.reshape(values.shape)).astype(jnp.bfloat16)
+    out = (values.astype(jnp.float32) + update.reshape(values.shape)).astype(jnp.bfloat16)
+    return out, (modulated, inv_rms, pre)
+
+
+def spatial_backward(saved, grad, stencil_taps, modulate, norm_gain, w_in, w_out):
+    modulated, inv_rms, pre = saved
+    clip_count, frame_count, pixel_count, channels = grad.shape
+    flat_grad = grad.reshape(-1, channels)
+    hidden_grad = jnp.dot(flat_grad, w_out.T, preferred_element_type=jnp.float32).astype(jnp.bfloat16)
+    gate = jax.nn.sigmoid(pre)
+    pre_grad = hidden_grad.astype(jnp.float32) * (gate * (1.0 + pre * (1.0 - gate)))
+    pre_grad = lax.optimization_barrier(pre_grad.astype(jnp.bfloat16))
+    normed_grad = jnp.dot(pre_grad, w_in.T, preferred_element_type=jnp.float32).astype(jnp.bfloat16)
+    scaled_grad = normed_grad.astype(jnp.float32).reshape(grad.shape) * norm_gain
+    inner = jnp.sum(scaled_grad * modulated, axis=-1, keepdims=True)
+    modulated_grad = inv_rms * scaled_grad - modulated * (inv_rms * inv_rms * inv_rms) * (inner / channels)
+    stencil_grad = modulated_grad * (1.0 + modulate[:, 0])[:, None, None, :]
+    spread = stencil(
+        stencil_grad.reshape(clip_count, frame_count, H, W, channels), stencil_taps[::-1]
+    ).reshape(grad.shape)
+    return (grad.astype(jnp.float32) + spread.astype(jnp.bfloat16).astype(jnp.float32)).astype(jnp.bfloat16)
 
 
 def band_frames(values, tap_table):
@@ -103,25 +120,20 @@
         [jnp.where(first, fetch_halves(p), p) for p in (weight_in, weight_out)]
     )
 
-    def spatial(values):
-        return spatial_block(values, taps, mod, gain, weight_in, weight_out)
+    first_params = (taps, mod, gain, weight_in, weight_out)
+    second_params = (second_taps, second_mod, second_gain, second_in, second_out)
 
-    def second_spatial(values):
-        return spatial_block(
-            values, second_taps, second_mod, second_gain, second_in, second_out
-        )
-
-    first_mixed, first_pull = jax.vjp(spatial, clips)
+    first_mixed, first_saved = spatial_forward(clips, *first_params)
     lead_in = jnp.where(first, first_mixed, cotangent)
     lead_taps = jnp.where(first, band, band[::-1])
     first_acts, second_seed = temporal_shared(lead_in, lead_taps[None])
-    second_mixed, second_pull = jax.vjp(second_spatial, first_acts)
-    second_grad = second_pull(second_seed)[0]
+    second_mixed, second_saved = spatial_forward(first_acts, *second_params)
+    second_grad = spatial_backward(second_saved, second_seed, *second_params)
 
     tail_in = jnp.where(first, second_grad, second_mixed)
     tail_taps = jnp.where(first, band[::-1], band)
     tail_out = temporal(tail_in, tail_taps[None])
-    first_grad = first_pull(tail_out)[0]
+    first_grad = spatial_backward(first_saved, tail_out, *first_params)
 
     activations = jnp.where(first, first_acts, tail_out)
     input_grads = jnp.where(first, first_grad, second_grad)

time: 167 us -> 164 us (0.982)
  local copies, waits for them, and re-layouts: 13.2 us -> 10.2 us
  other arithmetic: 26.6 us -> 28.9 us
  matrix products: 16.5 us -> 14.3 us
    convert_element_type x4 -> x5, other arithmetic: 2.65 us -> 5.38 us  [the longest x2 3.6 us: spatial_backward(): spread.astype(jnp.bfloat16).astype(jnp.float32)]
    unnamed x88 -> x80, local copies, waits for them, and re-layouts: 4.65 us -> 2.38 us
    dot_general x6 -> x8, matrix products: 16.5 us -> 14.3 us  [the longest x2 4.34 us: spatial_backward(): jnp.dot(pre_grad, w_in.T, preferred_element_type=jnp.float32)]
    reduce_sum x4 -> x2, other arithmetic: 5.82 us -> 3.83 us  [spatial_forward(): jnp.mean(modulated * modulated, axis=-1, keepdims=True) + EPSILON]
  transfers between devices with their start and end apart: 10 -> 10, of which waited for: 6 -> 6; matrix products, arithmetic and copies ran while one was open for 6% -> 7% of each run, Pallas kernels for 0% -> 0%
where the time goes in v8:
time: 164 us; the launch traced here: 163 us
  waiting for transfers between devices  58.6 us (36%)
  other arithmetic  28.9 us (18%)
  blocking collectives  25.7 us (16%)
  starting transfers between devices  23.7 us (14%)
  matrix products  14.3 us (9%)
  local copies, waits for them, and re-layouts  10.2 us (6%)
    all_to_all x1, blocking collectives, temporal(): lax.all_to_all(banded, 'seq', split_axis=1, concat_axis=2, tiled=True)  25.7 us
    all_to_all x1, waiting for transfers between devices, temporal(): lax.all_to_all(grouped, 'seq', split_axis=2, concat_axis=1, tiled=True)  18.7 us
    all_to_all x1, waiting for transfers between devices, temporal_shared(): lax.all_to_all(grouped, 'seq', split_axis=2, concat_axis=1, tiled=True)  17.9 us
    ppermute x2, waiting for transfers between devices, fetch_halves(): got = lax.ppermute(mine, 'section', perm=to_first)  17.8 us
    all_to_all x1, starting transfers between devices, temporal_shared(): lax.all_to_all(grouped, 'seq', split_axis=2, concat_axis=1, tiled=True)  7.38 us
    all_to_all x1, starting transfers between devices, temporal_shared(): lax.all_to_all(banded, ('section', 'seq'), split_axis=1, concat_axis=2, t...  5.39 us
    select_n x2, other arithmetic, on_device(): jnp.where(first, fetch_halves(p), p)  4.45 us
    dot_general x2, matrix products, spatial_backward(): jnp.dot(pre_grad, w_in.T, preferred_element_type=jnp.float32)  4.34 us
  transfers between devices with their start and end apart: 10, of which 6 were waited for; matrix products, arithmetic and copies ran while one was open for 7% of the time, Pallas kernels for 0%

profile of v8, /device:TPU:0, one launch (start us, length us, event | category | flops | bytes accessed | tf_op | source)
XLA Modules:
  0.0 162.7 jit_solution(14745148503818147642)
XLA Ops:
  3.6 1.9 %multiply_reduce_fusion.2 = (f32[2,32,16]{2,1,0:T(8,128)S(1)}, f32[2,1,32,16,384]{4,3,2,0,1:T(8,128)S(1)}) fusion(f32[2,384]{1,0:T(2,128)S(1)} %get-tuple-element.75, f32[2,384]{1,0:T(2,128)S(1)} %get-tuple-element.76, f32[384]{0:T(512)S(1)} %get-tuple-element.47, f32[384]{0:T(512)S(1)} %get-tuple-element.40, f32[384]{0:T(512)S(1)} %get-tuple-element.41, ...), kind=kLoop, calls=%fused_computation.183 | loop fusion | flops 8256512 | bytes 3169792 | tf_op jit(solution)/shard_map/reduce_sum | solution.py:32
  6.7 2.8 %multiply_convert_fusion.3 = (bf16[1024,768]{1,0:T(8,128)(2,1)S(1)}, f32[1024,768]{1,0:T(8,128)}) fusion(bf16[1024,384]{1,0:T(8,128)(2,1)S(1)} %bitcast.169, bf16[1,384,768]{2,1,0:T(8,128)(2,1)S(1)} %copy-done.6), kind=kOutput, calls=%fused_computation.52 | convolution fusion | flops 607911936 | bytes 6094848 | tf_op jit(solution)/shard_map/dot_general | solution.py:34
  11.6 7.4 %all-to-all-start = ((bf16[2,1,16,32,384]{4,3,0,1,2:T(8,128)(2,1)}), bf16[2,1,16,32,384]{4,3,0,1,2:T(8,128)(2,1)S(1)}, u32[]{:S(2)}, u32[]{:S(2)}) async-start(bf16[2,1,16,32,384]{4,3,0,1,2:T(8,128)(2,1)} %copy.29), calls=%async_computation | async-start | bytes 1572864 | tf_op jit(solution)/shard_map/all_to_all | solution.py:88
  19.8 17.9 %all-to-all-done = bf16[2,1,16,32,384]{4,3,0,1,2:T(8,128)(2,1)S(1)} async-done(((bf16[2,1,16,32,384]{4,3,0,1,2:T(8,128)(2,1)}), bf16[2,1,16,32,384]{4,3,0,1,2:T(8,128)(2,1)S(1)}, u32[]{:S(2)}, u32[]{:S(2)}) %all-to-all-start) | async-done | bytes 786464 | tf_op jit(solution)/shard_map/all_to_all | solution.py:88
  40.2 5.4 %all-to-all-start.1 = ((bf16[2,32,1,32,384]{4,3,0,2,1:T(8,128)(2,1)}), bf16[2,32,1,32,384]{4,3,0,2,1:T(8,128)(2,1)S(1)}, u32[]{:S(2)}, u32[]{:S(2)}) async-start(bf16[2,32,1,32,384]{4,3,0,2,1:T(8,128)(2,1)} %bitcast.159), calls=%async_computation.1 | async-start | bytes 3145728 | tf_op jit(solution)/shard_map/all_to_all | solution.py:94
  52.4 1.7 %dynamic-slice_bitcast_fusion.1 = bf16[192,768]{1,0:T(8,128)(2,1)} fusion(bf16[1,384,768]{2,1,0:T(8,128)(2,1)} %param.13, s32[]{:T(128)S(6)} %select_n.124), kind=kLoop, calls=%fused_computation.211 | loop fusion | bytes 589828 | tf_op jit(solution)/shard_map/dynamic_slice | solution.py:110
  58.1 10.4 %collective-permute-done.4 = bf16[384,384]{1,0:T(8,128)(2,1)} collective-permute-done((bf16[384,384]{1,0:T(8,128)(2,1)S(1)}, bf16[384,384]{1,0:T(8,128)(2,1)}, u32[]{:S(2)}, u32[]{:S(2)}) %collective-permute-start.4) | collective-permute-done | bytes 294944 | tf_op jit(solution)/shard_map/ppermute | solution.py:111
  69.2 7.4 %collective-permute-done.2 = bf16[192,768]{1,0:T(8,128)(2,1)} collective-permute-done((bf16[192,768]{1,0:T(8,128)(2,1)}, bf16[192,768]{1,0:T(8,128)(2,1)}, u32[]{:S(2)}, u32[]{:S(2)}) %collective-permute-start.2) | collective-permute-done | bytes 294944 | tf_op jit(solution)/shard_map/ppermute | solution.py:111
  76.7 2.4 %fusion.121 = bf16[768,384]{1,0:T(8,128)(2,1)} fusion(bf16[384,384]{1,0:T(8,128)(2,1)S(1)} %collective-permute-done.5, bf16[384,384]{1,0:T(8,128)(2,1)} %collective-permute-done.4, bf16[1,768,384]{2,1,0:T(8,128)(2,1)} %param.14, pred[]{:T(512)S(6)} %eq.10, pred[]{:T(512)S(6)} %eq.9), kind=kLoop, calls=%fused_computation.204 | loop fusion | flops 2949120 | bytes 1769474 | tf_op jit(solution)/shard_map/jit(_where)/select_n | solution.py:120
  79.1 2.1 %fusion.120 = bf16[384,768]{1,0:T(8,128)(2,1)} fusion(bf16[192,768]{1,0:T(8,128)(2,1)S(1)} %collective-permute-done.3, bf16[192,768]{1,0:T(8,128)(2,1)} %collective-permute-done.2, bf16[1,384,768]{2,1,0:T(8,128)(2,1)S(1)} %copy-done.7, pred[]{:T(512)S(6)} %eq.10, pred[]{:T(512)S(6)} %eq.9), kind=kLoop, calls=%fused_computation.202 | loop fusion | flops 2949120 | bytes 1769474 | tf_op jit(solution)/shard_map/jit(_where)/select_n | solution.py:120
  81.1 3.1 %all-to-all-done.1 = bf16[2,32,1,32,384]{4,3,0,2,1:T(8,128)(2,1)S(1)} async-done(((bf16[2,32,1,32,384]{4,3,0,2,1:T(8,128)(2,1)}), bf16[2,32,1,32,384]{4,3,0,2,1:T(8,128)(2,1)S(1)}, u32[]{:S(2)}, u32[]{:S(2)}) %all-to-all-start.1) | async-done | bytes 1572896 | tf_op jit(solution)/shard_map/all_to_all | solution.py:94
  84.4 1.9 %fusion.130 = (bf16[1,2,1,512,384]{4,3,0,1,2:T(8,128)(2,1)}, f32[1,2,1,512,384]{4,3,0,1,2:T(8,128)}, f32[1,2,1,512,384]{4,3,0,1,2:T(8,128)S(1)}) fusion(bf16[2,2,1,512,384]{4,3,0,1,2:T(8,128)(2,1)S(1)} %bitcast.157), kind=kLoop, calls=%fused_computation.269 | loop fusion | flops 786432 | bytes 5505024 | tf_op jit(solution)/shard_map/unstack | solution.py:129
  86.4 1.9 %multiply_reduce_fusion.1 = (f32[2,32,16]{2,1,0:T(8,128)S(1)}, f32[2,1,32,16,384]{4,3,2,0,1:T(8,128)S(1)}) fusion(f32[2,384]{1,0:T(2,128)S(1)} %get-tuple-element.73, f32[2,384]{1,0:T(2,128)S(1)} %get-tuple-element.74, f32[384]{0:T(512)S(1)} %get-tuple-element.21, f32[384]{0:T(512)S(1)} %get-tuple-element.22, f32[384]{0:T(512)S(1)} %get-tuple-element.23, ...), kind=kLoop, calls=%fused_computation.181 | loop fusion | flops 8256512 | bytes 3169792 | tf_op jit(solution)/shard_map/reduce_sum | solution.py:32
  90.5 2.2 %fusion.111 = f32[1024,384]{1,0:T(8,128)} fusion(bf16[768,384]{1,0:T(8,128)(2,1)S(1)} %copy-done.16, f32[1024,768]{1,0:T(8,128)S(1)} %fusion.131), kind=kOutput, calls=%fused_computation.185 | convolution fusion | flops 607911936 | bytes 5308416 | tf_op jit(solution)/shard_map/dot_general | solution.py:36
  94.2 2.2 %multiply_reduce_fusion = (f32[1024]{0:T(1024)S(1)}, f32[1024,384]{1,0:T(8,128)}) fusion(f32[2,1,32,16,384]{4,3,2,0,1:T(8,128)S(1)} %get-tuple-element.49, f32[384]{0:T(512)S(1)} %broadcast_select_fusion.2, f32[2,384]{1,0:T(2,128)S(1)} %get-tuple-element.73, f32[2,384]{1,0:T(2,128)S(1)} %get-tuple-element.74, ...), kind=kOutput, calls=%fused_computation.179 | convolution fusion | flops 606731264 | bytes 5320192 | tf_op jit(solution)/shard_map/dot_general | solution.py:49
  96.5 2.0 %subtract_multiply_fusion.1 = f32[2,1,32,16,384]{4,3,2,0,1:T(8,128)S(1)} fusion(f32[2,1,32,16,384]{4,3,2,0,1:T(8,128)} %bitcast.162, f32[2,1,32,16,384]{4,3,2,0,1:T(8,128)S(1)} %get-tuple-element.49, f32[2,32,16]{2,1,0:T(8,128)S(1)} %div.30, f32[2,32,16]{2,1,0:T(8,128)S(1)} %get-tuple-element.61, f32[384]{0:T(512)S(1)} %broadcast_select_fusion.2, ...), kind=kLoop, calls=%fused_computation.178 | loop fusion | flops 3145728 | bytes 4738560 | tf_op jit(solution)/shard_map/mul | solution.py:53
  98.6 1.8 %fusion.118 = f32[2,1,32,16,384]{4,3,2,0,1:T(8,128)S(1)} fusion(f32[2,1,32,16,384]{4,3,2,0,1:T(8,128)S(1)} %subtract_multiply_fusion.1, f32[384]{0:T(512)S(1)} %get-tuple-element.29, f32[384]{0:T(512)S(1)} %get-tuple-element.28, f32[384]{0:T(512)S(1)} %get-tuple-element.27, f32[384]{0:T(512)S(1)} %get-tuple-element.26, f32[384]{0:T(512)S(1)} %get-tuple-element.25, ...), kind=kLoop, calls=%fused_computation.198 | loop fusion | flops 7471104 | bytes 3159552 | tf_op jit(solution)/shard_map/convert_element_type | solution.py:57
  102.2 4.3 %all-to-all-start.2 = ((bf16[2,1,16,32,384]{4,3,0,1,2:T(8,128)(2,1)}), bf16[2,1,16,32,384]{4,3,0,1,2:T(8,128)(2,1)}, u32[]{:S(2)}, u32[]{:S(2)}) async-start(bf16[2,1,16,32,384]{4,3,0,1,2:T(8,128)(2,1)} %copy.31), calls=%async_computation.2 | async-start | bytes 1572864 | tf_op jit(solution)/shard_map/all_to_all | solution.py:75
  106.6 18.7 %all-to-all-done.2 = bf16[2,1,16,32,384]{4,3,0,1,2:T(8,128)(2,1)} async-done(((bf16[2,1,16,32,384]{4,3,0,1,2:T(8,128)(2,1)}), bf16[2,1,16,32,384]{4,3,0,1,2:T(8,128)(2,1)}, u32[]{:S(2)}, u32[]{:S(2)}) %all-to-all-start.2) | async-done | bytes 786464 | tf_op jit(solution)/shard_map/all_to_all | solution.py:75
  127.6 25.7 %all_to_all.16 = bf16[2,16,1,32,384]{4,3,0,2,1:T(8,128)(2,1)S(1)} all-to-all(bf16[2,16,1,32,384]{4,3,0,2,1:T(8,128)(2,1)S(1)} %fusion.119), channel_id=1, replica_groups=mesh['section'=2,'seq'=16] {'seq'}, dimensions={1} | all-to-all | bytes 1572864 | tf_op jit(solution)/shard_map/all_to_all | solution.py:79
  154.8 2.2 %fusion.104 = (f32[1024]{0:T(1024)S(1)}, f32[1024,384]{1,0:T(8,128)}) fusion(f32[2,1,32,16,384]{4,3,2,0,1:T(8,128)S(1)} %get-tuple-element.51, f32[384]{0:T(512)S(1)} %reduce.15, f32[2,384]{1,0:T(2,128)S(1)} %get-tuple-element.75, f32[2,384]{1,0:T(2,128)S(1)} %get-tuple-element.76, bf16[1024,768]{1,0:T(8,128)(2,1)S(1)} %multiply_convert_fusion, ...), kind=kOutput, calls=%fused_computation.162 | convolution fusion | flops 606731264 | bytes 5320192 | tf_op jit(solution)/shard_map/dot_general | solution.py:49
  157.1 1.9 %subtract_multiply_fusion = f32[2,1,32,16,384]{4,3,2,0,1:T(8,128)S(1)} fusion(f32[2,1,32,16,384]{4,3,2,0,1:T(8,128)} %bitcast.163, f32[2,1,32,16,384]{4,3,2,0,1:T(8,128)S(1)} %get-tuple-element.51, f32[2,32,16]{2,1,0:T(8,128)S(1)} %div.32, f32[2,32,16]{2,1,0:T(8,128)S(1)} %get-tuple-element.59, f32[384]{0:T(512)S(1)} %reduce.15, ...), kind=kLoop, calls=%fused_computation.176 | loop fusion | flops 3145728 | bytes 4738560 | tf_op jit(solution)/shard_map/mul | solution.py:53
  159.2 1.8 %fusion.94 = bf16[2,1,32,16,384]{4,3,2,0,1:T(8,128)(2,1)S(1)} fusion(f32[2,1,32,16,384]{4,3,2,0,1:T(8,128)S(1)} %subtract_multiply_fusion, f32[384]{0:T(512)S(1)} %copy-done.34, f32[384]{0:T(512)S(1)} %get-tuple-element.40, f32[384]{0:T(512)S(1)} %copy-done.22, f32[384]{0:T(512)S(1)} %copy-done.24, f32[384]{0:T(512)S(1)} %copy-done.26, ...), kind=kLoop, calls=%fused_computation.150 | loop fusion | flops 7077888 | bytes 2373120 | tf_op jit(solution)/shard_map/convert_element_type | solution.py:57
  161.0 1.7 %fusion.117 = (bf16[1,2,1,512,384]{4,3,2,1,0:T(8,128)(2,1)}, bf16[1,2,1,512,384]{4,3,2,1,0:T(8,128)(2,1)}) fusion(f32[1,2,1,512,384]{4,3,0,1,2:T(8,128)S(1)} %bitcast.154, bf16[1,2,1,512,384]{4,3,0,1,2:T(8,128)(2,1)S(1)} %bitcast.166, bf16[1,2,1,512,384]{4,3,0,1,2:T(8,128)(2,1)S(1)} %bitcast.165, pred[]{:T(512)S(6)} %eq.9, ...), kind=kLoop, calls=%fused_computation.193 | loop fusion | flops 3538944 | bytes 6291457
  (130 shorter events, 30.5 us)
Async XLA Ops:
  2.3 3.3 %copy-start.21 = (f32[384]{0:T(512)}, f32[384]{0:T(512)S(1)}, u32[]{:S(2)}) copy-start(f32[384]{0:T(512)S(1)} %get-tuple-element.41) | copy-start | bytes 4612
  2.3 3.3 %copy-start.23 = (f32[384]{0:T(512)}, f32[384]{0:T(512)S(1)}, u32[]{:S(2)}) copy-start(f32[384]{0:T(512)S(1)} %get-tuple-element.42) | copy-start | bytes 4612
  2.3 3.3 %copy-start.25 = (f32[384]{0:T(512)}, f32[384]{0:T(512)S(1)}, u32[]{:S(2)}) copy-start(f32[384]{0:T(512)S(1)} %get-tuple-element.43) | copy-start | bytes 4612
  2.3 3.3 %copy-start.27 = (f32[384]{0:T(512)}, f32[384]{0:T(512)S(1)}, u32[]{:S(2)}) copy-start(f32[384]{0:T(512)S(1)} %get-tuple-element.44) | copy-start | bytes 4612
  2.3 3.3 %copy-start.29 = (f32[384]{0:T(512)}, f32[384]{0:T(512)S(1)}, u32[]{:S(2)}) copy-start(f32[384]{0:T(512)S(1)} %get-tuple-element.45) | copy-start | bytes 4612
  2.3 3.3 %copy-start.31 = (f32[384]{0:T(512)}, f32[384]{0:T(512)S(1)}, u32[]{:S(2)}) copy-start(f32[384]{0:T(512)S(1)} %get-tuple-element.46) | copy-start | bytes 4612
  10.6 8.4 %copy-start.19 = (f32[1,9,384]{2,0,1:T(1,128)S(1)}, f32[1,9,384]{2,0,1:T(1,128)}, u32[]{:S(2)}) copy-start(f32[1,9,384]{2,0,1:T(1,128)} %param.15) | copy-start | bytes 41476
  11.6 26.1 %all-to-all-start = ((bf16[2,1,16,32,384]{4,3,0,1,2:T(8,128)(2,1)}), bf16[2,1,16,32,384]{4,3,0,1,2:T(8,128)(2,1)S(1)}, u32[]{:S(2)}, u32[]{:S(2)}) async-start(bf16[2,1,16,32,384]{4,3,0,1,2:T(8,128)(2,1)} %copy.29), calls=%async_computation | async-start | bytes 1572864 | tf_op jit(solution)/shard_map/all_to_all | solution.py:88
  40.2 6.7 %copy-start.20 = (f32[1,2,2,384]{3,2,1,0:T(2,128)S(1)}, f32[1,2,2,384]{3,2,1,0:T(2,128)}, u32[]{:S(2)}) copy-start(f32[1,2,2,384]{3,2,1,0:T(2,128)} %param.11) | copy-start | bytes 18436
  40.2 8.0 %copy-start.17 = (f32[1,9,384]{2,0,1:T(1,128)S(1)}, f32[1,9,384]{2,0,1:T(1,128)}, u32[]{:S(2)}) copy-start(f32[1,9,384]{2,0,1:T(1,128)} %param.10) | copy-start | bytes 41476
  40.2 44.0 %all-to-all-start.1 = ((bf16[2,32,1,32,384]{4,3,0,2,1:T(8,128)(2,1)}), bf16[2,32,1,32,384]{4,3,0,2,1:T(8,128)(2,1)S(1)}, u32[]{:S(2)}, u32[]{:S(2)}) async-start(bf16[2,32,1,32,384]{4,3,0,2,1:T(8,128)(2,1)} %bitcast.159), calls=%async_computation.1 | async-start | bytes 3145728 | tf_op jit(solution)/shard_map/all_to_all | solution.py:94
  45.6 11.1 %collective-permute-start.6 = (f32[384]{0:T(512)S(1)}, f32[384]{0:T(512)}, u32[]{:S(2)}, u32[]{:S(2)}) collective-permute-start(f32[384]{0:T(512)S(1)} %reduce.15), channel_id=1, source_target_pairs={{16,0},{17,1},{18,2},{19,3},{20,4},{21,5},{22,6},{23,7},{24,8},{25... | collective-permute-start | bytes 4616 | tf_op jit(solution)/shard_map/ppermute | solution.py:116
  46.9 10.4 %collective-permute-start.1 = (f32[2,2,384]{2,1,0:T(2,128)S(1)}, f32[2,2,384]{2,1,0:T(2,128)}, u32[]{:S(2)}, u32[]{:S(2)}) collective-permute-start(f32[2,2,384]{2,1,0:T(2,128)S(1)} %bitcast.173), channel_id=1, source_target_pairs={{16,0},{17,1},{18,2},{19,3},{20,4},{21,5},{22,6},{23,7},{24,8},{25... | collective-permute-start | bytes 18440 | tf_op jit(solution)/shard_map/ppermute | solution.py:116
  48.8 19.7 %collective-permute-start = (f32[9,384]{1,0:T(8,128)}, f32[9,384]{1,0:T(8,128)}, u32[]{:S(2)}, u32[]{:S(2)}) collective-permute-start(f32[9,384]{1,0:T(8,128)} %bitcast.150), channel_id=1, source_target_pairs={{16,0},{17,1},{18,2},{19,3},{20,4},{21,5},{22,6},{23,7},{24,8},{25... | collective-permute-start | bytes 41480 | tf_op jit(solution)/shard_map/ppermute | solution.py:116
  51.1 17.3 %collective-permute-start.4 = (bf16[384,384]{1,0:T(8,128)(2,1)S(1)}, bf16[384,384]{1,0:T(8,128)(2,1)}, u32[]{:S(2)}, u32[]{:S(2)}) collective-permute-start(bf16[384,384]{1,0:T(8,128)(2,1)S(1)} %dynamic-slice_bitcast_fusion), channel_id=1, source_target_pairs={{16,0},{17,1},{18,2},{19,3},{20,4},{21,5},{22,6},{23,7},{24,8},{25... | collective-permute-start | bytes 884744 | tf_op jit(solution)/shard_map/ppermute | solution.py:111
  54.1 22.5 %collective-permute-start.2 = (bf16[192,768]{1,0:T(8,128)(2,1)}, bf16[192,768]{1,0:T(8,128)(2,1)}, u32[]{:S(2)}, u32[]{:S(2)}) collective-permute-start(bf16[192,768]{1,0:T(8,128)(2,1)} %dynamic-slice_bitcast_fusion.1), channel_id=1, source_target_pairs={{16,0},{17,1},{18,2},{19,3},{20,4},{21,5},{22,6},{23,7},{24,8},{25... | collective-permute-start | bytes 884744 | tf_op jit(solution)/shard_map/ppermute | solution.py:111
  55.6 23.4 %copy-start.7 = (bf16[1,384,768]{2,1,0:T(8,128)(2,1)S(1)}, bf16[1,384,768]{2,1,0:T(8,128)(2,1)}, u32[]{:S(2)}) copy-start(bf16[1,384,768]{2,1,0:T(8,128)(2,1)} %param.13) | copy-start | bytes 1769476
  68.5 8.2 %collective-permute-start.5 = (bf16[384,384]{1,0:T(8,128)(2,1)}, bf16[384,384]{1,0:T(8,128)(2,1)S(1)}, u32[]{:S(2)}, u32[]{:S(2)}) collective-permute-start(bf16[384,384]{1,0:T(8,128)(2,1)} %collective-permute-done.4), channel_id=1, source_target_pairs={{0,1},{1,0},{2,3},{3,2},{4,5},{5,4},{6,7},{7,6},{8,9},{9,8},{10,11... | collective-permute-start | bytes 884744 | tf_op jit(solution)/shard_map/ppermute | solution.py:112
  76.6 2.4 %collective-permute-start.3 = (bf16[192,768]{1,0:T(8,128)(2,1)}, bf16[192,768]{1,0:T(8,128)(2,1)S(1)}, u32[]{:S(2)}, u32[]{:S(2)}) collective-permute-start(bf16[192,768]{1,0:T(8,128)(2,1)} %collective-permute-done.2), channel_id=1, source_target_pairs={{0,1},{1,0},{2,3},{3,2},{4,5},{5,4},{6,7},{7,6},{8,9},{9,8},{10,11... | collective-permute-start | bytes 884744 | tf_op jit(solution)/shard_map/ppermute | solution.py:112
  96.5 3.9 %copy-start.11 = (f32[1024,384]{1,0:T(8,128)S(1)}, f32[1024,384]{1,0:T(8,128)}, u32[]{:S(2)}) copy-start(f32[1024,384]{1,0:T(8,128)} %fusion.111) | copy-start | bytes 4718596
  101.2 5.3 %copy-start.18 = (f32[1,9,384]{2,1,0:T(8,128)S(1)}, f32[1,9,384]{2,1,0:T(8,128)}, u32[]{:S(2)}) copy-start(f32[1,9,384]{2,1,0:T(8,128)} %get-tuple-element.57) | copy-start | bytes 41476
  102.2 23.1 %all-to-all-start.2 = ((bf16[2,1,16,32,384]{4,3,0,1,2:T(8,128)(2,1)}), bf16[2,1,16,32,384]{4,3,0,1,2:T(8,128)(2,1)}, u32[]{:S(2)}, u32[]{:S(2)}) async-start(bf16[2,1,16,32,384]{4,3,0,1,2:T(8,128)(2,1)} %copy.31), calls=%async_computation.2 | async-start | bytes 1572864 | tf_op jit(solution)/shard_map/all_to_all | solution.py:75
  126.6 26.8 %copy-start.37 = (f32[1024,768]{1,0:T(8,128)S(1)}, f32[1024,768]{1,0:T(8,128)}, u32[]{:S(2)}) copy-start(f32[1024,768]{1,0:T(8,128)} %get-tuple-element.68) | copy-start | bytes 9437188
  127.6 25.8 %copy-start.13 = (bf16[1,768,384]{2,1,0:T(8,128)(2,1)S(1)}, bf16[1,768,384]{2,1,0:T(8,128)(2,1)}, u32[]{:S(2)}) copy-start(bf16[1,768,384]{2,1,0:T(8,128)(2,1)} %param.14) | copy-start | bytes 1769476
  (24 other events, 47.5 us)

commit v9 on v8

--- a/solution.py
+++ b/solution.py
@@ -68,74 +68,73 @@
     return total.astype(jnp.bfloat16)
 
 
-def temporal(values, tap_table):
+def temporal(values, tap_table, carried):
     clip_count, frame_count, pixel_count, channels = values.shape
     groups = lax.axis_size("seq")
     grouped = values.reshape(clip_count, frame_count, groups, pixel_count // groups, channels)
     pixel_view = lax.all_to_all(grouped, "seq", split_axis=2, concat_axis=1, tiled=True)
+    pixel_view, carried = lax.optimization_barrier((pixel_view, carried))
     pixel_view = pixel_view.reshape(clip_count, groups * frame_count, pixel_count // groups, channels)
     banded = band_frames(pixel_view, tap_table)
     banded = banded.reshape(clip_count, groups * frame_count, 1, pixel_count // groups, channels)
     back = lax.all_to_all(banded, "seq", split_axis=1, concat_axis=2, tiled=True)
-    return back.reshape(values.shape)
-
-
-def temporal_shared(values, tap_table):
-    clip_count, frame_count, pixel_count, channels = values.shape
-    groups = lax.axis_size("seq")
-    planes = lax.axis_size("section")
-    grouped = values.reshape(clip_count, frame_count, groups, pixel_count // groups, channels)
-    pixel_view = lax.all_to_all(grouped, "seq", split_axis=2, concat_axis=1, tiled=True)
-    pixel_view = pixel_view.reshape(clip_count, groups * frame_count, pixel_count // groups, channels)
-    banded = band_frames(pixel_view, tap_table)
-    banded = jnp.broadcast_to(
-        banded[:, None], (clip_count, planes) + banded.shape[1:]
-    ).reshape(clip_count, planes * groups * frame_count, 1, pixel_count // groups, channels)
-    back = lax.all_to_all(banded, ("section", "seq"), split_axis=1, concat_axis=2, tiled=True)
-    back = back.reshape(clip_count, frame_count, planes, pixel_count, channels)
-    return jnp.moveaxis(back, 2, 0)
+    return back.reshape(values.shape), carried
 
 
 def on_device(clips, cotangent, spatial_taps, modulation, norm_gain, w_in, w_out, band_taps):
     first = lax.axis_index("section") == 0
     taps, mod, gain = spatial_taps[0], modulation[0], norm_gain[0]
     weight_in, weight_out, band = w_in[0], w_out[0], band_taps[0]
-
-    to_first = [(1, 0)]
-    core = lax.axis_index("seq") % 2
-    siblings = [(q, q ^ 1) for q in range(lax.axis_size("seq"))]
-
-    def fetch_halves(p):
-        half = p.shape[0] // 2
-        mine = lax.dynamic_slice_in_dim(p, core * half, half, 0)
-        got = lax.ppermute(mine, "section", perm=to_first)
-        other = lax.ppermute(got, "seq", perm=siblings)
-        return jnp.where(core == 0, jnp.concatenate([got, other]), jnp.concatenate([other, got]))
-
-    second_taps, second_mod, second_gain = [
-        jnp.where(first, lax.ppermute(p, "section", perm=to_first), p)
-        for p in (taps, mod, gain)
-    ]
-    second_in, second_out = lax.optimization_barrier(
-        [jnp.where(first, fetch_halves(p), p) for p in (weight_in, weight_out)]
-    )
-
+    channels = taps.shape[-1]
     first_params = (taps, mod, gain, weight_in, weight_out)
-    second_params = (second_taps, second_mod, second_gain, second_in, second_out)
 
     first_mixed, first_saved = spatial_forward(clips, *first_params)
     lead_in = jnp.where(first, first_mixed, cotangent)
     lead_taps = jnp.where(first, band, band[::-1])
-    first_acts, second_seed = temporal_shared(lead_in, lead_taps[None])
+
+    lead_in, fetched = lax.optimization_barrier((lead_in, first_params))
+    to_first = [(1, 0)]
+    core = lax.axis_index("seq") % 2
+    siblings = [(q, q ^ 1) for q in range(lax.axis_size("seq"))]
+    f_taps, f_mod, f_gain, f_in, f_out = fetched
+    small = jnp.concatenate([f_taps, f_mod.reshape(-1, channels), f_gain[None]])
+    got_small = lax.ppermute(small, "section", perm=to_first)
+    in_half, out_half = f_in.shape[0] // 2, f_out.shape[0] // 2
+    halves = jnp.concatenate(
+        [
+            lax.dynamic_slice_in_dim(f_in, core * in_half, in_half, 0).reshape(-1),
+            lax.dynamic_slice_in_dim(f_out, core * out_half, out_half, 0).reshape(-1),
+        ]
+    )
+    got = lax.ppermute(halves, "section", perm=to_first)
+    other = lax.ppermute(got, "seq", perm=siblings)
+    low, high = jnp.where(core == 0, got, other), jnp.where(core == 0, other, got)
+    split = in_half * f_in.shape[1]
+    got_in = jnp.concatenate([low[:split], high[:split]]).reshape(f_in.shape)
+    got_out = jnp.concatenate([low[split:], high[split:]]).reshape(f_out.shape)
+    tap_count = f_taps.shape[0]
+    got_taps = got_small[:tap_count]
+    got_mod = got_small[tap_count:-1].reshape(f_mod.shape)
+    got_gain = got_small[-1]
+    second_params = tuple(
+        jnp.where(first, g, p)
+        for g, p in zip((got_taps, got_mod, got_gain, got_in, got_out), first_params)
+    )
+
+    lead_out, second_params = temporal(lead_in, lead_taps[None], second_params)
+
+    swapped = lax.ppermute(lead_out, "section", perm=[(0, 1), (1, 0)])
+    first_acts = jnp.where(first, lead_out, swapped)
+    second_seed = jnp.where(first, swapped, lead_out)
     second_mixed, second_saved = spatial_forward(first_acts, *second_params)
     second_grad = spatial_backward(second_saved, second_seed, *second_params)
 
     tail_in = jnp.where(first, second_grad, second_mixed)
     tail_taps = jnp.where(first, band[::-1], band)
-    tail_out = temporal(tail_in, tail_taps[None])
+    tail_out, _ = temporal(tail_in, tail_taps[None], ())
     first_grad = spatial_backward(first_saved, tail_out, *first_params)
 
-    activations = jnp.where(first, first_acts, tail_out)
+    activations = jnp.where(first, lead_out, tail_out)
     input_grads = jnp.where(first, first_grad, second_grad)
     return (activations[None], input_grads[None])
 

time: 164 us -> 189 us (1.15)
  blocking collectives: 25.7 us -> 51.8 us
  waiting for transfers between devices: 58.6 us -> 37.1 us
  local copies, waits for them, and re-layouts: 10.2 us -> 28.3 us
  other arithmetic: 28.9 us -> 34.4 us
  starting transfers between devices: 23.7 us -> 19 us
    all_to_all x1 -> x2, blocking collectives: 25.7 us -> 51.8 us  [temporal(): lax.all_to_all(banded, 'seq', split_axis=1, concat_axis=2, tiled=True)]
    all_to_all x2 -> x0, waiting for transfers between devices: 21 us -> none  [the longest x1 17.9 us: temporal_shared(): lax.all_to_all(grouped, 'seq', split_axis=2, concat_axis=1, tiled=True)]
    all_to_all x2 -> x0, starting transfers between devices: 12.8 us -> none  [the longest x1 7.38 us: temporal_shared(): lax.all_to_all(grouped, 'seq', split_axis=2, concat_axis=1, tiled=True)]
    slice x0 -> x8, local copies, waits for them, and re-layouts: none -> 11.2 us  [the longest x4 5.35 us: on_device(): got_out = jnp.concatenate([low[split:], high[split:]]).reshape(f_out.shape)]
    all_to_all x1 -> x2, starting transfers between devices: 4.31 us -> 11.7 us  [temporal(): lax.all_to_all(grouped, 'seq', split_axis=2, concat_axis=1, tiled=True)]
    reshape x1 -> x6, local copies, waits for them, and re-layouts: 1.01 us -> 5.75 us  [the longest x2 2.03 us: temporal(): values.reshape(clip_count, frame_count, groups, pixel_count // groups, ch...]
    select_n x5 -> x8, other arithmetic: 6.57 us -> 9.97 us  [the longest x5 6.23 us: on_device(): jnp.where(first, g, p)]
    unnamed x80 -> x135, local copies, waits for them, and re-layouts: 2.38 us -> 5.78 us
  transfers between devices with their start and end apart: 10 -> 6, of which waited for: 6 -> 3; matrix products, arithmetic and copies ran while one was open for 7% -> 16% of each run, Pallas kernels for 0% -> 0%
where the time goes in v9:
time: 189 us; the launch traced here: 187 us
  blocking collectives  51.8 us (27%)
  waiting for transfers between devices  37.1 us (20%)
  other arithmetic  34.4 us (18%)
  local copies, waits for them, and re-layouts  28.3 us (15%)
  starting transfers between devices  19 us (10%)
  matrix products  15.1 us (8%)
    all_to_all x2, blocking collectives, temporal(): lax.all_to_all(banded, 'seq', split_axis=1, concat_axis=2, tiled=True)  51.8 us
    all_to_all x2, waiting for transfers between devices, temporal(): lax.all_to_all(grouped, 'seq', split_axis=2, concat_axis=1, tiled=True)  18.7 us
    ppermute x1, waiting for transfers between devices, on_device(): swapped = lax.ppermute(lead_out, 'section', perm=[(0, 1), (1, 0)])  18.2 us
    all_to_all x2, starting transfers between devices, temporal(): lax.all_to_all(grouped, 'seq', split_axis=2, concat_axis=1, tiled=True)  11.7 us
    select_n x5, other arithmetic, on_device(): jnp.where(first, g, p)  6.23 us
    unnamed x135, local copies, waits for them, and re-layouts  5.78 us
    slice x4, local copies, waits for them, and re-layouts, on_device(): got_out = jnp.concatenate([low[split:], high[split:]]).reshape(f_out.shape)  5.35 us
    ppermute x1, starting transfers between devices, on_device(): swapped = lax.ppermute(lead_out, 'section', perm=[(0, 1), (1, 0)])  4.56 us
  transfers between devices with their start and end apart: 6, of which 3 were waited for; matrix products, arithmetic and copies ran while one was open for 16% of the time, Pallas kernels for 0%

profile of v9, /device:TPU:0, one launch (start us, length us, event | category | flops | bytes accessed | tf_op | source)
XLA Modules:
  0.0 187.2 jit_solution(611354665888858645)
XLA Ops:
  5.1 1.9 %multiply_reduce_fusion.2 = (f32[2,32,16]{2,1,0:T(8,128)S(1)}, f32[2,1,32,16,384]{4,3,2,0,1:T(8,128)S(1)}) fusion(f32[2,384]{1,0:T(2,128)S(1)} %get-tuple-element.100, f32[2,384]{1,0:T(2,128)S(1)} %get-tuple-element.101, f32[384]{0:T(512)S(1)} %get-tuple-element.69, f32[384]{0:T(512)S(1)} %get-tuple-element.62, f32[384]{0:T(512)S(1)} %get-tuple-element.63, ...), kind=kLoop, calls=%fused_computation.182 | loop fusion | flops 8256512 | bytes 3169792 | tf_op jit(solution)/shard_map/reduce_sum | solution.py:32
  8.4 2.8 %multiply_convert_fusion.3 = (bf16[1024,768]{1,0:T(8,128)(2,1)S(1)}, f32[1024,768]{1,0:T(8,128)}) fusion(bf16[1024,384]{1,0:T(8,128)(2,1)S(1)} %bitcast.175, bf16[1,384,768]{2,1,0:T(8,128)(2,1)S(1)} %copy-done.9), kind=kOutput, calls=%fused_computation.52 | convolution fusion | flops 607911936 | bytes 6094848 | tf_op jit(solution)/shard_map/dot_general | solution.py:34
  11.2 1.9 %fusion.114 = bf16[2,1,512,384]{3,2,0,1:T(8,128)(2,1)} fusion(bf16[2,512,768]{2,1,0:T(8,128)(2,1)S(1)} %bitcast.190, bf16[2,1,512,384]{3,2,1,0:T(8,128)(2,1)S(1)} %copy-done.63, pred[]{:T(512)S(6)} %eq.9, bf16[1,768,384]{2,1,0:T(8,128)(2,1)S(1)} %copy-done.14, bf16[2,1,512,384]{3,2,1,0:T(8,128)(2,1)S(1)} %copy-done.19), kind=kOutput, calls=%fused_computation.189 | convolution fusion | flops 605552640 | bytes 4521985 | tf_op jit(solution)/shard_map/dot_general | solution.py:36
  14.3 1.9 %pad_maximum_fusion = bf16[294912]{0:T(1024)(128)(2,1)} fusion(bf16[147456]{0:T(1024)(128)(2,1)} %reshape.732, bf16[147456]{0:T(1024)(128)(2,1)S(1)} %reshape.731), kind=kLoop, calls=%fused_computation.200 | loop fusion | flops 1179648 | bytes 1179648 | tf_op jit(solution)/shard_map/concatenate | solution.py:103
  18.5 7.4 %all-to-all-start = ((bf16[2,1,16,32,384]{4,3,0,1,2:T(8,128)(2,1)}), bf16[2,1,16,32,384]{4,3,0,1,2:T(8,128)(2,1)S(1)}, u32[]{:S(2)}, u32[]{:S(2)}) async-start(bf16[2,1,16,32,384]{4,3,0,1,2:T(8,128)(2,1)} %copy.27), calls=%async_computation | async-start | bytes 1572864 | tf_op jit(solution)/shard_map/all_to_all | solution.py:75
  32.4 2.0 %rev.2 = f32[9,384]{1,0:T(8,128)} reverse(f32[9,384]{1,0:T(8,128)} %bitcast.179), dimensions={0} | reverse | bytes 27648 | tf_op jit(solution)/shard_map/rev | solution.py:93
  48.1 1.9 %slice.410 = bf16[192,768]{1,0:T(8,128)(2,1)} reshape(bf16[147456]{0:T(1024)(128)(2,1)} %get-tuple-element.81) | data formatting | bytes 589824 | tf_op jit(solution)/shard_map/slice | solution.py:113
  50.1 1.8 slice.416
  51.9 1.9 %slice.412 = bf16[192,768]{1,0:T(8,128)(2,1)} reshape(bf16[147456]{0:T(1024)(128)(2,1)} %get-tuple-element.83) | data formatting | bytes 589824 | tf_op jit(solution)/shard_map/slice | solution.py:113
  53.8 2.1 %maximum_select_fusion.1 = bf16[768,384]{1,0:T(8,128)(2,1)} fusion(bf16[384,384]{1,0:T(8,128)(2,1)} %slice.416, bf16[384,384]{1,0:T(8,128)(2,1)} %slice.414, pred[]{:T(512)S(6)} %eq.9, bf16[1,768,384]{2,1,0:T(8,128)(2,1)S(1)} %copy-done.14), kind=kLoop, calls=%fused_computation.202 | loop fusion | flops 1474560 | bytes 1769473 | tf_op jit(solution)/shard_map/jit(_where)/select_n | solution.py:120
  58.5 26.0 %all_to_all.42 = bf16[2,16,1,32,384]{4,3,0,2,1:T(8,128)(2,1)S(1)} all-to-all(bf16[2,16,1,32,384]{4,3,0,2,1:T(8,128)(2,1)S(1)} %fusion.118), channel_id=1, replica_groups=mesh['section'=2,'seq'=16] {'seq'}, dimensions={1} | all-to-all | bytes 1572864 | tf_op jit(solution)/shard_map/all_to_all | solution.py:80
  85.5 4.6 %collective-permute-start.3 = (bf16[2,1,512,384]{3,2,0,1:T(8,128)(2,1)S(1)}, bf16[2,1,512,384]{3,2,0,1:T(8,128)(2,1)S(1)}, u32[]{:S(2)}, u32[]{:S(2)}) collective-permute-start(bf16[2,1,512,384]{3,2,0,1:T(8,128)(2,1)S(1)} %bitcast.163), channel_id=1, source_target_pairs={{0,16},{16,0},{1,17},{17,1},{2,18},{18,2},{3,19},{19,3},{4,20},{20... | collective-permute-start | bytes 2359304 | tf_op jit(solution)/shard_map/ppermute | solution.py:126
  90.2 18.2 %collective-permute-done.3 = bf16[2,1,512,384]{3,2,0,1:T(8,128)(2,1)S(1)} collective-permute-done((bf16[2,1,512,384]{3,2,0,1:T(8,128)(2,1)S(1)}, bf16[2,1,512,384]{3,2,0,1:T(8,128)(2,1)S(1)}, u32[]{:S(2)}, u32[]{:S(2)}) %collective-permute-start.3) | collective-permute-done | bytes 786464 | tf_op jit(solution)/shard_map/ppermute | solution.py:126
  109.5 1.9 %multiply_reduce_fusion.1 = (f32[2,32,16]{2,1,0:T(8,128)S(1)}, f32[2,1,32,16,384]{4,3,2,0,1:T(8,128)S(1)}) fusion(f32[2,384]{1,0:T(2,128)S(1)} %bitcast.184, f32[2,384]{1,0:T(2,128)S(1)} %bitcast.180, f32[384]{0:T(512)S(1)} %get-tuple-element.43, f32[384]{0:T(512)S(1)} %get-tuple-element.44, f32[384]{0:T(512)S(1)} %get-tuple-element.45, ...), kind=kLoop, calls=%fused_computation.180 | loop fusion | flops 8256512 | bytes 3169792 | tf_op jit(solution)/shard_map/reduce_sum | solution.py:32
  113.7 2.1 %fusion.111 = f32[1024,384]{1,0:T(8,128)} fusion(bf16[768,384]{1,0:T(8,128)(2,1)S(1)} %copy-done.20, f32[1024,768]{1,0:T(8,128)S(1)} %fusion.130), kind=kOutput, calls=%fused_computation.184 | convolution fusion | flops 607911936 | bytes 5308416 | tf_op jit(solution)/shard_map/dot_general | solution.py:36
  117.3 2.2 %multiply_reduce_fusion = (f32[1024]{0:T(1024)S(1)}, f32[1024,384]{1,0:T(8,128)}) fusion(f32[2,1,32,16,384]{4,3,2,0,1:T(8,128)S(1)} %get-tuple-element.71, f32[384]{0:T(512)S(1)} %copy-done.33, f32[2,384]{1,0:T(2,128)S(1)} %bitcast.186, f32[2,384]{1,0:T(2,128)S(1)} %bitcast.182, bf16[1024,768]{1,0:T(8,128)(2,1)S(1)} %multiply_convert_fusion.2, ...), kind=kOutput, calls=%fused_computation.178 | convolution fusion | flops 606731264 | bytes 5320192 | tf_op jit(solution)/shard_map/dot_general | solution.py:49
  119.6 2.0 %subtract_multiply_fusion.1 = f32[2,1,32,16,384]{4,3,2,0,1:T(8,128)S(1)} fusion(f32[2,1,32,16,384]{4,3,2,0,1:T(8,128)} %bitcast.166, f32[2,1,32,16,384]{4,3,2,0,1:T(8,128)S(1)} %get-tuple-element.71, f32[2,32,16]{2,1,0:T(8,128)S(1)} %div.30, f32[2,32,16]{2,1,0:T(8,128)S(1)} %get-tuple-element.88, f32[384]{0:T(512)S(1)} %copy-done.33, ...), kind=kLoop, calls=%fused_computation.177 | loop fusion | flops 3145728 | bytes 4738560 | tf_op jit(solution)/shard_map/mul | solution.py:53
  121.7 1.8 fusion.77
  125.2 4.3 %all-to-all-start.2 = ((bf16[2,1,16,32,384]{4,3,0,1,2:T(8,128)(2,1)}), bf16[2,1,16,32,384]{4,3,0,1,2:T(8,128)(2,1)}, u32[]{:S(2)}, u32[]{:S(2)}) async-start(bf16[2,1,16,32,384]{4,3,0,1,2:T(8,128)(2,1)} %copy.30), calls=%async_computation.2 | async-start | bytes 1572864 | tf_op jit(solution)/shard_map/all_to_all | solution.py:75
  129.6 18.6 %all-to-all-done.2 = bf16[2,1,16,32,384]{4,3,0,1,2:T(8,128)(2,1)} async-done(((bf16[2,1,16,32,384]{4,3,0,1,2:T(8,128)(2,1)}), bf16[2,1,16,32,384]{4,3,0,1,2:T(8,128)(2,1)}, u32[]{:S(2)}, u32[]{:S(2)}) %all-to-all-start.2) | async-done | bytes 786464 | tf_op jit(solution)/shard_map/all_to_all | solution.py:75
  150.6 25.8 %all_to_all.43 = bf16[2,16,1,32,384]{4,3,0,2,1:T(8,128)(2,1)S(1)} all-to-all(bf16[2,16,1,32,384]{4,3,0,2,1:T(8,128)(2,1)S(1)} %fusion.117), channel_id=1, replica_groups=mesh['section'=2,'seq'=16] {'seq'}, dimensions={1} | all-to-all | bytes 1572864 | tf_op jit(solution)/shard_map/all_to_all | solution.py:80
  179.3 2.2 %fusion.105 = (f32[1024]{0:T(1024)S(1)}, f32[1024,384]{1,0:T(8,128)}) fusion(f32[2,1,32,16,384]{4,3,2,0,1:T(8,128)S(1)} %get-tuple-element.73, f32[384]{0:T(512)S(1)} %copy-done.30, f32[2,384]{1,0:T(2,128)S(1)} %copy-done.26, f32[2,384]{1,0:T(2,128)S(1)} %copy-done.28, bf16[1024,768]{1,0:T(8,128)(2,1)S(1)} %multiply_convert_fusion, ...), kind=kOutput, calls=%fused_computation.164 | convolution fusion | flops 606731264 | bytes 5320192 | tf_op jit(solution)/shard_map/dot_general | solution.py:49
  181.7 1.9 %subtract_multiply_fusion = f32[2,1,32,16,384]{4,3,2,0,1:T(8,128)S(1)} fusion(f32[2,1,32,16,384]{4,3,2,0,1:T(8,128)} %bitcast.167, f32[2,1,32,16,384]{4,3,2,0,1:T(8,128)S(1)} %get-tuple-element.73, f32[2,32,16]{2,1,0:T(8,128)S(1)} %div.32, f32[2,32,16]{2,1,0:T(8,128)S(1)} %copy-done.23, f32[384]{0:T(512)S(1)} %copy-done.30, f32[2,32,16]{2,1,0:T(8,128)S(1)} %copy-done.22, ...), kind=kLoop, calls=%fused_computation.175 | loop fusion | flops 3145728 | bytes 4738560 | tf_op jit(solution)/shard_map/mul | solution.py:53
  183.7 1.8 fusion.94
  (194 shorter events, 46.5 us)
Async XLA Ops:
  1.5 3.5 %copy-start.35 = (f32[384]{0:T(512)}, f32[384]{0:T(512)S(1)}, u32[]{:S(2)}) copy-start(f32[384]{0:T(512)S(1)} %get-tuple-element.61) | copy-start | bytes 4612
  1.5 3.5 %copy-start.37 = (f32[384]{0:T(512)}, f32[384]{0:T(512)S(1)}, u32[]{:S(2)}) copy-start(f32[384]{0:T(512)S(1)} %get-tuple-element.62) | copy-start | bytes 4612
  1.5 3.5 %copy-start.39 = (f32[384]{0:T(512)}, f32[384]{0:T(512)S(1)}, u32[]{:S(2)}) copy-start(f32[384]{0:T(512)S(1)} %get-tuple-element.63) | copy-start | bytes 4612
  1.5 3.5 %copy-start.41 = (f32[384]{0:T(512)}, f32[384]{0:T(512)S(1)}, u32[]{:S(2)}) copy-start(f32[384]{0:T(512)S(1)} %get-tuple-element.64) | copy-start | bytes 4612
  1.5 3.5 %copy-start.43 = (f32[384]{0:T(512)}, f32[384]{0:T(512)S(1)}, u32[]{:S(2)}) copy-start(f32[384]{0:T(512)S(1)} %get-tuple-element.65) | copy-start | bytes 4612
  1.6 3.5 %copy-start.45 = (f32[384]{0:T(512)}, f32[384]{0:T(512)S(1)}, u32[]{:S(2)}) copy-start(f32[384]{0:T(512)S(1)} %get-tuple-element.66) | copy-start | bytes 4612
  1.6 3.5 %copy-start.47 = (f32[384]{0:T(512)}, f32[384]{0:T(512)S(1)}, u32[]{:S(2)}) copy-start(f32[384]{0:T(512)S(1)} %get-tuple-element.67) | copy-start | bytes 4612
  1.6 3.5 %copy-start.49 = (f32[384]{0:T(512)}, f32[384]{0:T(512)S(1)}, u32[]{:S(2)}) copy-start(f32[384]{0:T(512)S(1)} %get-tuple-element.68) | copy-start | bytes 4612
  1.6 3.5 %copy-start.51 = (f32[384]{0:T(512)}, f32[384]{0:T(512)S(1)}, u32[]{:S(2)}) copy-start(f32[384]{0:T(512)S(1)} %get-tuple-element.69) | copy-start | bytes 4612
  14.3 3.2 %copy-start.18 = (bf16[2,1,512,384]{3,2,0,1:T(8,128)(2,1)S(1)}, bf16[2,1,512,384]{3,2,0,1:T(8,128)(2,1)}, u32[]{:S(2)}) copy-start(bf16[2,1,512,384]{3,2,0,1:T(8,128)(2,1)} %fusion.114) | copy-start | bytes 2359300
  16.2 23.8 %collective-permute-start.1 = (bf16[294912]{0:T(1024)(128)(2,1)}, bf16[294912]{0:T(1024)(128)(2,1)}, u32[]{:S(2)}, u32[]{:S(2)}) collective-permute-start(bf16[294912]{0:T(1024)(128)(2,1)} %pad_maximum_fusion), channel_id=1, source_target_pairs={{16,0},{17,1},{18,2},{19,3},{20,4},{21,5},{22,6},{23,7},{24,8},{25... | collective-permute-start | bytes 1769480 | tf_op jit(solution)/shard_map/ppermute | solution.py:109
  17.5 24.6 %copy-start.24 = (f32[1,9,384]{2,0,1:T(1,128)S(1)}, f32[1,9,384]{2,0,1:T(1,128)}, u32[]{:S(2)}) copy-start(f32[1,9,384]{2,0,1:T(1,128)} %param.10) | copy-start | bytes 41476
  18.5 38.4 %all-to-all-start = ((bf16[2,1,16,32,384]{4,3,0,1,2:T(8,128)(2,1)}), bf16[2,1,16,32,384]{4,3,0,1,2:T(8,128)(2,1)S(1)}, u32[]{:S(2)}, u32[]{:S(2)}) async-start(bf16[2,1,16,32,384]{4,3,0,1,2:T(8,128)(2,1)} %copy.27), calls=%async_computation | async-start | bytes 1572864 | tf_op jit(solution)/shard_map/all_to_all | solution.py:75
  29.8 6.8 %collective-permute-start = (f32[14,384]{1,0:T(8,128)}, f32[14,384]{1,0:T(8,128)}, u32[]{:S(2)}, u32[]{:S(2)}) collective-permute-start(f32[14,384]{1,0:T(8,128)} %pad_maximum_fusion.1), channel_id=1, source_target_pairs={{16,0},{17,1},{18,2},{19,3},{20,4},{21,5},{22,6},{23,7},{24,8},{25... | collective-permute-start | bytes 64520 | tf_op jit(solution)/shard_map/ppermute | solution.py:101
  40.0 3.5 %collective-permute-start.2 = (bf16[294912]{0:T(1024)(128)(2,1)}, bf16[294912]{0:T(1024)(128)(2,1)S(1)}, u32[]{:S(2)}, u32[]{:S(2)}) collective-permute-start(bf16[294912]{0:T(1024)(128)(2,1)} %collective-permute-done.1), channel_id=1, source_target_pairs={{0,1},{1,0},{2,3},{3,2},{4,5},{5,4},{6,7},{7,6},{8,9},{9,8},{10,11... | collective-permute-start | bytes 1769480 | tf_op jit(solution)/shard_map/ppermute | solution.py:110
  58.5 31.6 %copy-start.34 = (f32[2,2,384]{2,1,0:T(2,128)S(1)}, f32[2,2,384]{2,1,0:T(2,128)}, u32[]{:S(2)}) copy-start(f32[2,2,384]{2,1,0:T(2,128)} %broadcast_select_fusion.4) | copy-start | bytes 18436
  58.5 31.6 %copy-start.32 = (f32[9,384]{1,0:T(8,128)S(1)}, f32[9,384]{1,0:T(8,128)}, u32[]{:S(2)}) copy-start(f32[9,384]{1,0:T(8,128)} %slice_select_fusion) | copy-start | bytes 41476
  85.5 24.0 %copy-start.4 = (bf16[2,16,1,32,384]{4,3,1,0,2:T(8,128)(2,1)}, bf16[2,16,1,32,384]{4,3,1,0,2:T(8,128)(2,1)S(1)}, u32[]{:S(2)}) copy-start(bf16[2,16,1,32,384]{4,3,1,0,2:T(8,128)(2,1)S(1)} %copy.32) | copy-start | bytes 2359300
  85.5 22.9 %collective-permute-start.3 = (bf16[2,1,512,384]{3,2,0,1:T(8,128)(2,1)S(1)}, bf16[2,1,512,384]{3,2,0,1:T(8,128)(2,1)S(1)}, u32[]{:S(2)}, u32[]{:S(2)}) collective-permute-start(bf16[2,1,512,384]{3,2,0,1:T(8,128)(2,1)S(1)} %bitcast.163), channel_id=1, source_target_pairs={{0,16},{16,0},{1,17},{17,1},{2,18},{18,2},{3,19},{19,3},{4,20},{20... | collective-permute-start | bytes 2359304 | tf_op jit(solution)/shard_map/ppermute | solution.py:126
  119.6 3.9 %copy-start.13 = (f32[1024,384]{1,0:T(8,128)S(1)}, f32[1024,384]{1,0:T(8,128)}, u32[]{:S(2)}) copy-start(f32[1024,384]{1,0:T(8,128)} %fusion.111) | copy-start | bytes 4718596
  124.2 5.3 %copy-start.31 = (f32[1,9,384]{2,1,0:T(8,128)S(1)}, f32[1,9,384]{2,1,0:T(8,128)}, u32[]{:S(2)}) copy-start(f32[1,9,384]{2,1,0:T(8,128)} %get-tuple-element.84) | copy-start | bytes 41476
  125.2 23.0 %all-to-all-start.2 = ((bf16[2,1,16,32,384]{4,3,0,1,2:T(8,128)(2,1)}), bf16[2,1,16,32,384]{4,3,0,1,2:T(8,128)(2,1)}, u32[]{:S(2)}, u32[]{:S(2)}) async-start(bf16[2,1,16,32,384]{4,3,0,1,2:T(8,128)(2,1)} %copy.30), calls=%async_computation.2 | async-start | bytes 1572864 | tf_op jit(solution)/shard_map/all_to_all | solution.py:75
  149.6 26.7 %copy-start.3 = (bf16[2,16,1,32,384]{4,3,0,2,1:T(8,128)(2,1)S(1)}, bf16[2,16,1,32,384]{4,3,0,2,1:T(8,128)(2,1)}, u32[]{:S(2)}) copy-start(bf16[2,16,1,32,384]{4,3,0,2,1:T(8,128)(2,1)} %copy-done.2) | copy-start | bytes 2359300
  150.5 26.9 %copy-start.64 = (f32[1024,768]{1,0:T(8,128)S(1)}, f32[1024,768]{1,0:T(8,128)}, u32[]{:S(2)}) copy-start(f32[1024,768]{1,0:T(8,128)} %get-tuple-element.95) | copy-start | bytes 9437188
  (47 other events, 76.6 us)

commit v10 on v8

--- a/solution.py
+++ b/solution.py
@@ -80,22 +80,6 @@
     return back.reshape(values.shape)
 
 
-def temporal_shared(values, tap_table):
-    clip_count, frame_count, pixel_count, channels = values.shape
-    groups = lax.axis_size("seq")
-    planes = lax.axis_size("section")
-    grouped = values.reshape(clip_count, frame_count, groups, pixel_count // groups, channels)
-    pixel_view = lax.all_to_all(grouped, "seq", split_axis=2, concat_axis=1, tiled=True)
-    pixel_view = pixel_view.reshape(clip_count, groups * frame_count, pixel_count // groups, channels)
-    banded = band_frames(pixel_view, tap_table)
-    banded = jnp.broadcast_to(
-        banded[:, None], (clip_count, planes) + banded.shape[1:]
-    ).reshape(clip_count, planes * groups * frame_count, 1, pixel_count // groups, channels)
-    back = lax.all_to_all(banded, ("section", "seq"), split_axis=1, concat_axis=2, tiled=True)
-    back = back.reshape(clip_count, frame_count, planes, pixel_count, channels)
-    return jnp.moveaxis(back, 2, 0)
-
-
 def on_device(clips, cotangent, spatial_taps, modulation, norm_gain, w_in, w_out, band_taps):
     first = lax.axis_index("section") == 0
     taps, mod, gain = spatial_taps[0], modulation[0], norm_gain[0]
@@ -126,17 +110,22 @@
     first_mixed, first_saved = spatial_forward(clips, *first_params)
     lead_in = jnp.where(first, first_mixed, cotangent)
     lead_taps = jnp.where(first, band, band[::-1])
-    first_acts, second_seed = temporal_shared(lead_in, lead_taps[None])
-    second_mixed, second_saved = spatial_forward(first_acts, *second_params)
+    lead_out = temporal(lead_in, lead_taps[None])
+
+    second_seed = lax.ppermute(lead_out, "section", perm=to_first)
+    second_mixed, second_saved = spatial_forward(lead_out, *second_params)
     second_grad = spatial_backward(second_saved, second_seed, *second_params)
 
-    tail_in = jnp.where(first, second_grad, second_mixed)
+    to_second = [(0, 1)]
+    sent_mixed = lax.ppermute(second_mixed, "section", perm=to_second)
+    sent_grad = lax.ppermute(second_grad, "section", perm=to_second)
+    tail_in = jnp.where(first, second_grad, sent_mixed)
     tail_taps = jnp.where(first, band[::-1], band)
     tail_out = temporal(tail_in, tail_taps[None])
     first_grad = spatial_backward(first_saved, tail_out, *first_params)
 
-    activations = jnp.where(first, first_acts, tail_out)
-    input_grads = jnp.where(first, first_grad, second_grad)
+    activations = jnp.where(first, lead_out, tail_out)
+    input_grads = jnp.where(first, first_grad, sent_grad)
     return (activations[None], input_grads[None])
 
 

time: 164 us -> 165 us (level)
  blocking collectives: 25.7 us -> 0 us
  starting transfers between devices: 23.7 us -> 41.8 us
  local copies, waits for them, and re-layouts: 10.2 us -> 14.8 us
    all_to_all x1 -> x0, blocking collectives: 25.7 us -> none  [temporal(): lax.all_to_all(banded, 'seq', split_axis=1, concat_axis=2, tiled=True)]
    ppermute x2, waiting for transfers between devices: 17.8 us -> 0.01 us  [fetch_halves(): got = lax.ppermute(mine, 'section', perm=to_first)]
    ppermute x0 -> x3, waiting for transfers between devices: none -> 11.6 us  [the longest x1 11.6 us: on_device(): second_seed = lax.ppermute(lead_out, 'section', perm=to_first)]
    ppermute x0 -> x3, starting transfers between devices: none -> 10.9 us  [the longest x1 5.62 us: on_device(): sent_mixed = lax.ppermute(second_mixed, 'section', perm=to_second)]
    all_to_all x1 -> x2, starting transfers between devices: 4.31 us -> 13 us  [temporal(): lax.all_to_all(grouped, 'seq', split_axis=2, concat_axis=1, tiled=True)]
    all_to_all x2, waiting for transfers between devices: 21 us -> 26.1 us  [temporal(): lax.all_to_all(banded, 'seq', split_axis=1, concat_axis=2, tiled=True)]
    unnamed x80 -> x128, local copies, waits for them, and re-layouts: 2.38 us -> 6.45 us
    all_to_all x1 -> x2, waiting for transfers between devices: 18.7 us -> 22.2 us  [temporal(): lax.all_to_all(grouped, 'seq', split_axis=2, concat_axis=1, tiled=True)]
  transfers between devices with their start and end apart: 10 -> 14, of which waited for: 6 -> 5; matrix products, arithmetic and copies ran while one was open for 7% -> 23% of each run, Pallas kernels for 0% -> 0%
where the time goes in v10:
time: 165 us; the launch traced here: 163 us
  waiting for transfers between devices  59.9 us (36%)
  starting transfers between devices  41.8 us (25%)
  other arithmetic  30.4 us (18%)
  matrix products  14.9 us (9%)
  local copies, waits for them, and re-layouts  14.8 us (9%)
    all_to_all x2, waiting for transfers between devices, temporal(): lax.all_to_all(banded, 'seq', split_axis=1, concat_axis=2, tiled=True)  26.1 us
    all_to_all x2, waiting for transfers between devices, temporal(): lax.all_to_all(grouped, 'seq', split_axis=2, concat_axis=1, tiled=True)  22.2 us
    all_to_all x2, starting transfers between devices, temporal(): lax.all_to_all(grouped, 'seq', split_axis=2, concat_axis=1, tiled=True)  13 us
    ppermute x1, waiting for transfers between devices, on_device(): second_seed = lax.ppermute(lead_out, 'section', perm=to_first)  11.6 us
    all_to_all x2, starting transfers between devices, temporal(): lax.all_to_all(banded, 'seq', split_axis=1, concat_axis=2, tiled=True)  10.9 us
    unnamed x128, local copies, waits for them, and re-layouts  6.45 us
    ppermute x1, starting transfers between devices, on_device(): sent_mixed = lax.ppermute(second_mixed, 'section', perm=to_second)  5.62 us
    dot_general x2, matrix products, spatial_backward(): jnp.dot(flat_grad, w_out.T, preferred_element_type=jnp.float32)  4.84 us
  transfers between devices with their start and end apart: 14, of which 5 were waited for; matrix products, arithmetic and copies ran while one was open for 23% of the time, Pallas kernels for 0%

profile of v10, /device:TPU:0, one launch (start us, length us, event | category | flops | bytes accessed | tf_op | source)
XLA Modules:
  0.0 163.3 jit_solution(12730402365250992904)
XLA Ops:
  3.6 1.9 %multiply_reduce_fusion.2 = (f32[2,32,16]{2,1,0:T(8,128)S(1)}, f32[2,1,32,16,384]{4,3,2,0,1:T(8,128)S(1)}) fusion(f32[2,384]{1,0:T(2,128)S(1)} %get-tuple-element.76, f32[2,384]{1,0:T(2,128)S(1)} %get-tuple-element.77, f32[384]{0:T(512)S(1)} %get-tuple-element.49, f32[384]{0:T(512)S(1)} %get-tuple-element.42, f32[384]{0:T(512)S(1)} %get-tuple-element.43, ...), kind=kLoop, calls=%fused_computation.182 | loop fusion | flops 8256512 | bytes 3169792 | tf_op jit(solution)/shard_map/reduce_sum | solution.py:32
  7.5 2.8 %multiply_convert_fusion.3 = (bf16[1024,768]{1,0:T(8,128)(2,1)S(1)}, f32[1024,768]{1,0:T(8,128)}) fusion(bf16[1024,384]{1,0:T(8,128)(2,1)S(1)} %bitcast.167, bf16[1,384,768]{2,1,0:T(8,128)(2,1)S(1)} %copy-done.6), kind=kOutput, calls=%fused_computation.52 | convolution fusion | flops 607911936 | bytes 6094848 | tf_op jit(solution)/shard_map/dot_general | solution.py:34
  12.3 7.5 %all-to-all-start = ((bf16[2,1,16,32,384]{4,3,0,1,2:T(8,128)(2,1)}), bf16[2,1,16,32,384]{4,3,0,1,2:T(8,128)(2,1)S(1)}, u32[]{:S(2)}, u32[]{:S(2)}) async-start(bf16[2,1,16,32,384]{4,3,0,1,2:T(8,128)(2,1)} %copy.27), calls=%async_computation | async-start | bytes 1572864 | tf_op jit(solution)/shard_map/all_to_all | solution.py:75
  29.8 2.0 %rev.2 = f32[9,384]{1,0:T(8,128)} reverse(f32[9,384]{1,0:T(8,128)} %bitcast.170), dimensions={0} | reverse | bytes 27648 | tf_op jit(solution)/shard_map/rev | solution.py:112
  35.1 3.5 %all-to-all-done = bf16[2,1,16,32,384]{4,3,0,1,2:T(8,128)(2,1)S(1)} async-done(((bf16[2,1,16,32,384]{4,3,0,1,2:T(8,128)(2,1)}), bf16[2,1,16,32,384]{4,3,0,1,2:T(8,128)(2,1)S(1)}, u32[]{:S(2)}, u32[]{:S(2)}) %all-to-all-start) | async-done | bytes 786464 | tf_op jit(solution)/shard_map/all_to_all | solution.py:75
  39.3 1.8 %fusion.117 = bf16[2,16,1,32,384]{4,3,0,2,1:T(8,128)(2,1)} fusion(f32[2,16,32,384]{3,2,0,1:T(8,128)S(1)} %bitcast_convert_fusion.1, f32[384]{0:T(512)S(1)} %copy-done.52, f32[384]{0:T(512)S(1)} %copy-done.53, f32[384]{0:T(512)S(1)} %copy-done.54, f32[384]{0:T(512)S(1)} %copy-done.55, f32[384]{0:T(512)S(1)} %copy-done.56, f32[384]{0:T(512)S(1)} %copy-done.57, ...), kind=kLoop, calls=%fused_computation.197 | loop fusion | flops 7471104 | bytes 2373120 | tf_op jit(solution)/shard_map/reshape | solution.py:78
  41.1 5.5 %all-to-all-start.1 = ((bf16[2,16,1,32,384]{4,3,0,2,1:T(8,128)(2,1)}), bf16[2,16,1,32,384]{4,3,0,2,1:T(8,128)(2,1)S(1)}, u32[]{:S(2)}, u32[]{:S(2)}) async-start(bf16[2,16,1,32,384]{4,3,0,2,1:T(8,128)(2,1)} %fusion.117), calls=%async_computation.1 | async-start | bytes 1572864 | tf_op jit(solution)/shard_map/all_to_all | solution.py:79
  49.9 2.1 %fusion.118 = bf16[384,768]{1,0:T(8,128)(2,1)} fusion(bf16[192,768]{1,0:T(8,128)(2,1)S(1)} %collective-permute-done.4, bf16[192,768]{1,0:T(8,128)(2,1)} %collective-permute-done.3, bf16[1,384,768]{2,1,0:T(8,128)(2,1)S(1)} %copy-done.6, pred[]{:T(512)S(6)} %eq.10, pred[]{:T(512)S(6)} %eq.9), kind=kLoop, calls=%fused_computation.199 | loop fusion | flops 2949120 | bytes 1769474 | tf_op jit(solution)/shard_map/jit(_where)/select_n | solution.py:104
  52.0 2.1 %fusion.119 = bf16[768,384]{1,0:T(8,128)(2,1)} fusion(bf16[384,384]{1,0:T(8,128)(2,1)S(1)} %collective-permute-done.6, bf16[384,384]{1,0:T(8,128)(2,1)} %collective-permute-done.5, bf16[1,768,384]{2,1,0:T(8,128)(2,1)S(1)} %copy-done.8, pred[]{:T(512)S(6)} %eq.10, pred[]{:T(512)S(6)} %eq.9), kind=kLoop, calls=%fused_computation.201 | loop fusion | flops 2949120 | bytes 1769474 | tf_op jit(solution)/shard_map/jit(_where)/select_n | solution.py:104
  54.1 11.2 %all-to-all-done.1 = bf16[2,16,1,32,384]{4,3,0,2,1:T(8,128)(2,1)S(1)} async-done(((bf16[2,16,1,32,384]{4,3,0,2,1:T(8,128)(2,1)}), bf16[2,16,1,32,384]{4,3,0,2,1:T(8,128)(2,1)S(1)}, u32[]{:S(2)}, u32[]{:S(2)}) %all-to-all-start.1) | async-done | bytes 786464 | tf_op jit(solution)/shard_map/all_to_all | solution.py:79
  66.5 1.9 %multiply_reduce_fusion.1 = (f32[2,32,16]{2,1,0:T(8,128)S(1)}, f32[2,1,32,16,384]{4,3,2,0,1:T(8,128)S(1)}) fusion(f32[2,384]{1,0:T(2,128)S(1)} %copy-done.22, f32[2,384]{1,0:T(2,128)S(1)} %copy-done.23, f32[384]{0:T(512)S(1)} %get-tuple-element.23, f32[384]{0:T(512)S(1)} %get-tuple-element.24, f32[384]{0:T(512)S(1)} %get-tuple-element.25, ...), kind=kLoop, calls=%fused_computation.180 | loop fusion | flops 8256512 | bytes 3169792 | tf_op jit(solution)/shard_map/reduce_sum | solution.py:32
  73.6 5.6 %collective-permute-start.8 = (bf16[2,1,512,384]{3,2,0,1:T(8,128)(2,1)}, bf16[2,1,512,384]{3,2,0,1:T(8,128)(2,1)}, u32[]{:S(2)}, u32[]{:S(2)}) collective-permute-start(bf16[2,1,512,384]{3,2,0,1:T(8,128)(2,1)} %add_convert_fusion), channel_id=1, source_target_pairs={{0,16},{1,17},{2,18},{3,19},{4,20},{5,21},{6,22},{7,23},{8,24},{9,... | collective-permute-start | bytes 2359304 | tf_op jit(solution)/shard_map/ppermute | solution.py:120
  79.3 11.6 %collective-permute-done = bf16[2,1,512,384]{3,2,0,1:T(8,128)(2,1)S(1)} collective-permute-done((bf16[2,1,512,384]{3,2,0,1:T(8,128)(2,1)}, bf16[2,1,512,384]{3,2,0,1:T(8,128)(2,1)S(1)}, u32[]{:S(2)}, u32[]{:S(2)}) %collective-permute-start) | collective-permute-done | bytes 786464 | tf_op jit(solution)/shard_map/ppermute | solution.py:115
  92.3 2.1 %multiply_reduce_fusion = (f32[1024]{0:T(1024)S(1)}, f32[1024,384]{1,0:T(8,128)}) fusion(f32[2,1,32,16,384]{4,3,2,0,1:T(8,128)S(1)} %get-tuple-element.53, f32[384]{0:T(512)S(1)} %copy-done.27, f32[2,384]{1,0:T(2,128)S(1)} %copy-done.22, f32[2,384]{1,0:T(2,128)S(1)} %copy-done.23, bf16[1024,768]{1,0:T(8,128)(2,1)S(1)} %multiply_convert_fusion.2, ...), kind=kOutput, calls=%fused_computation.178 | convolution fusion | flops 606731264 | bytes 5320192 | tf_op jit(solution)/shard_map/dot_general | solution.py:49
  94.6 1.9 %subtract_multiply_fusion.1 = f32[2,1,32,16,384]{4,3,2,0,1:T(8,128)S(1)} fusion(f32[2,1,32,16,384]{4,3,2,0,1:T(8,128)} %bitcast.161, f32[2,1,32,16,384]{4,3,2,0,1:T(8,128)S(1)} %get-tuple-element.53, f32[2,32,16]{2,1,0:T(8,128)S(1)} %div.30, f32[2,32,16]{2,1,0:T(8,128)S(1)} %get-tuple-element.62, f32[384]{0:T(512)S(1)} %copy-done.27, ...), kind=kLoop, calls=%fused_computation.177 | loop fusion | flops 3145728 | bytes 4738560 | tf_op jit(solution)/shard_map/mul | solution.py:53
  100.7 5.5 %all-to-all-start.2 = ((bf16[2,1,16,32,384]{4,3,0,1,2:T(8,128)(2,1)}), bf16[2,1,16,32,384]{4,3,0,1,2:T(8,128)(2,1)S(1)}, u32[]{:S(2)}, u32[]{:S(2)}) async-start(bf16[2,1,16,32,384]{4,3,0,1,2:T(8,128)(2,1)} %copy.31), calls=%async_computation.2 | async-start | bytes 1572864 | tf_op jit(solution)/shard_map/all_to_all | solution.py:75
  106.3 18.6 %all-to-all-done.2 = bf16[2,1,16,32,384]{4,3,0,1,2:T(8,128)(2,1)S(1)} async-done(((bf16[2,1,16,32,384]{4,3,0,1,2:T(8,128)(2,1)}), bf16[2,1,16,32,384]{4,3,0,1,2:T(8,128)(2,1)S(1)}, u32[]{:S(2)}, u32[]{:S(2)}) %all-to-all-start.2) | async-done | bytes 786464 | tf_op jit(solution)/shard_map/all_to_all | solution.py:75
  125.1 1.8 %fusion.116 = bf16[2,16,1,32,384]{4,3,0,2,1:T(8,128)(2,1)} fusion(f32[2,16,32,384]{3,2,0,1:T(8,128)S(1)} %bitcast_convert_fusion, f32[384]{0:T(512)S(1)} %get-tuple-element.15, f32[384]{0:T(512)S(1)} %get-tuple-element.16, f32[384]{0:T(512)S(1)} %get-tuple-element.17, f32[384]{0:T(512)S(1)} %get-tuple-element.18, f32[384]{0:T(512)S(1)} %get-tuple-element.19, ...), kind=kLoop, calls=%fused_computation.196 | loop fusion | flops 7471104 | bytes 2373120 | tf_op jit(solution)/shard_map/reshape | solution.py:78
  126.9 5.5 %all-to-all-start.3 = ((bf16[2,16,1,32,384]{4,3,0,2,1:T(8,128)(2,1)}), bf16[2,16,1,32,384]{4,3,0,2,1:T(8,128)(2,1)S(1)}, u32[]{:S(2)}, u32[]{:S(2)}) async-start(bf16[2,16,1,32,384]{4,3,0,2,1:T(8,128)(2,1)} %fusion.116), calls=%async_computation.3 | async-start | bytes 1572864 | tf_op jit(solution)/shard_map/all_to_all | solution.py:79
  132.4 3.8 %collective-permute-start.9 = (bf16[2,1,512,384]{3,2,0,1:T(8,128)(2,1)}, bf16[2,1,512,384]{3,2,0,1:T(8,128)(2,1)}, u32[]{:S(2)}, u32[]{:S(2)}) collective-permute-start(bf16[2,1,512,384]{3,2,0,1:T(8,128)(2,1)} %get-tuple-element.51), channel_id=1, source_target_pairs={{0,16},{1,17},{2,18},{3,19},{4,20},{5,21},{6,22},{7,23},{8,24},{9,... | collective-permute-start | bytes 2359304 | tf_op jit(solution)/shard_map/ppermute | solution.py:121
  136.3 14.9 %all-to-all-done.3 = bf16[2,16,1,32,384]{4,3,0,2,1:T(8,128)(2,1)S(1)} async-done(((bf16[2,16,1,32,384]{4,3,0,2,1:T(8,128)(2,1)}), bf16[2,16,1,32,384]{4,3,0,2,1:T(8,128)(2,1)S(1)}, u32[]{:S(2)}, u32[]{:S(2)}) %all-to-all-start.3) | async-done | bytes 786464 | tf_op jit(solution)/shard_map/all_to_all | solution.py:79
  152.3 3.4 %multiply_convert_fusion = bf16[1024,768]{1,0:T(8,128)(2,1)S(1)} fusion(f32[1024,768]{1,0:T(8,128)} %get-tuple-element.69, bf16[1024,384]{1,0:T(8,128)(2,1)S(1)} %bitcast.169, bf16[1,768,384]{2,1,0:T(8,128)(2,1)S(1)} %copy-done.9), kind=kOutput, calls=%fused_computation.48 | convolution fusion | flops 612630528 | bytes 6094848 | tf_op jit(solution)/shard_map/dot_general | solution.py:45
  155.7 2.2 %fusion.105 = (f32[1024]{0:T(1024)S(1)}, f32[1024,384]{1,0:T(8,128)}) fusion(f32[2,1,32,16,384]{4,3,2,0,1:T(8,128)S(1)} %get-tuple-element.55, f32[384]{0:T(512)S(1)} %copy-done.26, f32[2,384]{1,0:T(2,128)S(1)} %copy-done.19, f32[2,384]{1,0:T(2,128)S(1)} %copy-done.21, bf16[1024,768]{1,0:T(8,128)(2,1)S(1)} %multiply_convert_fusion, ...), kind=kOutput, calls=%fused_computation.164 | convolution fusion | flops 606731264 | bytes 5320192 | tf_op jit(solution)/shard_map/dot_general | solution.py:49
  160.1 1.8 %fusion.94 = bf16[2,1,32,16,384]{4,3,2,0,1:T(8,128)(2,1)S(1)} fusion(f32[2,1,32,16,384]{4,3,2,0,1:T(8,128)S(1)} %subtract_multiply_fusion, f32[384]{0:T(512)S(1)} %copy-done.45, f32[384]{0:T(512)S(1)} %copy-done.31, f32[384]{0:T(512)S(1)} %copy-done.33, f32[384]{0:T(512)S(1)} %copy-done.35, f32[384]{0:T(512)S(1)} %copy-done.37, f32[384]{0:T(512)S(1)} %copy-done.39, ...), kind=kLoop, calls=%fused_computation.150 | loop fusion | flops 7077888 | bytes 2373120 | tf_op jit(solution)/shard_map/convert_element_type | solution.py:57
  (186 shorter events, 40.6 us)
Async XLA Ops:
  2.3 3.3 %copy-start.28 = (f32[384]{0:T(512)}, f32[384]{0:T(512)S(1)}, u32[]{:S(2)}) copy-start(f32[384]{0:T(512)S(1)} %get-tuple-element.41) | copy-start | bytes 4612
  2.3 3.3 %copy-start.30 = (f32[384]{0:T(512)}, f32[384]{0:T(512)S(1)}, u32[]{:S(2)}) copy-start(f32[384]{0:T(512)S(1)} %get-tuple-element.42) | copy-start | bytes 4612
  12.3 14.2 %copy-start.17 = (f32[1,9,384]{2,0,1:T(1,128)S(1)}, f32[1,9,384]{2,0,1:T(1,128)}, u32[]{:S(2)}) copy-start(f32[1,9,384]{2,0,1:T(1,128)} %param.10) | copy-start | bytes 41476
  12.3 26.2 %all-to-all-start = ((bf16[2,1,16,32,384]{4,3,0,1,2:T(8,128)(2,1)}), bf16[2,1,16,32,384]{4,3,0,1,2:T(8,128)(2,1)S(1)}, u32[]{:S(2)}, u32[]{:S(2)}) async-start(bf16[2,1,16,32,384]{4,3,0,1,2:T(8,128)(2,1)} %copy.27), calls=%async_computation | async-start | bytes 1572864 | tf_op jit(solution)/shard_map/all_to_all | solution.py:75
  19.9 26.8 %collective-permute-start.2 = (f32[2,2,384]{2,1,0:T(2,128)}, f32[2,2,384]{2,1,0:T(2,128)}, u32[]{:S(2)}, u32[]{:S(2)}) collective-permute-start(f32[2,2,384]{2,1,0:T(2,128)} %bitcast.172), channel_id=1, source_target_pairs={{16,0},{17,1},{18,2},{19,3},{20,4},{21,5},{22,6},{23,7},{24,8},{25... | collective-permute-start | bytes 18440 | tf_op jit(solution)/shard_map/ppermute | solution.py:100
  21.2 12.6 %collective-permute-start.7 = (f32[384]{0:T(512)}, f32[384]{0:T(512)}, u32[]{:S(2)}, u32[]{:S(2)}) collective-permute-start(f32[384]{0:T(512)} %copy-done.25), channel_id=1, source_target_pairs={{16,0},{17,1},{18,2},{19,3},{20,4},{21,5},{22,6},{23,7},{24,8},{25... | collective-permute-start | bytes 4616 | tf_op jit(solution)/shard_map/ppermute | solution.py:100
  23.2 24.7 %collective-permute-start.3 = (bf16[192,768]{1,0:T(8,128)(2,1)}, bf16[192,768]{1,0:T(8,128)(2,1)}, u32[]{:S(2)}, u32[]{:S(2)}) collective-permute-start(bf16[192,768]{1,0:T(8,128)(2,1)} %dynamic-slice_bitcast_fusion.1), channel_id=1, source_target_pairs={{16,0},{17,1},{18,2},{19,3},{20,4},{21,5},{22,6},{23,7},{24,8},{25... | collective-permute-start | bytes 884744 | tf_op jit(solution)/shard_map/ppermute | solution.py:95
  25.3 23.8 %collective-permute-start.5 = (bf16[384,384]{1,0:T(8,128)(2,1)}, bf16[384,384]{1,0:T(8,128)(2,1)}, u32[]{:S(2)}, u32[]{:S(2)}) collective-permute-start(bf16[384,384]{1,0:T(8,128)(2,1)} %dynamic-slice_bitcast_fusion), channel_id=1, source_target_pairs={{16,0},{17,1},{18,2},{19,3},{20,4},{21,5},{22,6},{23,7},{24,8},{25... | collective-permute-start | bytes 884744 | tf_op jit(solution)/shard_map/ppermute | solution.py:95
  27.2 21.2 %collective-permute-start.1 = (f32[9,384]{1,0:T(8,128)}, f32[9,384]{1,0:T(8,128)}, u32[]{:S(2)}, u32[]{:S(2)}) collective-permute-start(f32[9,384]{1,0:T(8,128)} %bitcast.155), channel_id=1, source_target_pairs={{16,0},{17,1},{18,2},{19,3},{20,4},{21,5},{22,6},{23,7},{24,8},{25... | collective-permute-start | bytes 41480 | tf_op jit(solution)/shard_map/ppermute | solution.py:100
  41.1 24.2 %all-to-all-start.1 = ((bf16[2,16,1,32,384]{4,3,0,2,1:T(8,128)(2,1)}), bf16[2,16,1,32,384]{4,3,0,2,1:T(8,128)(2,1)S(1)}, u32[]{:S(2)}, u32[]{:S(2)}) async-start(bf16[2,16,1,32,384]{4,3,0,2,1:T(8,128)(2,1)} %fusion.117), calls=%async_computation.1 | async-start | bytes 1572864 | tf_op jit(solution)/shard_map/all_to_all | solution.py:79
  48.0 1.9 %collective-permute-start.4 = (bf16[192,768]{1,0:T(8,128)(2,1)}, bf16[192,768]{1,0:T(8,128)(2,1)S(1)}, u32[]{:S(2)}, u32[]{:S(2)}) collective-permute-start(bf16[192,768]{1,0:T(8,128)(2,1)} %collective-permute-done.3), channel_id=1, source_target_pairs={{0,1},{1,0},{2,3},{3,2},{4,5},{5,4},{6,7},{7,6},{8,9},{9,8},{10,11... | collective-permute-start | bytes 884744 | tf_op jit(solution)/shard_map/ppermute | solution.py:96
  49.1 2.9 %collective-permute-start.6 = (bf16[384,384]{1,0:T(8,128)(2,1)}, bf16[384,384]{1,0:T(8,128)(2,1)S(1)}, u32[]{:S(2)}, u32[]{:S(2)}) collective-permute-start(bf16[384,384]{1,0:T(8,128)(2,1)} %collective-permute-done.5), channel_id=1, source_target_pairs={{0,1},{1,0},{2,3},{3,2},{4,5},{5,4},{6,7},{7,6},{8,9},{9,8},{10,11... | collective-permute-start | bytes 884744 | tf_op jit(solution)/shard_map/ppermute | solution.py:96
  66.5 3.5 %copy-start.27 = (f32[384]{0:T(512)S(1)}, f32[384]{0:T(512)}, u32[]{:S(2)}) copy-start(f32[384]{0:T(512)} %broadcast_select_fusion.4) | copy-start | bytes 4612
  68.6 22.3 %collective-permute-start = (bf16[2,1,512,384]{3,2,0,1:T(8,128)(2,1)}, bf16[2,1,512,384]{3,2,0,1:T(8,128)(2,1)S(1)}, u32[]{:S(2)}, u32[]{:S(2)}) collective-permute-start(bf16[2,1,512,384]{3,2,0,1:T(8,128)(2,1)} %bitcast.158), channel_id=1, source_target_pairs={{16,0},{17,1},{18,2},{19,3},{20,4},{21,5},{22,6},{23,7},{24,8},{25... | collective-permute-start | bytes 2359304 | tf_op jit(solution)/shard_map/ppermute | solution.py:115
  73.6 24.7 %collective-permute-start.8 = (bf16[2,1,512,384]{3,2,0,1:T(8,128)(2,1)}, bf16[2,1,512,384]{3,2,0,1:T(8,128)(2,1)}, u32[]{:S(2)}, u32[]{:S(2)}) collective-permute-start(bf16[2,1,512,384]{3,2,0,1:T(8,128)(2,1)} %add_convert_fusion), channel_id=1, source_target_pairs={{0,16},{1,17},{2,18},{3,19},{4,20},{5,21},{6,22},{7,23},{8,24},{9,... | collective-permute-start | bytes 2359304 | tf_op jit(solution)/shard_map/ppermute | solution.py:120
  99.7 6.5 %copy-start.24 = (f32[1,9,384]{2,1,0:T(8,128)S(1)}, f32[1,9,384]{2,1,0:T(8,128)}, u32[]{:S(2)}) copy-start(f32[1,9,384]{2,1,0:T(8,128)} %get-tuple-element.58) | copy-start | bytes 41476
  100.7 24.2 %all-to-all-start.2 = ((bf16[2,1,16,32,384]{4,3,0,1,2:T(8,128)(2,1)}), bf16[2,1,16,32,384]{4,3,0,1,2:T(8,128)(2,1)S(1)}, u32[]{:S(2)}, u32[]{:S(2)}) async-start(bf16[2,1,16,32,384]{4,3,0,1,2:T(8,128)(2,1)} %copy.31), calls=%async_computation.2 | async-start | bytes 1572864 | tf_op jit(solution)/shard_map/all_to_all | solution.py:75
  125.1 26.0 %copy-start.1 = (bf16[2,16,1,32,384]{4,3,0,2,1:T(8,128)(2,1)S(1)}, bf16[2,16,1,32,384]{4,3,0,2,1:T(8,128)(2,1)}, u32[]{:S(2)}) copy-start(bf16[2,16,1,32,384]{4,3,0,2,1:T(8,128)(2,1)} %copy-done) | copy-start | bytes 2359300
  126.9 24.2 %all-to-all-start.3 = ((bf16[2,16,1,32,384]{4,3,0,2,1:T(8,128)(2,1)}), bf16[2,16,1,32,384]{4,3,0,2,1:T(8,128)(2,1)S(1)}, u32[]{:S(2)}, u32[]{:S(2)}) async-start(bf16[2,16,1,32,384]{4,3,0,2,1:T(8,128)(2,1)} %fusion.116), calls=%async_computation.3 | async-start | bytes 1572864 | tf_op jit(solution)/shard_map/all_to_all | solution.py:79
  132.4 29.5 %collective-permute-start.9 = (bf16[2,1,512,384]{3,2,0,1:T(8,128)(2,1)}, bf16[2,1,512,384]{3,2,0,1:T(8,128)(2,1)}, u32[]{:S(2)}, u32[]{:S(2)}) collective-permute-start(bf16[2,1,512,384]{3,2,0,1:T(8,128)(2,1)} %get-tuple-element.51), channel_id=1, source_target_pairs={{0,16},{1,17},{2,18},{3,19},{4,20},{5,21},{6,22},{7,23},{8,24},{9,... | collective-permute-start | bytes 2359304 | tf_op jit(solution)/shard_map/ppermute | solution.py:121
  152.2 3.4 %copy-start.7 = (bf16[1,384,768]{2,1,0:T(8,128)(2,1)S(1)}, bf16[1,384,768]{2,1,0:T(8,128)(2,1)}, u32[]{:S(2)}) copy-start(bf16[1,384,768]{2,1,0:T(8,128)(2,1)} %param.13) | copy-start | bytes 1769476
  152.3 3.4 %copy-start.19 = (f32[2,384]{1,0:T(2,128)S(1)}, f32[2,384]{1,0:T(2,128)}, u32[]{:S(2)}) copy-start(f32[2,384]{1,0:T(2,128)} %copy-done.18) | copy-start | bytes 9220
  152.3 3.4 %copy-start.21 = (f32[2,384]{1,0:T(2,128)S(1)}, f32[2,384]{1,0:T(2,128)}, u32[]{:S(2)}) copy-start(f32[2,384]{1,0:T(2,128)} %copy-done.20) | copy-start | bytes 9220
  152.3 3.4 %copy-start.26 = (f32[384]{0:T(512)S(1)}, f32[384]{0:T(512)}, u32[]{:S(2)}) copy-start(f32[384]{0:T(512)} %copy-done.25) | copy-start | bytes 4612
  (52 other events, 76.8 us)

commit v11 on v10

--- a/solution.py
+++ b/solution.py
@@ -84,6 +84,7 @@
     first = lax.axis_index("section") == 0
     taps, mod, gain = spatial_taps[0], modulation[0], norm_gain[0]
     weight_in, weight_out, band = w_in[0], w_out[0], band_taps[0]
+    clip_total = clips.shape[0]
 
     to_first = [(1, 0)]
     core = lax.axis_index("seq") % 2
@@ -112,9 +113,25 @@
     lead_taps = jnp.where(first, band, band[::-1])
     lead_out = temporal(lead_in, lead_taps[None])
 
-    second_seed = lax.ppermute(lead_out, "section", perm=to_first)
     second_mixed, second_saved = spatial_forward(lead_out, *second_params)
-    second_grad = spatial_backward(second_saved, second_seed, *second_params)
+    rows = second_saved[2].shape[0] // clip_total
+    second_grad = []
+    outgoing = lead_out[:1]
+    for clip in range(clip_total):
+        second_seed = lax.ppermute(outgoing, "section", perm=to_first)
+        if clip + 1 < clip_total:
+            second_seed, outgoing = lax.optimization_barrier(
+                (second_seed, lead_out[clip + 1 : clip + 2])
+            )
+        saved = (
+            second_saved[0][clip : clip + 1],
+            second_saved[1][clip : clip + 1],
+            second_saved[2][clip * rows : (clip + 1) * rows],
+        )
+        clip_params = list(second_params)
+        clip_params[1] = second_params[1][clip : clip + 1]
+        second_grad.append(spatial_backward(saved, second_seed, *clip_params))
+    second_grad = jnp.concatenate(second_grad)
 
     to_second = [(0, 1)]
     sent_mixed = lax.ppermute(second_mixed, "section", perm=to_second)

time: 165 us -> 179 us (1.085)
  local copies, waits for them, and re-layouts: 14.8 us -> 21.3 us
  other arithmetic: 30.4 us -> 33.3 us
  matrix products: 14.9 us -> 17.3 us
    slice x0 -> x4, local copies, waits for them, and re-layouts: none -> 3.62 us  [the longest x3 2.67 us: on_device(): second_saved[1][clip:clip + 1]]
    mul x2 -> x3, other arithmetic: 0.63 us -> 3.16 us  [spatial_backward(): inv_rms * inv_rms * inv_rms]
    mul x0 -> x2, local copies, waits for them, and re-layouts: none -> 2.03 us  [spatial_backward(): inv_rms * scaled_grad]
    ppermute x1 -> x2, waiting for transfers between devices: 11.6 us -> 13.1 us  [on_device(): second_seed = lax.ppermute(outgoing, 'section', perm=to_first)]
    dot_general x2 -> x3, matrix products: 4.84 us -> 5.95 us  [spatial_backward(): jnp.dot(flat_grad, w_out.T, preferred_element_type=jnp.float32)]
    unnamed x128 -> x176, local copies, waits for them, and re-layouts: 6.45 us -> 7.53 us
    dot_general x2 -> x3, matrix products: 4.31 us -> 3.46 us  [spatial_backward(): jnp.dot(pre_grad, w_in.T, preferred_element_type=jnp.float32)]
  transfers between devices with their start and end apart: 14 -> 15, of which waited for: 5 -> 6; matrix products, arithmetic and copies ran while one was open for 23% -> 24% of each run, Pallas kernels for 0% -> 0%
where the time goes in v11:
time: 179 us; the launch traced here: 177 us
  waiting for transfers between devices  61 us (34%)
  starting transfers between devices  42.8 us (24%)
  other arithmetic  33.3 us (19%)
  local copies, waits for them, and re-layouts  21.3 us (12%)
  matrix products  17.3 us (10%)
    all_to_all x2, waiting for transfers between devices, temporal(): lax.all_to_all(banded, 'seq', split_axis=1, concat_axis=2, tiled=True)  25.7 us
    all_to_all x2, waiting for transfers between devices, temporal(): lax.all_to_all(grouped, 'seq', split_axis=2, concat_axis=1, tiled=True)  22.2 us
    ppermute x2, waiting for transfers between devices, on_device(): second_seed = lax.ppermute(outgoing, 'section', perm=to_first)  13.1 us
    all_to_all x2, starting transfers between devices, temporal(): lax.all_to_all(grouped, 'seq', split_axis=2, concat_axis=1, tiled=True)  13 us
    all_to_all x2, starting transfers between devices, temporal(): lax.all_to_all(banded, 'seq', split_axis=1, concat_axis=2, tiled=True)  10.9 us
    unnamed x176, local copies, waits for them, and re-layouts  7.53 us
    dot_general x3, matrix products, spatial_backward(): jnp.dot(flat_grad, w_out.T, preferred_element_type=jnp.float32)  5.95 us
    ppermute x1, starting transfers between devices, on_device(): sent_mixed = lax.ppermute(second_mixed, 'section', perm=to_second)  5.53 us
  transfers between devices with their start and end apart: 15, of which 6 were waited for; matrix products, arithmetic and copies ran while one was open for 24% of the time, Pallas kernels for 0%

profile of v11, /device:TPU:0, one launch (start us, length us, event | category | flops | bytes accessed | tf_op | source)
XLA Modules:
  0.0 177.4 jit_solution(17827589977430625975)
XLA Ops:
  3.6 1.9 %multiply_reduce_fusion.1 = (f32[2,32,16]{2,1,0:T(8,128)S(1)}, f32[2,1,32,16,384]{4,3,2,0,1:T(8,128)S(1)}) fusion(f32[2,384]{1,0:T(2,128)S(1)} %get-tuple-element.87, f32[2,384]{1,0:T(2,128)S(1)} %get-tuple-element.88, f32[384]{0:T(512)S(1)} %get-tuple-element.55, f32[384]{0:T(512)S(1)} %get-tuple-element.48, f32[384]{0:T(512)S(1)} %get-tuple-element.49, ...), kind=kLoop, calls=%fused_computation.171 | loop fusion | flops 8256512 | bytes 3169792 | tf_op jit(solution)/shard_map/reduce_sum | solution.py:32
  7.0 3.3 %multiply_convert_fusion.2 = (bf16[1024,768]{1,0:T(8,128)(2,1)}, f32[1024,768]{1,0:T(8,128)}) fusion(bf16[1024,384]{1,0:T(8,128)(2,1)S(1)} %bitcast.193, bf16[1,384,768]{2,1,0:T(8,128)(2,1)S(1)} %copy-done.8), kind=kOutput, calls=%fused_computation.42 | convolution fusion | flops 607911936 | bytes 6094848 | tf_op jit(solution)/shard_map/dot_general | solution.py:34
  10.3 2.6 %fusion.99 = bf16[2,1,512,384]{3,2,0,1:T(8,128)(2,1)S(1)} fusion(bf16[2,512,768]{2,1,0:T(8,128)(2,1)} %bitcast.202, bf16[2,1,512,384]{3,2,1,0:T(8,128)(2,1)} %param.9, pred[]{:T(512)S(6)} %eq.9, bf16[1,768,384]{2,1,0:T(8,128)(2,1)S(1)} %copy-done.12, bf16[2,1,512,384]{3,2,1,0:T(8,128)(2,1)S(1)} %copy-done.14), kind=kOutput, calls=%fused_computation.178 | convolution fusion | flops 605552640 | bytes 4521985 | tf_op jit(solution)/shard_map/dot_general | solution.py:36
  13.9 7.4 %all-to-all-start = ((bf16[2,1,16,32,384]{4,3,0,1,2:T(8,128)(2,1)}), bf16[2,1,16,32,384]{4,3,0,1,2:T(8,128)(2,1)S(1)}, u32[]{:S(2)}, u32[]{:S(2)}) async-start(bf16[2,1,16,32,384]{4,3,0,1,2:T(8,128)(2,1)} %copy.27), calls=%async_computation | async-start | bytes 1572864 | tf_op jit(solution)/shard_map/all_to_all | solution.py:75
  31.2 2.0 %rev.2 = f32[9,384]{1,0:T(8,128)} reverse(f32[9,384]{1,0:T(8,128)} %bitcast.197), dimensions={0} | reverse | bytes 27648 | tf_op jit(solution)/shard_map/rev | solution.py:113
  36.5 3.6 %all-to-all-done = bf16[2,1,16,32,384]{4,3,0,1,2:T(8,128)(2,1)S(1)} async-done(((bf16[2,1,16,32,384]{4,3,0,1,2:T(8,128)(2,1)}), bf16[2,1,16,32,384]{4,3,0,1,2:T(8,128)(2,1)S(1)}, u32[]{:S(2)}, u32[]{:S(2)}) %all-to-all-start) | async-done | bytes 786464 | tf_op jit(solution)/shard_map/all_to_all | solution.py:75
  40.8 1.8 %fusion.146 = bf16[2,16,1,32,384]{4,3,0,2,1:T(8,128)(2,1)} fusion(f32[2,16,32,384]{3,2,0,1:T(8,128)S(1)} %bitcast_convert_fusion.1, f32[384]{0:T(512)S(1)} %copy-done.77, f32[384]{0:T(512)S(1)} %copy-done.78, f32[384]{0:T(512)S(1)} %copy-done.79, f32[384]{0:T(512)S(1)} %copy-done.80, f32[384]{0:T(512)S(1)} %copy-done.81, f32[384]{0:T(512)S(1)} %copy-done.82, ...), kind=kLoop, calls=%fused_computation.239 | loop fusion | flops 7471104 | bytes 2373120 | tf_op jit(solution)/shard_map/reshape | solution.py:78
  42.6 5.5 %all-to-all-start.1 = ((bf16[2,16,1,32,384]{4,3,0,2,1:T(8,128)(2,1)}), bf16[2,16,1,32,384]{4,3,0,2,1:T(8,128)(2,1)S(1)}, u32[]{:S(2)}, u32[]{:S(2)}) async-start(bf16[2,16,1,32,384]{4,3,0,2,1:T(8,128)(2,1)} %fusion.146), calls=%async_computation.1 | async-start | bytes 1572864 | tf_op jit(solution)/shard_map/all_to_all | solution.py:79
  52.0 2.1 %fusion.147 = bf16[384,768]{1,0:T(8,128)(2,1)} fusion(bf16[192,768]{1,0:T(8,128)(2,1)S(1)} %collective-permute-done.4, bf16[192,768]{1,0:T(8,128)(2,1)} %collective-permute-done.3, bf16[1,384,768]{2,1,0:T(8,128)(2,1)S(1)} %copy-done.8, pred[]{:T(512)S(6)} %eq.10, pred[]{:T(512)S(6)} %eq.9), kind=kLoop, calls=%fused_computation.242 | loop fusion | flops 2949120 | bytes 1769474 | tf_op jit(solution)/shard_map/jit(_where)/select_n | solution.py:105
  54.1 2.2 %fusion.148 = bf16[768,384]{1,0:T(8,128)(2,1)} fusion(bf16[384,384]{1,0:T(8,128)(2,1)S(1)} %collective-permute-done.6, bf16[384,384]{1,0:T(8,128)(2,1)} %collective-permute-done.5, bf16[1,768,384]{2,1,0:T(8,128)(2,1)S(1)} %copy-done.12, pred[]{:T(512)S(6)} %eq.10, pred[]{:T(512)S(6)} %eq.9), kind=kLoop, calls=%fused_computation.244 | loop fusion | flops 2949120 | bytes 1769474 | tf_op jit(solution)/shard_map/jit(_where)/select_n | solution.py:105
  56.2 10.5 %all-to-all-done.1 = bf16[2,16,1,32,384]{4,3,0,2,1:T(8,128)(2,1)S(1)} async-done(((bf16[2,16,1,32,384]{4,3,0,2,1:T(8,128)(2,1)}), bf16[2,16,1,32,384]{4,3,0,2,1:T(8,128)(2,1)S(1)}, u32[]{:S(2)}, u32[]{:S(2)}) %all-to-all-start.1) | async-done | bytes 786464 | tf_op jit(solution)/shard_map/all_to_all | solution.py:79
  67.8 1.9 %multiply_reduce_fusion = (f32[2,32,16]{2,1,0:T(8,128)S(1)}, f32[2,1,32,16,384]{4,3,2,0,1:T(8,128)S(1)}) fusion(f32[2,384]{1,0:T(2,128)S(1)} %copy-done.28, f32[2,384]{1,0:T(2,128)S(1)} %copy-done.30, f32[384]{0:T(512)S(1)} %copy-done.68, f32[384]{0:T(512)S(1)} %get-tuple-element.30, f32[384]{0:T(512)S(1)} %copy-done.56, f32[384]{0:T(512)S(1)} %copy-done.58, ...), kind=kLoop, calls=%fused_computation.170 | loop fusion | flops 8256512 | bytes 3169792 | tf_op jit(solution)/shard_map/reduce_sum | solution.py:32
  75.6 5.5 %collective-permute-start.9 = (bf16[2,1,512,384]{3,2,0,1:T(8,128)(2,1)}, bf16[2,1,512,384]{3,2,0,1:T(8,128)(2,1)}, u32[]{:S(2)}, u32[]{:S(2)}) collective-permute-start(bf16[2,1,512,384]{3,2,0,1:T(8,128)(2,1)} %fusion.88), channel_id=1, source_target_pairs={{0,16},{1,17},{2,18},{3,19},{4,20},{5,21},{6,22},{7,23},{8,24},{9,... | collective-permute-start | bytes 2359304 | tf_op jit(solution)/shard_map/ppermute | solution.py:137
  90.9 4.2 %collective-permute-done = bf16[1,1,512,384]{3,2,0,1:T(8,128)(2,1)S(1)} collective-permute-done((bf16[1,1,512,384]{3,2,0,1:T(8,128)(2,1)}, bf16[1,1,512,384]{3,2,0,1:T(8,128)(2,1)S(1)}, u32[]{:S(2)}, u32[]{:S(2)}) %collective-permute-start) | collective-permute-done | bytes 393248 | tf_op jit(solution)/shard_map/ppermute | solution.py:121
  98.6 8.9 %collective-permute-done.8 = bf16[1,1,512,384]{3,2,0,1:T(8,128)(2,1)S(1)} collective-permute-done((bf16[1,1,512,384]{3,2,0,1:T(8,128)(2,1)}, bf16[1,1,512,384]{3,2,0,1:T(8,128)(2,1)S(1)}, u32[]{:S(2)}, u32[]{:S(2)}) %collective-permute-start.8) | collective-permute-done | bytes 393248 | tf_op jit(solution)/shard_map/ppermute | solution.py:121
  110.5 1.9 %fusion.114 = (bf16[1,1,32,16,384]{4,3,2,1,0:T(8,128)(2,1)S(1)}, bf16[1,1,32,16,384]{4,3,2,1,0:T(8,128)(2,1)S(1)}) fusion(f32[1,1,32,16,384]{4,3,2,1,0:T(8,128)S(1)} %bitcast.187, f32[384]{0:T(512)S(1)} %copy-done.53, f32[384]{0:T(512)S(1)} %copy-done.67, f32[384]{0:T(512)S(1)} %copy-done.65, f32[384]{0:T(512)S(1)} %copy-done.63, f32[384]{0:T(512)S(1)} %copy-done.61, ...), kind=kLoop, calls=%fused_computation.195 | loop fusion | flops 7077888 | bytes 2373120 | tf_op jit(solution)/shard_map/convert_element_type | solution.py:57
  114.8 5.6 %all-to-all-start.2 = ((bf16[2,1,16,32,384]{4,3,0,1,2:T(8,128)(2,1)}), bf16[2,1,16,32,384]{4,3,0,1,2:T(8,128)(2,1)S(1)}, u32[]{:S(2)}, u32[]{:S(2)}) async-start(bf16[2,1,16,32,384]{4,3,0,1,2:T(8,128)(2,1)} %copy.30), calls=%async_computation.2 | async-start | bytes 1572864 | tf_op jit(solution)/shard_map/all_to_all | solution.py:75
  120.4 18.6 %all-to-all-done.2 = bf16[2,1,16,32,384]{4,3,0,1,2:T(8,128)(2,1)S(1)} async-done(((bf16[2,1,16,32,384]{4,3,0,1,2:T(8,128)(2,1)}), bf16[2,1,16,32,384]{4,3,0,1,2:T(8,128)(2,1)S(1)}, u32[]{:S(2)}, u32[]{:S(2)}) %all-to-all-start.2) | async-done | bytes 786464 | tf_op jit(solution)/shard_map/all_to_all | solution.py:75
  139.3 1.8 %fusion.145 = bf16[2,16,1,32,384]{4,3,0,2,1:T(8,128)(2,1)} fusion(f32[2,16,32,384]{3,2,0,1:T(8,128)S(1)} %bitcast_convert_fusion, f32[384]{0:T(512)S(1)} %get-tuple-element.21, f32[384]{0:T(512)S(1)} %get-tuple-element.22, f32[384]{0:T(512)S(1)} %get-tuple-element.23, f32[384]{0:T(512)S(1)} %get-tuple-element.24, f32[384]{0:T(512)S(1)} %get-tuple-element.25, ...), kind=kLoop, calls=%fused_computation.238 | loop fusion | flops 7471104 | bytes 2373120 | tf_op jit(solution)/shard_map/reshape | solution.py:78
  141.1 5.5 %all-to-all-start.3 = ((bf16[2,16,1,32,384]{4,3,0,2,1:T(8,128)(2,1)}), bf16[2,16,1,32,384]{4,3,0,2,1:T(8,128)(2,1)S(1)}, u32[]{:S(2)}, u32[]{:S(2)}) async-start(bf16[2,16,1,32,384]{4,3,0,2,1:T(8,128)(2,1)} %fusion.145), calls=%async_computation.3 | async-start | bytes 1572864 | tf_op jit(solution)/shard_map/all_to_all | solution.py:79
  146.6 3.6 %collective-permute-start.10 = (bf16[2,1,512,384]{3,2,0,1:T(8,128)(2,1)}, bf16[2,1,512,384]{3,2,0,1:T(8,128)(2,1)}, u32[]{:S(2)}, u32[]{:S(2)}) collective-permute-start(bf16[2,1,512,384]{3,2,0,1:T(8,128)(2,1)} %get-tuple-element.66), channel_id=1, source_target_pairs={{0,16},{1,17},{2,18},{3,19},{4,20},{5,21},{6,22},{7,23},{8,24},{9,... | collective-permute-start | bytes 2359304 | tf_op jit(solution)/shard_map/ppermute | solution.py:138
  150.2 15.1 %all-to-all-done.3 = bf16[2,16,1,32,384]{4,3,0,2,1:T(8,128)(2,1)S(1)} async-done(((bf16[2,16,1,32,384]{4,3,0,2,1:T(8,128)(2,1)}), bf16[2,16,1,32,384]{4,3,0,2,1:T(8,128)(2,1)S(1)}, u32[]{:S(2)}, u32[]{:S(2)}) %all-to-all-start.3) | async-done | bytes 786464 | tf_op jit(solution)/shard_map/all_to_all | solution.py:79
  166.4 3.4 %multiply_convert_fusion = bf16[1024,768]{1,0:T(8,128)(2,1)S(1)} fusion(f32[1024,768]{1,0:T(8,128)} %get-tuple-element.83, bf16[1024,384]{1,0:T(8,128)(2,1)S(1)} %bitcast.195, bf16[1,768,384]{2,1,0:T(8,128)(2,1)S(1)} %copy-done.13), kind=kOutput, calls=%fused_computation.40 | convolution fusion | flops 612630528 | bytes 6094848 | tf_op jit(solution)/shard_map/dot_general | solution.py:45
  169.9 2.2 %fusion.87 = (f32[1024]{0:T(1024)S(1)}, f32[1024,384]{1,0:T(8,128)}) fusion(f32[2,1,32,16,384]{4,3,2,0,1:T(8,128)S(1)} %get-tuple-element.61, f32[384]{0:T(512)S(1)} %copy-done.27, f32[2,384]{1,0:T(2,128)S(1)} %copy-done.22, f32[2,384]{1,0:T(2,128)S(1)} %copy-done.24, bf16[1024,768]{1,0:T(8,128)(2,1)S(1)} %multiply_convert_fusion, ...), kind=kOutput, calls=%fused_computation.150 | convolution fusion | flops 606731264 | bytes 5320192 | tf_op jit(solution)/shard_map/dot_general | solution.py:49
  (249 shorter events, 54.5 us)
Async XLA Ops:
  12.9 11.0 %copy-start.20 = (f32[1,9,384]{2,0,1:T(1,128)S(1)}, f32[1,9,384]{2,0,1:T(1,128)}, u32[]{:S(2)}) copy-start(f32[1,9,384]{2,0,1:T(1,128)} %param.10) | copy-start | bytes 41476
  13.9 26.1 %all-to-all-start = ((bf16[2,1,16,32,384]{4,3,0,1,2:T(8,128)(2,1)}), bf16[2,1,16,32,384]{4,3,0,1,2:T(8,128)(2,1)S(1)}, u32[]{:S(2)}, u32[]{:S(2)}) async-start(bf16[2,1,16,32,384]{4,3,0,1,2:T(8,128)(2,1)} %copy.27), calls=%async_computation | async-start | bytes 1572864 | tf_op jit(solution)/shard_map/all_to_all | solution.py:75
  21.3 26.8 %collective-permute-start.2 = (f32[2,2,384]{2,1,0:T(2,128)}, f32[2,2,384]{2,1,0:T(2,128)}, u32[]{:S(2)}, u32[]{:S(2)}) collective-permute-start(f32[2,2,384]{2,1,0:T(2,128)} %bitcast.199), channel_id=1, source_target_pairs={{16,0},{17,1},{18,2},{19,3},{20,4},{21,5},{22,6},{23,7},{24,8},{25... | collective-permute-start | bytes 18440 | tf_op jit(solution)/shard_map/ppermute | solution.py:101
  22.6 12.6 %collective-permute-start.7 = (f32[384]{0:T(512)}, f32[384]{0:T(512)}, u32[]{:S(2)}, u32[]{:S(2)}) collective-permute-start(f32[384]{0:T(512)} %copy-done.26), channel_id=1, source_target_pairs={{16,0},{17,1},{18,2},{19,3},{20,4},{21,5},{22,6},{23,7},{24,8},{25... | collective-permute-start | bytes 4616 | tf_op jit(solution)/shard_map/ppermute | solution.py:101
  24.5 25.9 %collective-permute-start.1 = (f32[9,384]{1,0:T(8,128)}, f32[9,384]{1,0:T(8,128)}, u32[]{:S(2)}, u32[]{:S(2)}) collective-permute-start(f32[9,384]{1,0:T(8,128)} %bitcast.181), channel_id=1, source_target_pairs={{16,0},{17,1},{18,2},{19,3},{20,4},{21,5},{22,6},{23,7},{24,8},{25... | collective-permute-start | bytes 41480 | tf_op jit(solution)/shard_map/ppermute | solution.py:101
  26.6 23.4 %collective-permute-start.3 = (bf16[192,768]{1,0:T(8,128)(2,1)}, bf16[192,768]{1,0:T(8,128)(2,1)}, u32[]{:S(2)}, u32[]{:S(2)}) collective-permute-start(bf16[192,768]{1,0:T(8,128)(2,1)} %dynamic-slice_bitcast_fusion.1), channel_id=1, source_target_pairs={{16,0},{17,1},{18,2},{19,3},{20,4},{21,5},{22,6},{23,7},{24,8},{25... | collective-permute-start | bytes 884744 | tf_op jit(solution)/shard_map/ppermute | solution.py:96
  28.6 22.6 %collective-permute-start.5 = (bf16[384,384]{1,0:T(8,128)(2,1)}, bf16[384,384]{1,0:T(8,128)(2,1)}, u32[]{:S(2)}, u32[]{:S(2)}) collective-permute-start(bf16[384,384]{1,0:T(8,128)(2,1)} %dynamic-slice_bitcast_fusion), channel_id=1, source_target_pairs={{16,0},{17,1},{18,2},{19,3},{20,4},{21,5},{22,6},{23,7},{24,8},{25... | collective-permute-start | bytes 884744 | tf_op jit(solution)/shard_map/ppermute | solution.py:96
  42.6 24.2 %all-to-all-start.1 = ((bf16[2,16,1,32,384]{4,3,0,2,1:T(8,128)(2,1)}), bf16[2,16,1,32,384]{4,3,0,2,1:T(8,128)(2,1)S(1)}, u32[]{:S(2)}, u32[]{:S(2)}) async-start(bf16[2,16,1,32,384]{4,3,0,2,1:T(8,128)(2,1)} %fusion.146), calls=%async_computation.1 | async-start | bytes 1572864 | tf_op jit(solution)/shard_map/all_to_all | solution.py:79
  50.0 1.9 %collective-permute-start.4 = (bf16[192,768]{1,0:T(8,128)(2,1)}, bf16[192,768]{1,0:T(8,128)(2,1)S(1)}, u32[]{:S(2)}, u32[]{:S(2)}) collective-permute-start(bf16[192,768]{1,0:T(8,128)(2,1)} %collective-permute-done.3), channel_id=1, source_target_pairs={{0,1},{1,0},{2,3},{3,2},{4,5},{5,4},{6,7},{7,6},{8,9},{9,8},{10,11... | collective-permute-start | bytes 884744 | tf_op jit(solution)/shard_map/ppermute | solution.py:97
  51.2 2.9 %collective-permute-start.6 = (bf16[384,384]{1,0:T(8,128)(2,1)}, bf16[384,384]{1,0:T(8,128)(2,1)S(1)}, u32[]{:S(2)}, u32[]{:S(2)}) collective-permute-start(bf16[384,384]{1,0:T(8,128)(2,1)} %collective-permute-done.5), channel_id=1, source_target_pairs={{0,1},{1,0},{2,3},{3,2},{4,5},{5,4},{6,7},{7,6},{8,9},{9,8},{10,11... | collective-permute-start | bytes 884744 | tf_op jit(solution)/shard_map/ppermute | solution.py:97
  51.9 15.7 %copy-start.52 = (f32[384]{0:T(512)}, f32[384]{0:T(512)S(1)}, u32[]{:S(2)}) copy-start(f32[384]{0:T(512)S(1)} %get-tuple-element.29) | copy-start | bytes 4612
  51.9 15.7 %copy-start.54 = (f32[384]{0:T(512)}, f32[384]{0:T(512)S(1)}, u32[]{:S(2)}) copy-start(f32[384]{0:T(512)S(1)} %get-tuple-element.30) | copy-start | bytes 4612
  56.2 11.4 %copy-start.28 = (f32[2,384]{1,0:T(2,128)S(1)}, f32[2,384]{1,0:T(2,128)}, u32[]{:S(2)}) copy-start(f32[2,384]{1,0:T(2,128)} %get-tuple-element.89) | copy-start | bytes 9220
  56.2 11.4 %copy-start.30 = (f32[2,384]{1,0:T(2,128)S(1)}, f32[2,384]{1,0:T(2,128)}, u32[]{:S(2)}) copy-start(f32[2,384]{1,0:T(2,128)} %get-tuple-element.90) | copy-start | bytes 9220
  75.6 37.1 %collective-permute-start.9 = (bf16[2,1,512,384]{3,2,0,1:T(8,128)(2,1)}, bf16[2,1,512,384]{3,2,0,1:T(8,128)(2,1)}, u32[]{:S(2)}, u32[]{:S(2)}) collective-permute-start(bf16[2,1,512,384]{3,2,0,1:T(8,128)(2,1)} %fusion.88), channel_id=1, source_target_pairs={{0,16},{1,17},{2,18},{3,19},{4,20},{5,21},{6,22},{7,23},{8,24},{9,... | collective-permute-start | bytes 2359304 | tf_op jit(solution)/shard_map/ppermute | solution.py:137
  82.0 13.1 %collective-permute-start = (bf16[1,1,512,384]{3,2,0,1:T(8,128)(2,1)}, bf16[1,1,512,384]{3,2,0,1:T(8,128)(2,1)S(1)}, u32[]{:S(2)}, u32[]{:S(2)}) collective-permute-start(bf16[1,1,512,384]{3,2,0,1:T(8,128)(2,1)} %bitcast.17), channel_id=1, source_target_pairs={{16,0},{17,1},{18,2},{19,3},{20,4},{21,5},{22,6},{23,7},{24,8},{25... | collective-permute-start | bytes 1179656 | tf_op jit(solution)/shard_map/ppermute | solution.py:121
  95.1 12.4 %copy-start.16 = (bf16[768,384]{1,0:T(8,128)(2,1)S(1)}, bf16[768,384]{1,0:T(8,128)(2,1)}, u32[]{:S(2)}) copy-start(bf16[768,384]{1,0:T(8,128)(2,1)} %fusion.148) | copy-start | bytes 1769476
  95.1 12.4 %collective-permute-start.8 = (bf16[1,1,512,384]{3,2,0,1:T(8,128)(2,1)}, bf16[1,1,512,384]{3,2,0,1:T(8,128)(2,1)S(1)}, u32[]{:S(2)}, u32[]{:S(2)}) collective-permute-start(bf16[1,1,512,384]{3,2,0,1:T(8,128)(2,1)} %bitcast.196), channel_id=1, source_target_pairs={{16,0},{17,1},{18,2},{19,3},{20,4},{21,5},{22,6},{23,7},{24,8},{25... | collective-permute-start | bytes 1179656 | tf_op jit(solution)/shard_map/ppermute | solution.py:121
  98.6 9.7 %copy-start.6 = (bf16[384,768]{1,0:T(8,128)(2,1)S(1)}, bf16[384,768]{1,0:T(8,128)(2,1)}, u32[]{:S(2)}) copy-start(bf16[384,768]{1,0:T(8,128)(2,1)} %fusion.147) | copy-start | bytes 1769476
  98.6 9.7 %copy-start.33 = (f32[384]{0:T(512)S(1)}, f32[384]{0:T(512)}, u32[]{:S(2)}) copy-start(f32[384]{0:T(512)} %broadcast_select_fusion.4) | copy-start | bytes 4612
  114.8 24.3 %all-to-all-start.2 = ((bf16[2,1,16,32,384]{4,3,0,1,2:T(8,128)(2,1)}), bf16[2,1,16,32,384]{4,3,0,1,2:T(8,128)(2,1)S(1)}, u32[]{:S(2)}, u32[]{:S(2)}) async-start(bf16[2,1,16,32,384]{4,3,0,1,2:T(8,128)(2,1)} %copy.30), calls=%async_computation.2 | async-start | bytes 1572864 | tf_op jit(solution)/shard_map/all_to_all | solution.py:75
  139.3 26.0 %copy-start.4 = (bf16[2,16,1,32,384]{4,3,0,2,1:T(8,128)(2,1)S(1)}, bf16[2,16,1,32,384]{4,3,0,2,1:T(8,128)(2,1)}, u32[]{:S(2)}) copy-start(bf16[2,16,1,32,384]{4,3,0,2,1:T(8,128)(2,1)} %copy-done.2) | copy-start | bytes 2359300
  141.1 24.2 %all-to-all-start.3 = ((bf16[2,16,1,32,384]{4,3,0,2,1:T(8,128)(2,1)}), bf16[2,16,1,32,384]{4,3,0,2,1:T(8,128)(2,1)S(1)}, u32[]{:S(2)}, u32[]{:S(2)}) async-start(bf16[2,16,1,32,384]{4,3,0,2,1:T(8,128)(2,1)} %fusion.145), calls=%async_computation.3 | async-start | bytes 1572864 | tf_op jit(solution)/shard_map/all_to_all | solution.py:79
  146.6 29.5 %collective-permute-start.10 = (bf16[2,1,512,384]{3,2,0,1:T(8,128)(2,1)}, bf16[2,1,512,384]{3,2,0,1:T(8,128)(2,1)}, u32[]{:S(2)}, u32[]{:S(2)}) collective-permute-start(bf16[2,1,512,384]{3,2,0,1:T(8,128)(2,1)} %get-tuple-element.66), channel_id=1, source_target_pairs={{0,16},{1,17},{2,18},{3,19},{4,20},{5,21},{6,22},{7,23},{8,24},{9,... | collective-permute-start | bytes 2359304 | tf_op jit(solution)/shard_map/ppermute | solution.py:138
  (77 other events, 139.4 us)

commit v12 on v8

--- a/solution.py
+++ b/solution.py
@@ -12,14 +12,17 @@
 
 
 def stencil(volume, stencil_taps):
-    padded = jnp.pad(volume, ((0, 0), (0, 0), (1, 1), (1, 1), (0, 0)))
-    total = jnp.zeros_like(volume)
-    for down_step in range(3):
-        for across in range(3):
-            total = total + stencil_taps[3 * down_step + across] * padded[
-                :, :, down_step : down_step + H, across : across + W
-            ]
-    return total
+    zero = ((0, 0), (0, 0))
+    padded = jnp.pad(volume, zero + ((1, 1), (0, 0), (0, 0)))
+    columns = []
+    for across in range(3):
+        column = stencil_taps[across] * padded[:, :, 0:H]
+        for down_step in range(1, 3):
+            column = column + stencil_taps[3 * down_step + across] * padded[:, :, down_step : down_step + H]
+        columns.append(column)
+    left = jnp.pad(columns[0], zero + ((0, 0), (1, 0), (0, 0)))[:, :, :, :W]
+    right = jnp.pad(columns[2], zero + ((0, 0), (0, 1), (0, 0)))[:, :, :, 1:]
+    return left + columns[1] + right
 
 
 def spatial_forward(values, stencil_taps, modulate, norm_gain, w_in, w_out):

time: 164 us -> 163 us (level)
  local copies, waits for them, and re-layouts: 10.2 us -> 12.9 us
  other arithmetic: 28.9 us -> 26.8 us
    unnamed x80 -> x82, local copies, waits for them, and re-layouts: 2.38 us -> 5.17 us
    convert_element_type x2, other arithmetic: 3.6 us -> 1.18 us  [spatial_backward(): spread.astype(jnp.bfloat16).astype(jnp.float32)]
    add x0 -> x4, other arithmetic: none -> 2.05 us  [stencil(): column + stencil_taps[3 * down_step + across] * padded[:, :, down_step:do...]
where the time goes in v12:
time: 163 us; the launch traced here: 162 us
  waiting for transfers between devices  58.5 us (36%)
  other arithmetic  26.8 us (16%)
  blocking collectives  25.7 us (16%)
  starting transfers between devices  23.7 us (15%)
  matrix products  13.2 us (8%)
  local copies, waits for them, and re-layouts  12.9 us (8%)
    all_to_all x1, blocking collectives, temporal(): lax.all_to_all(banded, 'seq', split_axis=1, concat_axis=2, tiled=True)  25.7 us
    all_to_all x1, waiting for transfers between devices, temporal(): lax.all_to_all(grouped, 'seq', split_axis=2, concat_axis=1, tiled=True)  18.6 us
    all_to_all x1, waiting for transfers between devices, temporal_shared(): lax.all_to_all(grouped, 'seq', split_axis=2, concat_axis=1, tiled=True)  17.9 us
    ppermute x2, waiting for transfers between devices, fetch_halves(): got = lax.ppermute(mine, 'section', perm=to_first)  17.8 us
    all_to_all x1, starting transfers between devices, temporal_shared(): lax.all_to_all(grouped, 'seq', split_axis=2, concat_axis=1, tiled=True)  7.39 us
    all_to_all x1, starting transfers between devices, temporal_shared(): lax.all_to_all(banded, ('section', 'seq'), split_axis=1, concat_axis=2, t...  5.39 us
    unnamed x82, local copies, waits for them, and re-layouts  5.17 us
    select_n x2, other arithmetic, on_device(): jnp.where(first, fetch_halves(p), p)  4.45 us
  transfers between devices with their start and end apart: 10, of which 6 were waited for; matrix products, arithmetic and copies ran while one was open for 7% of the time, Pallas kernels for 0%

profile of v12, /device:TPU:0, one launch (start us, length us, event | category | flops | bytes accessed | tf_op | source)
XLA Modules:
  0.0 162.0 jit_solution(7330167724675744691)
XLA Ops:
  6.1 2.8 %multiply_convert_fusion.3 = (bf16[1024,768]{1,0:T(8,128)(2,1)S(1)}, f32[1024,768]{1,0:T(8,128)}) fusion(bf16[1024,384]{1,0:T(8,128)(2,1)S(1)} %bitcast.171, bf16[1,384,768]{2,1,0:T(8,128)(2,1)S(1)} %copy-done.7), kind=kOutput, calls=%fused_computation.20 | convolution fusion | flops 607911936 | bytes 6094848 | tf_op jit(solution)/shard_map/dot_general | solution.py:37
  11.0 7.4 %all-to-all-start = ((bf16[2,1,16,32,384]{4,3,0,1,2:T(8,128)(2,1)}), bf16[2,1,16,32,384]{4,3,0,1,2:T(8,128)(2,1)S(1)}, u32[]{:S(2)}, u32[]{:S(2)}) async-start(bf16[2,1,16,32,384]{4,3,0,1,2:T(8,128)(2,1)} %copy.29), calls=%async_computation | async-start | bytes 1572864 | tf_op jit(solution)/shard_map/all_to_all | solution.py:91
  19.2 17.9 %all-to-all-done = bf16[2,1,16,32,384]{4,3,0,1,2:T(8,128)(2,1)S(1)} async-done(((bf16[2,1,16,32,384]{4,3,0,1,2:T(8,128)(2,1)}), bf16[2,1,16,32,384]{4,3,0,1,2:T(8,128)(2,1)S(1)}, u32[]{:S(2)}, u32[]{:S(2)}) %all-to-all-start) | async-done | bytes 786464 | tf_op jit(solution)/shard_map/all_to_all | solution.py:91
  38.2 1.4 broadcast_in_dim.7
  39.6 5.4 %all-to-all-start.1 = ((bf16[2,32,1,32,384]{4,3,0,2,1:T(8,128)(2,1)}), bf16[2,32,1,32,384]{4,3,0,2,1:T(8,128)(2,1)S(1)}, u32[]{:S(2)}, u32[]{:S(2)}) async-start(bf16[2,32,1,32,384]{4,3,0,2,1:T(8,128)(2,1)} %bitcast.162), calls=%async_computation.1 | async-start | bytes 3145728 | tf_op jit(solution)/shard_map/all_to_all | solution.py:97
  51.9 1.7 %dynamic-slice_bitcast_fusion.1 = bf16[192,768]{1,0:T(8,128)(2,1)} fusion(bf16[1,384,768]{2,1,0:T(8,128)(2,1)} %param.13, s32[]{:T(128)S(6)} %select_n.124), kind=kLoop, calls=%fused_computation.147 | loop fusion | bytes 589828 | tf_op jit(solution)/shard_map/dynamic_slice | solution.py:113
  53.6 1.5 collective-permute-start.2
  57.5 10.4 %collective-permute-done.4 = bf16[384,384]{1,0:T(8,128)(2,1)} collective-permute-done((bf16[384,384]{1,0:T(8,128)(2,1)S(1)}, bf16[384,384]{1,0:T(8,128)(2,1)}, u32[]{:S(2)}, u32[]{:S(2)}) %collective-permute-start.4) | collective-permute-done | bytes 294944 | tf_op jit(solution)/shard_map/ppermute | solution.py:114
  68.7 7.4 %collective-permute-done.2 = bf16[192,768]{1,0:T(8,128)(2,1)} collective-permute-done((bf16[192,768]{1,0:T(8,128)(2,1)}, bf16[192,768]{1,0:T(8,128)(2,1)}, u32[]{:S(2)}, u32[]{:S(2)}) %collective-permute-start.2) | collective-permute-done | bytes 294944 | tf_op jit(solution)/shard_map/ppermute | solution.py:114
  76.1 2.4 %fusion.65 = bf16[768,384]{1,0:T(8,128)(2,1)} fusion(bf16[384,384]{1,0:T(8,128)(2,1)S(1)} %collective-permute-done.5, bf16[384,384]{1,0:T(8,128)(2,1)} %collective-permute-done.4, bf16[1,768,384]{2,1,0:T(8,128)(2,1)} %param.14, pred[]{:T(512)S(6)} %eq.10, pred[]{:T(512)S(6)} %eq.9), kind=kLoop, calls=%fused_computation.140 | loop fusion | flops 2949120 | bytes 1769474 | tf_op jit(solution)/shard_map/jit(_where)/select_n | solution.py:123
  78.5 2.1 %fusion.64 = bf16[384,768]{1,0:T(8,128)(2,1)} fusion(bf16[192,768]{1,0:T(8,128)(2,1)S(1)} %collective-permute-done.3, bf16[192,768]{1,0:T(8,128)(2,1)} %collective-permute-done.2, bf16[1,384,768]{2,1,0:T(8,128)(2,1)S(1)} %copy-done.8, pred[]{:T(512)S(6)} %eq.10, pred[]{:T(512)S(6)} %eq.9), kind=kLoop, calls=%fused_computation.138 | loop fusion | flops 2949120 | bytes 1769474 | tf_op jit(solution)/shard_map/jit(_where)/select_n | solution.py:123
  80.6 3.1 %all-to-all-done.1 = bf16[2,32,1,32,384]{4,3,0,2,1:T(8,128)(2,1)S(1)} async-done(((bf16[2,32,1,32,384]{4,3,0,2,1:T(8,128)(2,1)}), bf16[2,32,1,32,384]{4,3,0,2,1:T(8,128)(2,1)S(1)}, u32[]{:S(2)}, u32[]{:S(2)}) %all-to-all-start.1) | async-done | bytes 1572896 | tf_op jit(solution)/shard_map/all_to_all | solution.py:97
  83.9 1.8 %fusion.74 = (bf16[1,2,1,512,384]{4,3,0,1,2:T(8,128)(2,1)}, f32[1,2,1,512,384]{4,3,0,1,2:T(8,128)}, f32[1,2,1,512,384]{4,3,0,1,2:T(8,128)S(1)}) fusion(bf16[2,2,1,512,384]{4,3,0,1,2:T(8,128)(2,1)S(1)} %bitcast.158), kind=kLoop, calls=%fused_computation.205 | loop fusion | flops 786432 | bytes 5505024 | tf_op jit(solution)/shard_map/unstack | solution.py:132
  86.3 1.9 %multiply_reduce_fusion.1 = (f32[2,32,16]{2,1,0:T(8,128)S(1)}, f32[2,1,32,16,384]{4,3,2,0,1:T(8,128)}) fusion(f32[2,384]{1,0:T(2,128)S(1)} %get-tuple-element.81, f32[2,384]{1,0:T(2,128)S(1)} %get-tuple-element.82, f32[2,1,32,16,384]{4,3,2,0,1:T(8,128)S(1)} %get-tuple-element.62, f32[384]{0:T(512)S(1)} %get-tuple-element.24, ...), kind=kLoop, calls=%fused_computation.113 | loop fusion | flops 4324352 | bytes 6306304 | tf_op jit(solution)/shard_map/reduce_sum | solution.py:35
  88.3 1.7 %multiply_convert_fusion.4 = bf16[1024,384]{1,0:T(8,128)(2,1)S(1)} fusion(f32[2,1,32,16,384]{4,3,2,0,1:T(8,128)} %get-tuple-element.49, f32[384]{0:T(512)S(1)} %broadcast_select_fusion.2, f32[1024]{0:T(1024)S(1)} %rsqrt.33, f32[2,384]{1,0:T(2,128)S(1)} %get-tuple-element.81, f32[2,384]{1,0:T(2,128)S(1)} %get-tuple-element.82), kind=kLoop, calls=%fused_computation.112 | loop fusion | flops 1966080 | bytes 2371072 | tf_op jit(solution)/shard_map/convert_element_type | solution.py:36
  91.1 2.2 %fusion.55 = f32[1024,384]{1,0:T(8,128)} fusion(bf16[768,384]{1,0:T(8,128)(2,1)S(1)} %copy-done.17, f32[1024,768]{1,0:T(8,128)S(1)} %fusion.75), kind=kOutput, calls=%fused_computation.121 | convolution fusion | flops 607911936 | bytes 5308416 | tf_op jit(solution)/shard_map/dot_general | solution.py:39
  93.4 1.5 multiply_convert_fusion.2
  94.8 2.2 %multiply_reduce_fusion = (f32[1024]{0:T(1024)S(1)}, f32[1024,384]{1,0:T(8,128)}) fusion(f32[2,1,32,16,384]{4,3,2,0,1:T(8,128)S(1)} %copy-done, f32[384]{0:T(512)S(1)} %broadcast_select_fusion.2, f32[2,384]{1,0:T(2,128)S(1)} %get-tuple-element.81, f32[2,384]{1,0:T(2,128)S(1)} %get-tuple-element.82, bf16[1024,768]{1,0:T(8,128)(2,1)S(1)} %multiply_convert_fusion.2, ...), kind=kOutput, calls=%fused_computation.111 | convolution fusion | flops 606731264 | bytes 5320192 | tf_op jit(solution)/shard_map/dot_general | solution.py:52
  97.1 2.4 %subtract_multiply_fusion.1 = f32[2,1,32,16,384]{4,3,2,0,1:T(8,128)S(1)} fusion(f32[2,1,32,16,384]{4,3,2,0,1:T(8,128)} %bitcast.164, f32[2,1,32,16,384]{4,3,2,0,1:T(8,128)} %get-tuple-element.49, f32[2,32,16]{2,1,0:T(8,128)S(1)} %div.30, f32[2,32,16]{2,1,0:T(8,128)S(1)} %get-tuple-element.69, f32[384]{0:T(512)S(1)} %broadcast_select_fusion.2, ...), kind=kLoop, calls=%fused_computation.110 | loop fusion | flops 3145728 | bytes 4738560 | tf_op jit(solution)/shard_map/mul | solution.py:56
  104.2 4.3 %all-to-all-start.2 = ((bf16[2,1,16,32,384]{4,3,0,1,2:T(8,128)(2,1)}), bf16[2,1,16,32,384]{4,3,0,1,2:T(8,128)(2,1)S(1)}, u32[]{:S(2)}, u32[]{:S(2)}) async-start(bf16[2,1,16,32,384]{4,3,0,1,2:T(8,128)(2,1)} %copy.31), calls=%async_computation.2 | async-start | bytes 1572864 | tf_op jit(solution)/shard_map/all_to_all | solution.py:78
  108.6 18.6 %all-to-all-done.2 = bf16[2,1,16,32,384]{4,3,0,1,2:T(8,128)(2,1)S(1)} async-done(((bf16[2,1,16,32,384]{4,3,0,1,2:T(8,128)(2,1)}), bf16[2,1,16,32,384]{4,3,0,1,2:T(8,128)(2,1)S(1)}, u32[]{:S(2)}, u32[]{:S(2)}) %all-to-all-start.2) | async-done | bytes 786464 | tf_op jit(solution)/shard_map/all_to_all | solution.py:78
  128.4 25.7 %all_to_all.16 = bf16[2,16,1,32,384]{4,3,0,2,1:T(8,128)(2,1)S(1)} all-to-all(bf16[2,16,1,32,384]{4,3,0,2,1:T(8,128)(2,1)S(1)} %fusion.63), channel_id=1, replica_groups=mesh['section'=2,'seq'=16] {'seq'}, dimensions={1} | all-to-all | bytes 1572864 | tf_op jit(solution)/shard_map/all_to_all | solution.py:82
  154.2 1.4 multiply_convert_fusion
  160.3 1.7 %fusion.61 = (bf16[1,2,1,512,384]{4,3,2,1,0:T(8,128)(2,1)}, bf16[1,2,1,512,384]{4,3,2,1,0:T(8,128)(2,1)}) fusion(f32[1,2,1,512,384]{4,3,0,1,2:T(8,128)S(1)} %bitcast.157, bf16[1,2,1,512,384]{4,3,0,1,2:T(8,128)(2,1)S(1)} %bitcast.168, bf16[1,2,1,512,384]{4,3,0,1,2:T(8,128)(2,1)S(1)} %bitcast.167, pred[]{:T(512)S(6)} %eq.9, ...), kind=kLoop, calls=%fused_computation.129 | loop fusion | flops 3538944 | bytes 6291457
  (136 shorter events, 31.8 us)
Async XLA Ops:
  6.1 2.8 %copy-start.13 = (bf16[1,768,384]{2,1,0:T(8,128)(2,1)S(1)}, bf16[1,768,384]{2,1,0:T(8,128)(2,1)}, u32[]{:S(2)}) copy-start(bf16[1,768,384]{2,1,0:T(8,128)(2,1)} %param.14) | copy-start | bytes 1769476
  6.1 2.8 %copy-start.15 = (bf16[2,1,512,384]{3,2,1,0:T(8,128)(2,1)S(1)}, bf16[2,1,512,384]{3,2,1,0:T(8,128)(2,1)}, u32[]{:S(2)}) copy-start(bf16[2,1,512,384]{3,2,1,0:T(8,128)(2,1)} %param.8) | copy-start | bytes 2359300
  6.1 2.8 %copy-start.37 = (bf16[2,1,512,384]{3,2,1,0:T(8,128)(2,1)S(1)}, bf16[2,1,512,384]{3,2,1,0:T(8,128)(2,1)}, u32[]{:S(2)}) copy-start(bf16[2,1,512,384]{3,2,1,0:T(8,128)(2,1)} %param.9) | copy-start | bytes 2359300
  10.0 8.4 %copy-start.20 = (f32[1,9,384]{2,0,1:T(1,128)S(1)}, f32[1,9,384]{2,0,1:T(1,128)}, u32[]{:S(2)}) copy-start(f32[1,9,384]{2,0,1:T(1,128)} %param.15) | copy-start | bytes 41476
  11.0 26.1 %all-to-all-start = ((bf16[2,1,16,32,384]{4,3,0,1,2:T(8,128)(2,1)}), bf16[2,1,16,32,384]{4,3,0,1,2:T(8,128)(2,1)S(1)}, u32[]{:S(2)}, u32[]{:S(2)}) async-start(bf16[2,1,16,32,384]{4,3,0,1,2:T(8,128)(2,1)} %copy.29), calls=%async_computation | async-start | bytes 1572864 | tf_op jit(solution)/shard_map/all_to_all | solution.py:91
  39.6 6.7 %copy-start.21 = (f32[1,2,2,384]{3,2,1,0:T(2,128)S(1)}, f32[1,2,2,384]{3,2,1,0:T(2,128)}, u32[]{:S(2)}) copy-start(f32[1,2,2,384]{3,2,1,0:T(2,128)} %param.11) | copy-start | bytes 18436
  39.6 8.0 %copy-start.18 = (f32[1,9,384]{2,0,1:T(1,128)S(1)}, f32[1,9,384]{2,0,1:T(1,128)}, u32[]{:S(2)}) copy-start(f32[1,9,384]{2,0,1:T(1,128)} %param.10) | copy-start | bytes 41476
  39.6 44.0 %all-to-all-start.1 = ((bf16[2,32,1,32,384]{4,3,0,2,1:T(8,128)(2,1)}), bf16[2,32,1,32,384]{4,3,0,2,1:T(8,128)(2,1)S(1)}, u32[]{:S(2)}, u32[]{:S(2)}) async-start(bf16[2,32,1,32,384]{4,3,0,2,1:T(8,128)(2,1)} %bitcast.162), calls=%async_computation.1 | async-start | bytes 3145728 | tf_op jit(solution)/shard_map/all_to_all | solution.py:97
  45.0 11.1 %collective-permute-start.6 = (f32[384]{0:T(512)S(1)}, f32[384]{0:T(512)}, u32[]{:S(2)}, u32[]{:S(2)}) collective-permute-start(f32[384]{0:T(512)S(1)} %reduce.15), channel_id=1, source_target_pairs={{16,0},{17,1},{18,2},{19,3},{20,4},{21,5},{22,6},{23,7},{24,8},{25... | collective-permute-start | bytes 4616 | tf_op jit(solution)/shard_map/ppermute | solution.py:119
  46.3 10.4 %collective-permute-start.1 = (f32[2,2,384]{2,1,0:T(2,128)S(1)}, f32[2,2,384]{2,1,0:T(2,128)}, u32[]{:S(2)}, u32[]{:S(2)}) collective-permute-start(f32[2,2,384]{2,1,0:T(2,128)S(1)} %bitcast.175), channel_id=1, source_target_pairs={{16,0},{17,1},{18,2},{19,3},{20,4},{21,5},{22,6},{23,7},{24,8},{25... | collective-permute-start | bytes 18440 | tf_op jit(solution)/shard_map/ppermute | solution.py:119
  48.3 19.7 %collective-permute-start = (f32[9,384]{1,0:T(8,128)}, f32[9,384]{1,0:T(8,128)}, u32[]{:S(2)}, u32[]{:S(2)}) collective-permute-start(f32[9,384]{1,0:T(8,128)} %bitcast.150), channel_id=1, source_target_pairs={{16,0},{17,1},{18,2},{19,3},{20,4},{21,5},{22,6},{23,7},{24,8},{25... | collective-permute-start | bytes 41480 | tf_op jit(solution)/shard_map/ppermute | solution.py:119
  50.6 17.3 %collective-permute-start.4 = (bf16[384,384]{1,0:T(8,128)(2,1)S(1)}, bf16[384,384]{1,0:T(8,128)(2,1)}, u32[]{:S(2)}, u32[]{:S(2)}) collective-permute-start(bf16[384,384]{1,0:T(8,128)(2,1)S(1)} %dynamic-slice_bitcast_fusion), channel_id=1, source_target_pairs={{16,0},{17,1},{18,2},{19,3},{20,4},{21,5},{22,6},{23,7},{24,8},{25... | collective-permute-start | bytes 884744 | tf_op jit(solution)/shard_map/ppermute | solution.py:114
  53.6 22.5 %collective-permute-start.2 = (bf16[192,768]{1,0:T(8,128)(2,1)}, bf16[192,768]{1,0:T(8,128)(2,1)}, u32[]{:S(2)}, u32[]{:S(2)}) collective-permute-start(bf16[192,768]{1,0:T(8,128)(2,1)} %dynamic-slice_bitcast_fusion.1), channel_id=1, source_target_pairs={{16,0},{17,1},{18,2},{19,3},{20,4},{21,5},{22,6},{23,7},{24,8},{25... | collective-permute-start | bytes 884744 | tf_op jit(solution)/shard_map/ppermute | solution.py:114
  55.0 23.4 %copy-start.8 = (bf16[1,384,768]{2,1,0:T(8,128)(2,1)S(1)}, bf16[1,384,768]{2,1,0:T(8,128)(2,1)}, u32[]{:S(2)}) copy-start(bf16[1,384,768]{2,1,0:T(8,128)(2,1)} %param.13) | copy-start | bytes 1769476
  67.9 8.2 %collective-permute-start.5 = (bf16[384,384]{1,0:T(8,128)(2,1)}, bf16[384,384]{1,0:T(8,128)(2,1)S(1)}, u32[]{:S(2)}, u32[]{:S(2)}) collective-permute-start(bf16[384,384]{1,0:T(8,128)(2,1)} %collective-permute-done.4), channel_id=1, source_target_pairs={{0,1},{1,0},{2,3},{3,2},{4,5},{5,4},{6,7},{7,6},{8,9},{9,8},{10,11... | collective-permute-start | bytes 884744 | tf_op jit(solution)/shard_map/ppermute | solution.py:115
  76.1 2.4 %collective-permute-start.3 = (bf16[192,768]{1,0:T(8,128)(2,1)}, bf16[192,768]{1,0:T(8,128)(2,1)S(1)}, u32[]{:S(2)}, u32[]{:S(2)}) collective-permute-start(bf16[192,768]{1,0:T(8,128)(2,1)} %collective-permute-done.2), channel_id=1, source_target_pairs={{0,1},{1,0},{2,3},{3,2},{4,5},{5,4},{6,7},{7,6},{8,9},{9,8},{10,11... | collective-permute-start | bytes 884744 | tf_op jit(solution)/shard_map/ppermute | solution.py:115
  91.1 2.2 %copy-start.16 = (bf16[1,2,1,512,384]{4,3,0,1,2:T(8,128)(2,1)S(1)}, bf16[1,2,1,512,384]{4,3,0,1,2:T(8,128)(2,1)}, u32[]{:S(2)}) copy-start(bf16[1,2,1,512,384]{4,3,0,1,2:T(8,128)(2,1)} %get-tuple-element.58) | copy-start | bytes 2359300
  100.0 2.4 %copy-start.12 = (f32[1024,384]{1,0:T(8,128)S(1)}, f32[1024,384]{1,0:T(8,128)}, u32[]{:S(2)}) copy-start(f32[1024,384]{1,0:T(8,128)} %fusion.55) | copy-start | bytes 4718596
  100.6 2.6 %copy-start.1 = (f32[2,1,32,16,384]{4,3,2,0,1:T(8,128)}, f32[2,1,32,16,384]{4,3,2,0,1:T(8,128)S(1)}, u32[]{:S(2)}) copy-start(f32[2,1,32,16,384]{4,3,2,0,1:T(8,128)S(1)} %fusion.62) | copy-start | bytes 4718596
  103.2 5.3 %copy-start.19 = (f32[1,9,384]{2,1,0:T(8,128)S(1)}, f32[1,9,384]{2,1,0:T(8,128)}, u32[]{:S(2)}) copy-start(f32[1,9,384]{2,1,0:T(8,128)} %get-tuple-element.65) | copy-start | bytes 41476
  104.2 23.0 %all-to-all-start.2 = ((bf16[2,1,16,32,384]{4,3,0,1,2:T(8,128)(2,1)}), bf16[2,1,16,32,384]{4,3,0,1,2:T(8,128)(2,1)S(1)}, u32[]{:S(2)}, u32[]{:S(2)}) async-start(bf16[2,1,16,32,384]{4,3,0,1,2:T(8,128)(2,1)} %copy.31), calls=%async_computation.2 | async-start | bytes 1572864 | tf_op jit(solution)/shard_map/all_to_all | solution.py:78
  127.4 26.8 %copy-start.38 = (f32[1024,768]{1,0:T(8,128)S(1)}, f32[1024,768]{1,0:T(8,128)}, u32[]{:S(2)}) copy-start(f32[1024,768]{1,0:T(8,128)} %get-tuple-element.76) | copy-start | bytes 9437188
  128.4 25.8 %copy-start.14 = (bf16[1,768,384]{2,1,0:T(8,128)(2,1)S(1)}, bf16[1,768,384]{2,1,0:T(8,128)(2,1)}, u32[]{:S(2)}) copy-start(bf16[1,768,384]{2,1,0:T(8,128)(2,1)} %param.14) | copy-start | bytes 1769476
  158.2 2.1 %copy-start.11 = (bf16[2,16,1,32,384]{4,3,1,0,2:T(8,128)(2,1)S(1)}, bf16[2,16,1,32,384]{4,3,1,0,2:T(8,128)(2,1)}, u32[]{:S(2)}) copy-start(bf16[2,16,1,32,384]{4,3,1,0,2:T(8,128)(2,1)} %copy-done.10) | copy-start | bytes 2359300
  (25 other events, 33.4 us)

commit v13 on v12

--- a/solution.py
+++ b/solution.py
@@ -100,46 +100,83 @@
 
 
 def on_device(clips, cotangent, spatial_taps, modulation, norm_gain, w_in, w_out, band_taps):
-    first = lax.axis_index("section") == 0
+    plane = lax.axis_index("section")
+    first = plane == 0
     taps, mod, gain = spatial_taps[0], modulation[0], norm_gain[0]
     weight_in, weight_out, band = w_in[0], w_out[0], band_taps[0]
-
-    to_first = [(1, 0)]
+    channels = taps.shape[-1]
+    tap_count = taps.shape[0]
+    own = (taps, mod, gain, weight_in, weight_out)
+
+    swap = [(0, 1), (1, 0)]
     core = lax.axis_index("seq") % 2
     siblings = [(q, q ^ 1) for q in range(lax.axis_size("seq"))]
 
     def fetch_halves(p):
         half = p.shape[0] // 2
         mine = lax.dynamic_slice_in_dim(p, core * half, half, 0)
-        got = lax.ppermute(mine, "section", perm=to_first)
+        got = lax.ppermute(mine, "section", perm=swap)
         other = lax.ppermute(got, "seq", perm=siblings)
         return jnp.where(core == 0, jnp.concatenate([got, other]), jnp.concatenate([other, got]))
 
-    second_taps, second_mod, second_gain = [
-        jnp.where(first, lax.ppermute(p, "section", perm=to_first), p)
-        for p in (taps, mod, gain)
-    ]
-    second_in, second_out = lax.optimization_barrier(
-        [jnp.where(first, fetch_halves(p), p) for p in (weight_in, weight_out)]
-    )
-
-    first_params = (taps, mod, gain, weight_in, weight_out)
-    second_params = (second_taps, second_mod, second_gain, second_in, second_out)
-
-    first_mixed, first_saved = spatial_forward(clips, *first_params)
+    small = jnp.concatenate([taps, mod.reshape(-1, channels), gain[None], band])
+    got_small = lax.ppermute(small, "section", perm=swap)
+    mod_rows = mod.shape[0] * mod.shape[1]
+    other = (
+        got_small[:tap_count],
+        got_small[tap_count : tap_count + mod_rows].reshape(mod.shape),
+        got_small[tap_count + mod_rows],
+        fetch_halves(weight_in),
+        fetch_halves(weight_out),
+    )
+    other_band = got_small[tap_count + mod_rows + 1 :]
+    first_seg = lax.optimization_barrier(
+        tuple(jnp.where(first, o, r) for o, r in zip(own, other))
+    )
+    second_seg = lax.optimization_barrier(
+        tuple(jnp.where(first, r, o) for o, r in zip(own, other))
+    )
+    first_band = jnp.where(first, band, other_band)
+    second_band = jnp.where(first, other_band, band)
+
+    def for_clip(params, clip):
+        clip_mod = lax.dynamic_index_in_dim(params[1], clip, 0, keepdims=True)
+        return (params[0], clip_mod) + tuple(params[2:])
+
+    first_mixed, _ = spatial_forward(clips, *own)
     lead_in = jnp.where(first, first_mixed, cotangent)
     lead_taps = jnp.where(first, band, band[::-1])
-    first_acts, second_seed = temporal_shared(lead_in, lead_taps[None])
-    second_mixed, second_saved = spatial_forward(first_acts, *second_params)
-    second_grad = spatial_backward(second_saved, second_seed, *second_params)
-
-    tail_in = jnp.where(first, second_grad, second_mixed)
-    tail_taps = jnp.where(first, band[::-1], band)
-    tail_out = temporal(tail_in, tail_taps[None])
-    first_grad = spatial_backward(first_saved, tail_out, *first_params)
-
-    activations = jnp.where(first, first_acts, tail_out)
-    input_grads = jnp.where(first, first_grad, second_grad)
+    lead_out = temporal(lead_in, lead_taps[None])
+
+    mine = lax.dynamic_index_in_dim(lead_out, plane, 0, keepdims=True)
+    theirs = lax.dynamic_index_in_dim(lead_out, 1 - plane, 0, keepdims=True)
+    got = lax.ppermute(theirs, "section", perm=swap)
+    clip_act = jnp.where(first, mine, got)
+    clip_seed = jnp.where(first, got, mine)
+    second_params = for_clip(second_seg, plane)
+    second_mixed, second_saved = spatial_forward(clip_act, *second_params)
+    second_grad = spatial_backward(second_saved, clip_seed, *second_params)
+
+    tail_out = temporal(
+        jnp.concatenate([second_grad, second_mixed]), jnp.stack([first_band[::-1], second_band])
+    )
+    first_params = for_clip(first_seg, plane)
+    start = lax.dynamic_index_in_dim(clips, plane, 0, keepdims=True)
+    _, first_saved = spatial_forward(start, *first_params)
+    first_grad = spatial_backward(first_saved, tail_out[:1], *first_params)
+
+    to_second, to_first = [(0, 1)], [(1, 0)]
+    sent_second_grad = lax.ppermute(second_grad, "section", perm=to_second)
+    sent_second_act = lax.ppermute(tail_out[1:], "section", perm=to_second)
+    sent_first_grad = lax.ppermute(first_grad, "section", perm=to_first)
+    activations = jnp.where(
+        first, lead_out, jnp.concatenate([sent_second_act, tail_out[1:]])
+    )
+    input_grads = jnp.where(
+        first,
+        jnp.concatenate([first_grad, sent_first_grad]),
+        jnp.concatenate([sent_second_grad, second_grad]),
+    )
     return (activations[None], input_grads[None])
 
 

time: 163 us -> 160 us (0.982)
  blocking collectives: 25.7 us -> 0 us
  waiting for transfers between devices: 58.5 us -> 76.4 us
  starting transfers between devices: 23.7 us -> 38.5 us
  local copies, waits for them, and re-layouts: 12.9 us -> 6.37 us
  matrix products: 13.2 us -> 10.5 us
    all_to_all x1 -> x0, blocking collectives: 25.7 us -> none  [temporal(): lax.all_to_all(banded, 'seq', split_axis=1, concat_axis=2, tiled=True)]
    all_to_all x1 -> x2, waiting for transfers between devices: 18.6 us -> 31.2 us  [temporal(): lax.all_to_all(grouped, 'seq', split_axis=2, concat_axis=1, tiled=True)]
    ppermute x5 -> x7, waiting for transfers between devices: 18.8 us -> 30.7 us  [the longest x2 12.3 us: fetch_halves(): got = lax.ppermute(mine, 'section', perm=swap)]
    all_to_all x1 -> x2, starting transfers between devices: 4.25 us -> 13.1 us  [temporal(): lax.all_to_all(grouped, 'seq', split_axis=2, concat_axis=1, tiled=True)]
    ppermute x5 -> x7, starting transfers between devices: 6.62 us -> 14.3 us  [the longest x1 4.28 us: on_device(): sent_second_grad = lax.ppermute(second_grad, 'section', perm=to_second)]
    all_to_all x2, waiting for transfers between devices: 21 us -> 14.5 us  [temporal(): lax.all_to_all(banded, 'seq', split_axis=1, concat_axis=2, tiled=True)]
    reshape x1 -> x2, other arithmetic: 0.94 us -> 4.18 us  [temporal(): banded.reshape(clip_count, groups * frame_count, 1, pixel_count // groups...]
    dynamic_slice x2, local copies, waits for them, and re-layouts: 2.7 us -> 0.06 us  [fetch_halves(): mine = lax.dynamic_slice_in_dim(p, core * half, half, 0)]
  transfers between devices with their start and end apart: 10 -> 13, of which waited for: 6 -> 10; matrix products, arithmetic and copies ran while one was open for 7% -> 10% of each run, Pallas kernels for 0% -> 0%
where the time goes in v13:
time: 160 us; the launch traced here: 159 us
  waiting for transfers between devices  76.4 us (48%)
  starting transfers between devices  38.5 us (24%)
  other arithmetic  25.2 us (16%)
  matrix products  10.5 us (7%)
  local copies, waits for them, and re-layouts  6.37 us (4%)
    all_to_all x2, waiting for transfers between devices, temporal(): lax.all_to_all(grouped, 'seq', split_axis=2, concat_axis=1, tiled=True)  31.2 us
    all_to_all x2, waiting for transfers between devices, temporal(): lax.all_to_all(banded, 'seq', split_axis=1, concat_axis=2, tiled=True)  14.5 us
    all_to_all x2, starting transfers between devices, temporal(): lax.all_to_all(grouped, 'seq', split_axis=2, concat_axis=1, tiled=True)  13.1 us
    ppermute x2, waiting for transfers between devices, fetch_halves(): got = lax.ppermute(mine, 'section', perm=swap)  12.3 us
    all_to_all x2, starting transfers between devices, temporal(): lax.all_to_all(banded, 'seq', split_axis=1, concat_axis=2, tiled=True)  11.1 us
    select_n x5, other arithmetic, on_device(): jnp.where(first, o, r)  5.93 us
    ppermute x1, waiting for transfers between devices, on_device(): sent_first_grad = lax.ppermute(first_grad, 'section', perm=to_first)  5.56 us
    ppermute x1, waiting for transfers between devices, on_device(): got = lax.ppermute(theirs, 'section', perm=swap)  5.53 us
  transfers between devices with their start and end apart: 13, of which 10 were waited for; matrix products, arithmetic and copies ran while one was open for 10% of the time, Pallas kernels for 0%

profile of v13, /device:TPU:0, one launch (start us, length us, event | category | flops | bytes accessed | tf_op | source)
XLA Modules:
  0.0 158.5 jit_solution(7944123514527663329)
XLA Ops:
  5.2 2.4 %multiply_convert_fusion = bf16[1024,768]{1,0:T(8,128)(2,1)} fusion(bf16[1024,384]{1,0:T(8,128)(2,1)S(1)} %bitcast.202, bf16[1,384,768]{2,1,0:T(8,128)(2,1)S(1)} %copy-done.4), kind=kOutput, calls=%fused_computation.16 | convolution fusion | flops 607911936 | bytes 2949120 | tf_op jit(solution)/shard_map/dot_general | solution.py:37
  7.6 2.4 %fusion.43 = bf16[2,1,512,384]{3,2,0,1:T(8,128)(2,1)S(1)} fusion(bf16[2,512,768]{2,1,0:T(8,128)(2,1)} %bitcast.217, bf16[2,1,512,384]{3,2,1,0:T(8,128)(2,1)S(1)} %copy-done.46, pred[]{:T(512)S(6)} %eq.9, bf16[1,768,384]{2,1,0:T(8,128)(2,1)S(1)} %copy-done.5, bf16[2,1,512,384]{3,2,1,0:T(8,128)(2,1)S(1)} %copy-done), kind=kOutput, calls=%fused_computation.76 | convolution fusion | flops 605552640 | bytes 4521985 | tf_op jit(solution)/shard_map/dot_general | solution.py:39
  11.0 7.4 %all-to-all-start = ((bf16[2,1,16,32,384]{4,3,0,1,2:T(8,128)(2,1)}), bf16[2,1,16,32,384]{4,3,0,1,2:T(8,128)(2,1)S(1)}, u32[]{:S(2)}, u32[]{:S(2)}) async-start(bf16[2,1,16,32,384]{4,3,0,1,2:T(8,128)(2,1)} %copy.16), calls=%async_computation | async-start | bytes 1572864 | tf_op jit(solution)/shard_map/all_to_all | solution.py:78
  20.1 2.4 %collective-permute-done.1 = f32[23,384]{1,0:T(8,128)S(1)} collective-permute-done((f32[23,384]{1,0:T(8,128)S(1)}, f32[23,384]{1,0:T(8,128)S(1)}, u32[]{:S(2)}, u32[]{:S(2)}) %collective-permute-start.1) | collective-permute-done | bytes 35360 | tf_op jit(solution)/shard_map/ppermute | solution.py:123
  23.2 13.9 %all-to-all-done = bf16[2,1,16,32,384]{4,3,0,1,2:T(8,128)(2,1)S(1)} async-done(((bf16[2,1,16,32,384]{4,3,0,1,2:T(8,128)(2,1)}), bf16[2,1,16,32,384]{4,3,0,1,2:T(8,128)(2,1)S(1)}, u32[]{:S(2)}, u32[]{:S(2)}) %all-to-all-start) | async-done | bytes 786464 | tf_op jit(solution)/shard_map/all_to_all | solution.py:78
  37.3 1.8 %fusion.66 = bf16[2,16,1,32,384]{4,3,0,2,1:T(8,128)(2,1)} fusion(f32[2,16,32,384]{3,2,0,1:T(8,128)S(1)} %bitcast_convert_fusion.1, f32[384]{0:T(512)S(1)} %get-tuple-element.41, f32[384]{0:T(512)S(1)} %get-tuple-element.42, f32[384]{0:T(512)S(1)} %get-tuple-element.43, f32[384]{0:T(512)S(1)} %get-tuple-element.44, f32[384]{0:T(512)S(1)} %get-tuple-element.45, ...), kind=kLoop, calls=%fused_computation.144 | loop fusion | flops 7471104 | bytes 2373120 | tf_op jit(solution)/shard_map/reshape | solution.py:81
  39.2 5.6 %all-to-all-start.1 = ((bf16[2,16,1,32,384]{4,3,0,2,1:T(8,128)(2,1)}), bf16[2,16,1,32,384]{4,3,0,2,1:T(8,128)(2,1)S(1)}, u32[]{:S(2)}, u32[]{:S(2)}) async-start(bf16[2,16,1,32,384]{4,3,0,2,1:T(8,128)(2,1)} %fusion.66), calls=%async_computation.1 | async-start | bytes 1572864 | tf_op jit(solution)/shard_map/all_to_all | solution.py:82
  44.8 1.6 collective-permute-start.2
  47.7 7.1 %collective-permute-done.2 = bf16[192,768]{1,0:T(8,128)(2,1)S(1)} collective-permute-done((bf16[192,768]{1,0:T(8,128)(2,1)S(1)}, bf16[192,768]{1,0:T(8,128)(2,1)S(1)}, u32[]{:S(2)}, u32[]{:S(2)}) %collective-permute-start.2) | collective-permute-done | bytes 294944 | tf_op jit(solution)/shard_map/ppermute | solution.py:118
  55.4 5.2 %collective-permute-done.4 = bf16[384,384]{1,0:T(8,128)(2,1)} collective-permute-done((bf16[384,384]{1,0:T(8,128)(2,1)S(1)}, bf16[384,384]{1,0:T(8,128)(2,1)}, u32[]{:S(2)}, u32[]{:S(2)}) %collective-permute-start.4) | collective-permute-done | bytes 294944 | tf_op jit(solution)/shard_map/ppermute | solution.py:118
  60.6 2.9 %all-to-all-done.1 = bf16[2,16,1,32,384]{4,3,0,2,1:T(8,128)(2,1)S(1)} async-done(((bf16[2,16,1,32,384]{4,3,0,2,1:T(8,128)(2,1)}), bf16[2,16,1,32,384]{4,3,0,2,1:T(8,128)(2,1)S(1)}, u32[]{:S(2)}, u32[]{:S(2)}) %all-to-all-start.1) | async-done | bytes 786464 | tf_op jit(solution)/shard_map/all_to_all | solution.py:82
  66.7 2.5 %bitcast_select_fusion.1 = (bf16[768,384]{1,0:T(8,128)(2,1)}, bf16[768,384]{1,0:T(8,128)(2,1)}) fusion(bf16[1,768,384]{2,1,0:T(8,128)(2,1)S(1)} %copy-done.5, pred[]{:T(512)S(6)} %eq.9, bf16[384,384]{1,0:T(8,128)(2,1)} %collective-permute-done.4, bf16[384,384]{1,0:T(8,128)(2,1)} %collective-permute-done.5, pred[]{:T(512)S(6)} %eq.10), kind=kLoop, calls=%fused_computation.149 | loop fusion | flops 3244032 | bytes 2359298 | tf_op jit(solution)/shard_map/jit(_where)/select_n | solution.py:134
  69.5 5.5 %collective-permute-done = bf16[1,1,512,384]{3,2,1,0:T(8,128)(2,1)S(1)} collective-permute-done((bf16[1,1,512,384]{3,2,1,0:T(8,128)(2,1)S(1)}, bf16[1,1,512,384]{3,2,1,0:T(8,128)(2,1)S(1)}, u32[]{:S(2)}, u32[]{:S(2)}) %collective-permute-start) | collective-permute-done | bytes 393248 | tf_op jit(solution)/shard_map/ppermute | solution.py:153
  85.1 5.7 %all-to-all-start.2 = ((bf16[2,1,16,32,384]{4,3,0,1,2:T(8,128)(2,1)}), bf16[2,1,16,32,384]{4,3,0,1,2:T(8,128)(2,1)S(1)}, u32[]{:S(2)}, u32[]{:S(2)}) async-start(bf16[2,1,16,32,384]{4,3,0,1,2:T(8,128)(2,1)} %copy.20), calls=%async_computation.2 | async-start | bytes 1572864 | tf_op jit(solution)/shard_map/all_to_all | solution.py:78
  92.2 17.3 %all-to-all-done.2 = bf16[2,1,16,32,384]{4,3,0,1,2:T(8,128)(2,1)S(1)} async-done(((bf16[2,1,16,32,384]{4,3,0,1,2:T(8,128)(2,1)}), bf16[2,1,16,32,384]{4,3,0,1,2:T(8,128)(2,1)S(1)}, u32[]{:S(2)}, u32[]{:S(2)}) %all-to-all-start.2) | async-done | bytes 786464 | tf_op jit(solution)/shard_map/all_to_all | solution.py:78
  109.7 2.4 %fusion.65 = bf16[2,16,1,32,384]{4,3,0,2,1:T(8,128)(2,1)} fusion(f32[2,16,32,384]{3,2,0,1:T(8,128)S(1)} %bitcast_convert_fusion, f32[2,384]{1,0:T(2,128)S(1)} %bitcast.208, f32[2,384]{1,0:T(2,128)S(1)} %bitcast.209, f32[2,384]{1,0:T(2,128)S(1)} %bitcast.210, f32[2,384]{1,0:T(2,128)S(1)} %bitcast.211, f32[2,384]{1,0:T(2,128)S(1)} %bitcast.212, ...), kind=kLoop, calls=%fused_computation.143 | loop fusion | flops 7471104 | bytes 2386944 | tf_op jit(solution)/shard_map/reshape | solution.py:81
  112.0 5.5 %all-to-all-start.3 = ((bf16[2,16,1,32,384]{4,3,0,2,1:T(8,128)(2,1)}), bf16[2,16,1,32,384]{4,3,0,2,1:T(8,128)(2,1)}, u32[]{:S(2)}, u32[]{:S(2)}) async-start(bf16[2,16,1,32,384]{4,3,0,2,1:T(8,128)(2,1)} %fusion.65), calls=%async_computation.3 | async-start | bytes 1572864 | tf_op jit(solution)/shard_map/all_to_all | solution.py:82
  118.7 1.7 %fusion.84 = f32[512,768]{1,0:T(8,128)} fusion(bf16[512,384]{1,0:T(8,128)(2,1)S(1)} %multiply_convert_fusion.4, bf16[384,768]{1,0:T(8,128)(2,1)S(1)} %get-tuple-element.21), kind=kOutput, calls=%fused_computation.254 | convolution fusion | flops 301989888 | bytes 2555904 | tf_op jit(solution)/shard_map/dot_general | solution.py:37
  120.4 4.3 %collective-permute-start.8 = (bf16[1,1,512,384]{3,2,1,0:T(8,128)(2,1)S(1)}, bf16[1,1,512,384]{3,2,1,0:T(8,128)(2,1)}, u32[]{:S(2)}, u32[]{:S(2)}) collective-permute-start(bf16[1,1,512,384]{3,2,1,0:T(8,128)(2,1)S(1)} %fusion.60), channel_id=1, source_target_pairs={{0,16},{1,17},{2,18},{3,19},{4,20},{5,21},{6,22},{7,23},{8,24},{9,... | collective-permute-start | bytes 1179656 | tf_op jit(solution)/shard_map/ppermute | solution.py:169
  124.7 11.7 %all-to-all-done.3 = bf16[2,16,1,32,384]{4,3,0,2,1:T(8,128)(2,1)} async-done(((bf16[2,16,1,32,384]{4,3,0,2,1:T(8,128)(2,1)}), bf16[2,16,1,32,384]{4,3,0,2,1:T(8,128)(2,1)}, u32[]{:S(2)}, u32[]{:S(2)}) %all-to-all-start.3) | async-done | bytes 786464 | tf_op jit(solution)/shard_map/all_to_all | solution.py:82
  137.7 3.4 %collective-permute-start.6 = (bf16[1,1,512,384]{3,2,1,0:T(8,128)(2,1)S(1)}, bf16[1,1,512,384]{3,2,1,0:T(8,128)(2,1)S(1)}, u32[]{:S(2)}, u32[]{:S(2)}) collective-permute-start(bf16[1,1,512,384]{3,2,1,0:T(8,128)(2,1)S(1)} %bitcast.198), channel_id=1, source_target_pairs={{0,16},{1,17},{2,18},{3,19},{4,20},{5,21},{6,22},{7,23},{8,24},{9,... | collective-permute-start | bytes 1179656 | tf_op jit(solution)/shard_map/ppermute | solution.py:170
  145.0 4.9 %collective-permute-done.6 = bf16[1,1,512,384]{3,2,1,0:T(8,128)(2,1)S(1)} collective-permute-done((bf16[1,1,512,384]{3,2,1,0:T(8,128)(2,1)S(1)}, bf16[1,1,512,384]{3,2,1,0:T(8,128)(2,1)S(1)}, u32[]{:S(2)}, u32[]{:S(2)}) %collective-permute-start.6) | collective-permute-done | bytes 393248 | tf_op jit(solution)/shard_map/ppermute | solution.py:170
  150.9 5.6 %collective-permute-done.7 = bf16[1,1,512,384]{3,2,1,0:T(8,128)(2,1)S(1)} collective-permute-done((bf16[1,1,512,384]{3,2,1,0:T(8,128)(2,1)S(1)}, bf16[1,1,512,384]{3,2,1,0:T(8,128)(2,1)S(1)}, u32[]{:S(2)}, u32[]{:S(2)}) %collective-permute-start.7) | collective-permute-done | bytes 393248 | tf_op jit(solution)/shard_map/ppermute | solution.py:171
  156.5 2.0 %maximum_select_fusion.1 = bf16[1,2,1,512,384]{4,3,2,1,0:T(8,128)(2,1)} fusion(bf16[1,1,1,512,384]{4,3,2,1,0:T(8,128)(2,1)S(1)} %bitcast.204, bf16[1,1,1,512,384]{4,3,2,1,0:T(8,128)(2,1)S(1)} %bitcast.200, bf16[1,1,1,512,384]{4,3,2,1,0:T(8,128)(2,1)S(1)} %bitcast.196, bf16[1,1,1,512,384]{4,3,2,1,0:T(8,128)(2,1)} %bitcast.48, pred[]{:T(512)S(6)} %eq.9), kind=kLoop, calls=%fused_computation.113 | loop fusion | flops 1179648 | bytes 2359297 | tf_op jit(solution)/shard_map/jit(_where)/select_n | solution.py:175
  (182 shorter events, 31.9 us)
Async XLA Ops:
  10.0 8.4 %copy-start.15 = (f32[1,2,2,384]{3,2,1,0:T(2,128)S(1)}, f32[1,2,2,384]{3,2,1,0:T(2,128)}, u32[]{:S(2)}) copy-start(f32[1,2,2,384]{3,2,1,0:T(2,128)} %param.11) | copy-start | bytes 18436
  10.0 8.5 %copy-start.14 = (f32[1,9,384]{2,0,1:T(1,128)S(1)}, f32[1,9,384]{2,0,1:T(1,128)}, u32[]{:S(2)}) copy-start(f32[1,9,384]{2,0,1:T(1,128)} %param.15) | copy-start | bytes 41476
  10.0 8.5 %copy-start.45 = (f32[1,384]{1,0:T(1,128)S(1)}, f32[1,384]{1,0:T(1,128)}, u32[]{:S(2)}) copy-start(f32[1,384]{1,0:T(1,128)} %param.12) | copy-start | bytes 4612
  11.0 26.1 %all-to-all-start = ((bf16[2,1,16,32,384]{4,3,0,1,2:T(8,128)(2,1)}), bf16[2,1,16,32,384]{4,3,0,1,2:T(8,128)(2,1)S(1)}, u32[]{:S(2)}, u32[]{:S(2)}) async-start(bf16[2,1,16,32,384]{4,3,0,1,2:T(8,128)(2,1)} %copy.16), calls=%async_computation | async-start | bytes 1572864 | tf_op jit(solution)/shard_map/all_to_all | solution.py:78
  18.5 4.0 %collective-permute-start.1 = (f32[23,384]{1,0:T(8,128)S(1)}, f32[23,384]{1,0:T(8,128)S(1)}, u32[]{:S(2)}, u32[]{:S(2)}) collective-permute-start(f32[23,384]{1,0:T(8,128)S(1)} %pad_maximum_fusion.1), channel_id=1, source_target_pairs={{0,16},{16,0},{1,17},{17,1},{2,18},{18,2},{3,19},{19,3},{4,20},{20... | collective-permute-start | bytes 105992 | tf_op jit(solution)/shard_map/ppermute | solution.py:123
  39.2 15.6 %copy-start.34 = (f32[384]{0:T(512)S(1)}, f32[384]{0:T(512)}, u32[]{:S(2)}) copy-start(f32[384]{0:T(512)} %copy-done.33) | copy-start | bytes 4612
  39.2 24.3 %all-to-all-start.1 = ((bf16[2,16,1,32,384]{4,3,0,2,1:T(8,128)(2,1)}), bf16[2,16,1,32,384]{4,3,0,2,1:T(8,128)(2,1)S(1)}, u32[]{:S(2)}, u32[]{:S(2)}) async-start(bf16[2,16,1,32,384]{4,3,0,2,1:T(8,128)(2,1)} %fusion.66), calls=%async_computation.1 | async-start | bytes 1572864 | tf_op jit(solution)/shard_map/all_to_all | solution.py:82
  44.8 9.9 %collective-permute-start.2 = (bf16[192,768]{1,0:T(8,128)(2,1)S(1)}, bf16[192,768]{1,0:T(8,128)(2,1)S(1)}, u32[]{:S(2)}, u32[]{:S(2)}) collective-permute-start(bf16[192,768]{1,0:T(8,128)(2,1)S(1)} %dynamic-slice_bitcast_fusion.1), channel_id=1, source_target_pairs={{0,16},{16,0},{1,17},{17,1},{2,18},{18,2},{3,19},{19,3},{4,20},{20... | collective-permute-start | bytes 884744 | tf_op jit(solution)/shard_map/ppermute | solution.py:118
  46.4 14.2 %collective-permute-start.4 = (bf16[384,384]{1,0:T(8,128)(2,1)S(1)}, bf16[384,384]{1,0:T(8,128)(2,1)}, u32[]{:S(2)}, u32[]{:S(2)}) collective-permute-start(bf16[384,384]{1,0:T(8,128)(2,1)S(1)} %dynamic-slice_bitcast_fusion), channel_id=1, source_target_pairs={{0,16},{16,0},{1,17},{17,1},{2,18},{18,2},{3,19},{19,3},{4,20},{20... | collective-permute-start | bytes 884744 | tf_op jit(solution)/shard_map/ppermute | solution.py:118
  54.7 10.4 %copy-start.8 = (bf16[192,768]{1,0:T(8,128)(2,1)}, bf16[192,768]{1,0:T(8,128)(2,1)S(1)}, u32[]{:S(2)}) copy-start(bf16[192,768]{1,0:T(8,128)(2,1)S(1)} %collective-permute-done.2) | copy-start | bytes 884740
  54.7 10.4 %collective-permute-start.3 = (bf16[192,768]{1,0:T(8,128)(2,1)S(1)}, bf16[192,768]{1,0:T(8,128)(2,1)}, u32[]{:S(2)}, u32[]{:S(2)}) collective-permute-start(bf16[192,768]{1,0:T(8,128)(2,1)S(1)} %collective-permute-done.2), channel_id=1, source_target_pairs={{0,1},{1,0},{2,3},{3,2},{4,5},{5,4},{6,7},{7,6},{8,9},{9,8},{10,11... | collective-permute-start | bytes 884744 | tf_op jit(solution)/shard_map/ppermute | solution.py:119
  60.6 6.1 %collective-permute-start.5 = (bf16[384,384]{1,0:T(8,128)(2,1)}, bf16[384,384]{1,0:T(8,128)(2,1)}, u32[]{:S(2)}, u32[]{:S(2)}) collective-permute-start(bf16[384,384]{1,0:T(8,128)(2,1)} %collective-permute-done.4), channel_id=1, source_target_pairs={{0,1},{1,0},{2,3},{3,2},{4,5},{5,4},{6,7},{7,6},{8,9},{9,8},{10,11... | collective-permute-start | bytes 884744 | tf_op jit(solution)/shard_map/ppermute | solution.py:119
  63.6 11.3 %collective-permute-start = (bf16[1,1,512,384]{3,2,1,0:T(8,128)(2,1)S(1)}, bf16[1,1,512,384]{3,2,1,0:T(8,128)(2,1)S(1)}, u32[]{:S(2)}, u32[]{:S(2)}) collective-permute-start(bf16[1,1,512,384]{3,2,1,0:T(8,128)(2,1)S(1)} %constant_dynamic-slice_fusion.5), channel_id=1, source_target_pairs={{0,16},{16,0},{1,17},{17,1},{2,18},{18,2},{3,19},{19,3},{4,20},{20... | collective-permute-start | bytes 1179656 | tf_op jit(solution)/shard_map/ppermute | solution.py:153
  69.3 7.2 %copy-start.16 = (f32[384]{0:T(512)}, f32[384]{0:T(512)S(1)}, u32[]{:S(2)}) copy-start(f32[384]{0:T(512)S(1)} %get-tuple-element.60) | copy-start | bytes 4612
  69.3 7.2 %copy-start.18 = (f32[384]{0:T(512)}, f32[384]{0:T(512)S(1)}, u32[]{:S(2)}) copy-start(f32[384]{0:T(512)S(1)} %get-tuple-element.61) | copy-start | bytes 4612
  85.1 6.9 %copy-start.10 = (f32[1,9,384]{2,1,0:T(8,128)S(1)}, f32[1,9,384]{2,1,0:T(8,128)}, u32[]{:S(2)}) copy-start(f32[1,9,384]{2,1,0:T(8,128)} %get-tuple-element.98) | copy-start | bytes 41476
  85.1 7.0 %copy-start.43 = (f32[2,2,384]{2,1,0:T(2,128)S(1)}, f32[2,2,384]{2,1,0:T(2,128)}, u32[]{:S(2)}) copy-start(f32[2,2,384]{2,1,0:T(2,128)} %get-tuple-element.18) | copy-start | bytes 18436
  85.1 7.0 %copy-start.12 = (f32[9,384]{1,0:T(8,128)S(1)}, f32[9,384]{1,0:T(8,128)}, u32[]{:S(2)}) copy-start(f32[9,384]{1,0:T(8,128)} %get-tuple-element.17) | copy-start | bytes 41476
  85.1 24.4 %all-to-all-start.2 = ((bf16[2,1,16,32,384]{4,3,0,1,2:T(8,128)(2,1)}), bf16[2,1,16,32,384]{4,3,0,1,2:T(8,128)(2,1)S(1)}, u32[]{:S(2)}, u32[]{:S(2)}) async-start(bf16[2,1,16,32,384]{4,3,0,1,2:T(8,128)(2,1)} %copy.20), calls=%async_computation.2 | async-start | bytes 1572864 | tf_op jit(solution)/shard_map/all_to_all | solution.py:78
  112.0 24.3 %all-to-all-start.3 = ((bf16[2,16,1,32,384]{4,3,0,2,1:T(8,128)(2,1)}), bf16[2,16,1,32,384]{4,3,0,2,1:T(8,128)(2,1)}, u32[]{:S(2)}, u32[]{:S(2)}) async-start(bf16[2,16,1,32,384]{4,3,0,2,1:T(8,128)(2,1)} %fusion.65), calls=%async_computation.3 | async-start | bytes 1572864 | tf_op jit(solution)/shard_map/all_to_all | solution.py:82
  120.4 20.8 %copy-start.6 = (bf16[768,384]{1,0:T(8,128)(2,1)S(1)}, bf16[768,384]{1,0:T(8,128)(2,1)}, u32[]{:S(2)}) copy-start(bf16[768,384]{1,0:T(8,128)(2,1)} %get-tuple-element.19) | copy-start | bytes 1769476
  120.4 30.5 %collective-permute-start.8 = (bf16[1,1,512,384]{3,2,1,0:T(8,128)(2,1)S(1)}, bf16[1,1,512,384]{3,2,1,0:T(8,128)(2,1)}, u32[]{:S(2)}, u32[]{:S(2)}) collective-permute-start(bf16[1,1,512,384]{3,2,1,0:T(8,128)(2,1)S(1)} %fusion.60), channel_id=1, source_target_pairs={{0,16},{1,17},{2,18},{3,19},{4,20},{5,21},{6,22},{7,23},{8,24},{9,... | collective-permute-start | bytes 1179656 | tf_op jit(solution)/shard_map/ppermute | solution.py:169
  137.7 12.2 %collective-permute-start.6 = (bf16[1,1,512,384]{3,2,1,0:T(8,128)(2,1)S(1)}, bf16[1,1,512,384]{3,2,1,0:T(8,128)(2,1)S(1)}, u32[]{:S(2)}, u32[]{:S(2)}) collective-permute-start(bf16[1,1,512,384]{3,2,1,0:T(8,128)(2,1)S(1)} %bitcast.198), channel_id=1, source_target_pairs={{0,16},{1,17},{2,18},{3,19},{4,20},{5,21},{6,22},{7,23},{8,24},{9,... | collective-permute-start | bytes 1179656 | tf_op jit(solution)/shard_map/ppermute | solution.py:170
  143.6 12.9 %collective-permute-start.7 = (bf16[1,1,512,384]{3,2,1,0:T(8,128)(2,1)S(1)}, bf16[1,1,512,384]{3,2,1,0:T(8,128)(2,1)S(1)}, u32[]{:S(2)}, u32[]{:S(2)}) collective-permute-start(bf16[1,1,512,384]{3,2,1,0:T(8,128)(2,1)S(1)} %fusion.61), channel_id=1, source_target_pairs={{16,0},{17,1},{18,2},{19,3},{20,4},{21,5},{22,6},{23,7},{24,8},{25... | collective-permute-start | bytes 1179656 | tf_op jit(solution)/shard_map/ppermute | solution.py:171
  (36 other events, 98.3 us)

commit v14 on v13

--- a/solution.py
+++ b/solution.py
@@ -119,7 +119,7 @@
         other = lax.ppermute(got, "seq", perm=siblings)
         return jnp.where(core == 0, jnp.concatenate([got, other]), jnp.concatenate([other, got]))
 
-    small = jnp.concatenate([taps, mod.reshape(-1, channels), gain[None], band])
+    small = jnp.concatenate([taps, mod.reshape(-1, channels), gain[None]])
     got_small = lax.ppermute(small, "section", perm=swap)
     mod_rows = mod.shape[0] * mod.shape[1]
     other = (
@@ -129,21 +129,15 @@
         fetch_halves(weight_in),
         fetch_halves(weight_out),
     )
-    other_band = got_small[tap_count + mod_rows + 1 :]
-    first_seg = lax.optimization_barrier(
-        tuple(jnp.where(first, o, r) for o, r in zip(own, other))
-    )
     second_seg = lax.optimization_barrier(
         tuple(jnp.where(first, r, o) for o, r in zip(own, other))
     )
-    first_band = jnp.where(first, band, other_band)
-    second_band = jnp.where(first, other_band, band)
 
     def for_clip(params, clip):
         clip_mod = lax.dynamic_index_in_dim(params[1], clip, 0, keepdims=True)
         return (params[0], clip_mod) + tuple(params[2:])
 
-    first_mixed, _ = spatial_forward(clips, *own)
+    first_mixed, first_saved = spatial_forward(clips, *own)
     lead_in = jnp.where(first, first_mixed, cotangent)
     lead_taps = jnp.where(first, band, band[::-1])
     lead_out = temporal(lead_in, lead_taps[None])
@@ -157,26 +151,19 @@
     second_mixed, second_saved = spatial_forward(clip_act, *second_params)
     second_grad = spatial_backward(second_saved, clip_seed, *second_params)
 
-    tail_out = temporal(
-        jnp.concatenate([second_grad, second_mixed]), jnp.stack([first_band[::-1], second_band])
+    got_tail = lax.ppermute(jnp.where(first, second_mixed, second_grad), "section", perm=swap)
+    tail_in = jnp.where(
+        first,
+        jnp.concatenate([second_grad, got_tail]),
+        jnp.concatenate([got_tail, second_mixed]),
     )
-    first_params = for_clip(first_seg, plane)
-    start = lax.dynamic_index_in_dim(clips, plane, 0, keepdims=True)
-    _, first_saved = spatial_forward(start, *first_params)
-    first_grad = spatial_backward(first_saved, tail_out[:1], *first_params)
+    tail_taps = jnp.where(first, band[::-1], band)
+    tail_out = temporal(tail_in, tail_taps[None])
+    first_grad = spatial_backward(first_saved, tail_out, *own)
 
-    to_second, to_first = [(0, 1)], [(1, 0)]
-    sent_second_grad = lax.ppermute(second_grad, "section", perm=to_second)
-    sent_second_act = lax.ppermute(tail_out[1:], "section", perm=to_second)
-    sent_first_grad = lax.ppermute(first_grad, "section", perm=to_first)
-    activations = jnp.where(
-        first, lead_out, jnp.concatenate([sent_second_act, tail_out[1:]])
-    )
-    input_grads = jnp.where(
-        first,
-        jnp.concatenate([first_grad, sent_first_grad]),
-        jnp.concatenate([sent_second_grad, second_grad]),
-    )
+    sent_second_grad = lax.ppermute(second_grad, "section", perm=[(0, 1)])
+    activations = jnp.where(first, lead_out, tail_out)
+    input_grads = jnp.where(first, first_grad, jnp.concatenate([sent_second_grad, second_grad]))
     return (activations[None], input_grads[None])
 
 

time: 160 us -> 164 us (1.025)
  local copies, waits for them, and re-layouts: 6.37 us -> 19.1 us
  starting transfers between devices: 38.5 us -> 32.1 us
  waiting for transfers between devices: 76.4 us -> 70.7 us
  matrix products: 10.5 us -> 12.2 us
    ppermute x3 -> x2, starting transfers between devices: 8.99 us -> 3.89 us  [the longest x1 3.29 us: on_device(): sent_second_grad = lax.ppermute(second_grad, 'section', perm=[(0, 1)])]
    ppermute x2, waiting for transfers between devices: 12.3 us -> 7.54 us  [fetch_halves(): got = lax.ppermute(mine, 'section', perm=swap)]
    unnamed x105 -> x121, local copies, waits for them, and re-layouts: 2.9 us -> 6.29 us
    dot_general x2, matrix products: 1.52 us -> 4.16 us  [spatial_backward(): jnp.dot(flat_grad, w_out.T, preferred_element_type=jnp.float32)]
    ppermute x1, waiting for transfers between devices: 2.4 us -> 0.01 us  [on_device(): got_small = lax.ppermute(small, 'section', perm=swap)]
    slice x1 -> x2, local copies, waits for them, and re-layouts: 0.05 us -> 2.28 us  [band_frames(): tap_table[:, offset, None, None, :] * padded[:, offset:offset + frame_count]]
    rev x1, local copies, waits for them, and re-layouts: 0.06 us -> 2.01 us  [on_device(): lead_taps = jnp.where(first, band, band[::-1])]
    mul x2, other arithmetic: 0.55 us -> 2.2 us  [spatial_backward(): stencil_grad = modulated_grad * (1.0 + modulate[:, 0])[:, None, None, :]]
  transfers between devices with their start and end apart: 13 -> 12, of which waited for: 10 -> 7; matrix products, arithmetic and copies ran while one was open for 10% -> 19% of each run, Pallas kernels for 0% -> 0%
where the time goes in v14:
time: 164 us; the launch traced here: 162 us
  waiting for transfers between devices  70.7 us (43%)
  starting transfers between devices  32.1 us (20%)
  other arithmetic  26.6 us (16%)
  local copies, waits for them, and re-layouts  19.1 us (12%)
  matrix products  12.2 us (7%)
    all_to_all x2, waiting for transfers between devices, temporal(): lax.all_to_all(grouped, 'seq', split_axis=2, concat_axis=1, tiled=True)  31.2 us
    all_to_all x2, waiting for transfers between devices, temporal(): lax.all_to_all(banded, 'seq', split_axis=1, concat_axis=2, tiled=True)  15.4 us
    all_to_all x2, starting transfers between devices, temporal(): lax.all_to_all(grouped, 'seq', split_axis=2, concat_axis=1, tiled=True)  13.1 us
    all_to_all x2, starting transfers between devices, temporal(): lax.all_to_all(banded, 'seq', split_axis=1, concat_axis=2, tiled=True)  11 us
    ppermute x1, waiting for transfers between devices, on_device(): lax.ppermute(jnp.where(first, second_mixed, second_grad), 'section', perm...  10.2 us
    ppermute x2, waiting for transfers between devices, fetch_halves(): got = lax.ppermute(mine, 'section', perm=swap)  7.54 us
    select_n x5, other arithmetic, on_device(): jnp.where(first, r, o)  6.61 us
    ppermute x1, waiting for transfers between devices, on_device(): got = lax.ppermute(theirs, 'section', perm=swap)  6.35 us
  transfers between devices with their start and end apart: 12, of which 7 were waited for; matrix products, arithmetic and copies ran while one was open for 19% of the time, Pallas kernels for 0%

profile of v14, /device:TPU:0, one launch (start us, length us, event | category | flops | bytes accessed | tf_op | source)
XLA Modules:
  0.0 162.0 jit_solution(228415537292152101)
XLA Ops:
  6.9 2.8 %multiply_convert_fusion.1 = (bf16[1024,768]{1,0:T(8,128)(2,1)S(1)}, f32[1024,768]{1,0:T(8,128)}) fusion(bf16[1024,384]{1,0:T(8,128)(2,1)S(1)} %bitcast.167, bf16[1,384,768]{2,1,0:T(8,128)(2,1)S(1)} %copy-done.3), kind=kOutput, calls=%fused_computation.17 | convolution fusion | flops 607911936 | bytes 6094848 | tf_op jit(solution)/shard_map/dot_general | solution.py:37
  11.8 7.4 %all-to-all-start = ((bf16[2,1,16,32,384]{4,3,0,1,2:T(8,128)(2,1)}), bf16[2,1,16,32,384]{4,3,0,1,2:T(8,128)(2,1)S(1)}, u32[]{:S(2)}, u32[]{:S(2)}) async-start(bf16[2,1,16,32,384]{4,3,0,1,2:T(8,128)(2,1)} %copy.35), calls=%async_computation | async-start | bytes 1572864 | tf_op jit(solution)/shard_map/all_to_all | solution.py:78
  19.8 2.0 %rev.2 = f32[9,384]{1,0:T(8,128)} reverse(f32[9,384]{1,0:T(8,128)} %bitcast.173), dimensions={0} | reverse | bytes 27648 | tf_op jit(solution)/shard_map/rev | solution.py:142
  23.8 14.1 %all-to-all-done = bf16[2,1,16,32,384]{4,3,0,1,2:T(8,128)(2,1)S(1)} async-done(((bf16[2,1,16,32,384]{4,3,0,1,2:T(8,128)(2,1)}), bf16[2,1,16,32,384]{4,3,0,1,2:T(8,128)(2,1)S(1)}, u32[]{:S(2)}, u32[]{:S(2)}) %all-to-all-start) | async-done | bytes 786464 | tf_op jit(solution)/shard_map/all_to_all | solution.py:78
  38.6 1.8 %fusion.64 = bf16[2,16,1,32,384]{4,3,0,2,1:T(8,128)(2,1)} fusion(f32[2,16,32,384]{3,2,0,1:T(8,128)S(1)} %bitcast_convert_fusion.1, f32[384]{0:T(512)S(1)} %copy-done.44, f32[384]{0:T(512)S(1)} %copy-done.45, f32[384]{0:T(512)S(1)} %copy-done.46, f32[384]{0:T(512)S(1)} %copy-done.47, f32[384]{0:T(512)S(1)} %copy-done.48, f32[384]{0:T(512)S(1)} %copy-done.49, ...), kind=kLoop, calls=%fused_computation.134 | loop fusion | flops 7471104 | bytes 2373120 | tf_op jit(solution)/shard_map/reshape | solution.py:81
  40.5 5.5 %all-to-all-start.1 = ((bf16[2,16,1,32,384]{4,3,0,2,1:T(8,128)(2,1)}), bf16[2,16,1,32,384]{4,3,0,2,1:T(8,128)(2,1)S(1)}, u32[]{:S(2)}, u32[]{:S(2)}) async-start(bf16[2,16,1,32,384]{4,3,0,2,1:T(8,128)(2,1)} %fusion.64), calls=%async_computation.1 | async-start | bytes 1572864 | tf_op jit(solution)/shard_map/all_to_all | solution.py:82
  48.6 1.5 collective-permute-start.1
  59.0 2.0 %collective-permute-done.4 = bf16[384,384]{1,0:T(8,128)(2,1)} collective-permute-done((bf16[384,384]{1,0:T(8,128)(2,1)}, bf16[384,384]{1,0:T(8,128)(2,1)}, u32[]{:S(2)}, u32[]{:S(2)}) %collective-permute-start.4) | collective-permute-done | bytes 294944 | tf_op jit(solution)/shard_map/ppermute | solution.py:118
  61.0 5.5 %collective-permute-done.2 = bf16[192,768]{1,0:T(8,128)(2,1)} collective-permute-done((bf16[192,768]{1,0:T(8,128)(2,1)}, bf16[192,768]{1,0:T(8,128)(2,1)}, u32[]{:S(2)}, u32[]{:S(2)}) %collective-permute-start.2) | collective-permute-done | bytes 294944 | tf_op jit(solution)/shard_map/ppermute | solution.py:118
  67.3 2.3 %fusion.66 = bf16[768,384]{1,0:T(8,128)(2,1)} fusion(bf16[384,384]{1,0:T(8,128)(2,1)} %collective-permute-done.5, bf16[384,384]{1,0:T(8,128)(2,1)} %collective-permute-done.4, bf16[1,768,384]{2,1,0:T(8,128)(2,1)S(1)} %copy-done.7, pred[]{:T(512)S(6)} %eq.10, pred[]{:T(512)S(6)} %eq.9), kind=kLoop, calls=%fused_computation.138 | loop fusion | flops 2949120 | bytes 1769474 | tf_op jit(solution)/shard_map/jit(_where)/select_n | solution.py:133
  69.6 2.3 %fusion.65 = bf16[384,768]{1,0:T(8,128)(2,1)} fusion(bf16[192,768]{1,0:T(8,128)(2,1)} %collective-permute-done.3, bf16[192,768]{1,0:T(8,128)(2,1)} %collective-permute-done.2, bf16[1,384,768]{2,1,0:T(8,128)(2,1)S(1)} %copy-done.3, pred[]{:T(512)S(6)} %eq.10, pred[]{:T(512)S(6)} %eq.9), kind=kLoop, calls=%fused_computation.136 | loop fusion | flops 2949120 | bytes 1769474 | tf_op jit(solution)/shard_map/jit(_where)/select_n | solution.py:133
  71.9 6.3 %collective-permute-done = bf16[1,1,512,384]{3,2,1,0:T(8,128)(2,1)S(1)} collective-permute-done((bf16[1,1,512,384]{3,2,1,0:T(8,128)(2,1)S(1)}, bf16[1,1,512,384]{3,2,1,0:T(8,128)(2,1)S(1)}, u32[]{:S(2)}, u32[]{:S(2)}) %collective-permute-start) | collective-permute-done | bytes 393248 | tf_op jit(solution)/shard_map/ppermute | solution.py:147
  86.8 10.2 %collective-permute-done.6 = bf16[1,1,512,384]{3,2,1,0:T(8,128)(2,1)S(1)} collective-permute-done((bf16[1,1,512,384]{3,2,1,0:T(8,128)(2,1)S(1)}, bf16[1,1,512,384]{3,2,1,0:T(8,128)(2,1)S(1)}, u32[]{:S(2)}, u32[]{:S(2)}) %collective-permute-start.6) | collective-permute-done | bytes 393248 | tf_op jit(solution)/shard_map/ppermute | solution.py:154
  98.0 5.7 %all-to-all-start.2 = ((bf16[2,1,16,32,384]{4,3,0,1,2:T(8,128)(2,1)}), bf16[2,1,16,32,384]{4,3,0,1,2:T(8,128)(2,1)S(1)}, u32[]{:S(2)}, u32[]{:S(2)}) async-start(bf16[2,1,16,32,384]{4,3,0,1,2:T(8,128)(2,1)} %maximum_select_fusion), calls=%async_computation.2 | async-start | bytes 1572864 | tf_op jit(solution)/shard_map/all_to_all | solution.py:78
  103.8 1.6 %slice_reduce_fusion.8 = (f32[384]{0:T(512)S(1)}, f32[384]{0:T(512)S(1)}, f32[384]{0:T(512)S(1)}, f32[384]{0:T(512)S(1)}, f32[384]{0:T(512)}, /*index=5*/f32[384]{0:T(512)}, f32[384]{0:T(512)}, f32[384]{0:T(512)}, f32[384]{0:T(512)}) fusion(f32[1,9,384]{2,1,0:T(8,128)} %get-tuple-element.68), kind=kLoop, calls=%fused_computation.173 | loop fusion | bytes 27648 | tf_op jit(solution)/shard_map/slice | solution.py:70
  105.4 17.1 %all-to-all-done.2 = bf16[2,1,16,32,384]{4,3,0,1,2:T(8,128)(2,1)S(1)} async-done(((bf16[2,1,16,32,384]{4,3,0,1,2:T(8,128)(2,1)}), bf16[2,1,16,32,384]{4,3,0,1,2:T(8,128)(2,1)S(1)}, u32[]{:S(2)}, u32[]{:S(2)}) %all-to-all-start.2) | async-done | bytes 786464 | tf_op jit(solution)/shard_map/all_to_all | solution.py:78
  123.2 1.8 %fusion.63 = bf16[2,16,1,32,384]{4,3,0,2,1:T(8,128)(2,1)} fusion(f32[2,16,32,384]{3,2,0,1:T(8,128)S(1)} %bitcast_convert_fusion, f32[384]{0:T(512)S(1)} %get-tuple-element.15, f32[384]{0:T(512)S(1)} %get-tuple-element.16, f32[384]{0:T(512)S(1)} %get-tuple-element.17, f32[384]{0:T(512)S(1)} %copy-done.52, f32[384]{0:T(512)S(1)} %copy-done.53, ...), kind=kLoop, calls=%fused_computation.133 | loop fusion | flops 7471104 | bytes 2373120 | tf_op jit(solution)/shard_map/reshape | solution.py:81
  125.0 5.5 %all-to-all-start.3 = ((bf16[2,16,1,32,384]{4,3,0,2,1:T(8,128)(2,1)}), bf16[2,16,1,32,384]{4,3,0,2,1:T(8,128)(2,1)S(1)}, u32[]{:S(2)}, u32[]{:S(2)}) async-start(bf16[2,16,1,32,384]{4,3,0,2,1:T(8,128)(2,1)} %fusion.63), calls=%async_computation.3 | async-start | bytes 1572864 | tf_op jit(solution)/shard_map/all_to_all | solution.py:82
  130.5 3.3 %collective-permute-start.7 = (bf16[1,1,512,384]{3,2,1,0:T(8,128)(2,1)S(1)}, bf16[1,1,512,384]{3,2,1,0:T(8,128)(2,1)}, u32[]{:S(2)}, u32[]{:S(2)}) collective-permute-start(bf16[1,1,512,384]{3,2,1,0:T(8,128)(2,1)S(1)} %get-tuple-element.53), channel_id=1, source_target_pairs={{0,16},{1,17},{2,18},{3,19},{4,20},{5,21},{6,22},{7,23},{8,24},{9,... | collective-permute-start | bytes 1179656 | tf_op jit(solution)/shard_map/ppermute | solution.py:164
  133.8 15.4 %all-to-all-done.3 = bf16[2,16,1,32,384]{4,3,0,2,1:T(8,128)(2,1)S(1)} async-done(((bf16[2,16,1,32,384]{4,3,0,2,1:T(8,128)(2,1)}), bf16[2,16,1,32,384]{4,3,0,2,1:T(8,128)(2,1)S(1)}, u32[]{:S(2)}, u32[]{:S(2)}) %all-to-all-start.3) | async-done | bytes 786464 | tf_op jit(solution)/shard_map/all_to_all | solution.py:82
  150.3 3.4 %multiply_convert_fusion = bf16[1024,768]{1,0:T(8,128)(2,1)S(1)} fusion(f32[1024,768]{1,0:T(8,128)} %get-tuple-element.75, bf16[1024,384]{1,0:T(8,128)(2,1)S(1)} %bitcast.169, bf16[1,768,384]{2,1,0:T(8,128)(2,1)S(1)} %copy-done.8), kind=kOutput, calls=%fused_computation.16 | convolution fusion | flops 612630528 | bytes 6094848 | tf_op jit(solution)/shard_map/dot_general | solution.py:48
  153.8 2.2 %fusion.43 = (f32[1024]{0:T(1024)S(1)}, f32[1024,384]{1,0:T(8,128)}) fusion(f32[2,1,32,16,384]{4,3,2,0,1:T(8,128)S(1)} %get-tuple-element.57, f32[384]{0:T(512)S(1)} %copy-done.24, f32[2,384]{1,0:T(2,128)S(1)} %copy-done.18, f32[2,384]{1,0:T(2,128)S(1)} %copy-done.20, bf16[1024,768]{1,0:T(8,128)(2,1)S(1)} %multiply_convert_fusion, ...), kind=kOutput, calls=%fused_computation.73 | convolution fusion | flops 606731264 | bytes 5320192 | tf_op jit(solution)/shard_map/dot_general | solution.py:52
  156.1 1.9 %subtract_multiply_fusion = f32[2,1,32,16,384]{4,3,2,0,1:T(8,128)S(1)} fusion(f32[2,1,32,16,384]{4,3,2,0,1:T(8,128)} %bitcast.158, f32[2,1,32,16,384]{4,3,2,0,1:T(8,128)S(1)} %get-tuple-element.57, f32[2,32,16]{2,1,0:T(8,128)S(1)} %div.30, f32[2,32,16]{2,1,0:T(8,128)S(1)} %copy-done.15, f32[384]{0:T(512)S(1)} %copy-done.24, f32[2,32,16]{2,1,0:T(8,128)S(1)} %copy-done.14, ...), kind=kLoop, calls=%fused_computation.84 | loop fusion | flops 3145728 | bytes 4738560 | tf_op jit(solution)/shard_map/mul | solution.py:56
  159.9 2.1 %fusion.60 = bf16[1,2,1,512,384]{4,3,2,1,0:T(8,128)(2,1)} fusion(f32[1,2,1,512,384]{4,3,2,1,0:T(8,128)S(1)} %bitcast.157, bf16[1,2,1,512,384]{4,3,2,1,0:T(8,128)(2,1)S(1)} %bitcast.163, bf16[1,1,1,512,384]{4,3,2,1,0:T(8,128)(2,1)S(1)} %bitcast.165, bf16[1,1,1,512,384]{4,3,2,1,0:T(8,128)(2,1)} %bitcast.47, pred[]{:T(512)S(6)} %eq.9), kind=kLoop, calls=%fused_computation.115 | loop fusion | flops 1966080 | bytes 3932161 | tf_op jit(solution)/shard_map/jit(_where)/select_n | solution.py:166
  (183 shorter events, 36.9 us)
Async XLA Ops:
  3.6 2.7 %copy-start.17 = (f32[2,384]{1,0:T(2,128)}, f32[2,384]{1,0:T(2,128)S(1)}, u32[]{:S(2)}) copy-start(f32[2,384]{1,0:T(2,128)S(1)} %get-tuple-element.81) | copy-start | bytes 9220
  6.9 2.8 %copy-start.7 = (bf16[1,768,384]{2,1,0:T(8,128)(2,1)S(1)}, bf16[1,768,384]{2,1,0:T(8,128)(2,1)}, u32[]{:S(2)}) copy-start(bf16[1,768,384]{2,1,0:T(8,128)(2,1)} %param.14) | copy-start | bytes 1769476
  6.9 2.8 %copy-start.9 = (bf16[2,1,512,384]{3,2,1,0:T(8,128)(2,1)S(1)}, bf16[2,1,512,384]{3,2,1,0:T(8,128)(2,1)}, u32[]{:S(2)}) copy-start(bf16[2,1,512,384]{3,2,1,0:T(8,128)(2,1)} %param.8) | copy-start | bytes 2359300
  6.9 2.8 %copy-start.58 = (bf16[2,1,512,384]{3,2,1,0:T(8,128)(2,1)S(1)}, bf16[2,1,512,384]{3,2,1,0:T(8,128)(2,1)}, u32[]{:S(2)}) copy-start(bf16[2,1,512,384]{3,2,1,0:T(8,128)(2,1)} %param.9) | copy-start | bytes 2359300
  10.8 8.4 %copy-start.22 = (f32[1,9,384]{2,0,1:T(1,128)S(1)}, f32[1,9,384]{2,0,1:T(1,128)}, u32[]{:S(2)}) copy-start(f32[1,9,384]{2,0,1:T(1,128)} %param.15) | copy-start | bytes 41476
  11.8 26.1 %all-to-all-start = ((bf16[2,1,16,32,384]{4,3,0,1,2:T(8,128)(2,1)}), bf16[2,1,16,32,384]{4,3,0,1,2:T(8,128)(2,1)S(1)}, u32[]{:S(2)}, u32[]{:S(2)}) async-start(bf16[2,1,16,32,384]{4,3,0,1,2:T(8,128)(2,1)} %copy.35), calls=%async_computation | async-start | bytes 1572864 | tf_op jit(solution)/shard_map/all_to_all | solution.py:78
  38.6 8.6 %copy-start.16 = (f32[1,9,384]{2,0,1:T(1,128)S(1)}, f32[1,9,384]{2,0,1:T(1,128)}, u32[]{:S(2)}) copy-start(f32[1,9,384]{2,0,1:T(1,128)} %param.10) | copy-start | bytes 41476
  40.5 26.0 %all-to-all-start.1 = ((bf16[2,16,1,32,384]{4,3,0,2,1:T(8,128)(2,1)}), bf16[2,16,1,32,384]{4,3,0,2,1:T(8,128)(2,1)S(1)}, u32[]{:S(2)}, u32[]{:S(2)}) async-start(bf16[2,16,1,32,384]{4,3,0,2,1:T(8,128)(2,1)} %fusion.64), calls=%async_computation.1 | async-start | bytes 1572864 | tf_op jit(solution)/shard_map/all_to_all | solution.py:82
  48.6 5.0 %collective-permute-start.1 = (f32[14,384]{1,0:T(8,128)}, f32[14,384]{1,0:T(8,128)}, u32[]{:S(2)}, u32[]{:S(2)}) collective-permute-start(f32[14,384]{1,0:T(8,128)} %pad_maximum_fusion), channel_id=1, source_target_pairs={{0,16},{16,0},{1,17},{17,1},{2,18},{18,2},{3,19},{19,3},{4,20},{20... | collective-permute-start | bytes 64520 | tf_op jit(solution)/shard_map/ppermute | solution.py:123
  50.8 10.2 %collective-permute-start.4 = (bf16[384,384]{1,0:T(8,128)(2,1)}, bf16[384,384]{1,0:T(8,128)(2,1)}, u32[]{:S(2)}, u32[]{:S(2)}) collective-permute-start(bf16[384,384]{1,0:T(8,128)(2,1)} %dynamic-slice_bitcast_fusion), channel_id=1, source_target_pairs={{0,16},{16,0},{1,17},{17,1},{2,18},{18,2},{3,19},{19,3},{4,20},{20... | collective-permute-start | bytes 884744 | tf_op jit(solution)/shard_map/ppermute | solution.py:118
  52.1 14.4 %collective-permute-start.2 = (bf16[192,768]{1,0:T(8,128)(2,1)}, bf16[192,768]{1,0:T(8,128)(2,1)}, u32[]{:S(2)}, u32[]{:S(2)}) collective-permute-start(bf16[192,768]{1,0:T(8,128)(2,1)} %dynamic-slice_bitcast_fusion.1), channel_id=1, source_target_pairs={{0,16},{16,0},{1,17},{17,1},{2,18},{18,2},{3,19},{19,3},{4,20},{20... | collective-permute-start | bytes 884744 | tf_op jit(solution)/shard_map/ppermute | solution.py:118
  61.0 6.3 %collective-permute-start.5 = (bf16[384,384]{1,0:T(8,128)(2,1)}, bf16[384,384]{1,0:T(8,128)(2,1)}, u32[]{:S(2)}, u32[]{:S(2)}) collective-permute-start(bf16[384,384]{1,0:T(8,128)(2,1)} %collective-permute-done.4), channel_id=1, source_target_pairs={{0,1},{1,0},{2,3},{3,2},{4,5},{5,4},{6,7},{7,6},{8,9},{9,8},{10,11... | collective-permute-start | bytes 884744 | tf_op jit(solution)/shard_map/ppermute | solution.py:119
  66.5 3.1 %collective-permute-start.3 = (bf16[192,768]{1,0:T(8,128)(2,1)}, bf16[192,768]{1,0:T(8,128)(2,1)}, u32[]{:S(2)}, u32[]{:S(2)}) collective-permute-start(bf16[192,768]{1,0:T(8,128)(2,1)} %collective-permute-done.2), channel_id=1, source_target_pairs={{0,1},{1,0},{2,3},{3,2},{4,5},{5,4},{6,7},{7,6},{8,9},{9,8},{10,11... | collective-permute-start | bytes 884744 | tf_op jit(solution)/shard_map/ppermute | solution.py:119
  66.6 11.7 %copy-start.5 = (bf16[2,16,1,32,384]{4,3,1,0,2:T(8,128)(2,1)}, bf16[2,16,1,32,384]{4,3,1,0,2:T(8,128)(2,1)S(1)}, u32[]{:S(2)}) copy-start(bf16[2,16,1,32,384]{4,3,1,0,2:T(8,128)(2,1)S(1)} %copy.43) | copy-start | bytes 2359300
  66.7 5.2 %copy-start.21 = (f32[9,384]{1,0:T(8,128)S(1)}, f32[9,384]{1,0:T(8,128)}, u32[]{:S(2)}) copy-start(f32[9,384]{1,0:T(8,128)} %slice_select_fusion) | copy-start | bytes 41476
  66.7 11.6 %collective-permute-start = (bf16[1,1,512,384]{3,2,1,0:T(8,128)(2,1)S(1)}, bf16[1,1,512,384]{3,2,1,0:T(8,128)(2,1)S(1)}, u32[]{:S(2)}, u32[]{:S(2)}) collective-permute-start(bf16[1,1,512,384]{3,2,1,0:T(8,128)(2,1)S(1)} %constant_dynamic-slice_fusion), channel_id=1, source_target_pairs={{0,16},{16,0},{1,17},{17,1},{2,18},{18,2},{3,19},{19,3},{4,20},{20... | collective-permute-start | bytes 1179656 | tf_op jit(solution)/shard_map/ppermute | solution.py:147
  86.2 10.8 %collective-permute-start.6 = (bf16[1,1,512,384]{3,2,1,0:T(8,128)(2,1)S(1)}, bf16[1,1,512,384]{3,2,1,0:T(8,128)(2,1)S(1)}, u32[]{:S(2)}, u32[]{:S(2)}) collective-permute-start(bf16[1,1,512,384]{3,2,1,0:T(8,128)(2,1)S(1)} %get-tuple-element.52), channel_id=1, source_target_pairs={{0,16},{16,0},{1,17},{17,1},{2,18},{18,2},{3,19},{19,3},{4,20},{20... | collective-permute-start | bytes 1179656 | tf_op jit(solution)/shard_map/ppermute | solution.py:154
  98.0 24.4 %all-to-all-start.2 = ((bf16[2,1,16,32,384]{4,3,0,1,2:T(8,128)(2,1)}), bf16[2,1,16,32,384]{4,3,0,1,2:T(8,128)(2,1)S(1)}, u32[]{:S(2)}, u32[]{:S(2)}) async-start(bf16[2,1,16,32,384]{4,3,0,1,2:T(8,128)(2,1)} %maximum_select_fusion), calls=%async_computation.2 | async-start | bytes 1572864 | tf_op jit(solution)/shard_map/all_to_all | solution.py:78
  125.0 24.2 %all-to-all-start.3 = ((bf16[2,16,1,32,384]{4,3,0,2,1:T(8,128)(2,1)}), bf16[2,16,1,32,384]{4,3,0,2,1:T(8,128)(2,1)S(1)}, u32[]{:S(2)}, u32[]{:S(2)}) async-start(bf16[2,16,1,32,384]{4,3,0,2,1:T(8,128)(2,1)} %fusion.63), calls=%async_computation.3 | async-start | bytes 1572864 | tf_op jit(solution)/shard_map/all_to_all | solution.py:82
  130.5 29.4 %collective-permute-start.7 = (bf16[1,1,512,384]{3,2,1,0:T(8,128)(2,1)S(1)}, bf16[1,1,512,384]{3,2,1,0:T(8,128)(2,1)}, u32[]{:S(2)}, u32[]{:S(2)}) collective-permute-start(bf16[1,1,512,384]{3,2,1,0:T(8,128)(2,1)S(1)} %get-tuple-element.53), channel_id=1, source_target_pairs={{0,16},{1,17},{2,18},{3,19},{4,20},{5,21},{6,22},{7,23},{8,24},{9,... | collective-permute-start | bytes 1179656 | tf_op jit(solution)/shard_map/ppermute | solution.py:164
  150.3 3.4 %copy-start.4 = (bf16[1,384,768]{2,1,0:T(8,128)(2,1)S(1)}, bf16[1,384,768]{2,1,0:T(8,128)(2,1)}, u32[]{:S(2)}) copy-start(bf16[1,384,768]{2,1,0:T(8,128)(2,1)} %param.13) | copy-start | bytes 1769476
  150.3 3.4 %copy-start.18 = (f32[2,384]{1,0:T(2,128)S(1)}, f32[2,384]{1,0:T(2,128)}, u32[]{:S(2)}) copy-start(f32[2,384]{1,0:T(2,128)} %copy-done.17) | copy-start | bytes 9220
  150.3 3.4 %copy-start.20 = (f32[2,384]{1,0:T(2,128)S(1)}, f32[2,384]{1,0:T(2,128)}, u32[]{:S(2)}) copy-start(f32[2,384]{1,0:T(2,128)} %copy-done.19) | copy-start | bytes 9220
  150.3 3.4 %copy-start.24 = (f32[384]{0:T(512)S(1)}, f32[384]{0:T(512)}, u32[]{:S(2)}) copy-start(f32[384]{0:T(512)} %copy-done.23) | copy-start | bytes 4612
  (47 other events, 61.6 us)

commit v15 on v13

--- a/solution.py
+++ b/solution.py
@@ -167,16 +167,16 @@
 
     to_second, to_first = [(0, 1)], [(1, 0)]
     sent_second_grad = lax.ppermute(second_grad, "section", perm=to_second)
+    early = lax.optimization_barrier(
+        (
+            jnp.where(first, lead_out[1:], tail_out[1:]),
+            jnp.where(first, first_grad, sent_second_grad),
+        )
+    )
     sent_second_act = lax.ppermute(tail_out[1:], "section", perm=to_second)
     sent_first_grad = lax.ppermute(first_grad, "section", perm=to_first)
-    activations = jnp.where(
-        first, lead_out, jnp.concatenate([sent_second_act, tail_out[1:]])
-    )
-    input_grads = jnp.where(
-        first,
-        jnp.concatenate([first_grad, sent_first_grad]),
-        jnp.concatenate([sent_second_grad, second_grad]),
-    )
+    activations = jnp.concatenate([jnp.where(first, lead_out[:1], sent_second_act), early[0]])
+    input_grads = jnp.concatenate([early[1], jnp.where(first, sent_first_grad, second_grad)])
     return (activations[None], input_grads[None])
 
 

time: 160 us -> 159 us (level)
  waiting for transfers between devices: 76.4 us -> 73.1 us
  local copies, waits for them, and re-layouts: 6.37 us -> 9.15 us
    select_n x2 -> x4, other arithmetic: 3.04 us -> 0.4 us  [the longest x1 0.22 us: on_device(): jnp.where(first, first_grad, sent_second_grad)]
    slice x0 -> x2, local copies, waits for them, and re-layouts: none -> 2.29 us  [the longest x1 1.32 us: on_device(): first_grad = spatial_backward(first_saved, tail_out[:1], *first_params)]
    unnamed x1 -> x3, other arithmetic: 0.02 us -> 1.96 us
    all_to_all x2, waiting for transfers between devices: 14.5 us -> 12.7 us  [temporal(): lax.all_to_all(banded, 'seq', split_axis=1, concat_axis=2, tiled=True)]
    ppermute x1, waiting for transfers between devices: 5.56 us -> 3.71 us  [on_device(): sent_first_grad = lax.ppermute(first_grad, 'section', perm=to_first)]
    ppermute x1, waiting for transfers between devices: 4.93 us -> 6.78 us  [on_device(): sent_second_act = lax.ppermute(tail_out[1:], 'section', perm=to_second)]
    unnamed x105 -> x113, local copies, waits for them, and re-layouts: 2.9 us -> 3.38 us
  transfers between devices with their start and end apart: 13 -> 13, of which waited for: 10 -> 10; matrix products, arithmetic and copies ran while one was open for 10% -> 12% of each run, Pallas kernels for 0% -> 0%
where the time goes in v15:
time: 159 us; the launch traced here: 158 us
  waiting for transfers between devices  73.1 us (46%)
  starting transfers between devices  38.3 us (24%)
  other arithmetic  25.5 us (16%)
  matrix products  10.5 us (7%)
  local copies, waits for them, and re-layouts  9.15 us (6%)
    all_to_all x2, waiting for transfers between devices, temporal(): lax.all_to_all(grouped, 'seq', split_axis=2, concat_axis=1, tiled=True)  29.8 us
    all_to_all x2, starting transfers between devices, temporal(): lax.all_to_all(grouped, 'seq', split_axis=2, concat_axis=1, tiled=True)  13.1 us
    all_to_all x2, waiting for transfers between devices, temporal(): lax.all_to_all(banded, 'seq', split_axis=1, concat_axis=2, tiled=True)  12.7 us
    ppermute x2, waiting for transfers between devices, fetch_halves(): got = lax.ppermute(mine, 'section', perm=swap)  12.3 us
    all_to_all x2, starting transfers between devices, temporal(): lax.all_to_all(banded, 'seq', split_axis=1, concat_axis=2, tiled=True)  11.1 us
    ppermute x1, waiting for transfers between devices, on_device(): sent_second_act = lax.ppermute(tail_out[1:], 'section', perm=to_second)  6.78 us
    select_n x5, other arithmetic, on_device(): jnp.where(first, o, r)  5.93 us
    ppermute x1, waiting for transfers between devices, on_device(): got = lax.ppermute(theirs, 'section', perm=swap)  5.53 us
  transfers between devices with their start and end apart: 13, of which 10 were waited for; matrix products, arithmetic and copies ran while one was open for 12% of the time, Pallas kernels for 0%

profile of v15, /device:TPU:0, one launch (start us, length us, event | category | flops | bytes accessed | tf_op | source)
XLA Modules:
  0.0 158.2 jit_solution(16130848970011561440)
XLA Ops:
  5.2 2.4 %multiply_convert_fusion = bf16[1024,768]{1,0:T(8,128)(2,1)} fusion(bf16[1024,384]{1,0:T(8,128)(2,1)S(1)} %bitcast.200, bf16[1,384,768]{2,1,0:T(8,128)(2,1)S(1)} %copy-done.8), kind=kOutput, calls=%fused_computation.16 | convolution fusion | flops 607911936 | bytes 2949120 | tf_op jit(solution)/shard_map/dot_general | solution.py:37
  7.6 2.4 %fusion.43 = bf16[2,1,512,384]{3,2,0,1:T(8,128)(2,1)S(1)} fusion(bf16[2,512,768]{2,1,0:T(8,128)(2,1)} %bitcast.212, bf16[2,1,512,384]{3,2,1,0:T(8,128)(2,1)S(1)} %copy-done.50, pred[]{:T(512)S(6)} %eq.9, bf16[1,768,384]{2,1,0:T(8,128)(2,1)S(1)} %copy-done.9, bf16[2,1,512,384]{3,2,1,0:T(8,128)(2,1)S(1)} %copy-done.2), kind=kOutput, calls=%fused_computation.76 | convolution fusion | flops 605552640 | bytes 4521985 | tf_op jit(solution)/shard_map/dot_general | solution.py:39
  11.0 7.4 %all-to-all-start = ((bf16[2,1,16,32,384]{4,3,0,1,2:T(8,128)(2,1)}), bf16[2,1,16,32,384]{4,3,0,1,2:T(8,128)(2,1)S(1)}, u32[]{:S(2)}, u32[]{:S(2)}) async-start(bf16[2,1,16,32,384]{4,3,0,1,2:T(8,128)(2,1)} %copy.20), calls=%async_computation | async-start | bytes 1572864 | tf_op jit(solution)/shard_map/all_to_all | solution.py:78
  20.1 2.4 %collective-permute-done.1 = f32[23,384]{1,0:T(8,128)S(1)} collective-permute-done((f32[23,384]{1,0:T(8,128)S(1)}, f32[23,384]{1,0:T(8,128)S(1)}, u32[]{:S(2)}, u32[]{:S(2)}) %collective-permute-start.1) | collective-permute-done | bytes 35360 | tf_op jit(solution)/shard_map/ppermute | solution.py:123
  23.2 13.9 %all-to-all-done = bf16[2,1,16,32,384]{4,3,0,1,2:T(8,128)(2,1)S(1)} async-done(((bf16[2,1,16,32,384]{4,3,0,1,2:T(8,128)(2,1)}), bf16[2,1,16,32,384]{4,3,0,1,2:T(8,128)(2,1)S(1)}, u32[]{:S(2)}, u32[]{:S(2)}) %all-to-all-start) | async-done | bytes 786464 | tf_op jit(solution)/shard_map/all_to_all | solution.py:78
  37.3 1.8 %fusion.65 = bf16[2,16,1,32,384]{4,3,0,2,1:T(8,128)(2,1)} fusion(f32[2,16,32,384]{3,2,0,1:T(8,128)S(1)} %bitcast_convert_fusion.1, f32[384]{0:T(512)S(1)} %get-tuple-element.51, f32[384]{0:T(512)S(1)} %get-tuple-element.52, f32[384]{0:T(512)S(1)} %get-tuple-element.53, f32[384]{0:T(512)S(1)} %get-tuple-element.54, f32[384]{0:T(512)S(1)} %get-tuple-element.55, ...), kind=kLoop, calls=%fused_computation.142 | loop fusion | flops 7471104 | bytes 2373120 | tf_op jit(solution)/shard_map/reshape | solution.py:81
  39.2 5.6 %all-to-all-start.1 = ((bf16[2,16,1,32,384]{4,3,0,2,1:T(8,128)(2,1)}), bf16[2,16,1,32,384]{4,3,0,2,1:T(8,128)(2,1)S(1)}, u32[]{:S(2)}, u32[]{:S(2)}) async-start(bf16[2,16,1,32,384]{4,3,0,2,1:T(8,128)(2,1)} %fusion.65), calls=%async_computation.1 | async-start | bytes 1572864 | tf_op jit(solution)/shard_map/all_to_all | solution.py:82
  44.8 1.6 collective-permute-start.2
  47.7 7.1 %collective-permute-done.2 = bf16[192,768]{1,0:T(8,128)(2,1)S(1)} collective-permute-done((bf16[192,768]{1,0:T(8,128)(2,1)S(1)}, bf16[192,768]{1,0:T(8,128)(2,1)S(1)}, u32[]{:S(2)}, u32[]{:S(2)}) %collective-permute-start.2) | collective-permute-done | bytes 294944 | tf_op jit(solution)/shard_map/ppermute | solution.py:118
  55.4 5.2 %collective-permute-done.4 = bf16[384,384]{1,0:T(8,128)(2,1)} collective-permute-done((bf16[384,384]{1,0:T(8,128)(2,1)S(1)}, bf16[384,384]{1,0:T(8,128)(2,1)}, u32[]{:S(2)}, u32[]{:S(2)}) %collective-permute-start.4) | collective-permute-done | bytes 294944 | tf_op jit(solution)/shard_map/ppermute | solution.py:118
  60.6 2.9 %all-to-all-done.1 = bf16[2,16,1,32,384]{4,3,0,2,1:T(8,128)(2,1)S(1)} async-done(((bf16[2,16,1,32,384]{4,3,0,2,1:T(8,128)(2,1)}), bf16[2,16,1,32,384]{4,3,0,2,1:T(8,128)(2,1)S(1)}, u32[]{:S(2)}, u32[]{:S(2)}) %all-to-all-start.1) | async-done | bytes 786464 | tf_op jit(solution)/shard_map/all_to_all | solution.py:82
  66.7 2.5 %bitcast_select_fusion.1 = (bf16[768,384]{1,0:T(8,128)(2,1)}, bf16[768,384]{1,0:T(8,128)(2,1)}) fusion(bf16[1,768,384]{2,1,0:T(8,128)(2,1)S(1)} %copy-done.9, pred[]{:T(512)S(6)} %eq.9, bf16[384,384]{1,0:T(8,128)(2,1)} %collective-permute-done.4, bf16[384,384]{1,0:T(8,128)(2,1)} %collective-permute-done.5, pred[]{:T(512)S(6)} %eq.10), kind=kLoop, calls=%fused_computation.147 | loop fusion | flops 3244032 | bytes 2359298 | tf_op jit(solution)/shard_map/jit(_where)/select_n | solution.py:134
  69.5 5.5 %collective-permute-done = bf16[1,1,512,384]{3,2,1,0:T(8,128)(2,1)S(1)} collective-permute-done((bf16[1,1,512,384]{3,2,1,0:T(8,128)(2,1)S(1)}, bf16[1,1,512,384]{3,2,1,0:T(8,128)(2,1)S(1)}, u32[]{:S(2)}, u32[]{:S(2)}) %collective-permute-start) | collective-permute-done | bytes 393248 | tf_op jit(solution)/shard_map/ppermute | solution.py:153
  85.4 5.7 %all-to-all-start.2 = ((bf16[2,1,16,32,384]{4,3,0,1,2:T(8,128)(2,1)}), bf16[2,1,16,32,384]{4,3,0,1,2:T(8,128)(2,1)S(1)}, u32[]{:S(2)}, u32[]{:S(2)}) async-start(bf16[2,1,16,32,384]{4,3,0,1,2:T(8,128)(2,1)} %copy.23), calls=%async_computation.2 | async-start | bytes 1572864 | tf_op jit(solution)/shard_map/all_to_all | solution.py:78
  93.9 15.9 %all-to-all-done.2 = bf16[2,1,16,32,384]{4,3,0,1,2:T(8,128)(2,1)S(1)} async-done(((bf16[2,1,16,32,384]{4,3,0,1,2:T(8,128)(2,1)}), bf16[2,1,16,32,384]{4,3,0,1,2:T(8,128)(2,1)S(1)}, u32[]{:S(2)}, u32[]{:S(2)}) %all-to-all-start.2) | async-done | bytes 786464 | tf_op jit(solution)/shard_map/all_to_all | solution.py:78
  109.9 2.4 %fusion.64 = bf16[2,16,1,32,384]{4,3,0,2,1:T(8,128)(2,1)} fusion(f32[2,16,32,384]{3,2,0,1:T(8,128)S(1)} %bitcast_convert_fusion, f32[2,384]{1,0:T(2,128)S(1)} %bitcast.203, f32[2,384]{1,0:T(2,128)S(1)} %bitcast.204, f32[2,384]{1,0:T(2,128)S(1)} %bitcast.205, f32[2,384]{1,0:T(2,128)S(1)} %bitcast.206, f32[2,384]{1,0:T(2,128)S(1)} %bitcast.207, ...), kind=kLoop, calls=%fused_computation.141 | loop fusion | flops 7471104 | bytes 2386944 | tf_op jit(solution)/shard_map/reshape | solution.py:81
  112.3 5.5 %all-to-all-start.3 = ((bf16[2,16,1,32,384]{4,3,0,2,1:T(8,128)(2,1)}), bf16[2,16,1,32,384]{4,3,0,2,1:T(8,128)(2,1)}, u32[]{:S(2)}, u32[]{:S(2)}) async-start(bf16[2,16,1,32,384]{4,3,0,2,1:T(8,128)(2,1)} %fusion.64), calls=%async_computation.3 | async-start | bytes 1572864 | tf_op jit(solution)/shard_map/all_to_all | solution.py:82
  117.8 1.8 %multiply_reduce_fusion.2 = (f32[32,16]{1,0:T(8,128)S(1)}, f32[1,1,32,16,384]{4,3,2,1,0:T(8,128)S(1)}) fusion(f32[384]{0:T(512)S(1)} %get-tuple-element.69, f32[384]{0:T(512)S(1)} %get-tuple-element.68, f32[1,1,32,16,384]{4,3,2,1,0:T(8,128)} %get-tuple-element.93, f32[384]{0:T(512)S(1)} %get-tuple-element.35, ...), kind=kLoop, calls=%fused_computation.130 | loop fusion | flops 2162176 | bytes 3155456 | tf_op jit(solution)/shard_map/reduce_sum | solution.py:35
  119.9 1.7 %fusion.84 = f32[512,768]{1,0:T(8,128)} fusion(bf16[512,384]{1,0:T(8,128)(2,1)S(1)} %multiply_convert_fusion.4, bf16[384,768]{1,0:T(8,128)(2,1)S(1)} %get-tuple-element.23), kind=kOutput, calls=%fused_computation.255 | convolution fusion | flops 301989888 | bytes 2555904 | tf_op jit(solution)/shard_map/dot_general | solution.py:37
  122.6 4.2 %collective-permute-start.7 = (bf16[1,1,512,384]{3,2,1,0:T(8,128)(2,1)S(1)}, bf16[1,1,512,384]{3,2,1,0:T(8,128)(2,1)}, u32[]{:S(2)}, u32[]{:S(2)}) collective-permute-start(bf16[1,1,512,384]{3,2,1,0:T(8,128)(2,1)S(1)} %fusion.61), channel_id=1, source_target_pairs={{0,16},{1,17},{2,18},{3,19},{4,20},{5,21},{6,22},{7,23},{8,24},{9,... | collective-permute-start | bytes 1179656 | tf_op jit(solution)/shard_map/ppermute | solution.py:169
  126.8 9.8 %all-to-all-done.3 = bf16[2,16,1,32,384]{4,3,0,2,1:T(8,128)(2,1)} async-done(((bf16[2,16,1,32,384]{4,3,0,2,1:T(8,128)(2,1)}), bf16[2,16,1,32,384]{4,3,0,2,1:T(8,128)(2,1)}, u32[]{:S(2)}, u32[]{:S(2)}) %all-to-all-start.3) | async-done | bytes 786464 | tf_op jit(solution)/shard_map/all_to_all | solution.py:82
  140.2 3.4 %collective-permute-start.6 = (bf16[1,1,512,384]{3,2,1,0:T(8,128)(2,1)S(1)}, bf16[1,1,512,384]{3,2,1,0:T(8,128)(2,1)S(1)}, u32[]{:S(2)}, u32[]{:S(2)}) collective-permute-start(bf16[1,1,512,384]{3,2,1,0:T(8,128)(2,1)S(1)} %bitcast.195), channel_id=1, source_target_pairs={{0,16},{1,17},{2,18},{3,19},{4,20},{5,21},{6,22},{7,23},{8,24},{9,... | collective-permute-start | bytes 1179656 | tf_op jit(solution)/shard_map/ppermute | solution.py:176
  145.6 6.8 %collective-permute-done.6 = bf16[1,1,512,384]{3,2,1,0:T(8,128)(2,1)S(1)} collective-permute-done((bf16[1,1,512,384]{3,2,1,0:T(8,128)(2,1)S(1)}, bf16[1,1,512,384]{3,2,1,0:T(8,128)(2,1)S(1)}, u32[]{:S(2)}, u32[]{:S(2)}) %collective-permute-start.6) | collective-permute-done | bytes 393248 | tf_op jit(solution)/shard_map/ppermute | solution.py:176
  153.4 3.7 %collective-permute-done.8 = bf16[1,1,512,384]{3,2,1,0:T(8,128)(2,1)S(1)} collective-permute-done((bf16[1,1,512,384]{3,2,1,0:T(8,128)(2,1)S(1)}, bf16[1,1,512,384]{3,2,1,0:T(8,128)(2,1)S(1)}, u32[]{:S(2)}, u32[]{:S(2)}) %collective-permute-start.8) | collective-permute-done | bytes 393248 | tf_op jit(solution)/shard_map/ppermute | solution.py:177
  (193 shorter events, 35.1 us)
Async XLA Ops:
  10.0 8.4 %copy-start.19 = (f32[1,2,2,384]{3,2,1,0:T(2,128)S(1)}, f32[1,2,2,384]{3,2,1,0:T(2,128)}, u32[]{:S(2)}) copy-start(f32[1,2,2,384]{3,2,1,0:T(2,128)} %param.11) | copy-start | bytes 18436
  10.0 8.5 %copy-start.18 = (f32[1,9,384]{2,0,1:T(1,128)S(1)}, f32[1,9,384]{2,0,1:T(1,128)}, u32[]{:S(2)}) copy-start(f32[1,9,384]{2,0,1:T(1,128)} %param.15) | copy-start | bytes 41476
  10.0 8.5 %copy-start.49 = (f32[1,384]{1,0:T(1,128)S(1)}, f32[1,384]{1,0:T(1,128)}, u32[]{:S(2)}) copy-start(f32[1,384]{1,0:T(1,128)} %param.12) | copy-start | bytes 4612
  11.0 26.1 %all-to-all-start = ((bf16[2,1,16,32,384]{4,3,0,1,2:T(8,128)(2,1)}), bf16[2,1,16,32,384]{4,3,0,1,2:T(8,128)(2,1)S(1)}, u32[]{:S(2)}, u32[]{:S(2)}) async-start(bf16[2,1,16,32,384]{4,3,0,1,2:T(8,128)(2,1)} %copy.20), calls=%async_computation | async-start | bytes 1572864 | tf_op jit(solution)/shard_map/all_to_all | solution.py:78
  18.5 4.0 %collective-permute-start.1 = (f32[23,384]{1,0:T(8,128)S(1)}, f32[23,384]{1,0:T(8,128)S(1)}, u32[]{:S(2)}, u32[]{:S(2)}) collective-permute-start(f32[23,384]{1,0:T(8,128)S(1)} %pad_maximum_fusion.1), channel_id=1, source_target_pairs={{0,16},{16,0},{1,17},{17,1},{2,18},{18,2},{3,19},{19,3},{4,20},{20... | collective-permute-start | bytes 105992 | tf_op jit(solution)/shard_map/ppermute | solution.py:123
  39.2 15.6 %copy-start.38 = (f32[384]{0:T(512)S(1)}, f32[384]{0:T(512)}, u32[]{:S(2)}) copy-start(f32[384]{0:T(512)} %copy-done.37) | copy-start | bytes 4612
  39.2 24.3 %all-to-all-start.1 = ((bf16[2,16,1,32,384]{4,3,0,2,1:T(8,128)(2,1)}), bf16[2,16,1,32,384]{4,3,0,2,1:T(8,128)(2,1)S(1)}, u32[]{:S(2)}, u32[]{:S(2)}) async-start(bf16[2,16,1,32,384]{4,3,0,2,1:T(8,128)(2,1)} %fusion.65), calls=%async_computation.1 | async-start | bytes 1572864 | tf_op jit(solution)/shard_map/all_to_all | solution.py:82
  44.8 9.9 %collective-permute-start.2 = (bf16[192,768]{1,0:T(8,128)(2,1)S(1)}, bf16[192,768]{1,0:T(8,128)(2,1)S(1)}, u32[]{:S(2)}, u32[]{:S(2)}) collective-permute-start(bf16[192,768]{1,0:T(8,128)(2,1)S(1)} %dynamic-slice_bitcast_fusion.1), channel_id=1, source_target_pairs={{0,16},{16,0},{1,17},{17,1},{2,18},{18,2},{3,19},{19,3},{4,20},{20... | collective-permute-start | bytes 884744 | tf_op jit(solution)/shard_map/ppermute | solution.py:118
  46.4 14.2 %collective-permute-start.4 = (bf16[384,384]{1,0:T(8,128)(2,1)S(1)}, bf16[384,384]{1,0:T(8,128)(2,1)}, u32[]{:S(2)}, u32[]{:S(2)}) collective-permute-start(bf16[384,384]{1,0:T(8,128)(2,1)S(1)} %dynamic-slice_bitcast_fusion), channel_id=1, source_target_pairs={{0,16},{16,0},{1,17},{17,1},{2,18},{18,2},{3,19},{19,3},{4,20},{20... | collective-permute-start | bytes 884744 | tf_op jit(solution)/shard_map/ppermute | solution.py:118
  54.7 10.5 %copy-start.12 = (bf16[192,768]{1,0:T(8,128)(2,1)}, bf16[192,768]{1,0:T(8,128)(2,1)S(1)}, u32[]{:S(2)}) copy-start(bf16[192,768]{1,0:T(8,128)(2,1)S(1)} %collective-permute-done.2) | copy-start | bytes 884740
  54.7 10.5 %collective-permute-start.3 = (bf16[192,768]{1,0:T(8,128)(2,1)S(1)}, bf16[192,768]{1,0:T(8,128)(2,1)}, u32[]{:S(2)}, u32[]{:S(2)}) collective-permute-start(bf16[192,768]{1,0:T(8,128)(2,1)S(1)} %collective-permute-done.2), channel_id=1, source_target_pairs={{0,1},{1,0},{2,3},{3,2},{4,5},{5,4},{6,7},{7,6},{8,9},{9,8},{10,11... | collective-permute-start | bytes 884744 | tf_op jit(solution)/shard_map/ppermute | solution.py:119
  60.6 6.1 %collective-permute-start.5 = (bf16[384,384]{1,0:T(8,128)(2,1)}, bf16[384,384]{1,0:T(8,128)(2,1)}, u32[]{:S(2)}, u32[]{:S(2)}) collective-permute-start(bf16[384,384]{1,0:T(8,128)(2,1)} %collective-permute-done.4), channel_id=1, source_target_pairs={{0,1},{1,0},{2,3},{3,2},{4,5},{5,4},{6,7},{7,6},{8,9},{9,8},{10,11... | collective-permute-start | bytes 884744 | tf_op jit(solution)/shard_map/ppermute | solution.py:119
  63.6 11.4 %copy-start = (bf16[2,16,1,32,384]{4,3,1,0,2:T(8,128)(2,1)}, bf16[2,16,1,32,384]{4,3,1,0,2:T(8,128)(2,1)S(1)}, u32[]{:S(2)}) copy-start(bf16[2,16,1,32,384]{4,3,1,0,2:T(8,128)(2,1)S(1)} %copy.22) | copy-start | bytes 2359300
  63.6 11.3 %collective-permute-start = (bf16[1,1,512,384]{3,2,1,0:T(8,128)(2,1)S(1)}, bf16[1,1,512,384]{3,2,1,0:T(8,128)(2,1)S(1)}, u32[]{:S(2)}, u32[]{:S(2)}) collective-permute-start(bf16[1,1,512,384]{3,2,1,0:T(8,128)(2,1)S(1)} %constant_dynamic-slice_fusion.5), channel_id=1, source_target_pairs={{0,16},{16,0},{1,17},{17,1},{2,18},{18,2},{3,19},{19,3},{4,20},{20... | collective-permute-start | bytes 1179656 | tf_op jit(solution)/shard_map/ppermute | solution.py:153
  85.4 6.9 %copy-start.14 = (f32[1,9,384]{2,1,0:T(8,128)S(1)}, f32[1,9,384]{2,1,0:T(8,128)}, u32[]{:S(2)}) copy-start(f32[1,9,384]{2,1,0:T(8,128)} %get-tuple-element.111) | copy-start | bytes 41476
  85.4 7.0 %copy-start.47 = (f32[2,2,384]{2,1,0:T(2,128)S(1)}, f32[2,2,384]{2,1,0:T(2,128)}, u32[]{:S(2)}) copy-start(f32[2,2,384]{2,1,0:T(2,128)} %get-tuple-element.20) | copy-start | bytes 18436
  85.4 7.0 %copy-start.16 = (f32[9,384]{1,0:T(8,128)S(1)}, f32[9,384]{1,0:T(8,128)}, u32[]{:S(2)}) copy-start(f32[9,384]{1,0:T(8,128)} %get-tuple-element.19) | copy-start | bytes 41476
  85.4 24.4 %all-to-all-start.2 = ((bf16[2,1,16,32,384]{4,3,0,1,2:T(8,128)(2,1)}), bf16[2,1,16,32,384]{4,3,0,1,2:T(8,128)(2,1)S(1)}, u32[]{:S(2)}, u32[]{:S(2)}) async-start(bf16[2,1,16,32,384]{4,3,0,1,2:T(8,128)(2,1)} %copy.23), calls=%async_computation.2 | async-start | bytes 1572864 | tf_op jit(solution)/shard_map/all_to_all | solution.py:78
  112.3 24.3 %all-to-all-start.3 = ((bf16[2,16,1,32,384]{4,3,0,2,1:T(8,128)(2,1)}), bf16[2,16,1,32,384]{4,3,0,2,1:T(8,128)(2,1)}, u32[]{:S(2)}, u32[]{:S(2)}) async-start(bf16[2,16,1,32,384]{4,3,0,2,1:T(8,128)(2,1)} %fusion.64), calls=%async_computation.3 | async-start | bytes 1572864 | tf_op jit(solution)/shard_map/all_to_all | solution.py:82
  121.7 16.3 %copy-start.10 = (bf16[768,384]{1,0:T(8,128)(2,1)S(1)}, bf16[768,384]{1,0:T(8,128)(2,1)}, u32[]{:S(2)}) copy-start(bf16[768,384]{1,0:T(8,128)(2,1)} %get-tuple-element.21) | copy-start | bytes 1769476
  122.6 21.4 %collective-permute-start.7 = (bf16[1,1,512,384]{3,2,1,0:T(8,128)(2,1)S(1)}, bf16[1,1,512,384]{3,2,1,0:T(8,128)(2,1)}, u32[]{:S(2)}, u32[]{:S(2)}) collective-permute-start(bf16[1,1,512,384]{3,2,1,0:T(8,128)(2,1)S(1)} %fusion.61), channel_id=1, source_target_pairs={{0,16},{1,17},{2,18},{3,19},{4,20},{5,21},{6,22},{7,23},{8,24},{9,... | collective-permute-start | bytes 1179656 | tf_op jit(solution)/shard_map/ppermute | solution.py:169
  140.2 12.2 %collective-permute-start.6 = (bf16[1,1,512,384]{3,2,1,0:T(8,128)(2,1)S(1)}, bf16[1,1,512,384]{3,2,1,0:T(8,128)(2,1)S(1)}, u32[]{:S(2)}, u32[]{:S(2)}) collective-permute-start(bf16[1,1,512,384]{3,2,1,0:T(8,128)(2,1)S(1)} %bitcast.195), channel_id=1, source_target_pairs={{0,16},{1,17},{2,18},{3,19},{4,20},{5,21},{6,22},{7,23},{8,24},{9,... | collective-permute-start | bytes 1179656 | tf_op jit(solution)/shard_map/ppermute | solution.py:176
  144.0 8.4 %copy-start.6 = (bf16[1,16,1,32,384]{4,3,0,2,1:T(8,128)(2,1)S(1)}, bf16[1,16,1,32,384]{4,3,0,2,1:T(8,128)(2,1)}, u32[]{:S(2)}) copy-start(bf16[1,16,1,32,384]{4,3,0,2,1:T(8,128)(2,1)} %get-tuple-element.86) | copy-start | bytes 1179652
  144.3 12.9 %collective-permute-start.8 = (bf16[1,1,512,384]{3,2,1,0:T(8,128)(2,1)S(1)}, bf16[1,1,512,384]{3,2,1,0:T(8,128)(2,1)S(1)}, u32[]{:S(2)}, u32[]{:S(2)}) collective-permute-start(bf16[1,1,512,384]{3,2,1,0:T(8,128)(2,1)S(1)} %get-tuple-element.73), channel_id=1, source_target_pairs={{16,0},{17,1},{18,2},{19,3},{20,4},{21,5},{22,6},{23,7},{24,8},{25... | collective-permute-start | bytes 1179656 | tf_op jit(solution)/shard_map/ppermute | solution.py:177
  (40 other events, 112.9 us)

commit v16 on v14

--- a/solution.py
+++ b/solution.py
@@ -99,6 +99,19 @@
     return jnp.moveaxis(back, 2, 0)
 
 
+def temporal_cross(values, tap_table):
+    piece_count, frame_count, pixel_count, channels = values.shape
+    groups = lax.axis_size("seq")
+    grouped = values.reshape(piece_count, frame_count, groups, pixel_count // groups, channels)
+    pixel_view = lax.all_to_all(grouped, "seq", split_axis=2, concat_axis=1, tiled=True)
+    pixel_view = pixel_view.reshape(piece_count, groups * frame_count, pixel_count // groups, channels)
+    banded = band_frames(pixel_view, tap_table)
+    banded = banded.reshape(1, piece_count * groups * frame_count, 1, pixel_count // groups, channels)
+    back = lax.all_to_all(banded, ("section", "seq"), split_axis=1, concat_axis=2, tiled=True)
+    back = back.reshape(frame_count, piece_count, pixel_count, channels)
+    return jnp.moveaxis(back, 1, 0)
+
+
 def on_device(clips, cotangent, spatial_taps, modulation, norm_gain, w_in, w_out, band_taps):
     plane = lax.axis_index("section")
     first = plane == 0
@@ -119,7 +132,7 @@
         other = lax.ppermute(got, "seq", perm=siblings)
         return jnp.where(core == 0, jnp.concatenate([got, other]), jnp.concatenate([other, got]))
 
-    small = jnp.concatenate([taps, mod.reshape(-1, channels), gain[None]])
+    small = jnp.concatenate([taps, mod.reshape(-1, channels), gain[None], band])
     got_small = lax.ppermute(small, "section", perm=swap)
     mod_rows = mod.shape[0] * mod.shape[1]
     other = (
@@ -129,9 +142,12 @@
         fetch_halves(weight_in),
         fetch_halves(weight_out),
     )
+    other_band = got_small[tap_count + mod_rows + 1 :]
     second_seg = lax.optimization_barrier(
         tuple(jnp.where(first, r, o) for o, r in zip(own, other))
     )
+    first_band = jnp.where(first, band, other_band)
+    second_band = jnp.where(first, other_band, band)
 
     def for_clip(params, clip):
         clip_mod = lax.dynamic_index_in_dim(params[1], clip, 0, keepdims=True)
@@ -151,14 +167,9 @@
     second_mixed, second_saved = spatial_forward(clip_act, *second_params)
     second_grad = spatial_backward(second_saved, clip_seed, *second_params)
 
-    got_tail = lax.ppermute(jnp.where(first, second_mixed, second_grad), "section", perm=swap)
-    tail_in = jnp.where(
-        first,
-        jnp.concatenate([second_grad, got_tail]),
-        jnp.concatenate([got_tail, second_mixed]),
+    tail_out = temporal_cross(
+        jnp.concatenate([second_grad, second_mixed]), jnp.stack([first_band[::-1], second_band])
     )
-    tail_taps = jnp.where(first, band[::-1], band)
-    tail_out = temporal(tail_in, tail_taps[None])
     first_grad = spatial_backward(first_saved, tail_out, *own)
 
     sent_second_grad = lax.ppermute(second_grad, "section", perm=[(0, 1)])

time: 164 us -> 155 us (0.945)
  waiting for transfers between devices: 70.7 us -> 57.7 us
    all_to_all x0 -> x2, waiting for transfers between devices: none -> 29.2 us  [the longest x1 17.1 us: temporal_cross(): lax.all_to_all(banded, ('section', 'seq'), split_axis=1, concat_axis=2, t...]
    all_to_all x2 -> x1, waiting for transfers between devices: 31.2 us -> 8.36 us  [temporal(): lax.all_to_all(grouped, 'seq', split_axis=2, concat_axis=1, tiled=True)]
    all_to_all x2 -> x1, waiting for transfers between devices: 15.4 us -> 2.95 us  [temporal(): lax.all_to_all(banded, 'seq', split_axis=1, concat_axis=2, tiled=True)]
    all_to_all x0 -> x2, starting transfers between devices: none -> 10.9 us  [the longest x1 5.53 us: temporal_cross(): lax.all_to_all(grouped, 'seq', split_axis=2, concat_axis=1, tiled=True)]
    ppermute x1 -> x0, waiting for transfers between devices: 10.2 us -> none  [on_device(): lax.ppermute(jnp.where(first, second_mixed, second_grad), 'section', perm...]
    all_to_all x2 -> x1, starting transfers between devices: 13.1 us -> 7.38 us  [temporal(): lax.all_to_all(grouped, 'seq', split_axis=2, concat_axis=1, tiled=True)]
    all_to_all x2 -> x1, starting transfers between devices: 11 us -> 5.66 us  [temporal(): lax.all_to_all(banded, 'seq', split_axis=1, concat_axis=2, tiled=True)]
    ppermute x2, waiting for transfers between devices: 7.54 us -> 11.5 us  [fetch_halves(): got = lax.ppermute(mine, 'section', perm=swap)]
  transfers between devices with their start and end apart: 12 -> 11, of which waited for: 7 -> 8; matrix products, arithmetic and copies ran while one was open for 19% -> 21% of each run, Pallas kernels for 0% -> 0%
where the time goes in v16:
time: 155 us; the launch traced here: 153 us
  waiting for transfers between devices  57.7 us (37%)
  starting transfers between devices  33.6 us (22%)
  other arithmetic  27.8 us (18%)
  local copies, waits for them, and re-layouts  20 us (13%)
  matrix products  12.1 us (8%)
  between operations  1.69 us (1%)
    all_to_all x1, waiting for transfers between devices, temporal_cross(): lax.all_to_all(banded, ('section', 'seq'), split_axis=1, concat_axis=2, t...  17.1 us
    all_to_all x1, waiting for transfers between devices, temporal_cross(): lax.all_to_all(grouped, 'seq', split_axis=2, concat_axis=1, tiled=True)  12.2 us
    ppermute x2, waiting for transfers between devices, fetch_halves(): got = lax.ppermute(mine, 'section', perm=swap)  11.5 us
    all_to_all x1, waiting for transfers between devices, temporal(): lax.all_to_all(grouped, 'seq', split_axis=2, concat_axis=1, tiled=True)  8.36 us
    all_to_all x1, starting transfers between devices, temporal(): lax.all_to_all(grouped, 'seq', split_axis=2, concat_axis=1, tiled=True)  7.38 us
    unnamed x159, local copies, waits for them, and re-layouts  6.85 us
    all_to_all x1, starting transfers between devices, temporal(): lax.all_to_all(banded, 'seq', split_axis=1, concat_axis=2, tiled=True)  5.66 us
    all_to_all x1, starting transfers between devices, temporal_cross(): lax.all_to_all(grouped, 'seq', split_axis=2, concat_axis=1, tiled=True)  5.53 us
  transfers between devices with their start and end apart: 11, of which 8 were waited for; matrix products, arithmetic and copies ran while one was open for 21% of the time, Pallas kernels for 0%

profile of v16, /device:TPU:0, one launch (start us, length us, event | category | flops | bytes accessed | tf_op | source)
XLA Modules:
  0.0 152.9 jit_solution(16812609872882320519)
XLA Ops:
  6.2 2.8 %multiply_convert_fusion.1 = (bf16[1024,768]{1,0:T(8,128)(2,1)S(1)}, f32[1024,768]{1,0:T(8,128)}) fusion(bf16[1024,384]{1,0:T(8,128)(2,1)S(1)} %bitcast.185, bf16[1,384,768]{2,1,0:T(8,128)(2,1)S(1)} %copy-done.3), kind=kOutput, calls=%fused_computation.17 | convolution fusion | flops 607911936 | bytes 6094848 | tf_op jit(solution)/shard_map/dot_general | solution.py:37
  11.1 7.4 %all-to-all-start = ((bf16[2,1,16,32,384]{4,3,0,1,2:T(8,128)(2,1)}), bf16[2,1,16,32,384]{4,3,0,1,2:T(8,128)(2,1)S(1)}, u32[]{:S(2)}, u32[]{:S(2)}) async-start(bf16[2,1,16,32,384]{4,3,0,1,2:T(8,128)(2,1)} %copy.23), calls=%async_computation | async-start | bytes 1572864 | tf_op jit(solution)/shard_map/all_to_all | solution.py:78
  23.9 2.0 %rev.8 = f32[9,384]{1,0:T(8,128)} reverse(f32[9,384]{1,0:T(8,128)} %copy-done.9), dimensions={0} | reverse | bytes 27648 | tf_op jit(solution)/shard_map/rev | solution.py:158
  28.8 8.4 %all-to-all-done = bf16[2,1,16,32,384]{4,3,0,1,2:T(8,128)(2,1)S(1)} async-done(((bf16[2,1,16,32,384]{4,3,0,1,2:T(8,128)(2,1)}), bf16[2,1,16,32,384]{4,3,0,1,2:T(8,128)(2,1)S(1)}, u32[]{:S(2)}, u32[]{:S(2)}) %all-to-all-start) | async-done | bytes 786464 | tf_op jit(solution)/shard_map/all_to_all | solution.py:78
  37.9 1.8 %fusion.63 = bf16[2,16,1,32,384]{4,3,0,2,1:T(8,128)(2,1)} fusion(f32[2,16,32,384]{3,2,0,1:T(8,128)S(1)} %bitcast_convert_fusion.1, f32[384]{0:T(512)S(1)} %get-tuple-element.22, f32[384]{0:T(512)S(1)} %get-tuple-element.23, f32[384]{0:T(512)S(1)} %get-tuple-element.24, f32[384]{0:T(512)S(1)} %copy-done.67, f32[384]{0:T(512)S(1)} %copy-done.68, ...), kind=kLoop, calls=%fused_computation.133 | loop fusion | flops 7471104 | bytes 2373120 | tf_op jit(solution)/shard_map/reshape | solution.py:81
  39.7 5.7 %all-to-all-start.1 = ((bf16[2,16,1,32,384]{4,3,0,2,1:T(8,128)(2,1)}), bf16[2,16,1,32,384]{4,3,0,2,1:T(8,128)(2,1)}, u32[]{:S(2)}, u32[]{:S(2)}) async-start(bf16[2,16,1,32,384]{4,3,0,2,1:T(8,128)(2,1)} %fusion.63), calls=%async_computation.1 | async-start | bytes 1572864 | tf_op jit(solution)/shard_map/all_to_all | solution.py:82
  45.4 1.6 %collective-permute-start.4 = (bf16[384,384]{1,0:T(8,128)(2,1)S(1)}, bf16[384,384]{1,0:T(8,128)(2,1)}, u32[]{:S(2)}, u32[]{:S(2)}) collective-permute-start(bf16[384,384]{1,0:T(8,128)(2,1)S(1)} %dynamic-slice_bitcast_fusion), channel_id=1, source_target_pairs={{0,16},{16,0},{1,17},{17,1},{2,18},{18,2},{3,19},{19,3},{4,20},{20... | collective-permute-start | bytes 884744 | tf_op jit(solution)/shard_map/ppermute | solution.py:131
  49.1 6.3 %collective-permute-done.4 = bf16[384,384]{1,0:T(8,128)(2,1)} collective-permute-done((bf16[384,384]{1,0:T(8,128)(2,1)S(1)}, bf16[384,384]{1,0:T(8,128)(2,1)}, u32[]{:S(2)}, u32[]{:S(2)}) %collective-permute-start.4) | collective-permute-done | bytes 294944 | tf_op jit(solution)/shard_map/ppermute | solution.py:131
  56.0 5.2 %collective-permute-done.2 = bf16[192,768]{1,0:T(8,128)(2,1)} collective-permute-done((bf16[192,768]{1,0:T(8,128)(2,1)S(1)}, bf16[192,768]{1,0:T(8,128)(2,1)}, u32[]{:S(2)}, u32[]{:S(2)}) %collective-permute-start.2) | collective-permute-done | bytes 294944 | tf_op jit(solution)/shard_map/ppermute | solution.py:131
  61.2 3.0 %all-to-all-done.1 = bf16[2,16,1,32,384]{4,3,0,2,1:T(8,128)(2,1)} async-done(((bf16[2,16,1,32,384]{4,3,0,2,1:T(8,128)(2,1)}), bf16[2,16,1,32,384]{4,3,0,2,1:T(8,128)(2,1)}, u32[]{:S(2)}, u32[]{:S(2)}) %all-to-all-start.1) | async-done | bytes 786464 | tf_op jit(solution)/shard_map/all_to_all | solution.py:82
  67.0 2.5 %fusion.65 = bf16[768,384]{1,0:T(8,128)(2,1)} fusion(bf16[384,384]{1,0:T(8,128)(2,1)} %collective-permute-done.5, bf16[384,384]{1,0:T(8,128)(2,1)} %collective-permute-done.4, bf16[1,768,384]{2,1,0:T(8,128)(2,1)} %param.14, pred[]{:T(512)S(6)} %eq.10, pred[]{:T(512)S(6)} %eq.9), kind=kLoop, calls=%fused_computation.137 | loop fusion | flops 2949120 | bytes 1769474 | tf_op jit(solution)/shard_map/jit(_where)/select_n | solution.py:147
  69.4 2.3 %fusion.64 = bf16[384,768]{1,0:T(8,128)(2,1)} fusion(bf16[192,768]{1,0:T(8,128)(2,1)} %collective-permute-done.3, bf16[192,768]{1,0:T(8,128)(2,1)} %collective-permute-done.2, bf16[1,384,768]{2,1,0:T(8,128)(2,1)S(1)} %copy-done.3, pred[]{:T(512)S(6)} %eq.10, pred[]{:T(512)S(6)} %eq.9), kind=kLoop, calls=%fused_computation.135 | loop fusion | flops 2949120 | bytes 1769474 | tf_op jit(solution)/shard_map/jit(_where)/select_n | solution.py:147
  71.9 4.9 %collective-permute-done = bf16[1,1,512,384]{3,2,1,0:T(8,128)(2,1)S(1)} collective-permute-done((bf16[1,1,512,384]{3,2,1,0:T(8,128)(2,1)S(1)}, bf16[1,1,512,384]{3,2,1,0:T(8,128)(2,1)S(1)}, u32[]{:S(2)}, u32[]{:S(2)}) %collective-permute-start) | collective-permute-done | bytes 393248 | tf_op jit(solution)/shard_map/ppermute | solution.py:163
  86.2 5.5 %all-to-all-start.2 = ((bf16[2,1,16,32,384]{4,3,0,1,2:T(8,128)(2,1)}), bf16[2,1,16,32,384]{4,3,0,1,2:T(8,128)(2,1)S(1)}, u32[]{:S(2)}, u32[]{:S(2)}) async-start(bf16[2,1,16,32,384]{4,3,0,1,2:T(8,128)(2,1)} %copy.27), calls=%async_computation.2 | async-start | bytes 1572864 | tf_op jit(solution)/shard_map/all_to_all | solution.py:106
  91.7 2.0 %rev.9 = f32[9,384]{1,0:T(8,128)} reverse(f32[9,384]{1,0:T(8,128)} %get-tuple-element.55), dimensions={0} | reverse | bytes 27648 | tf_op jit(solution)/shard_map/rev | solution.py:171
  98.3 12.2 %all-to-all-done.2 = bf16[2,1,16,32,384]{4,3,0,1,2:T(8,128)(2,1)S(1)} async-done(((bf16[2,1,16,32,384]{4,3,0,1,2:T(8,128)(2,1)}), bf16[2,1,16,32,384]{4,3,0,1,2:T(8,128)(2,1)S(1)}, u32[]{:S(2)}, u32[]{:S(2)}) %all-to-all-start.2) | async-done | bytes 786464 | tf_op jit(solution)/shard_map/all_to_all | solution.py:106
  111.2 2.3 %fusion.33 = bf16[2,16,32,384]{3,2,1,0:T(8,128)(2,1)} fusion(f32[2,16,32,384]{3,2,1,0:T(8,128)S(1)} %bitcast_convert_fusion, f32[2,384]{1,0:T(2,128)S(1)} %bitcast.196, f32[2,384]{1,0:T(2,128)S(1)} %bitcast.189, f32[2,384]{1,0:T(2,128)S(1)} %bitcast.190, f32[2,384]{1,0:T(2,128)S(1)} %bitcast.191, f32[2,384]{1,0:T(2,128)S(1)} %bitcast.192, ...), kind=kLoop, calls=%fused_computation.61 | loop fusion | flops 7471104 | bytes 2386944 | tf_op jit(solution)/shard_map/convert_element_type | solution.py:71
  113.5 5.4 %all-to-all-start.3 = ((bf16[1,32,1,32,384]{4,3,2,0,1:T(8,128)(2,1)}), bf16[1,32,1,32,384]{4,3,2,0,1:T(8,128)(2,1)S(1)}, u32[]{:S(2)}, u32[]{:S(2)}) async-start(bf16[1,32,1,32,384]{4,3,2,0,1:T(8,128)(2,1)} %bitcast.181), calls=%async_computation.3 | async-start | bytes 1572864 | tf_op jit(solution)/shard_map/all_to_all | solution.py:110
  118.9 4.4 %collective-permute-start.6 = (bf16[1,1,512,384]{3,2,1,0:T(8,128)(2,1)S(1)}, bf16[1,1,512,384]{3,2,1,0:T(8,128)(2,1)}, u32[]{:S(2)}, u32[]{:S(2)}) collective-permute-start(bf16[1,1,512,384]{3,2,1,0:T(8,128)(2,1)S(1)} %fusion.61), channel_id=1, source_target_pairs={{0,16},{1,17},{2,18},{3,19},{4,20},{5,21},{6,22},{7,23},{8,24},{9,... | collective-permute-start | bytes 1179656 | tf_op jit(solution)/shard_map/ppermute | solution.py:175
  123.3 17.1 %all-to-all-done.3 = bf16[1,32,1,32,384]{4,3,2,0,1:T(8,128)(2,1)S(1)} async-done(((bf16[1,32,1,32,384]{4,3,2,0,1:T(8,128)(2,1)}), bf16[1,32,1,32,384]{4,3,2,0,1:T(8,128)(2,1)S(1)}, u32[]{:S(2)}, u32[]{:S(2)}) %all-to-all-start.3) | async-done | bytes 786464 | tf_op jit(solution)/shard_map/all_to_all | solution.py:110
  140.4 3.5 %multiply_convert_fusion = bf16[1024,768]{1,0:T(8,128)(2,1)S(1)} fusion(f32[1024,768]{1,0:T(8,128)} %get-tuple-element.73, bf16[1024,384]{1,0:T(8,128)(2,1)S(1)} %bitcast.179, bf16[1,768,384]{2,1,0:T(8,128)(2,1)} %param.14), kind=kOutput, calls=%fused_computation.16 | convolution fusion | flops 612630528 | bytes 6094848 | tf_op jit(solution)/shard_map/dot_general | solution.py:48
  144.0 2.2 %fusion.43 = (f32[1024]{0:T(1024)S(1)}, f32[1024,384]{1,0:T(8,128)}) fusion(f32[2,1,32,16,384]{4,3,2,0,1:T(8,128)S(1)} %get-tuple-element.44, f32[384]{0:T(512)S(1)} %copy-done.19, f32[2,384]{1,0:T(2,128)S(1)} %copy-done.12, f32[2,384]{1,0:T(2,128)S(1)} %copy-done.14, bf16[1024,768]{1,0:T(8,128)(2,1)S(1)} %multiply_convert_fusion, ...), kind=kOutput, calls=%fused_computation.73 | convolution fusion | flops 606731264 | bytes 5320192 | tf_op jit(solution)/shard_map/dot_general | solution.py:52
  146.9 1.9 %subtract_multiply_fusion = f32[2,1,32,16,384]{4,3,2,0,1:T(8,128)S(1)} fusion(f32[2,1,32,16,384]{4,3,2,0,1:T(8,128)} %bitcast.177, f32[2,1,32,16,384]{4,3,2,0,1:T(8,128)S(1)} %get-tuple-element.44, f32[2,32,16]{2,1,0:T(8,128)} %div.30, f32[2,32,16]{2,1,0:T(8,128)} %get-tuple-element.67, f32[384]{0:T(512)S(1)} %copy-done.19, f32[2,32,16]{2,1,0:T(8,128)} %copy-done.8, ...), kind=kLoop, calls=%fused_computation.84 | loop fusion | flops 3145728 | bytes 4738560 | tf_op jit(solution)/shard_map/mul | solution.py:56
  150.3 2.6 %fusion.60 = (bf16[1,2,1,512,384]{4,3,2,1,0:T(8,128)(2,1)}, bf16[1,2,1,512,384]{4,3,2,1,0:T(8,128)(2,1)}) fusion(bf16[1,2,1,512,384]{4,3,2,1,0:T(8,128)(2,1)S(1)} %bitcast.183, bf16[1,2,1,512,384]{4,3,2,1,0:T(8,128)(2,1)S(1)} %bitcast.180, bf16[1,1,1,512,384]{4,3,2,1,0:T(8,128)(2,1)S(1)} %bitcast.178, bf16[1,1,1,512,384]{4,3,2,1,0:T(8,128)(2,1)} %bitcast.41, ...), kind=kLoop, calls=%fused_computation.115 | loop fusion | flops 2752512 | bytes 4718593 | tf_op jit(solution)/shard_map/jit(_where)/select_n | solution.py:177
  (219 shorter events, 38.4 us)
Async XLA Ops:
  10.0 9.7 %copy-start.10 = (f32[1,9,384]{2,0,1:T(1,128)S(1)}, f32[1,9,384]{2,0,1:T(1,128)}, u32[]{:S(2)}) copy-start(f32[1,9,384]{2,0,1:T(1,128)} %param.10) | copy-start | bytes 41476
  11.1 26.1 %all-to-all-start = ((bf16[2,1,16,32,384]{4,3,0,1,2:T(8,128)(2,1)}), bf16[2,1,16,32,384]{4,3,0,1,2:T(8,128)(2,1)S(1)}, u32[]{:S(2)}, u32[]{:S(2)}) async-start(bf16[2,1,16,32,384]{4,3,0,1,2:T(8,128)(2,1)} %copy.23), calls=%async_computation | async-start | bytes 1572864 | tf_op jit(solution)/shard_map/all_to_all | solution.py:78
  22.4 4.3 %collective-permute-start.1 = (f32[23,384]{1,0:T(8,128)}, f32[23,384]{1,0:T(8,128)}, u32[]{:S(2)}, u32[]{:S(2)}) collective-permute-start(f32[23,384]{1,0:T(8,128)} %pad_maximum_fusion.1), channel_id=1, source_target_pairs={{0,16},{16,0},{1,17},{17,1},{2,18},{18,2},{3,19},{19,3},{4,20},{20... | collective-permute-start | bytes 105992 | tf_op jit(solution)/shard_map/ppermute | solution.py:136
  39.7 8.6 %copy-start.16 = (f32[1,2,2,384]{3,2,1,0:T(2,128)S(1)}, f32[1,2,2,384]{3,2,1,0:T(2,128)}, u32[]{:S(2)}) copy-start(f32[1,2,2,384]{3,2,1,0:T(2,128)} %param.11) | copy-start | bytes 18436
  39.7 15.7 %copy-start.18 = (f32[384]{0:T(512)S(1)}, f32[384]{0:T(512)}, u32[]{:S(2)}) copy-start(f32[384]{0:T(512)} %copy-done.17) | copy-start | bytes 4612
  39.7 24.4 %all-to-all-start.1 = ((bf16[2,16,1,32,384]{4,3,0,2,1:T(8,128)(2,1)}), bf16[2,16,1,32,384]{4,3,0,2,1:T(8,128)(2,1)}, u32[]{:S(2)}, u32[]{:S(2)}) async-start(bf16[2,16,1,32,384]{4,3,0,2,1:T(8,128)(2,1)} %fusion.63), calls=%async_computation.1 | async-start | bytes 1572864 | tf_op jit(solution)/shard_map/all_to_all | solution.py:82
  45.4 10.0 %collective-permute-start.4 = (bf16[384,384]{1,0:T(8,128)(2,1)S(1)}, bf16[384,384]{1,0:T(8,128)(2,1)}, u32[]{:S(2)}, u32[]{:S(2)}) collective-permute-start(bf16[384,384]{1,0:T(8,128)(2,1)S(1)} %dynamic-slice_bitcast_fusion), channel_id=1, source_target_pairs={{0,16},{16,0},{1,17},{17,1},{2,18},{18,2},{3,19},{19,3},{4,20},{20... | collective-permute-start | bytes 884744 | tf_op jit(solution)/shard_map/ppermute | solution.py:131
  47.0 14.2 %collective-permute-start.2 = (bf16[192,768]{1,0:T(8,128)(2,1)S(1)}, bf16[192,768]{1,0:T(8,128)(2,1)}, u32[]{:S(2)}, u32[]{:S(2)}) collective-permute-start(bf16[192,768]{1,0:T(8,128)(2,1)S(1)} %dynamic-slice_bitcast_fusion.1), channel_id=1, source_target_pairs={{0,16},{16,0},{1,17},{17,1},{2,18},{18,2},{3,19},{19,3},{4,20},{20... | collective-permute-start | bytes 884744 | tf_op jit(solution)/shard_map/ppermute | solution.py:131
  55.4 11.6 %collective-permute-start.5 = (bf16[384,384]{1,0:T(8,128)(2,1)}, bf16[384,384]{1,0:T(8,128)(2,1)}, u32[]{:S(2)}, u32[]{:S(2)}) collective-permute-start(bf16[384,384]{1,0:T(8,128)(2,1)} %collective-permute-done.4), channel_id=1, source_target_pairs={{0,1},{1,0},{2,3},{3,2},{4,5},{5,4},{6,7},{7,6},{8,9},{9,8},{10,11... | collective-permute-start | bytes 884744 | tf_op jit(solution)/shard_map/ppermute | solution.py:132
  61.2 8.3 %collective-permute-start.3 = (bf16[192,768]{1,0:T(8,128)(2,1)}, bf16[192,768]{1,0:T(8,128)(2,1)}, u32[]{:S(2)}, u32[]{:S(2)}) collective-permute-start(bf16[192,768]{1,0:T(8,128)(2,1)} %collective-permute-done.2), channel_id=1, source_target_pairs={{0,1},{1,0},{2,3},{3,2},{4,5},{5,4},{6,7},{7,6},{8,9},{9,8},{10,11... | collective-permute-start | bytes 884744 | tf_op jit(solution)/shard_map/ppermute | solution.py:132
  65.4 6.3 %copy-start.15 = (f32[9,384]{1,0:T(8,128)S(1)}, f32[9,384]{1,0:T(8,128)}, u32[]{:S(2)}) copy-start(f32[9,384]{1,0:T(8,128)} %get-tuple-element.7) | copy-start | bytes 41476
  65.4 11.3 %collective-permute-start = (bf16[1,1,512,384]{3,2,1,0:T(8,128)(2,1)S(1)}, bf16[1,1,512,384]{3,2,1,0:T(8,128)(2,1)S(1)}, u32[]{:S(2)}, u32[]{:S(2)}) collective-permute-start(bf16[1,1,512,384]{3,2,1,0:T(8,128)(2,1)S(1)} %constant_dynamic-slice_fusion), channel_id=1, source_target_pairs={{0,16},{16,0},{1,17},{17,1},{2,18},{18,2},{3,19},{19,3},{4,20},{20... | collective-permute-start | bytes 1179656 | tf_op jit(solution)/shard_map/ppermute | solution.py:163
  71.7 5.4 %copy-start.20 = (f32[384]{0:T(512)}, f32[384]{0:T(512)S(1)}, u32[]{:S(2)}) copy-start(f32[384]{0:T(512)S(1)} %get-tuple-element.39) | copy-start | bytes 4612
  71.8 5.4 %copy-start.22 = (f32[384]{0:T(512)}, f32[384]{0:T(512)S(1)}, u32[]{:S(2)}) copy-start(f32[384]{0:T(512)S(1)} %get-tuple-element.40) | copy-start | bytes 4612
  71.8 5.3 %copy-start.45 = (f32[384]{0:T(512)}, f32[384]{0:T(512)S(1)}, u32[]{:S(2)}) copy-start(f32[384]{0:T(512)S(1)} %get-tuple-element.14) | copy-start | bytes 4612
  71.8 5.3 %copy-start.47 = (f32[384]{0:T(512)}, f32[384]{0:T(512)S(1)}, u32[]{:S(2)}) copy-start(f32[384]{0:T(512)S(1)} %get-tuple-element.17) | copy-start | bytes 4612
  71.8 5.3 %copy-start.49 = (f32[384]{0:T(512)}, f32[384]{0:T(512)S(1)}, u32[]{:S(2)}) copy-start(f32[384]{0:T(512)S(1)} %get-tuple-element.18) | copy-start | bytes 4612
  71.9 5.3 %copy-start.51 = (f32[384]{0:T(512)}, f32[384]{0:T(512)S(1)}, u32[]{:S(2)}) copy-start(f32[384]{0:T(512)S(1)} %get-tuple-element.19) | copy-start | bytes 4612
  71.9 5.3 %copy-start.55 = (f32[384]{0:T(512)}, f32[384]{0:T(512)S(1)}, u32[]{:S(2)}) copy-start(f32[384]{0:T(512)S(1)} %get-tuple-element.12) | copy-start | bytes 4612
  71.9 5.3 %copy-start.57 = (f32[384]{0:T(512)}, f32[384]{0:T(512)S(1)}, u32[]{:S(2)}) copy-start(f32[384]{0:T(512)S(1)} %get-tuple-element.15) | copy-start | bytes 4612
  71.9 5.3 %copy-start.59 = (f32[384]{0:T(512)}, f32[384]{0:T(512)S(1)}, u32[]{:S(2)}) copy-start(f32[384]{0:T(512)S(1)} %get-tuple-element.16) | copy-start | bytes 4612
  86.2 24.2 %all-to-all-start.2 = ((bf16[2,1,16,32,384]{4,3,0,1,2:T(8,128)(2,1)}), bf16[2,1,16,32,384]{4,3,0,1,2:T(8,128)(2,1)S(1)}, u32[]{:S(2)}, u32[]{:S(2)}) async-start(bf16[2,1,16,32,384]{4,3,0,1,2:T(8,128)(2,1)} %copy.27), calls=%async_computation.2 | async-start | bytes 1572864 | tf_op jit(solution)/shard_map/all_to_all | solution.py:106
  113.5 26.9 %all-to-all-start.3 = ((bf16[1,32,1,32,384]{4,3,2,0,1:T(8,128)(2,1)}), bf16[1,32,1,32,384]{4,3,2,0,1:T(8,128)(2,1)S(1)}, u32[]{:S(2)}, u32[]{:S(2)}) async-start(bf16[1,32,1,32,384]{4,3,2,0,1:T(8,128)(2,1)} %bitcast.181), calls=%async_computation.3 | async-start | bytes 1572864 | tf_op jit(solution)/shard_map/all_to_all | solution.py:110
  118.9 31.4 %collective-permute-start.6 = (bf16[1,1,512,384]{3,2,1,0:T(8,128)(2,1)S(1)}, bf16[1,1,512,384]{3,2,1,0:T(8,128)(2,1)}, u32[]{:S(2)}, u32[]{:S(2)}) collective-permute-start(bf16[1,1,512,384]{3,2,1,0:T(8,128)(2,1)S(1)} %fusion.61), channel_id=1, source_target_pairs={{0,16},{1,17},{2,18},{3,19},{4,20},{5,21},{6,22},{7,23},{8,24},{9,... | collective-permute-start | bytes 1179656 | tf_op jit(solution)/shard_map/ppermute | solution.py:175
  (61 other events, 99.7 us)

commit v17 on v16

--- a/solution.py
+++ b/solution.py
@@ -156,13 +156,8 @@
     first_mixed, first_saved = spatial_forward(clips, *own)
     lead_in = jnp.where(first, first_mixed, cotangent)
     lead_taps = jnp.where(first, band, band[::-1])
-    lead_out = temporal(lead_in, lead_taps[None])
-
-    mine = lax.dynamic_index_in_dim(lead_out, plane, 0, keepdims=True)
-    theirs = lax.dynamic_index_in_dim(lead_out, 1 - plane, 0, keepdims=True)
-    got = lax.ppermute(theirs, "section", perm=swap)
-    clip_act = jnp.where(first, mine, got)
-    clip_seed = jnp.where(first, got, mine)
+    clip_act, clip_seed = temporal_cross(lead_in, lead_taps[None])
+    clip_act, clip_seed = clip_act[None], clip_seed[None]
     second_params = for_clip(second_seg, plane)
     second_mixed, second_saved = spatial_forward(clip_act, *second_params)
     second_grad = spatial_backward(second_saved, clip_seed, *second_params)
@@ -173,7 +168,8 @@
     first_grad = spatial_backward(first_saved, tail_out, *own)
 
     sent_second_grad = lax.ppermute(second_grad, "section", perm=[(0, 1)])
-    activations = jnp.where(first, lead_out, tail_out)
+    other_act = lax.ppermute(clip_act, "section", perm=[(1, 0)])
+    activations = jnp.where(first, jnp.concatenate([clip_act, other_act]), tail_out)
     input_grads = jnp.where(first, first_grad, jnp.concatenate([sent_second_grad, second_grad]))
     return (activations[None], input_grads[None])
 

time: 155 us -> 155 us (level)
  waiting for transfers between devices: 57.7 us -> 52.4 us
  local copies, waits for them, and re-layouts: 20 us -> 23.1 us
  other arithmetic: 27.8 us -> 30.4 us
    all_to_all x2 -> x0, starting transfers between devices: 13 us -> none  [the longest x1 7.38 us: temporal(): lax.all_to_all(grouped, 'seq', split_axis=2, concat_axis=1, tiled=True)]
    all_to_all x2 -> x0, waiting for transfers between devices: 11.3 us -> none  [the longest x1 8.36 us: temporal(): lax.all_to_all(grouped, 'seq', split_axis=2, concat_axis=1, tiled=True)]
    all_to_all x1 -> x2, waiting for transfers between devices: 12.2 us -> 20.9 us  [temporal_cross(): lax.all_to_all(grouped, 'seq', split_axis=2, concat_axis=1, tiled=True)]
    all_to_all x1 -> x2, starting transfers between devices: 5.53 us -> 13.3 us  [temporal_cross(): lax.all_to_all(grouped, 'seq', split_axis=2, concat_axis=1, tiled=True)]
    ppermute x2, waiting for transfers between devices: 11.5 us -> 16.5 us  [fetch_halves(): got = lax.ppermute(mine, 'section', perm=swap)]
    ppermute x1, waiting for transfers between devices: 4.86 us -> 0.01 us  [on_device(): other_act = lax.ppermute(clip_act, 'section', perm=[(1, 0)])]
    all_to_all x1 -> x2, starting transfers between devices: 5.39 us -> 9.96 us  [temporal_cross(): lax.all_to_all(banded, ('section', 'seq'), split_axis=1, concat_axis=2, t...]
    all_to_all x1 -> x2, waiting for transfers between devices: 17.1 us -> 14.2 us  [temporal_cross(): lax.all_to_all(banded, ('section', 'seq'), split_axis=1, concat_axis=2, t...]
  transfers between devices with their start and end apart: 11 -> 11, of which waited for: 8 -> 6; matrix products, arithmetic and copies ran while one was open for 21% -> 22% of each run, Pallas kernels for 0% -> 0%
where the time goes in v17:
time: 155 us; the launch traced here: 154 us
  waiting for transfers between devices  52.4 us (34%)
  starting transfers between devices  32.5 us (21%)
  other arithmetic  30.4 us (20%)
  local copies, waits for them, and re-layouts  23.1 us (15%)
  matrix products  13.5 us (9%)
  between operations  1.63 us (1%)
    all_to_all x2, waiting for transfers between devices, temporal_cross(): lax.all_to_all(grouped, 'seq', split_axis=2, concat_axis=1, tiled=True)  20.9 us
    ppermute x2, waiting for transfers between devices, fetch_halves(): got = lax.ppermute(mine, 'section', perm=swap)  16.5 us
    all_to_all x2, waiting for transfers between devices, temporal_cross(): lax.all_to_all(banded, ('section', 'seq'), split_axis=1, concat_axis=2, t...  14.2 us
    all_to_all x2, starting transfers between devices, temporal_cross(): lax.all_to_all(grouped, 'seq', split_axis=2, concat_axis=1, tiled=True)  13.3 us
    all_to_all x2, starting transfers between devices, temporal_cross(): lax.all_to_all(banded, ('section', 'seq'), split_axis=1, concat_axis=2, t...  9.96 us
    unnamed x157, local copies, waits for them, and re-layouts  8.21 us
    select_n x4, other arithmetic, on_device(): jnp.where(first, r, o)  5.49 us
    dot_general x2, matrix products, spatial_backward(): jnp.dot(flat_grad, w_out.T, preferred_element_type=jnp.float32)  4.5 us
  transfers between devices with their start and end apart: 11, of which 6 were waited for; matrix products, arithmetic and copies ran while one was open for 22% of the time, Pallas kernels for 0%

profile of v17, /device:TPU:0, one launch (start us, length us, event | category | flops | bytes accessed | tf_op | source)
XLA Modules:
  0.0 153.6 jit_solution(6151780698539810464)
XLA Ops:
  6.1 3.3 %multiply_convert_fusion.1 = (bf16[1024,768]{1,0:T(8,128)(2,1)}, f32[1024,768]{1,0:T(8,128)}) fusion(bf16[1024,384]{1,0:T(8,128)(2,1)S(1)} %bitcast.197, bf16[1,384,768]{2,1,0:T(8,128)(2,1)S(1)} %copy-done.3), kind=kOutput, calls=%fused_computation.17 | convolution fusion | flops 607911936 | bytes 6094848 | tf_op jit(solution)/shard_map/dot_general | solution.py:37
  9.4 2.8 %fusion.50 = bf16[2,1,512,384]{3,2,0,1:T(8,128)(2,1)S(1)} fusion(bf16[2,512,768]{2,1,0:T(8,128)(2,1)} %bitcast.211, bf16[2,1,512,384]{3,2,1,0:T(8,128)(2,1)} %param.9, pred[]{:T(512)S(6)} %eq.9, bf16[1,768,384]{2,1,0:T(8,128)(2,1)S(1)} %copy-done.6, bf16[2,1,512,384]{3,2,1,0:T(8,128)(2,1)} %param.8), kind=kOutput, calls=%fused_computation.96 | convolution fusion | flops 605552640 | bytes 4521985 | tf_op jit(solution)/shard_map/dot_general | solution.py:39
  13.3 7.4 %all-to-all-start = ((bf16[2,1,16,32,384]{4,3,0,1,2:T(8,128)(2,1)}), bf16[2,1,16,32,384]{4,3,0,1,2:T(8,128)(2,1)S(1)}, u32[]{:S(2)}, u32[]{:S(2)}) async-start(bf16[2,1,16,32,384]{4,3,0,1,2:T(8,128)(2,1)} %copy.22), calls=%async_computation | async-start | bytes 1572864 | tf_op jit(solution)/shard_map/all_to_all | solution.py:106
  23.2 1.3 pad_maximum_fusion.1
  24.6 1.5 collective-permute-start.1
  26.1 2.0 %rev.8 = f32[9,384]{1,0:T(8,128)} reverse(f32[9,384]{1,0:T(8,128)} %copy-done.9), dimensions={0} | reverse | bytes 27648 | tf_op jit(solution)/shard_map/rev | solution.py:158
  28.9 1.4 slice_select_fusion.1
  30.9 8.4 %all-to-all-done = bf16[2,1,16,32,384]{4,3,0,1,2:T(8,128)(2,1)S(1)} async-done(((bf16[2,1,16,32,384]{4,3,0,1,2:T(8,128)(2,1)}), bf16[2,1,16,32,384]{4,3,0,1,2:T(8,128)(2,1)S(1)}, u32[]{:S(2)}, u32[]{:S(2)}) %all-to-all-start) | async-done | bytes 786464 | tf_op jit(solution)/shard_map/all_to_all | solution.py:106
  40.1 1.8 %fusion.15 = bf16[2,16,32,384]{3,2,1,0:T(8,128)(2,1)} fusion(f32[2,16,32,384]{3,2,1,0:T(8,128)S(1)} %bitcast_convert_fusion.1, f32[384]{0:T(512)S(1)} %get-tuple-element.22, f32[384]{0:T(512)S(1)} %get-tuple-element.23, f32[384]{0:T(512)S(1)} %get-tuple-element.24, f32[384]{0:T(512)S(1)} %copy-done.67, f32[384]{0:T(512)S(1)} %copy-done.68, ...), kind=kLoop, calls=%fused_computation.43 | loop fusion | flops 7471104 | bytes 2373120 | tf_op jit(solution)/shard_map/convert_element_type | solution.py:71
  41.9 5.4 %all-to-all-start.1 = ((bf16[1,32,1,32,384]{4,3,2,0,1:T(8,128)(2,1)}), bf16[1,32,1,32,384]{4,3,2,0,1:T(8,128)(2,1)S(1)}, u32[]{:S(2)}, u32[]{:S(2)}) async-start(bf16[1,32,1,32,384]{4,3,2,0,1:T(8,128)(2,1)} %bitcast.191), calls=%async_computation.1 | async-start | bytes 1572864 | tf_op jit(solution)/shard_map/all_to_all | solution.py:110
  48.0 1.8 %collective-permute-start.2 = (bf16[192,768]{1,0:T(8,128)(2,1)}, bf16[192,768]{1,0:T(8,128)(2,1)}, u32[]{:S(2)}, u32[]{:S(2)}) collective-permute-start(bf16[192,768]{1,0:T(8,128)(2,1)} %dynamic-slice_bitcast_fusion.1), channel_id=1, source_target_pairs={{0,16},{16,0},{1,17},{17,1},{2,18},{18,2},{3,19},{19,3},{4,20},{20... | collective-permute-start | bytes 884744 | tf_op jit(solution)/shard_map/ppermute | solution.py:131
  54.1 10.0 %collective-permute-done.2 = bf16[192,768]{1,0:T(8,128)(2,1)} collective-permute-done((bf16[192,768]{1,0:T(8,128)(2,1)}, bf16[192,768]{1,0:T(8,128)(2,1)}, u32[]{:S(2)}, u32[]{:S(2)}) %collective-permute-start.2) | collective-permute-done | bytes 294944 | tf_op jit(solution)/shard_map/ppermute | solution.py:131
  64.9 6.4 %collective-permute-done.4 = bf16[384,384]{1,0:T(8,128)(2,1)} collective-permute-done((bf16[384,384]{1,0:T(8,128)(2,1)}, bf16[384,384]{1,0:T(8,128)(2,1)}, u32[]{:S(2)}, u32[]{:S(2)}) %collective-permute-start.4) | collective-permute-done | bytes 294944 | tf_op jit(solution)/shard_map/ppermute | solution.py:131
  71.9 2.1 %fusion.64 = bf16[384,768]{1,0:T(8,128)(2,1)} fusion(bf16[192,768]{1,0:T(8,128)(2,1)S(1)} %collective-permute-done.3, bf16[192,768]{1,0:T(8,128)(2,1)} %collective-permute-done.2, bf16[1,384,768]{2,1,0:T(8,128)(2,1)S(1)} %copy-done.3, pred[]{:T(512)S(6)} %eq.10, pred[]{:T(512)S(6)} %eq.9), kind=kLoop, calls=%fused_computation.137 | loop fusion | flops 2949120 | bytes 1769474 | tf_op jit(solution)/shard_map/jit(_where)/select_n | solution.py:147
  74.0 2.1 %fusion.65 = bf16[768,384]{1,0:T(8,128)(2,1)} fusion(bf16[384,384]{1,0:T(8,128)(2,1)S(1)} %collective-permute-done.5, bf16[384,384]{1,0:T(8,128)(2,1)} %collective-permute-done.4, bf16[1,768,384]{2,1,0:T(8,128)(2,1)S(1)} %copy-done.6, pred[]{:T(512)S(6)} %eq.10, pred[]{:T(512)S(6)} %eq.9), kind=kLoop, calls=%fused_computation.139 | loop fusion | flops 2949120 | bytes 1769474 | tf_op jit(solution)/shard_map/jit(_where)/select_n | solution.py:147
  87.1 6.0 %all-to-all-start.2 = ((bf16[2,1,16,32,384]{4,3,1,0,2:T(8,128)(2,1)}), bf16[2,1,16,32,384]{4,3,1,0,2:T(8,128)(2,1)}, u32[]{:S(2)}, u32[]{:S(2)}) async-start(bf16[2,1,16,32,384]{4,3,1,0,2:T(8,128)(2,1)} %copy.25), calls=%async_computation.2 | async-start | bytes 1572864 | tf_op jit(solution)/shard_map/all_to_all | solution.py:106
  93.1 2.0 %rev.9 = f32[9,384]{1,0:T(8,128)} reverse(f32[9,384]{1,0:T(8,128)} %get-tuple-element.59), dimensions={0} | reverse | bytes 27648 | tf_op jit(solution)/shard_map/rev | solution.py:166
  99.3 12.5 %all-to-all-done.2 = bf16[2,1,16,32,384]{4,3,1,0,2:T(8,128)(2,1)} async-done(((bf16[2,1,16,32,384]{4,3,1,0,2:T(8,128)(2,1)}), bf16[2,1,16,32,384]{4,3,1,0,2:T(8,128)(2,1)}, u32[]{:S(2)}, u32[]{:S(2)}) %all-to-all-start.2) | async-done | bytes 786464 | tf_op jit(solution)/shard_map/all_to_all | solution.py:106
  113.2 2.4 %fusion.33 = bf16[2,16,32,384]{3,2,1,0:T(8,128)(2,1)} fusion(f32[2,16,32,384]{3,2,1,0:T(8,128)S(1)} %bitcast_convert_fusion, f32[2,384]{1,0:T(2,128)S(1)} %bitcast.202, f32[2,384]{1,0:T(2,128)S(1)} %bitcast.203, f32[2,384]{1,0:T(2,128)S(1)} %bitcast.204, f32[2,384]{1,0:T(2,128)S(1)} %bitcast.205, f32[2,384]{1,0:T(2,128)S(1)} %bitcast.206, ...), kind=kLoop, calls=%fused_computation.61 | loop fusion | flops 7471104 | bytes 2386944 | tf_op jit(solution)/shard_map/convert_element_type | solution.py:71
  115.6 4.6 %all-to-all-start.3 = ((bf16[1,32,1,32,384]{4,3,2,0,1:T(8,128)(2,1)}), bf16[1,32,1,32,384]{4,3,2,0,1:T(8,128)(2,1)}, u32[]{:S(2)}, u32[]{:S(2)}) async-start(bf16[1,32,1,32,384]{4,3,2,0,1:T(8,128)(2,1)} %bitcast.190), calls=%async_computation.3 | async-start | bytes 1572864 | tf_op jit(solution)/shard_map/all_to_all | solution.py:110
  121.0 4.3 %collective-permute-start.6 = (bf16[1,1,512,384]{3,2,1,0:T(8,128)(2,1)}, bf16[1,1,512,384]{3,2,1,0:T(8,128)(2,1)}, u32[]{:S(2)}, u32[]{:S(2)}) collective-permute-start(bf16[1,1,512,384]{3,2,1,0:T(8,128)(2,1)} %fusion.61), channel_id=1, source_target_pairs={{0,16},{1,17},{2,18},{3,19},{4,20},{5,21},{6,22},{7,23},{8,24},{9,... | collective-permute-start | bytes 1179656 | tf_op jit(solution)/shard_map/ppermute | solution.py:170
  127.5 14.2 %all-to-all-done.3 = bf16[1,32,1,32,384]{4,3,2,0,1:T(8,128)(2,1)} async-done(((bf16[1,32,1,32,384]{4,3,2,0,1:T(8,128)(2,1)}), bf16[1,32,1,32,384]{4,3,2,0,1:T(8,128)(2,1)}, u32[]{:S(2)}, u32[]{:S(2)}) %all-to-all-start.3) | async-done | bytes 786464 | tf_op jit(solution)/shard_map/all_to_all | solution.py:110
  141.7 3.8 %multiply_convert_fusion = bf16[1024,768]{1,0:T(8,128)(2,1)S(1)} fusion(f32[1024,768]{1,0:T(8,128)} %get-tuple-element.77, bf16[1024,384]{1,0:T(8,128)(2,1)} %bitcast.40, bf16[1,768,384]{2,1,0:T(8,128)(2,1)} %param.14), kind=kOutput, calls=%fused_computation.16 | convolution fusion | flops 612630528 | bytes 6094848 | tf_op jit(solution)/shard_map/dot_general | solution.py:48
  150.4 3.1 %fusion.59 = (bf16[1,2,1,512,384]{4,3,2,1,0:T(8,128)(2,1)}, bf16[1,2,1,512,384]{4,3,2,1,0:T(8,128)(2,1)}) fusion(bf16[1,2,1,512,384]{4,3,2,1,0:T(8,128)(2,1)S(1)} %bitcast.192, bf16[1,2,1,512,384]{4,3,2,1,0:T(8,128)(2,1)} %bitcast.38, bf16[1,1,1,512,384]{4,3,2,1,0:T(8,128)(2,1)S(1)} %bitcast.195, bf16[1,1,1,512,384]{4,3,2,1,0:T(8,128)(2,1)} %bitcast.48, ...), kind=kLoop, calls=%fused_computation.114 | loop fusion | flops 3145728 | bytes 4718593 | tf_op jit(solution)/shard_map/jit(_where)/select_n | solution.py:173
  (218 shorter events, 41.2 us)
Async XLA Ops:
  0.6 2.0 %copy-start.10 = (f32[1,9,384]{2,0,1:T(1,128)S(1)}, f32[1,9,384]{2,0,1:T(1,128)}, u32[]{:S(2)}) copy-start(f32[1,9,384]{2,0,1:T(1,128)} %param.10) | copy-start | bytes 41476
  2.8 2.7 %copy-start.11 = (f32[2,384]{1,0:T(2,128)}, f32[2,384]{1,0:T(2,128)S(1)}, u32[]{:S(2)}) copy-start(f32[2,384]{1,0:T(2,128)S(1)} %get-tuple-element.82) | copy-start | bytes 9220
  2.8 2.7 %copy-start.13 = (f32[2,384]{1,0:T(2,128)}, f32[2,384]{1,0:T(2,128)S(1)}, u32[]{:S(2)}) copy-start(f32[2,384]{1,0:T(2,128)S(1)} %get-tuple-element.83) | copy-start | bytes 9220
  4.3 1.8 %copy-start.3 = (bf16[1,384,768]{2,1,0:T(8,128)(2,1)S(1)}, bf16[1,384,768]{2,1,0:T(8,128)(2,1)}, u32[]{:S(2)}) copy-start(bf16[1,384,768]{2,1,0:T(8,128)(2,1)} %param.13) | copy-start | bytes 1769476
  6.1 3.3 %copy-start.6 = (bf16[1,768,384]{2,1,0:T(8,128)(2,1)S(1)}, bf16[1,768,384]{2,1,0:T(8,128)(2,1)}, u32[]{:S(2)}) copy-start(bf16[1,768,384]{2,1,0:T(8,128)(2,1)} %param.14) | copy-start | bytes 1769476
  13.3 26.1 %all-to-all-start = ((bf16[2,1,16,32,384]{4,3,0,1,2:T(8,128)(2,1)}), bf16[2,1,16,32,384]{4,3,0,1,2:T(8,128)(2,1)S(1)}, u32[]{:S(2)}, u32[]{:S(2)}) async-start(bf16[2,1,16,32,384]{4,3,0,1,2:T(8,128)(2,1)} %copy.22), calls=%async_computation | async-start | bytes 1572864 | tf_op jit(solution)/shard_map/all_to_all | solution.py:106
  24.6 4.3 %collective-permute-start.1 = (f32[23,384]{1,0:T(8,128)}, f32[23,384]{1,0:T(8,128)}, u32[]{:S(2)}, u32[]{:S(2)}) collective-permute-start(f32[23,384]{1,0:T(8,128)} %pad_maximum_fusion.1), channel_id=1, source_target_pairs={{0,16},{16,0},{1,17},{17,1},{2,18},{18,2},{3,19},{19,3},{4,20},{20... | collective-permute-start | bytes 105992 | tf_op jit(solution)/shard_map/ppermute | solution.py:136
  41.9 11.5 %copy-start.16 = (f32[1,2,2,384]{3,2,1,0:T(2,128)S(1)}, f32[1,2,2,384]{3,2,1,0:T(2,128)}, u32[]{:S(2)}) copy-start(f32[1,2,2,384]{3,2,1,0:T(2,128)} %param.11) | copy-start | bytes 18436
  41.9 29.4 %copy-start.18 = (f32[384]{0:T(512)S(1)}, f32[384]{0:T(512)}, u32[]{:S(2)}) copy-start(f32[384]{0:T(512)} %copy-done.17) | copy-start | bytes 4612
  41.9 35.0 %all-to-all-start.1 = ((bf16[1,32,1,32,384]{4,3,2,0,1:T(8,128)(2,1)}), bf16[1,32,1,32,384]{4,3,2,0,1:T(8,128)(2,1)S(1)}, u32[]{:S(2)}, u32[]{:S(2)}) async-start(bf16[1,32,1,32,384]{4,3,2,0,1:T(8,128)(2,1)} %bitcast.191), calls=%async_computation.1 | async-start | bytes 1572864 | tf_op jit(solution)/shard_map/all_to_all | solution.py:110
  48.0 16.1 %collective-permute-start.2 = (bf16[192,768]{1,0:T(8,128)(2,1)}, bf16[192,768]{1,0:T(8,128)(2,1)}, u32[]{:S(2)}, u32[]{:S(2)}) collective-permute-start(bf16[192,768]{1,0:T(8,128)(2,1)} %dynamic-slice_bitcast_fusion.1), channel_id=1, source_target_pairs={{0,16},{16,0},{1,17},{17,1},{2,18},{18,2},{3,19},{19,3},{4,20},{20... | collective-permute-start | bytes 884744 | tf_op jit(solution)/shard_map/ppermute | solution.py:131
  50.5 20.8 %collective-permute-start.4 = (bf16[384,384]{1,0:T(8,128)(2,1)}, bf16[384,384]{1,0:T(8,128)(2,1)}, u32[]{:S(2)}, u32[]{:S(2)}) collective-permute-start(bf16[384,384]{1,0:T(8,128)(2,1)} %dynamic-slice_bitcast_fusion), channel_id=1, source_target_pairs={{0,16},{16,0},{1,17},{17,1},{2,18},{18,2},{3,19},{19,3},{4,20},{20... | collective-permute-start | bytes 884744 | tf_op jit(solution)/shard_map/ppermute | solution.py:131
  64.1 7.8 %collective-permute-start.3 = (bf16[192,768]{1,0:T(8,128)(2,1)}, bf16[192,768]{1,0:T(8,128)(2,1)S(1)}, u32[]{:S(2)}, u32[]{:S(2)}) collective-permute-start(bf16[192,768]{1,0:T(8,128)(2,1)} %collective-permute-done.2), channel_id=1, source_target_pairs={{0,1},{1,0},{2,3},{3,2},{4,5},{5,4},{6,7},{7,6},{8,9},{9,8},{10,11... | collective-permute-start | bytes 884744 | tf_op jit(solution)/shard_map/ppermute | solution.py:132
  71.3 2.7 %collective-permute-start.5 = (bf16[384,384]{1,0:T(8,128)(2,1)}, bf16[384,384]{1,0:T(8,128)(2,1)S(1)}, u32[]{:S(2)}, u32[]{:S(2)}) collective-permute-start(bf16[384,384]{1,0:T(8,128)(2,1)} %collective-permute-done.4), channel_id=1, source_target_pairs={{0,1},{1,0},{2,3},{3,2},{4,5},{5,4},{6,7},{7,6},{8,9},{9,8},{10,11... | collective-permute-start | bytes 884744 | tf_op jit(solution)/shard_map/ppermute | solution.py:132
  71.9 4.3 %copy-start.15 = (f32[9,384]{1,0:T(8,128)S(1)}, f32[9,384]{1,0:T(8,128)}, u32[]{:S(2)}) copy-start(f32[9,384]{1,0:T(8,128)} %get-tuple-element.7) | copy-start | bytes 41476
  76.2 1.7 %copy-start.20 = (f32[384]{0:T(512)}, f32[384]{0:T(512)S(1)}, u32[]{:S(2)}) copy-start(f32[384]{0:T(512)S(1)} %get-tuple-element.39) | copy-start | bytes 4612
  87.1 24.7 %all-to-all-start.2 = ((bf16[2,1,16,32,384]{4,3,1,0,2:T(8,128)(2,1)}), bf16[2,1,16,32,384]{4,3,1,0,2:T(8,128)(2,1)}, u32[]{:S(2)}, u32[]{:S(2)}) async-start(bf16[2,1,16,32,384]{4,3,1,0,2:T(8,128)(2,1)} %copy.25), calls=%async_computation.2 | async-start | bytes 1572864 | tf_op jit(solution)/shard_map/all_to_all | solution.py:106
  115.6 26.1 %all-to-all-start.3 = ((bf16[1,32,1,32,384]{4,3,2,0,1:T(8,128)(2,1)}), bf16[1,32,1,32,384]{4,3,2,0,1:T(8,128)(2,1)}, u32[]{:S(2)}, u32[]{:S(2)}) async-start(bf16[1,32,1,32,384]{4,3,2,0,1:T(8,128)(2,1)} %bitcast.190), calls=%async_computation.3 | async-start | bytes 1572864 | tf_op jit(solution)/shard_map/all_to_all | solution.py:110
  121.0 29.0 %collective-permute-start.6 = (bf16[1,1,512,384]{3,2,1,0:T(8,128)(2,1)}, bf16[1,1,512,384]{3,2,1,0:T(8,128)(2,1)}, u32[]{:S(2)}, u32[]{:S(2)}) collective-permute-start(bf16[1,1,512,384]{3,2,1,0:T(8,128)(2,1)} %fusion.61), channel_id=1, source_target_pairs={{0,16},{1,17},{2,18},{3,19},{4,20},{5,21},{6,22},{7,23},{8,24},{9,... | collective-permute-start | bytes 1179656 | tf_op jit(solution)/shard_map/ppermute | solution.py:170
  125.4 24.7 %collective-permute-start = (bf16[1,1,512,384]{3,2,1,0:T(8,128)(2,1)S(1)}, bf16[1,1,512,384]{3,2,1,0:T(8,128)(2,1)}, u32[]{:S(2)}, u32[]{:S(2)}) collective-permute-start(bf16[1,1,512,384]{3,2,1,0:T(8,128)(2,1)S(1)} %bitcast.193), channel_id=1, source_target_pairs={{16,0},{17,1},{18,2},{19,3},{20,4},{21,5},{22,6},{23,7},{24,8},{25... | collective-permute-start | bytes 1179656 | tf_op jit(solution)/shard_map/ppermute | solution.py:171
  141.7 3.8 %copy-start.4 = (bf16[1,384,768]{2,1,0:T(8,128)(2,1)S(1)}, bf16[1,384,768]{2,1,0:T(8,128)(2,1)}, u32[]{:S(2)}) copy-start(bf16[1,384,768]{2,1,0:T(8,128)(2,1)} %param.13) | copy-start | bytes 1769476
  141.7 3.8 %copy-start.12 = (f32[2,384]{1,0:T(2,128)S(1)}, f32[2,384]{1,0:T(2,128)}, u32[]{:S(2)}) copy-start(f32[2,384]{1,0:T(2,128)} %copy-done.11) | copy-start | bytes 9220
  141.7 3.8 %copy-start.14 = (f32[2,384]{1,0:T(2,128)S(1)}, f32[2,384]{1,0:T(2,128)}, u32[]{:S(2)}) copy-start(f32[2,384]{1,0:T(2,128)} %copy-done.13) | copy-start | bytes 9220
  141.7 3.8 %copy-start.19 = (f32[384]{0:T(512)S(1)}, f32[384]{0:T(512)}, u32[]{:S(2)}) copy-start(f32[384]{0:T(512)} %copy-done.17) | copy-start | bytes 4612
  (60 other events, 53.6 us)

commit v18 on v17

--- a/solution.py
+++ b/solution.py
@@ -99,17 +99,18 @@
     return jnp.moveaxis(back, 2, 0)
 
 
-def temporal_cross(values, tap_table):
+def temporal_cross(values, tap_table, carried):
     piece_count, frame_count, pixel_count, channels = values.shape
     groups = lax.axis_size("seq")
     grouped = values.reshape(piece_count, frame_count, groups, pixel_count // groups, channels)
     pixel_view = lax.all_to_all(grouped, "seq", split_axis=2, concat_axis=1, tiled=True)
     pixel_view = pixel_view.reshape(piece_count, groups * frame_count, pixel_count // groups, channels)
+    pixel_view, carried = lax.optimization_barrier((pixel_view, carried))
     banded = band_frames(pixel_view, tap_table)
     banded = banded.reshape(1, piece_count * groups * frame_count, 1, pixel_count // groups, channels)
     back = lax.all_to_all(banded, ("section", "seq"), split_axis=1, concat_axis=2, tiled=True)
     back = back.reshape(frame_count, piece_count, pixel_count, channels)
-    return jnp.moveaxis(back, 1, 0)
+    return jnp.moveaxis(back, 1, 0), carried
 
 
 def on_device(clips, cotangent, spatial_taps, modulation, norm_gain, w_in, w_out, band_taps):
@@ -121,6 +122,10 @@
     tap_count = taps.shape[0]
     own = (taps, mod, gain, weight_in, weight_out)
 
+    first_mixed, first_saved = spatial_forward(clips, *own)
+    first_mixed, (taps, mod, gain, weight_in, weight_out, band) = lax.optimization_barrier(
+        (first_mixed, own + (band,))
+    )
     swap = [(0, 1), (1, 0)]
     core = lax.axis_index("seq") % 2
     siblings = [(q, q ^ 1) for q in range(lax.axis_size("seq"))]
@@ -153,17 +158,18 @@
         clip_mod = lax.dynamic_index_in_dim(params[1], clip, 0, keepdims=True)
         return (params[0], clip_mod) + tuple(params[2:])
 
-    first_mixed, first_saved = spatial_forward(clips, *own)
     lead_in = jnp.where(first, first_mixed, cotangent)
     lead_taps = jnp.where(first, band, band[::-1])
-    clip_act, clip_seed = temporal_cross(lead_in, lead_taps[None])
+    (clip_act, clip_seed), (second_seg, first_band, second_band) = temporal_cross(
+        lead_in, lead_taps[None], (second_seg, first_band, second_band)
+    )
     clip_act, clip_seed = clip_act[None], clip_seed[None]
     second_params = for_clip(second_seg, plane)
     second_mixed, second_saved = spatial_forward(clip_act, *second_params)
     second_grad = spatial_backward(second_saved, clip_seed, *second_params)
 
-    tail_out = temporal_cross(
-        jnp.concatenate([second_grad, second_mixed]), jnp.stack([first_band[::-1], second_band])
+    tail_out, _ = temporal_cross(
+        jnp.concatenate([second_grad, second_mixed]), jnp.stack([first_band[::-1], second_band]), ()
     )
     first_grad = spatial_backward(first_saved, tail_out, *own)
 

time: 155 us -> 154 us (level)
  starting transfers between devices: 32.5 us -> 30.7 us
  local copies, waits for them, and re-layouts: 23.1 us -> 24.9 us
    all_to_all x2, waiting for transfers between devices: 14.2 us -> 34.8 us  [temporal_cross(): lax.all_to_all(banded, ('section', 'seq'), split_axis=1, concat_axis=2, t...]
    ppermute x2, waiting for transfers between devices: 16.5 us -> 4.88 us  [fetch_halves(): got = lax.ppermute(mine, 'section', perm=swap)]
    all_to_all x2, waiting for transfers between devices: 20.9 us -> 12.4 us  [temporal_cross(): lax.all_to_all(grouped, 'seq', split_axis=2, concat_axis=1, tiled=True)]
    all_to_all x2, starting transfers between devices: 13.3 us -> 11.7 us  [temporal_cross(): lax.all_to_all(grouped, 'seq', split_axis=2, concat_axis=1, tiled=True)]
    unnamed x157 -> x161, local copies, waits for them, and re-layouts: 8.21 us -> 7.44 us
  transfers between devices with their start and end apart: 11 -> 11, of which waited for: 6 -> 4; matrix products, arithmetic and copies ran while one was open for 22% -> 23% of each run, Pallas kernels for 0% -> 0%
where the time goes in v18:
time: 154 us; the launch traced here: 152 us
  waiting for transfers between devices  52.2 us (34%)
  starting transfers between devices  30.7 us (20%)
  other arithmetic  30.5 us (20%)
  local copies, waits for them, and re-layouts  24.9 us (16%)
  matrix products  12.1 us (8%)
  between operations  1.67 us (1%)
    all_to_all x2, waiting for transfers between devices, temporal_cross(): lax.all_to_all(banded, ('section', 'seq'), split_axis=1, concat_axis=2, t...  34.8 us
    all_to_all x2, waiting for transfers between devices, temporal_cross(): lax.all_to_all(grouped, 'seq', split_axis=2, concat_axis=1, tiled=True)  12.4 us
    all_to_all x2, starting transfers between devices, temporal_cross(): lax.all_to_all(grouped, 'seq', split_axis=2, concat_axis=1, tiled=True)  11.7 us
    all_to_all x2, starting transfers between devices, temporal_cross(): lax.all_to_all(banded, ('section', 'seq'), split_axis=1, concat_axis=2, t...  11 us
    unnamed x161, local copies, waits for them, and re-layouts  7.44 us
    select_n x4, other arithmetic, on_device(): jnp.where(first, r, o)  5.53 us
    ppermute x2, waiting for transfers between devices, fetch_halves(): got = lax.ppermute(mine, 'section', perm=swap)  4.88 us
    dot_general x2, matrix products, spatial_backward(): jnp.dot(flat_grad, w_out.T, preferred_element_type=jnp.float32)  4.48 us
  transfers between devices with their start and end apart: 11, of which 4 were waited for; matrix products, arithmetic and copies ran while one was open for 23% of the time, Pallas kernels for 0%

profile of v18, /device:TPU:0, one launch (start us, length us, event | category | flops | bytes accessed | tf_op | source)
XLA Modules:
  0.0 152.0 jit_solution(8950951055446876569)
XLA Ops:
  6.2 2.8 %multiply_convert_fusion.1 = (bf16[1024,768]{1,0:T(8,128)(2,1)S(1)}, f32[1024,768]{1,0:T(8,128)}) fusion(bf16[1024,384]{1,0:T(8,128)(2,1)S(1)} %bitcast.187, bf16[1,384,768]{2,1,0:T(8,128)(2,1)S(1)} %copy-done.3), kind=kOutput, calls=%fused_computation.17 | convolution fusion | flops 607911936 | bytes 6094848 | tf_op jit(solution)/shard_map/dot_general | solution.py:37
  9.1 1.9 %fusion.44 = bf16[2,1,512,384]{3,2,0,1:T(8,128)(2,1)} fusion(bf16[2,512,768]{2,1,0:T(8,128)(2,1)S(1)} %bitcast.203, bf16[1,768,384]{2,1,0:T(8,128)(2,1)S(1)} %copy-done.6, bf16[2,1,512,384]{3,2,1,0:T(8,128)(2,1)S(1)} %copy-done.8), kind=kOutput, calls=%fused_computation.76 | convolution fusion | flops 605159424 | bytes 3735552 | tf_op jit(solution)/shard_map/dot_general | solution.py:39
  13.2 7.4 %all-to-all-start = ((bf16[2,1,16,32,384]{4,3,0,1,2:T(8,128)(2,1)}), bf16[2,1,16,32,384]{4,3,0,1,2:T(8,128)(2,1)S(1)}, u32[]{:S(2)}, u32[]{:S(2)}) async-start(bf16[2,1,16,32,384]{4,3,0,1,2:T(8,128)(2,1)} %copy.22), calls=%async_computation | async-start | bytes 1572864 | tf_op jit(solution)/shard_map/all_to_all | solution.py:106
  23.1 1.4 pad_maximum_fusion.1
  25.6 1.7 %collective-permute-start.1 = (bf16[192,768]{1,0:T(8,128)(2,1)}, bf16[192,768]{1,0:T(8,128)(2,1)}, u32[]{:S(2)}, u32[]{:S(2)}) collective-permute-start(bf16[192,768]{1,0:T(8,128)(2,1)} %constant_dynamic-slice_fusion.1), channel_id=1, source_target_pairs={{0,16},{16,0},{1,17},{17,1},{2,18},{18,2},{3,19},{19,3},{4,20},{20... | collective-permute-start | bytes 884744 | tf_op jit(solution)/shard_map/ppermute | solution.py:136
  28.3 2.0 %rev.8 = f32[9,384]{1,0:T(8,128)} reverse(f32[9,384]{1,0:T(8,128)} %get-tuple-element.26), dimensions={0} | reverse | bytes 27648 | tf_op jit(solution)/shard_map/rev | solution.py:162
  30.3 1.3 slice.395
  32.9 1.4 slice_select_fusion.1
  36.5 4.9 %collective-permute-done.3 = bf16[384,384]{1,0:T(8,128)(2,1)} collective-permute-done((bf16[384,384]{1,0:T(8,128)(2,1)}, bf16[384,384]{1,0:T(8,128)(2,1)}, u32[]{:S(2)}, u32[]{:S(2)}) %collective-permute-start.3) | collective-permute-done | bytes 294944 | tf_op jit(solution)/shard_map/ppermute | solution.py:136
  42.0 2.1 %fusion.63 = bf16[384,768]{1,0:T(8,128)(2,1)} fusion(bf16[192,768]{1,0:T(8,128)(2,1)S(1)} %collective-permute-done.2, bf16[192,768]{1,0:T(8,128)(2,1)} %collective-permute-done.1, pred[]{:T(512)S(6)} %eq.10, pred[]{:T(512)S(6)} %eq.9, bf16[1,384,768]{2,1,0:T(8,128)(2,1)S(1)} %copy-done.3), kind=kLoop, calls=%fused_computation.137 | loop fusion | flops 2949120 | bytes 1769474 | tf_op jit(solution)/shard_map/jit(_where)/select_n | solution.py:152
  44.1 2.1 %fusion.64 = bf16[768,384]{1,0:T(8,128)(2,1)} fusion(bf16[384,384]{1,0:T(8,128)(2,1)S(1)} %collective-permute-done.4, bf16[384,384]{1,0:T(8,128)(2,1)} %collective-permute-done.3, pred[]{:T(512)S(6)} %eq.10, pred[]{:T(512)S(6)} %eq.9, bf16[1,768,384]{2,1,0:T(8,128)(2,1)S(1)} %copy-done.6), kind=kLoop, calls=%fused_computation.139 | loop fusion | flops 2949120 | bytes 1769474 | tf_op jit(solution)/shard_map/jit(_where)/select_n | solution.py:152
  47.1 1.8 %fusion.15 = bf16[2,16,32,384]{3,2,1,0:T(8,128)(2,1)} fusion(f32[2,16,32,384]{3,2,1,0:T(8,128)S(1)} %convert_element_type.357, f32[384]{0:T(512)S(1)} %get-tuple-element.52, f32[384]{0:T(512)S(1)} %copy-done.67, f32[384]{0:T(512)S(1)} %copy-done.68, f32[384]{0:T(512)S(1)} %copy-done.69, f32[384]{0:T(512)S(1)} %copy-done.70, f32[384]{0:T(512)S(1)} %copy-done.71, ...), kind=kLoop, calls=%fused_computation.43 | loop fusion | flops 7471104 | bytes 2373120 | tf_op jit(solution)/shard_map/convert_element_type | solution.py:71
  48.9 6.0 %all-to-all-start.1 = ((bf16[1,32,1,32,384]{4,3,2,0,1:T(8,128)(2,1)}), bf16[1,32,1,32,384]{4,3,2,0,1:T(8,128)(2,1)S(1)}, u32[]{:S(2)}, u32[]{:S(2)}) async-start(bf16[1,32,1,32,384]{4,3,2,0,1:T(8,128)(2,1)} %bitcast.15), calls=%async_computation.1 | async-start | bytes 1572864 | tf_op jit(solution)/shard_map/all_to_all | solution.py:111
  55.6 20.6 %all-to-all-done.1 = bf16[1,32,1,32,384]{4,3,2,0,1:T(8,128)(2,1)S(1)} async-done(((bf16[1,32,1,32,384]{4,3,2,0,1:T(8,128)(2,1)}), bf16[1,32,1,32,384]{4,3,2,0,1:T(8,128)(2,1)S(1)}, u32[]{:S(2)}, u32[]{:S(2)}) %all-to-all-start.1) | async-done | bytes 786464 | tf_op jit(solution)/shard_map/all_to_all | solution.py:111
  86.4 4.3 %all-to-all-start.2 = ((bf16[2,1,16,32,384]{4,3,1,0,2:T(8,128)(2,1)}), bf16[2,1,16,32,384]{4,3,1,0,2:T(8,128)(2,1)}, u32[]{:S(2)}, u32[]{:S(2)}) async-start(bf16[2,1,16,32,384]{4,3,1,0,2:T(8,128)(2,1)} %copy.25), calls=%async_computation.2 | async-start | bytes 1572864 | tf_op jit(solution)/shard_map/all_to_all | solution.py:106
  90.7 2.0 %rev.9 = f32[9,384]{1,0:T(8,128)} reverse(f32[9,384]{1,0:T(8,128)} %get-tuple-element.40), dimensions={0} | reverse | bytes 27648 | tf_op jit(solution)/shard_map/rev | solution.py:172
  97.0 12.4 %all-to-all-done.2 = bf16[2,1,16,32,384]{4,3,1,0,2:T(8,128)(2,1)} async-done(((bf16[2,1,16,32,384]{4,3,1,0,2:T(8,128)(2,1)}), bf16[2,1,16,32,384]{4,3,1,0,2:T(8,128)(2,1)}, u32[]{:S(2)}, u32[]{:S(2)}) %all-to-all-start.2) | async-done | bytes 786464 | tf_op jit(solution)/shard_map/all_to_all | solution.py:106
  111.4 2.3 %fusion.33 = bf16[2,16,32,384]{3,2,1,0:T(8,128)(2,1)} fusion(f32[2,16,32,384]{3,2,1,0:T(8,128)S(1)} %convert_element_type.377, f32[2,384]{1,0:T(2,128)S(1)} %bitcast.194, f32[2,384]{1,0:T(2,128)S(1)} %bitcast.195, f32[2,384]{1,0:T(2,128)S(1)} %bitcast.196, f32[2,384]{1,0:T(2,128)S(1)} %bitcast.197, f32[2,384]{1,0:T(2,128)S(1)} %bitcast.198, ...), kind=kLoop, calls=%fused_computation.61 | loop fusion | flops 7471104 | bytes 2386944 | tf_op jit(solution)/shard_map/convert_element_type | solution.py:71
  113.7 5.0 %all-to-all-start.3 = ((bf16[1,32,1,32,384]{4,3,2,0,1:T(8,128)(2,1)}), bf16[1,32,1,32,384]{4,3,2,0,1:T(8,128)(2,1)}, u32[]{:S(2)}, u32[]{:S(2)}) async-start(bf16[1,32,1,32,384]{4,3,2,0,1:T(8,128)(2,1)} %bitcast.178), calls=%async_computation.3 | async-start | bytes 1572864 | tf_op jit(solution)/shard_map/all_to_all | solution.py:111
  119.6 4.3 %collective-permute-start.6 = (bf16[1,1,512,384]{3,2,1,0:T(8,128)(2,1)}, bf16[1,1,512,384]{3,2,1,0:T(8,128)(2,1)}, u32[]{:S(2)}, u32[]{:S(2)}) collective-permute-start(bf16[1,1,512,384]{3,2,1,0:T(8,128)(2,1)} %fusion.60), channel_id=1, source_target_pairs={{0,16},{1,17},{2,18},{3,19},{4,20},{5,21},{6,22},{7,23},{8,24},{9,... | collective-permute-start | bytes 1179656 | tf_op jit(solution)/shard_map/ppermute | solution.py:176
  126.0 14.2 %all-to-all-done.3 = bf16[1,32,1,32,384]{4,3,2,0,1:T(8,128)(2,1)} async-done(((bf16[1,32,1,32,384]{4,3,2,0,1:T(8,128)(2,1)}), bf16[1,32,1,32,384]{4,3,2,0,1:T(8,128)(2,1)}, u32[]{:S(2)}, u32[]{:S(2)}) %all-to-all-start.3) | async-done | bytes 786464 | tf_op jit(solution)/shard_map/all_to_all | solution.py:111
  140.3 3.8 %multiply_convert_fusion = bf16[1024,768]{1,0:T(8,128)(2,1)S(1)} fusion(f32[1024,768]{1,0:T(8,128)} %get-tuple-element.107, bf16[1024,384]{1,0:T(8,128)(2,1)} %bitcast.36, bf16[1,768,384]{2,1,0:T(8,128)(2,1)} %param.14), kind=kOutput, calls=%fused_computation.16 | convolution fusion | flops 612630528 | bytes 6094848 | tf_op jit(solution)/shard_map/dot_general | solution.py:48
  145.9 1.3 subtract_multiply_fusion
  148.9 3.1 %fusion.58 = (bf16[1,2,1,512,384]{4,3,2,1,0:T(8,128)(2,1)}, bf16[1,2,1,512,384]{4,3,2,1,0:T(8,128)(2,1)}) fusion(bf16[1,2,1,512,384]{4,3,2,1,0:T(8,128)(2,1)S(1)} %bitcast.182, bf16[1,2,1,512,384]{4,3,2,1,0:T(8,128)(2,1)} %bitcast.34, bf16[1,1,1,512,384]{4,3,2,1,0:T(8,128)(2,1)S(1)} %bitcast.185, bf16[1,1,1,512,384]{4,3,2,1,0:T(8,128)(2,1)} %bitcast.44, ...), kind=kLoop, calls=%fused_computation.113 | loop fusion | flops 3145728 | bytes 4718593 | tf_op jit(solution)/shard_map/jit(_where)/select_n | solution.py:179
  (226 shorter events, 40.2 us)
Async XLA Ops:
  2.8 2.9 %copy-start.12 = (f32[2,384]{1,0:T(2,128)}, f32[2,384]{1,0:T(2,128)S(1)}, u32[]{:S(2)}) copy-start(f32[2,384]{1,0:T(2,128)S(1)} %get-tuple-element.112) | copy-start | bytes 9220
  2.8 2.9 %copy-start.14 = (f32[2,384]{1,0:T(2,128)}, f32[2,384]{1,0:T(2,128)S(1)}, u32[]{:S(2)}) copy-start(f32[2,384]{1,0:T(2,128)S(1)} %get-tuple-element.113) | copy-start | bytes 9220
  6.2 2.8 %copy-start.6 = (bf16[1,768,384]{2,1,0:T(8,128)(2,1)S(1)}, bf16[1,768,384]{2,1,0:T(8,128)(2,1)}, u32[]{:S(2)}) copy-start(bf16[1,768,384]{2,1,0:T(8,128)(2,1)} %param.14) | copy-start | bytes 1769476
  6.2 2.8 %copy-start.8 = (bf16[2,1,512,384]{3,2,1,0:T(8,128)(2,1)S(1)}, bf16[2,1,512,384]{3,2,1,0:T(8,128)(2,1)}, u32[]{:S(2)}) copy-start(bf16[2,1,512,384]{3,2,1,0:T(8,128)(2,1)} %param.8) | copy-start | bytes 2359300
  13.2 33.0 %all-to-all-start = ((bf16[2,1,16,32,384]{4,3,0,1,2:T(8,128)(2,1)}), bf16[2,1,16,32,384]{4,3,0,1,2:T(8,128)(2,1)S(1)}, u32[]{:S(2)}, u32[]{:S(2)}) async-start(bf16[2,1,16,32,384]{4,3,0,1,2:T(8,128)(2,1)} %copy.22), calls=%async_computation | async-start | bytes 1572864 | tf_op jit(solution)/shard_map/all_to_all | solution.py:106
  24.5 5.9 %collective-permute-start = (f32[23,384]{1,0:T(8,128)}, f32[23,384]{1,0:T(8,128)}, u32[]{:S(2)}, u32[]{:S(2)}) collective-permute-start(f32[23,384]{1,0:T(8,128)} %pad_maximum_fusion.1), channel_id=1, source_target_pairs={{0,16},{16,0},{1,17},{17,1},{2,18},{18,2},{3,19},{19,3},{4,20},{20... | collective-permute-start | bytes 105992 | tf_op jit(solution)/shard_map/ppermute | solution.py:141
  25.6 10.3 %collective-permute-start.1 = (bf16[192,768]{1,0:T(8,128)(2,1)}, bf16[192,768]{1,0:T(8,128)(2,1)}, u32[]{:S(2)}, u32[]{:S(2)}) collective-permute-start(bf16[192,768]{1,0:T(8,128)(2,1)} %constant_dynamic-slice_fusion.1), channel_id=1, source_target_pairs={{0,16},{16,0},{1,17},{17,1},{2,18},{18,2},{3,19},{19,3},{4,20},{20... | collective-permute-start | bytes 884744 | tf_op jit(solution)/shard_map/ppermute | solution.py:136
  28.0 13.4 %collective-permute-start.3 = (bf16[384,384]{1,0:T(8,128)(2,1)}, bf16[384,384]{1,0:T(8,128)(2,1)}, u32[]{:S(2)}, u32[]{:S(2)}) collective-permute-start(bf16[384,384]{1,0:T(8,128)(2,1)} %constant_dynamic-slice_fusion), channel_id=1, source_target_pairs={{0,16},{16,0},{1,17},{17,1},{2,18},{18,2},{3,19},{19,3},{4,20},{20... | collective-permute-start | bytes 884744 | tf_op jit(solution)/shard_map/ppermute | solution.py:136
  35.8 6.2 %collective-permute-start.2 = (bf16[192,768]{1,0:T(8,128)(2,1)}, bf16[192,768]{1,0:T(8,128)(2,1)S(1)}, u32[]{:S(2)}, u32[]{:S(2)}) collective-permute-start(bf16[192,768]{1,0:T(8,128)(2,1)} %collective-permute-done.1), channel_id=1, source_target_pairs={{0,1},{1,0},{2,3},{3,2},{4,5},{5,4},{6,7},{7,6},{8,9},{9,8},{10,11... | collective-permute-start | bytes 884744 | tf_op jit(solution)/shard_map/ppermute | solution.py:137
  41.4 2.7 %collective-permute-start.4 = (bf16[384,384]{1,0:T(8,128)(2,1)}, bf16[384,384]{1,0:T(8,128)(2,1)S(1)}, u32[]{:S(2)}, u32[]{:S(2)}) collective-permute-start(bf16[384,384]{1,0:T(8,128)(2,1)} %collective-permute-done.3), channel_id=1, source_target_pairs={{0,1},{1,0},{2,3},{3,2},{4,5},{5,4},{6,7},{7,6},{8,9},{9,8},{10,11... | collective-permute-start | bytes 884744 | tf_op jit(solution)/shard_map/ppermute | solution.py:137
  47.1 7.8 %copy-start.18 = (f32[9,384]{1,0:T(8,128)S(1)}, f32[9,384]{1,0:T(8,128)}, u32[]{:S(2)}) copy-start(f32[9,384]{1,0:T(8,128)} %get-tuple-element.35) | copy-start | bytes 41476
  48.9 27.3 %all-to-all-start.1 = ((bf16[1,32,1,32,384]{4,3,2,0,1:T(8,128)(2,1)}), bf16[1,32,1,32,384]{4,3,2,0,1:T(8,128)(2,1)S(1)}, u32[]{:S(2)}, u32[]{:S(2)}) async-start(bf16[1,32,1,32,384]{4,3,2,0,1:T(8,128)(2,1)} %bitcast.15), calls=%async_computation.1 | async-start | bytes 1572864 | tf_op jit(solution)/shard_map/all_to_all | solution.py:111
  54.9 22.3 %copy-start.19 = (f32[384]{0:T(512)}, f32[384]{0:T(512)S(1)}, u32[]{:S(2)}) copy-start(f32[384]{0:T(512)S(1)} %get-tuple-element.69) | copy-start | bytes 4612
  54.9 22.3 %copy-start.21 = (f32[384]{0:T(512)}, f32[384]{0:T(512)S(1)}, u32[]{:S(2)}) copy-start(f32[384]{0:T(512)S(1)} %get-tuple-element.70) | copy-start | bytes 4612
  55.6 21.6 %copy-start.42 = (f32[384]{0:T(512)}, f32[384]{0:T(512)S(1)}, u32[]{:S(2)}) copy-start(f32[384]{0:T(512)S(1)} %get-tuple-element.43) | copy-start | bytes 4612
  55.6 21.6 %copy-start.44 = (f32[384]{0:T(512)}, f32[384]{0:T(512)S(1)}, u32[]{:S(2)}) copy-start(f32[384]{0:T(512)S(1)} %get-tuple-element.44) | copy-start | bytes 4612
  86.4 23.0 %all-to-all-start.2 = ((bf16[2,1,16,32,384]{4,3,1,0,2:T(8,128)(2,1)}), bf16[2,1,16,32,384]{4,3,1,0,2:T(8,128)(2,1)}, u32[]{:S(2)}, u32[]{:S(2)}) async-start(bf16[2,1,16,32,384]{4,3,1,0,2:T(8,128)(2,1)} %copy.25), calls=%async_computation.2 | async-start | bytes 1572864 | tf_op jit(solution)/shard_map/all_to_all | solution.py:106
  113.7 26.5 %all-to-all-start.3 = ((bf16[1,32,1,32,384]{4,3,2,0,1:T(8,128)(2,1)}), bf16[1,32,1,32,384]{4,3,2,0,1:T(8,128)(2,1)}, u32[]{:S(2)}, u32[]{:S(2)}) async-start(bf16[1,32,1,32,384]{4,3,2,0,1:T(8,128)(2,1)} %bitcast.178), calls=%async_computation.3 | async-start | bytes 1572864 | tf_op jit(solution)/shard_map/all_to_all | solution.py:111
  119.6 29.0 %collective-permute-start.6 = (bf16[1,1,512,384]{3,2,1,0:T(8,128)(2,1)}, bf16[1,1,512,384]{3,2,1,0:T(8,128)(2,1)}, u32[]{:S(2)}, u32[]{:S(2)}) collective-permute-start(bf16[1,1,512,384]{3,2,1,0:T(8,128)(2,1)} %fusion.60), channel_id=1, source_target_pairs={{0,16},{1,17},{2,18},{3,19},{4,20},{5,21},{6,22},{7,23},{8,24},{9,... | collective-permute-start | bytes 1179656 | tf_op jit(solution)/shard_map/ppermute | solution.py:176
  123.9 24.6 %collective-permute-start.5 = (bf16[1,1,512,384]{3,2,1,0:T(8,128)(2,1)S(1)}, bf16[1,1,512,384]{3,2,1,0:T(8,128)(2,1)}, u32[]{:S(2)}, u32[]{:S(2)}) collective-permute-start(bf16[1,1,512,384]{3,2,1,0:T(8,128)(2,1)S(1)} %bitcast.183), channel_id=1, source_target_pairs={{16,0},{17,1},{18,2},{19,3},{20,4},{21,5},{22,6},{23,7},{24,8},{25... | collective-permute-start | bytes 1179656 | tf_op jit(solution)/shard_map/ppermute | solution.py:177
  140.2 3.8 %copy-start.4 = (bf16[1,384,768]{2,1,0:T(8,128)(2,1)S(1)}, bf16[1,384,768]{2,1,0:T(8,128)(2,1)}, u32[]{:S(2)}) copy-start(bf16[1,384,768]{2,1,0:T(8,128)(2,1)} %param.13) | copy-start | bytes 1769476
  140.2 3.8 %copy-start.13 = (f32[2,384]{1,0:T(2,128)S(1)}, f32[2,384]{1,0:T(2,128)}, u32[]{:S(2)}) copy-start(f32[2,384]{1,0:T(2,128)} %copy-done.12) | copy-start | bytes 9220
  140.2 3.8 %copy-start.15 = (f32[2,384]{1,0:T(2,128)S(1)}, f32[2,384]{1,0:T(2,128)}, u32[]{:S(2)}) copy-start(f32[2,384]{1,0:T(2,128)} %copy-done.14) | copy-start | bytes 9220
  140.3 3.8 %copy-start.17 = (f32[384]{0:T(512)S(1)}, f32[384]{0:T(512)}, u32[]{:S(2)}) copy-start(f32[384]{0:T(512)} %copy-done.16) | copy-start | bytes 4612
  (62 other events, 55.3 us)

commit v19 on v18

--- a/solution.py
+++ b/solution.py
@@ -41,13 +41,18 @@
     return out, (modulated, inv_rms, pre)
 
 
+def silu_slope(saved):
+    modulated, inv_rms, pre = saved
+    gate = jax.nn.sigmoid(pre)
+    return modulated, inv_rms, gate * (1.0 + pre * (1.0 - gate))
+
+
 def spatial_backward(saved, grad, stencil_taps, modulate, norm_gain, w_in, w_out):
-    modulated, inv_rms, pre = saved
+    modulated, inv_rms, slope = saved
     clip_count, frame_count, pixel_count, channels = grad.shape
     flat_grad = grad.reshape(-1, channels)
     hidden_grad = jnp.dot(flat_grad, w_out.T, preferred_element_type=jnp.float32).astype(jnp.bfloat16)
-    gate = jax.nn.sigmoid(pre)
-    pre_grad = hidden_grad.astype(jnp.float32) * (gate * (1.0 + pre * (1.0 - gate)))
+    pre_grad = hidden_grad.astype(jnp.float32) * slope
     pre_grad = lax.optimization_barrier(pre_grad.astype(jnp.bfloat16))
     normed_grad = jnp.dot(pre_grad, w_in.T, preferred_element_type=jnp.float32).astype(jnp.bfloat16)
     scaled_grad = normed_grad.astype(jnp.float32).reshape(grad.shape) * norm_gain
@@ -166,12 +171,12 @@
     clip_act, clip_seed = clip_act[None], clip_seed[None]
     second_params = for_clip(second_seg, plane)
     second_mixed, second_saved = spatial_forward(clip_act, *second_params)
-    second_grad = spatial_backward(second_saved, clip_seed, *second_params)
-
-    tail_out, _ = temporal_cross(
-        jnp.concatenate([second_grad, second_mixed]), jnp.stack([first_band[::-1], second_band]), ()
-    )
-    first_grad = spatial_backward(first_saved, tail_out, *own)
+    second_grad = spatial_backward(silu_slope(second_saved), clip_seed, *second_params)
+
+    tail_out, first_prepared = temporal_cross(
+        jnp.concatenate([second_grad, second_mixed]), jnp.stack([first_band[::-1], second_band]), silu_slope(first_saved)
+    )
+    first_grad = spatial_backward(first_prepared, tail_out, *own)
 
     sent_second_grad = lax.ppermute(second_grad, "section", perm=[(0, 1)])
     other_act = lax.ppermute(clip_act, "section", perm=[(1, 0)])

time: 154 us -> 151 us (0.981)
  waiting for transfers between devices: 52.2 us -> 49.6 us
    unnamed x161 -> x163, local copies, waits for them, and re-layouts: 7.44 us -> 8.98 us
  transfers between devices with their start and end apart: 11 -> 11, of which waited for: 4 -> 4; matrix products, arithmetic and copies ran while one was open for 23% -> 24% of each run, Pallas kernels for 0% -> 0%
where the time goes in v19:
time: 151 us; the launch traced here: 150 us
  waiting for transfers between devices  49.6 us (33%)
  other arithmetic  31.1 us (21%)
  starting transfers between devices  30 us (20%)
  local copies, waits for them, and re-layouts  25.5 us (17%)
  matrix products  11.8 us (8%)
  between operations  1.62 us (1%)
    all_to_all x2, waiting for transfers between devices, temporal_cross(): lax.all_to_all(banded, ('section', 'seq'), split_axis=1, concat_axis=2, t...  33.7 us
    all_to_all x2, waiting for transfers between devices, temporal_cross(): lax.all_to_all(grouped, 'seq', split_axis=2, concat_axis=1, tiled=True)  11 us
    all_to_all x2, starting transfers between devices, temporal_cross(): lax.all_to_all(grouped, 'seq', split_axis=2, concat_axis=1, tiled=True)  11 us
    all_to_all x2, starting transfers between devices, temporal_cross(): lax.all_to_all(banded, ('section', 'seq'), split_axis=1, concat_axis=2, t...  10.9 us
    unnamed x163, local copies, waits for them, and re-layouts  8.98 us
    select_n x4, other arithmetic, on_device(): jnp.where(first, r, o)  5.53 us
    ppermute x2, waiting for transfers between devices, fetch_halves(): got = lax.ppermute(mine, 'section', perm=swap)  4.87 us
    ppermute x1, starting transfers between devices, on_device(): sent_second_grad = lax.ppermute(second_grad, 'section', perm=[(0, 1)])  4.41 us
  transfers between devices with their start and end apart: 11, of which 4 were waited for; matrix products, arithmetic and copies ran while one was open for 24% of the time, Pallas kernels for 0%

profile of v19, /device:TPU:0, one launch (start us, length us, event | category | flops | bytes accessed | tf_op | source)
XLA Modules:
  0.0 149.6 jit_solution(11242576046616777178)
XLA Ops:
  6.2 3.2 %add_multiply_fusion = (f32[1024,768]{1,0:T(8,128)}, bf16[1024,768]{1,0:T(8,128)(2,1)S(1)}) fusion(bf16[1024,384]{1,0:T(8,128)(2,1)S(1)} %bitcast.178, bf16[1,384,768]{2,1,0:T(8,128)(2,1)S(1)} %copy-done.6), kind=kOutput, calls=%fused_computation.17 | convolution fusion | flops 611057664 | bytes 6094848 | tf_op jit(solution)/shard_map/dot_general | solution.py:37
  9.4 1.9 %fusion.47 = bf16[2,1,512,384]{3,2,0,1:T(8,128)(2,1)} fusion(bf16[2,512,768]{2,1,0:T(8,128)(2,1)S(1)} %bitcast.195, bf16[1,768,384]{2,1,0:T(8,128)(2,1)S(1)} %copy-done.4, bf16[2,1,512,384]{3,2,1,0:T(8,128)(2,1)S(1)} %copy-done.10), kind=kOutput, calls=%fused_computation.79 | convolution fusion | flops 605159424 | bytes 3735552 | tf_op jit(solution)/shard_map/dot_general | solution.py:39
  13.6 7.4 %all-to-all-start = ((bf16[2,1,16,32,384]{4,3,0,1,2:T(8,128)(2,1)}), bf16[2,1,16,32,384]{4,3,0,1,2:T(8,128)(2,1)S(1)}, u32[]{:S(2)}, u32[]{:S(2)}) async-start(bf16[2,1,16,32,384]{4,3,0,1,2:T(8,128)(2,1)} %copy.22), calls=%async_computation | async-start | bytes 1572864 | tf_op jit(solution)/shard_map/all_to_all | solution.py:111
  23.5 1.4 pad_maximum_fusion.1
  25.9 1.7 %collective-permute-start.1 = (bf16[192,768]{1,0:T(8,128)(2,1)}, bf16[192,768]{1,0:T(8,128)(2,1)}, u32[]{:S(2)}, u32[]{:S(2)}) collective-permute-start(bf16[192,768]{1,0:T(8,128)(2,1)} %constant_dynamic-slice_fusion.1), channel_id=1, source_target_pairs={{0,16},{16,0},{1,17},{17,1},{2,18},{18,2},{3,19},{19,3},{4,20},{20... | collective-permute-start | bytes 884744 | tf_op jit(solution)/shard_map/ppermute | solution.py:141
  28.7 2.0 %rev.8 = f32[9,384]{1,0:T(8,128)} reverse(f32[9,384]{1,0:T(8,128)} %get-tuple-element.30), dimensions={0} | reverse | bytes 27648 | tf_op jit(solution)/shard_map/rev | solution.py:167
  30.7 1.3 slice.395
  33.3 1.5 slice_select_fusion.1
  36.9 4.9 %collective-permute-done.3 = bf16[384,384]{1,0:T(8,128)(2,1)} collective-permute-done((bf16[384,384]{1,0:T(8,128)(2,1)}, bf16[384,384]{1,0:T(8,128)(2,1)}, u32[]{:S(2)}, u32[]{:S(2)}) %collective-permute-start.3) | collective-permute-done | bytes 294944 | tf_op jit(solution)/shard_map/ppermute | solution.py:141
  42.4 2.1 %fusion.62 = bf16[384,768]{1,0:T(8,128)(2,1)} fusion(bf16[192,768]{1,0:T(8,128)(2,1)S(1)} %collective-permute-done.2, bf16[192,768]{1,0:T(8,128)(2,1)} %collective-permute-done.1, pred[]{:T(512)S(6)} %eq.10, pred[]{:T(512)S(6)} %eq.9, bf16[1,384,768]{2,1,0:T(8,128)(2,1)S(1)} %copy-done.7), kind=kLoop, calls=%fused_computation.135 | loop fusion | flops 2949120 | bytes 1769474 | tf_op jit(solution)/shard_map/jit(_where)/select_n | solution.py:157
  44.5 2.1 %fusion.63 = bf16[768,384]{1,0:T(8,128)(2,1)} fusion(bf16[384,384]{1,0:T(8,128)(2,1)S(1)} %collective-permute-done.4, bf16[384,384]{1,0:T(8,128)(2,1)} %collective-permute-done.3, pred[]{:T(512)S(6)} %eq.10, pred[]{:T(512)S(6)} %eq.9, bf16[1,768,384]{2,1,0:T(8,128)(2,1)S(1)} %copy-done.4), kind=kLoop, calls=%fused_computation.137 | loop fusion | flops 2949120 | bytes 1769474 | tf_op jit(solution)/shard_map/jit(_where)/select_n | solution.py:157
  47.5 1.8 %fusion.15 = bf16[2,16,32,384]{3,2,1,0:T(8,128)(2,1)} fusion(f32[2,16,32,384]{3,2,1,0:T(8,128)S(1)} %convert_element_type.355, f32[384]{0:T(512)S(1)} %get-tuple-element.60, f32[384]{0:T(512)S(1)} %copy-done.68, f32[384]{0:T(512)S(1)} %copy-done.69, f32[384]{0:T(512)S(1)} %copy-done.70, f32[384]{0:T(512)S(1)} %copy-done.71, f32[384]{0:T(512)S(1)} %copy-done.72, ...), kind=kLoop, calls=%fused_computation.44 | loop fusion | flops 7471104 | bytes 2373120 | tf_op jit(solution)/shard_map/convert_element_type | solution.py:76
  49.3 6.0 %all-to-all-start.1 = ((bf16[1,32,1,32,384]{4,3,2,0,1:T(8,128)(2,1)}), bf16[1,32,1,32,384]{4,3,2,0,1:T(8,128)(2,1)S(1)}, u32[]{:S(2)}, u32[]{:S(2)}) async-start(bf16[1,32,1,32,384]{4,3,2,0,1:T(8,128)(2,1)} %bitcast.15), calls=%async_computation.1 | async-start | bytes 1572864 | tf_op jit(solution)/shard_map/all_to_all | solution.py:116
  56.0 20.6 %all-to-all-done.1 = bf16[1,32,1,32,384]{4,3,2,0,1:T(8,128)(2,1)S(1)} async-done(((bf16[1,32,1,32,384]{4,3,2,0,1:T(8,128)(2,1)}), bf16[1,32,1,32,384]{4,3,2,0,1:T(8,128)(2,1)S(1)}, u32[]{:S(2)}, u32[]{:S(2)}) %all-to-all-start.1) | async-done | bytes 786464 | tf_op jit(solution)/shard_map/all_to_all | solution.py:116
  87.7 3.6 %all-to-all-start.2 = ((bf16[2,1,16,32,384]{4,3,1,0,2:T(8,128)(2,1)}), bf16[2,1,16,32,384]{4,3,1,0,2:T(8,128)(2,1)S(1)}, u32[]{:S(2)}, u32[]{:S(2)}) async-start(bf16[2,1,16,32,384]{4,3,1,0,2:T(8,128)(2,1)} %copy.25), calls=%async_computation.2 | async-start | bytes 1572864 | tf_op jit(solution)/shard_map/all_to_all | solution.py:111
  92.2 2.0 %rev.9 = f32[9,384]{1,0:T(8,128)} reverse(f32[9,384]{1,0:T(8,128)} %get-tuple-element.45), dimensions={0} | reverse | bytes 27648 | tf_op jit(solution)/shard_map/rev | solution.py:177
  99.0 11.0 %all-to-all-done.2 = bf16[2,1,16,32,384]{4,3,1,0,2:T(8,128)(2,1)S(1)} async-done(((bf16[2,1,16,32,384]{4,3,1,0,2:T(8,128)(2,1)}), bf16[2,1,16,32,384]{4,3,1,0,2:T(8,128)(2,1)S(1)}, u32[]{:S(2)}, u32[]{:S(2)}) %all-to-all-start.2) | async-done | bytes 786464 | tf_op jit(solution)/shard_map/all_to_all | solution.py:111
  110.8 2.3 %fusion.33 = bf16[2,16,32,384]{3,2,1,0:T(8,128)(2,1)} fusion(f32[2,16,32,384]{3,2,1,0:T(8,128)S(1)} %convert_element_type.375, f32[2,384]{1,0:T(2,128)S(1)} %bitcast.186, f32[2,384]{1,0:T(2,128)S(1)} %bitcast.187, f32[2,384]{1,0:T(2,128)S(1)} %bitcast.188, f32[2,384]{1,0:T(2,128)S(1)} %bitcast.189, f32[2,384]{1,0:T(2,128)S(1)} %bitcast.190, ...), kind=kLoop, calls=%fused_computation.62 | loop fusion | flops 7471104 | bytes 2386944 | tf_op jit(solution)/shard_map/convert_element_type | solution.py:76
  113.2 4.9 %all-to-all-start.3 = ((bf16[1,32,1,32,384]{4,3,2,0,1:T(8,128)(2,1)}), bf16[1,32,1,32,384]{4,3,2,0,1:T(8,128)(2,1)S(1)}, u32[]{:S(2)}, u32[]{:S(2)}) async-start(bf16[1,32,1,32,384]{4,3,2,0,1:T(8,128)(2,1)} %bitcast.168), calls=%async_computation.3 | async-start | bytes 1572864 | tf_op jit(solution)/shard_map/all_to_all | solution.py:116
  118.1 2.0 %fusion.59 = bf16[1,1,512,384]{3,2,1,0:T(8,128)(2,1)} fusion(f32[1,1,512,384]{3,2,1,0:T(8,128)} %bitcast.159, f32[1,1,32,16,384]{4,3,2,1,0:T(8,128)S(1)} %fusion.65), kind=kLoop, calls=%fused_computation.117 | loop fusion | flops 393216 | bytes 1966080 | tf_op jit(solution)/shard_map/convert_element_type | solution.py:65
  120.1 4.4 %collective-permute-start.6 = (bf16[1,1,512,384]{3,2,1,0:T(8,128)(2,1)}, bf16[1,1,512,384]{3,2,1,0:T(8,128)(2,1)}, u32[]{:S(2)}, u32[]{:S(2)}) collective-permute-start(bf16[1,1,512,384]{3,2,1,0:T(8,128)(2,1)} %fusion.59), channel_id=1, source_target_pairs={{0,16},{1,17},{2,18},{3,19},{4,20},{5,21},{6,22},{7,23},{8,24},{9,... | collective-permute-start | bytes 1179656 | tf_op jit(solution)/shard_map/ppermute | solution.py:181
  126.6 13.1 %all-to-all-done.3 = bf16[1,32,1,32,384]{4,3,2,0,1:T(8,128)(2,1)S(1)} async-done(((bf16[1,32,1,32,384]{4,3,2,0,1:T(8,128)(2,1)}), bf16[1,32,1,32,384]{4,3,2,0,1:T(8,128)(2,1)S(1)}, u32[]{:S(2)}, u32[]{:S(2)}) %all-to-all-start.3) | async-done | bytes 786464 | tf_op jit(solution)/shard_map/all_to_all | solution.py:116
  139.7 3.1 %multiply_convert_fusion = bf16[1024,768]{1,0:T(8,128)(2,1)S(1)} fusion(f32[1024,768]{1,0:T(8,128)} %get-tuple-element.48, bf16[1024,384]{1,0:T(8,128)(2,1)S(1)} %bitcast.157, bf16[1,768,384]{2,1,0:T(8,128)(2,1)} %param.14), kind=kOutput, calls=%fused_computation.16 | convolution fusion | flops 607125504 | bytes 6094848 | tf_op jit(solution)/shard_map/dot_general | solution.py:54
  146.9 2.6 %fusion.57 = (bf16[1,2,1,512,384]{4,3,2,1,0:T(8,128)(2,1)}, bf16[1,2,1,512,384]{4,3,2,1,0:T(8,128)(2,1)}) fusion(bf16[1,2,1,512,384]{4,3,2,1,0:T(8,128)(2,1)S(1)} %bitcast.172, bf16[1,2,1,512,384]{4,3,2,1,0:T(8,128)(2,1)S(1)} %bitcast.158, bf16[1,1,1,512,384]{4,3,2,1,0:T(8,128)(2,1)S(1)} %bitcast.176, bf16[1,1,1,512,384]{4,3,2,1,0:T(8,128)(2,1)} %bitcast.44, ...), kind=kLoop, calls=%fused_computation.111 | loop fusion | flops 3145728 | bytes 4718593 | tf_op jit(solution)/shard_map/jit(_where)/select_n | solution.py:184
  (230 shorter events, 41.0 us)
Async XLA Ops:
  0.6 2.0 %copy-start.13 = (f32[1,9,384]{2,0,1:T(1,128)S(1)}, f32[1,9,384]{2,0,1:T(1,128)}, u32[]{:S(2)}) copy-start(f32[1,9,384]{2,0,1:T(1,128)} %param.10) | copy-start | bytes 41476
  2.8 2.3 %copy-start.21 = (f32[2,384]{1,0:T(2,128)}, f32[2,384]{1,0:T(2,128)S(1)}, u32[]{:S(2)}) copy-start(f32[2,384]{1,0:T(2,128)S(1)} %get-tuple-element.119) | copy-start | bytes 9220
  6.2 3.2 %copy-start.4 = (bf16[1,768,384]{2,1,0:T(8,128)(2,1)S(1)}, bf16[1,768,384]{2,1,0:T(8,128)(2,1)}, u32[]{:S(2)}) copy-start(bf16[1,768,384]{2,1,0:T(8,128)(2,1)} %param.14) | copy-start | bytes 1769476
  6.2 3.2 %copy-start.10 = (bf16[2,1,512,384]{3,2,1,0:T(8,128)(2,1)S(1)}, bf16[2,1,512,384]{3,2,1,0:T(8,128)(2,1)}, u32[]{:S(2)}) copy-start(bf16[2,1,512,384]{3,2,1,0:T(8,128)(2,1)} %param.8) | copy-start | bytes 2359300
  9.4 1.9 %copy-start.9 = (bf16[2,1,512,384]{3,2,1,0:T(8,128)(2,1)S(1)}, bf16[2,1,512,384]{3,2,1,0:T(8,128)(2,1)}, u32[]{:S(2)}) copy-start(bf16[2,1,512,384]{3,2,1,0:T(8,128)(2,1)} %param.9) | copy-start | bytes 2359300
  12.5 12.7 %copy-start.7 = (bf16[1,384,768]{2,1,0:T(8,128)(2,1)S(1)}, bf16[1,384,768]{2,1,0:T(8,128)(2,1)}, u32[]{:S(2)}) copy-start(bf16[1,384,768]{2,1,0:T(8,128)(2,1)} %param.13) | copy-start | bytes 1769476
  13.6 33.1 %all-to-all-start = ((bf16[2,1,16,32,384]{4,3,0,1,2:T(8,128)(2,1)}), bf16[2,1,16,32,384]{4,3,0,1,2:T(8,128)(2,1)S(1)}, u32[]{:S(2)}, u32[]{:S(2)}) async-start(bf16[2,1,16,32,384]{4,3,0,1,2:T(8,128)(2,1)} %copy.22), calls=%async_computation | async-start | bytes 1572864 | tf_op jit(solution)/shard_map/all_to_all | solution.py:111
  24.9 5.9 %collective-permute-start = (f32[23,384]{1,0:T(8,128)}, f32[23,384]{1,0:T(8,128)}, u32[]{:S(2)}, u32[]{:S(2)}) collective-permute-start(f32[23,384]{1,0:T(8,128)} %pad_maximum_fusion.1), channel_id=1, source_target_pairs={{0,16},{16,0},{1,17},{17,1},{2,18},{18,2},{3,19},{19,3},{4,20},{20... | collective-permute-start | bytes 105992 | tf_op jit(solution)/shard_map/ppermute | solution.py:146
  25.9 10.3 %collective-permute-start.1 = (bf16[192,768]{1,0:T(8,128)(2,1)}, bf16[192,768]{1,0:T(8,128)(2,1)}, u32[]{:S(2)}, u32[]{:S(2)}) collective-permute-start(bf16[192,768]{1,0:T(8,128)(2,1)} %constant_dynamic-slice_fusion.1), channel_id=1, source_target_pairs={{0,16},{16,0},{1,17},{17,1},{2,18},{18,2},{3,19},{19,3},{4,20},{20... | collective-permute-start | bytes 884744 | tf_op jit(solution)/shard_map/ppermute | solution.py:141
  28.4 13.4 %collective-permute-start.3 = (bf16[384,384]{1,0:T(8,128)(2,1)}, bf16[384,384]{1,0:T(8,128)(2,1)}, u32[]{:S(2)}, u32[]{:S(2)}) collective-permute-start(bf16[384,384]{1,0:T(8,128)(2,1)} %constant_dynamic-slice_fusion), channel_id=1, source_target_pairs={{0,16},{16,0},{1,17},{17,1},{2,18},{18,2},{3,19},{19,3},{4,20},{20... | collective-permute-start | bytes 884744 | tf_op jit(solution)/shard_map/ppermute | solution.py:141
  36.2 6.2 %collective-permute-start.2 = (bf16[192,768]{1,0:T(8,128)(2,1)}, bf16[192,768]{1,0:T(8,128)(2,1)S(1)}, u32[]{:S(2)}, u32[]{:S(2)}) collective-permute-start(bf16[192,768]{1,0:T(8,128)(2,1)} %collective-permute-done.1), channel_id=1, source_target_pairs={{0,1},{1,0},{2,3},{3,2},{4,5},{5,4},{6,7},{7,6},{8,9},{9,8},{10,11... | collective-permute-start | bytes 884744 | tf_op jit(solution)/shard_map/ppermute | solution.py:142
  41.8 2.8 %collective-permute-start.4 = (bf16[384,384]{1,0:T(8,128)(2,1)}, bf16[384,384]{1,0:T(8,128)(2,1)S(1)}, u32[]{:S(2)}, u32[]{:S(2)}) collective-permute-start(bf16[384,384]{1,0:T(8,128)(2,1)} %collective-permute-done.3), channel_id=1, source_target_pairs={{0,1},{1,0},{2,3},{3,2},{4,5},{5,4},{6,7},{7,6},{8,9},{9,8},{10,11... | collective-permute-start | bytes 884744 | tf_op jit(solution)/shard_map/ppermute | solution.py:142
  47.5 7.9 %copy-start.16 = (f32[9,384]{1,0:T(8,128)S(1)}, f32[9,384]{1,0:T(8,128)}, u32[]{:S(2)}) copy-start(f32[9,384]{1,0:T(8,128)} %get-tuple-element.39) | copy-start | bytes 41476
  49.3 27.3 %all-to-all-start.1 = ((bf16[1,32,1,32,384]{4,3,2,0,1:T(8,128)(2,1)}), bf16[1,32,1,32,384]{4,3,2,0,1:T(8,128)(2,1)S(1)}, u32[]{:S(2)}, u32[]{:S(2)}) async-start(bf16[1,32,1,32,384]{4,3,2,0,1:T(8,128)(2,1)} %bitcast.15), calls=%async_computation.1 | async-start | bytes 1572864 | tf_op jit(solution)/shard_map/all_to_all | solution.py:116
  55.3 22.3 %copy-start.17 = (f32[384]{0:T(512)}, f32[384]{0:T(512)S(1)}, u32[]{:S(2)}) copy-start(f32[384]{0:T(512)S(1)} %get-tuple-element.77) | copy-start | bytes 4612
  55.4 22.3 %copy-start.19 = (f32[384]{0:T(512)}, f32[384]{0:T(512)S(1)}, u32[]{:S(2)}) copy-start(f32[384]{0:T(512)S(1)} %get-tuple-element.78) | copy-start | bytes 4612
  56.0 21.6 %copy-start.42 = (f32[384]{0:T(512)}, f32[384]{0:T(512)S(1)}, u32[]{:S(2)}) copy-start(f32[384]{0:T(512)S(1)} %get-tuple-element.51) | copy-start | bytes 4612
  56.0 21.6 %copy-start.44 = (f32[384]{0:T(512)}, f32[384]{0:T(512)S(1)}, u32[]{:S(2)}) copy-start(f32[384]{0:T(512)S(1)} %get-tuple-element.52) | copy-start | bytes 4612
  87.7 22.3 %all-to-all-start.2 = ((bf16[2,1,16,32,384]{4,3,1,0,2:T(8,128)(2,1)}), bf16[2,1,16,32,384]{4,3,1,0,2:T(8,128)(2,1)S(1)}, u32[]{:S(2)}, u32[]{:S(2)}) async-start(bf16[2,1,16,32,384]{4,3,1,0,2:T(8,128)(2,1)} %copy.25), calls=%async_computation.2 | async-start | bytes 1572864 | tf_op jit(solution)/shard_map/all_to_all | solution.py:111
  113.2 26.5 %all-to-all-start.3 = ((bf16[1,32,1,32,384]{4,3,2,0,1:T(8,128)(2,1)}), bf16[1,32,1,32,384]{4,3,2,0,1:T(8,128)(2,1)S(1)}, u32[]{:S(2)}, u32[]{:S(2)}) async-start(bf16[1,32,1,32,384]{4,3,2,0,1:T(8,128)(2,1)} %bitcast.168), calls=%async_computation.3 | async-start | bytes 1572864 | tf_op jit(solution)/shard_map/all_to_all | solution.py:116
  118.1 7.7 %copy-start = (f32[1,16,1,32,384]{4,3,2,0,1:T(8,128)S(1)}, f32[1,16,1,32,384]{4,3,2,0,1:T(8,128)}, u32[]{:S(2)}) copy-start(f32[1,16,1,32,384]{4,3,2,0,1:T(8,128)} %get-tuple-element.93) | copy-start | bytes 2359300
  120.1 26.5 %collective-permute-start.6 = (bf16[1,1,512,384]{3,2,1,0:T(8,128)(2,1)}, bf16[1,1,512,384]{3,2,1,0:T(8,128)(2,1)}, u32[]{:S(2)}, u32[]{:S(2)}) collective-permute-start(bf16[1,1,512,384]{3,2,1,0:T(8,128)(2,1)} %fusion.59), channel_id=1, source_target_pairs={{0,16},{1,17},{2,18},{3,19},{4,20},{5,21},{6,22},{7,23},{8,24},{9,... | collective-permute-start | bytes 1179656 | tf_op jit(solution)/shard_map/ppermute | solution.py:181
  124.5 22.1 %collective-permute-start.5 = (bf16[1,1,512,384]{3,2,1,0:T(8,128)(2,1)S(1)}, bf16[1,1,512,384]{3,2,1,0:T(8,128)(2,1)}, u32[]{:S(2)}, u32[]{:S(2)}) collective-permute-start(bf16[1,1,512,384]{3,2,1,0:T(8,128)(2,1)S(1)} %bitcast.174), channel_id=1, source_target_pairs={{16,0},{17,1},{18,2},{19,3},{20,4},{21,5},{22,6},{23,7},{24,8},{25... | collective-permute-start | bytes 1179656 | tf_op jit(solution)/shard_map/ppermute | solution.py:182
  139.7 3.1 %copy-start.8 = (bf16[1,384,768]{2,1,0:T(8,128)(2,1)S(1)}, bf16[1,384,768]{2,1,0:T(8,128)(2,1)}, u32[]{:S(2)}) copy-start(bf16[1,384,768]{2,1,0:T(8,128)(2,1)} %param.13) | copy-start | bytes 1769476
  (63 other events, 47.5 us)

commit v20 on v19

--- a/solution.py
+++ b/solution.py
@@ -44,11 +44,12 @@
 def silu_slope(saved):
     modulated, inv_rms, pre = saved
     gate = jax.nn.sigmoid(pre)
-    return modulated, inv_rms, gate * (1.0 + pre * (1.0 - gate))
+    coefficient = modulated * (inv_rms * inv_rms * inv_rms / modulated.shape[-1])
+    return modulated, inv_rms, gate * (1.0 + pre * (1.0 - gate)), coefficient
 
 
 def spatial_backward(saved, grad, stencil_taps, modulate, norm_gain, w_in, w_out):
-    modulated, inv_rms, slope = saved
+    modulated, inv_rms, slope, coefficient = saved
     clip_count, frame_count, pixel_count, channels = grad.shape
     flat_grad = grad.reshape(-1, channels)
     hidden_grad = jnp.dot(flat_grad, w_out.T, preferred_element_type=jnp.float32).astype(jnp.bfloat16)
@@ -57,7 +58,7 @@
     normed_grad = jnp.dot(pre_grad, w_in.T, preferred_element_type=jnp.float32).astype(jnp.bfloat16)
     scaled_grad = normed_grad.astype(jnp.float32).reshape(grad.shape) * norm_gain
     inner = jnp.sum(scaled_grad * modulated, axis=-1, keepdims=True)
-    modulated_grad = inv_rms * scaled_grad - modulated * (inv_rms * inv_rms * inv_rms) * (inner / channels)
+    modulated_grad = inv_rms * scaled_grad - coefficient * inner
     stencil_grad = modulated_grad * (1.0 + modulate[:, 0])[:, None, None, :]
     spread = stencil(
         stencil_grad.reshape(clip_count, frame_count, H, W, channels), stencil_taps[::-1]

time: 151 us -> 154 us (1.020)
  other arithmetic: 31.1 us -> 33.7 us
  transfers between devices with their start and end apart: 11 -> 11, of which waited for: 4 -> 4; matrix products, arithmetic and copies ran while one was open for 24% -> 23% of each run, Pallas kernels for 0% -> 0%
where the time goes in v20:
time: 154 us; the launch traced here: 152 us
  waiting for transfers between devices  49.5 us (32%)
  other arithmetic  33.7 us (22%)
  starting transfers between devices  30 us (19%)
  local copies, waits for them, and re-layouts  25.7 us (17%)
  matrix products  11.8 us (8%)
  between operations  1.64 us (1%)
    all_to_all x2, waiting for transfers between devices, temporal_cross(): lax.all_to_all(banded, ('section', 'seq'), split_axis=1, concat_axis=2, t...  33.6 us
    all_to_all x2, starting transfers between devices, temporal_cross(): lax.all_to_all(grouped, 'seq', split_axis=2, concat_axis=1, tiled=True)  11 us
    all_to_all x2, waiting for transfers between devices, temporal_cross(): lax.all_to_all(grouped, 'seq', split_axis=2, concat_axis=1, tiled=True)  11 us
    all_to_all x2, starting transfers between devices, temporal_cross(): lax.all_to_all(banded, ('section', 'seq'), split_axis=1, concat_axis=2, t...  10.8 us
    unnamed x163, local copies, waits for them, and re-layouts  9.18 us
    select_n x4, other arithmetic, on_device(): jnp.where(first, r, o)  5.5 us
    ppermute x2, waiting for transfers between devices, fetch_halves(): got = lax.ppermute(mine, 'section', perm=swap)  4.87 us
    ppermute x1, starting transfers between devices, on_device(): sent_second_grad = lax.ppermute(second_grad, 'section', perm=[(0, 1)])  4.41 us
  transfers between devices with their start and end apart: 11, of which 4 were waited for; matrix products, arithmetic and copies ran while one was open for 23% of the time, Pallas kernels for 0%

profile of v20, /device:TPU:0, one launch (start us, length us, event | category | flops | bytes accessed | tf_op | source)
XLA Modules:
  0.0 152.3 jit_solution(4108836171583910866)
XLA Ops:
  5.1 1.4 broadcast_multiply_fusion
  8.2 3.2 %add_multiply_fusion = (f32[1024,768]{1,0:T(8,128)}, bf16[1024,768]{1,0:T(8,128)(2,1)S(1)}) fusion(bf16[1024,384]{1,0:T(8,128)(2,1)S(1)} %bitcast.176, bf16[1,384,768]{2,1,0:T(8,128)(2,1)S(1)} %copy-done.7), kind=kOutput, calls=%fused_computation.17 | convolution fusion | flops 611057664 | bytes 6094848 | tf_op jit(solution)/shard_map/dot_general | solution.py:37
  11.4 1.9 %fusion.47 = bf16[2,1,512,384]{3,2,0,1:T(8,128)(2,1)} fusion(bf16[2,512,768]{2,1,0:T(8,128)(2,1)S(1)} %bitcast.193, bf16[1,768,384]{2,1,0:T(8,128)(2,1)S(1)} %copy-done.5, bf16[2,1,512,384]{3,2,1,0:T(8,128)(2,1)S(1)} %copy-done.10), kind=kOutput, calls=%fused_computation.79 | convolution fusion | flops 605159424 | bytes 3735552 | tf_op jit(solution)/shard_map/dot_general | solution.py:39
  15.6 7.4 %all-to-all-start = ((bf16[2,1,16,32,384]{4,3,0,1,2:T(8,128)(2,1)}), bf16[2,1,16,32,384]{4,3,0,1,2:T(8,128)(2,1)S(1)}, u32[]{:S(2)}, u32[]{:S(2)}) async-start(bf16[2,1,16,32,384]{4,3,0,1,2:T(8,128)(2,1)} %copy.22), calls=%async_computation | async-start | bytes 1572864 | tf_op jit(solution)/shard_map/all_to_all | solution.py:112
  25.5 1.4 pad_maximum_fusion.1
  28.0 1.7 %collective-permute-start.1 = (bf16[192,768]{1,0:T(8,128)(2,1)}, bf16[192,768]{1,0:T(8,128)(2,1)}, u32[]{:S(2)}, u32[]{:S(2)}) collective-permute-start(bf16[192,768]{1,0:T(8,128)(2,1)} %constant_dynamic-slice_fusion.1), channel_id=1, source_target_pairs={{0,16},{16,0},{1,17},{17,1},{2,18},{18,2},{3,19},{19,3},{4,20},{20... | collective-permute-start | bytes 884744 | tf_op jit(solution)/shard_map/ppermute | solution.py:142
  30.8 2.0 %rev.8 = f32[9,384]{1,0:T(8,128)} reverse(f32[9,384]{1,0:T(8,128)} %get-tuple-element.31), dimensions={0} | reverse | bytes 27648 | tf_op jit(solution)/shard_map/rev | solution.py:168
  35.4 1.4 slice_select_fusion.1
  39.0 4.9 %collective-permute-done.3 = bf16[384,384]{1,0:T(8,128)(2,1)} collective-permute-done((bf16[384,384]{1,0:T(8,128)(2,1)}, bf16[384,384]{1,0:T(8,128)(2,1)}, u32[]{:S(2)}, u32[]{:S(2)}) %collective-permute-start.3) | collective-permute-done | bytes 294944 | tf_op jit(solution)/shard_map/ppermute | solution.py:142
  44.5 2.1 %fusion.62 = bf16[384,768]{1,0:T(8,128)(2,1)} fusion(bf16[192,768]{1,0:T(8,128)(2,1)S(1)} %collective-permute-done.2, bf16[192,768]{1,0:T(8,128)(2,1)} %collective-permute-done.1, pred[]{:T(512)S(6)} %eq.10, pred[]{:T(512)S(6)} %eq.9, bf16[1,384,768]{2,1,0:T(8,128)(2,1)S(1)} %copy-done.7), kind=kLoop, calls=%fused_computation.136 | loop fusion | flops 2949120 | bytes 1769474 | tf_op jit(solution)/shard_map/jit(_where)/select_n | solution.py:158
  46.6 2.1 %fusion.63 = bf16[768,384]{1,0:T(8,128)(2,1)} fusion(bf16[384,384]{1,0:T(8,128)(2,1)S(1)} %collective-permute-done.4, bf16[384,384]{1,0:T(8,128)(2,1)} %collective-permute-done.3, pred[]{:T(512)S(6)} %eq.10, pred[]{:T(512)S(6)} %eq.9, bf16[1,768,384]{2,1,0:T(8,128)(2,1)S(1)} %copy-done.5), kind=kLoop, calls=%fused_computation.138 | loop fusion | flops 2949120 | bytes 1769474 | tf_op jit(solution)/shard_map/jit(_where)/select_n | solution.py:158
  49.5 1.8 %fusion.15 = bf16[2,16,32,384]{3,2,1,0:T(8,128)(2,1)} fusion(f32[2,16,32,384]{3,2,1,0:T(8,128)S(1)} %convert_element_type.355, f32[384]{0:T(512)S(1)} %get-tuple-element.62, f32[384]{0:T(512)S(1)} %copy-done.69, f32[384]{0:T(512)S(1)} %copy-done.70, f32[384]{0:T(512)S(1)} %copy-done.71, f32[384]{0:T(512)S(1)} %copy-done.72, f32[384]{0:T(512)S(1)} %copy-done.73, ...), kind=kLoop, calls=%fused_computation.44 | loop fusion | flops 7471104 | bytes 2373120 | tf_op jit(solution)/shard_map/convert_element_type | solution.py:77
  51.3 6.0 %all-to-all-start.1 = ((bf16[1,32,1,32,384]{4,3,2,0,1:T(8,128)(2,1)}), bf16[1,32,1,32,384]{4,3,2,0,1:T(8,128)(2,1)S(1)}, u32[]{:S(2)}, u32[]{:S(2)}) async-start(bf16[1,32,1,32,384]{4,3,2,0,1:T(8,128)(2,1)} %bitcast.15), calls=%async_computation.1 | async-start | bytes 1572864 | tf_op jit(solution)/shard_map/all_to_all | solution.py:117
  58.1 20.6 %all-to-all-done.1 = bf16[1,32,1,32,384]{4,3,2,0,1:T(8,128)(2,1)S(1)} async-done(((bf16[1,32,1,32,384]{4,3,2,0,1:T(8,128)(2,1)}), bf16[1,32,1,32,384]{4,3,2,0,1:T(8,128)(2,1)S(1)}, u32[]{:S(2)}, u32[]{:S(2)}) %all-to-all-start.1) | async-done | bytes 786464 | tf_op jit(solution)/shard_map/all_to_all | solution.py:117
  89.8 3.6 %all-to-all-start.2 = ((bf16[2,1,16,32,384]{4,3,1,0,2:T(8,128)(2,1)}), bf16[2,1,16,32,384]{4,3,1,0,2:T(8,128)(2,1)S(1)}, u32[]{:S(2)}, u32[]{:S(2)}) async-start(bf16[2,1,16,32,384]{4,3,1,0,2:T(8,128)(2,1)} %copy.25), calls=%async_computation.2 | async-start | bytes 1572864 | tf_op jit(solution)/shard_map/all_to_all | solution.py:112
  94.2 2.0 %rev.9 = f32[9,384]{1,0:T(8,128)} reverse(f32[9,384]{1,0:T(8,128)} %get-tuple-element.46), dimensions={0} | reverse | bytes 27648 | tf_op jit(solution)/shard_map/rev | solution.py:178
  101.1 10.9 %all-to-all-done.2 = bf16[2,1,16,32,384]{4,3,1,0,2:T(8,128)(2,1)S(1)} async-done(((bf16[2,1,16,32,384]{4,3,1,0,2:T(8,128)(2,1)}), bf16[2,1,16,32,384]{4,3,1,0,2:T(8,128)(2,1)S(1)}, u32[]{:S(2)}, u32[]{:S(2)}) %all-to-all-start.2) | async-done | bytes 786464 | tf_op jit(solution)/shard_map/all_to_all | solution.py:112
  112.9 2.3 %fusion.33 = bf16[2,16,32,384]{3,2,1,0:T(8,128)(2,1)} fusion(f32[2,16,32,384]{3,2,1,0:T(8,128)S(1)} %convert_element_type.375, f32[2,384]{1,0:T(2,128)S(1)} %bitcast.184, f32[2,384]{1,0:T(2,128)S(1)} %bitcast.185, f32[2,384]{1,0:T(2,128)S(1)} %bitcast.186, f32[2,384]{1,0:T(2,128)S(1)} %bitcast.187, f32[2,384]{1,0:T(2,128)S(1)} %bitcast.188, ...), kind=kLoop, calls=%fused_computation.62 | loop fusion | flops 7471104 | bytes 2386944 | tf_op jit(solution)/shard_map/convert_element_type | solution.py:77
  115.2 4.9 %all-to-all-start.3 = ((bf16[1,32,1,32,384]{4,3,2,0,1:T(8,128)(2,1)}), bf16[1,32,1,32,384]{4,3,2,0,1:T(8,128)(2,1)S(1)}, u32[]{:S(2)}, u32[]{:S(2)}) async-start(bf16[1,32,1,32,384]{4,3,2,0,1:T(8,128)(2,1)} %bitcast.166), calls=%async_computation.3 | async-start | bytes 1572864 | tf_op jit(solution)/shard_map/all_to_all | solution.py:117
  120.1 2.1 %fusion.59 = bf16[1,1,512,384]{3,2,1,0:T(8,128)(2,1)} fusion(f32[1,1,512,384]{3,2,1,0:T(8,128)} %bitcast.157, f32[1,1,32,16,384]{4,3,2,1,0:T(8,128)S(1)} %fusion.65), kind=kLoop, calls=%fused_computation.117 | loop fusion | flops 393216 | bytes 1966080 | tf_op jit(solution)/shard_map/convert_element_type | solution.py:66
  122.1 4.4 %collective-permute-start.6 = (bf16[1,1,512,384]{3,2,1,0:T(8,128)(2,1)}, bf16[1,1,512,384]{3,2,1,0:T(8,128)(2,1)}, u32[]{:S(2)}, u32[]{:S(2)}) collective-permute-start(bf16[1,1,512,384]{3,2,1,0:T(8,128)(2,1)} %fusion.59), channel_id=1, source_target_pairs={{0,16},{1,17},{2,18},{3,19},{4,20},{5,21},{6,22},{7,23},{8,24},{9,... | collective-permute-start | bytes 1179656 | tf_op jit(solution)/shard_map/ppermute | solution.py:182
  128.7 13.0 %all-to-all-done.3 = bf16[1,32,1,32,384]{4,3,2,0,1:T(8,128)(2,1)S(1)} async-done(((bf16[1,32,1,32,384]{4,3,2,0,1:T(8,128)(2,1)}), bf16[1,32,1,32,384]{4,3,2,0,1:T(8,128)(2,1)S(1)}, u32[]{:S(2)}, u32[]{:S(2)}) %all-to-all-start.3) | async-done | bytes 786464 | tf_op jit(solution)/shard_map/all_to_all | solution.py:117
  141.7 3.1 %multiply_convert_fusion = bf16[1024,768]{1,0:T(8,128)(2,1)S(1)} fusion(f32[1024,768]{1,0:T(8,128)} %get-tuple-element.49, bf16[1024,384]{1,0:T(8,128)(2,1)S(1)} %bitcast.155, bf16[1,768,384]{2,1,0:T(8,128)(2,1)} %param.14), kind=kOutput, calls=%fused_computation.16 | convolution fusion | flops 607125504 | bytes 6094848 | tf_op jit(solution)/shard_map/dot_general | solution.py:55
  149.7 2.6 %fusion.57 = (bf16[1,2,1,512,384]{4,3,2,1,0:T(8,128)(2,1)}, bf16[1,2,1,512,384]{4,3,2,1,0:T(8,128)(2,1)}) fusion(bf16[1,2,1,512,384]{4,3,2,1,0:T(8,128)(2,1)S(1)} %bitcast.171, bf16[1,2,1,512,384]{4,3,2,1,0:T(8,128)(2,1)S(1)} %bitcast.156, bf16[1,1,1,512,384]{4,3,2,1,0:T(8,128)(2,1)S(1)} %bitcast.174, bf16[1,1,1,512,384]{4,3,2,1,0:T(8,128)(2,1)} %bitcast.43, ...), kind=kLoop, calls=%fused_computation.111 | loop fusion | flops 3145728 | bytes 4718593 | tf_op jit(solution)/shard_map/jit(_where)/select_n | solution.py:185
  (229 shorter events, 43.8 us)
Async XLA Ops:
  0.6 2.0 %copy-start.13 = (f32[1,9,384]{2,0,1:T(1,128)S(1)}, f32[1,9,384]{2,0,1:T(1,128)}, u32[]{:S(2)}) copy-start(f32[1,9,384]{2,0,1:T(1,128)} %param.10) | copy-start | bytes 41476
  2.8 2.3 %copy-start.21 = (f32[2,384]{1,0:T(2,128)}, f32[2,384]{1,0:T(2,128)S(1)}, u32[]{:S(2)}) copy-start(f32[2,384]{1,0:T(2,128)S(1)} %get-tuple-element.121) | copy-start | bytes 9220
  6.5 1.7 %copy-start.7 = (bf16[1,384,768]{2,1,0:T(8,128)(2,1)S(1)}, bf16[1,384,768]{2,1,0:T(8,128)(2,1)}, u32[]{:S(2)}) copy-start(bf16[1,384,768]{2,1,0:T(8,128)(2,1)} %param.13) | copy-start | bytes 1769476
  8.2 3.2 %copy-start.5 = (bf16[1,768,384]{2,1,0:T(8,128)(2,1)S(1)}, bf16[1,768,384]{2,1,0:T(8,128)(2,1)}, u32[]{:S(2)}) copy-start(bf16[1,768,384]{2,1,0:T(8,128)(2,1)} %param.14) | copy-start | bytes 1769476
  8.2 3.2 %copy-start.10 = (bf16[2,1,512,384]{3,2,1,0:T(8,128)(2,1)S(1)}, bf16[2,1,512,384]{3,2,1,0:T(8,128)(2,1)}, u32[]{:S(2)}) copy-start(bf16[2,1,512,384]{3,2,1,0:T(8,128)(2,1)} %param.8) | copy-start | bytes 2359300
  11.4 1.9 %copy-start.9 = (bf16[2,1,512,384]{3,2,1,0:T(8,128)(2,1)S(1)}, bf16[2,1,512,384]{3,2,1,0:T(8,128)(2,1)}, u32[]{:S(2)}) copy-start(bf16[2,1,512,384]{3,2,1,0:T(8,128)(2,1)} %param.9) | copy-start | bytes 2359300
  15.6 33.1 %all-to-all-start = ((bf16[2,1,16,32,384]{4,3,0,1,2:T(8,128)(2,1)}), bf16[2,1,16,32,384]{4,3,0,1,2:T(8,128)(2,1)S(1)}, u32[]{:S(2)}, u32[]{:S(2)}) async-start(bf16[2,1,16,32,384]{4,3,0,1,2:T(8,128)(2,1)} %copy.22), calls=%async_computation | async-start | bytes 1572864 | tf_op jit(solution)/shard_map/all_to_all | solution.py:112
  26.9 5.9 %collective-permute-start = (f32[23,384]{1,0:T(8,128)}, f32[23,384]{1,0:T(8,128)}, u32[]{:S(2)}, u32[]{:S(2)}) collective-permute-start(f32[23,384]{1,0:T(8,128)} %pad_maximum_fusion.1), channel_id=1, source_target_pairs={{0,16},{16,0},{1,17},{17,1},{2,18},{18,2},{3,19},{19,3},{4,20},{20... | collective-permute-start | bytes 105992 | tf_op jit(solution)/shard_map/ppermute | solution.py:147
  28.0 10.3 %collective-permute-start.1 = (bf16[192,768]{1,0:T(8,128)(2,1)}, bf16[192,768]{1,0:T(8,128)(2,1)}, u32[]{:S(2)}, u32[]{:S(2)}) collective-permute-start(bf16[192,768]{1,0:T(8,128)(2,1)} %constant_dynamic-slice_fusion.1), channel_id=1, source_target_pairs={{0,16},{16,0},{1,17},{17,1},{2,18},{18,2},{3,19},{19,3},{4,20},{20... | collective-permute-start | bytes 884744 | tf_op jit(solution)/shard_map/ppermute | solution.py:142
  30.4 13.4 %collective-permute-start.3 = (bf16[384,384]{1,0:T(8,128)(2,1)}, bf16[384,384]{1,0:T(8,128)(2,1)}, u32[]{:S(2)}, u32[]{:S(2)}) collective-permute-start(bf16[384,384]{1,0:T(8,128)(2,1)} %constant_dynamic-slice_fusion), channel_id=1, source_target_pairs={{0,16},{16,0},{1,17},{17,1},{2,18},{18,2},{3,19},{19,3},{4,20},{20... | collective-permute-start | bytes 884744 | tf_op jit(solution)/shard_map/ppermute | solution.py:142
  38.3 6.2 %collective-permute-start.2 = (bf16[192,768]{1,0:T(8,128)(2,1)}, bf16[192,768]{1,0:T(8,128)(2,1)S(1)}, u32[]{:S(2)}, u32[]{:S(2)}) collective-permute-start(bf16[192,768]{1,0:T(8,128)(2,1)} %collective-permute-done.1), channel_id=1, source_target_pairs={{0,1},{1,0},{2,3},{3,2},{4,5},{5,4},{6,7},{7,6},{8,9},{9,8},{10,11... | collective-permute-start | bytes 884744 | tf_op jit(solution)/shard_map/ppermute | solution.py:143
  43.8 2.7 %collective-permute-start.4 = (bf16[384,384]{1,0:T(8,128)(2,1)}, bf16[384,384]{1,0:T(8,128)(2,1)S(1)}, u32[]{:S(2)}, u32[]{:S(2)}) collective-permute-start(bf16[384,384]{1,0:T(8,128)(2,1)} %collective-permute-done.3), channel_id=1, source_target_pairs={{0,1},{1,0},{2,3},{3,2},{4,5},{5,4},{6,7},{7,6},{8,9},{9,8},{10,11... | collective-permute-start | bytes 884744 | tf_op jit(solution)/shard_map/ppermute | solution.py:143
  49.5 7.9 %copy-start.16 = (f32[9,384]{1,0:T(8,128)S(1)}, f32[9,384]{1,0:T(8,128)}, u32[]{:S(2)}) copy-start(f32[9,384]{1,0:T(8,128)} %get-tuple-element.40) | copy-start | bytes 41476
  51.3 27.3 %all-to-all-start.1 = ((bf16[1,32,1,32,384]{4,3,2,0,1:T(8,128)(2,1)}), bf16[1,32,1,32,384]{4,3,2,0,1:T(8,128)(2,1)S(1)}, u32[]{:S(2)}, u32[]{:S(2)}) async-start(bf16[1,32,1,32,384]{4,3,2,0,1:T(8,128)(2,1)} %bitcast.15), calls=%async_computation.1 | async-start | bytes 1572864 | tf_op jit(solution)/shard_map/all_to_all | solution.py:117
  57.4 22.3 %copy-start.17 = (f32[384]{0:T(512)}, f32[384]{0:T(512)S(1)}, u32[]{:S(2)}) copy-start(f32[384]{0:T(512)S(1)} %get-tuple-element.79) | copy-start | bytes 4612
  57.4 22.3 %copy-start.19 = (f32[384]{0:T(512)}, f32[384]{0:T(512)S(1)}, u32[]{:S(2)}) copy-start(f32[384]{0:T(512)S(1)} %get-tuple-element.80) | copy-start | bytes 4612
  58.1 21.6 %copy-start.43 = (f32[384]{0:T(512)}, f32[384]{0:T(512)S(1)}, u32[]{:S(2)}) copy-start(f32[384]{0:T(512)S(1)} %get-tuple-element.53) | copy-start | bytes 4612
  58.1 21.6 %copy-start.45 = (f32[384]{0:T(512)}, f32[384]{0:T(512)S(1)}, u32[]{:S(2)}) copy-start(f32[384]{0:T(512)S(1)} %get-tuple-element.54) | copy-start | bytes 4612
  89.8 22.3 %all-to-all-start.2 = ((bf16[2,1,16,32,384]{4,3,1,0,2:T(8,128)(2,1)}), bf16[2,1,16,32,384]{4,3,1,0,2:T(8,128)(2,1)S(1)}, u32[]{:S(2)}, u32[]{:S(2)}) async-start(bf16[2,1,16,32,384]{4,3,1,0,2:T(8,128)(2,1)} %copy.25), calls=%async_computation.2 | async-start | bytes 1572864 | tf_op jit(solution)/shard_map/all_to_all | solution.py:112
  115.2 26.5 %all-to-all-start.3 = ((bf16[1,32,1,32,384]{4,3,2,0,1:T(8,128)(2,1)}), bf16[1,32,1,32,384]{4,3,2,0,1:T(8,128)(2,1)S(1)}, u32[]{:S(2)}, u32[]{:S(2)}) async-start(bf16[1,32,1,32,384]{4,3,2,0,1:T(8,128)(2,1)} %bitcast.166), calls=%async_computation.3 | async-start | bytes 1572864 | tf_op jit(solution)/shard_map/all_to_all | solution.py:117
  120.1 7.8 %copy-start = (f32[1,16,1,32,384]{4,3,2,0,1:T(8,128)S(1)}, f32[1,16,1,32,384]{4,3,2,0,1:T(8,128)}, u32[]{:S(2)}) copy-start(f32[1,16,1,32,384]{4,3,2,0,1:T(8,128)} %get-tuple-element.95) | copy-start | bytes 2359300
  122.1 27.2 %collective-permute-start.6 = (bf16[1,1,512,384]{3,2,1,0:T(8,128)(2,1)}, bf16[1,1,512,384]{3,2,1,0:T(8,128)(2,1)}, u32[]{:S(2)}, u32[]{:S(2)}) collective-permute-start(bf16[1,1,512,384]{3,2,1,0:T(8,128)(2,1)} %fusion.59), channel_id=1, source_target_pairs={{0,16},{1,17},{2,18},{3,19},{4,20},{5,21},{6,22},{7,23},{8,24},{9,... | collective-permute-start | bytes 1179656 | tf_op jit(solution)/shard_map/ppermute | solution.py:182
  126.6 22.8 %collective-permute-start.5 = (bf16[1,1,512,384]{3,2,1,0:T(8,128)(2,1)S(1)}, bf16[1,1,512,384]{3,2,1,0:T(8,128)(2,1)}, u32[]{:S(2)}, u32[]{:S(2)}) collective-permute-start(bf16[1,1,512,384]{3,2,1,0:T(8,128)(2,1)S(1)} %bitcast.172), channel_id=1, source_target_pairs={{16,0},{17,1},{18,2},{19,3},{20,4},{21,5},{22,6},{23,7},{24,8},{25... | collective-permute-start | bytes 1179656 | tf_op jit(solution)/shard_map/ppermute | solution.py:183
  141.7 3.1 %copy-start.8 = (bf16[1,384,768]{2,1,0:T(8,128)(2,1)S(1)}, bf16[1,384,768]{2,1,0:T(8,128)(2,1)}, u32[]{:S(2)}) copy-start(bf16[1,384,768]{2,1,0:T(8,128)(2,1)} %param.13) | copy-start | bytes 1769476
  (63 other events, 48.1 us)

commit v21 on v19

--- a/solution.py
+++ b/solution.py
@@ -127,7 +127,7 @@
     tap_count = taps.shape[0]
     own = (taps, mod, gain, weight_in, weight_out)
 
-    first_mixed, first_saved = spatial_forward(clips, *own)
+    first_mixed, _ = spatial_forward(clips, *own)
     first_mixed, (taps, mod, gain, weight_in, weight_out, band) = lax.optimization_barrier(
         (first_mixed, own + (band,))
     )
@@ -169,6 +169,8 @@
         lead_in, lead_taps[None], (second_seg, first_band, second_band)
     )
     clip_act, clip_seed = clip_act[None], clip_seed[None]
+    again, _ = lax.optimization_barrier((clips, clip_act))
+    _, first_saved = spatial_forward(again, *own)
     second_params = for_clip(second_seg, plane)
     second_mixed, second_saved = spatial_forward(clip_act, *second_params)
     second_grad = spatial_backward(silu_slope(second_saved), clip_seed, *second_params)

time: 151 us -> 146 us (0.967)
  local copies, waits for them, and re-layouts: 25.5 us -> 17.8 us
  waiting for transfers between devices: 49.6 us -> 47.9 us
  other arithmetic: 31.1 us -> 32.8 us
    all_to_all x2, waiting for transfers between devices: 33.7 us -> 25.3 us  [temporal_cross(): lax.all_to_all(banded, ('section', 'seq'), split_axis=1, concat_axis=2, t...]
    ppermute x2, waiting for transfers between devices: 4.87 us -> 11.6 us  [fetch_halves(): got = lax.ppermute(mine, 'section', perm=swap)]
    rev x1, local copies, waits for them, and re-layouts: 2 us -> 0.06 us  [on_device(): lead_taps = jnp.where(first, band, band[::-1])]
    reduce_sum x2 -> x3, other arithmetic: 1.3 us -> 3.21 us  [spatial_forward(): jnp.mean(modulated * modulated, axis=-1, keepdims=True) + EPSILON]
    rev x1, local copies, waits for them, and re-layouts: 2 us -> 0.1 us  [on_device(): first_band[::-1]]
    unnamed x163 -> x149, local copies, waits for them, and re-layouts: 8.98 us -> 10.9 us
    convert_element_type x2 -> x3, other arithmetic: 1.19 us -> 2.86 us  [spatial_forward(): (modulated * inv_rms * norm_gain).astype(jnp.bfloat16).reshape(-1, channels)]
    ppermute x1, starting transfers between devices: 4.41 us -> 6.02 us  [on_device(): sent_second_grad = lax.ppermute(second_grad, 'section', perm=[(0, 1)])]
  transfers between devices with their start and end apart: 11 -> 11, of which waited for: 4 -> 6; matrix products, arithmetic and copies ran while one was open for 24% -> 21% of each run, Pallas kernels for 0% -> 0%
where the time goes in v21:
time: 146 us; the launch traced here: 144 us
  waiting for transfers between devices  47.9 us (33%)
  other arithmetic  32.8 us (22%)
  starting transfers between devices  31.5 us (22%)
  local copies, waits for them, and re-layouts  17.8 us (12%)
  matrix products  12.8 us (9%)
  between operations  1.64 us (1%)
    all_to_all x2, waiting for transfers between devices, temporal_cross(): lax.all_to_all(banded, ('section', 'seq'), split_axis=1, concat_axis=2, t...  25.3 us
    ppermute x2, waiting for transfers between devices, fetch_halves(): got = lax.ppermute(mine, 'section', perm=swap)  11.6 us
    all_to_all x2, starting transfers between devices, temporal_cross(): lax.all_to_all(grouped, 'seq', split_axis=2, concat_axis=1, tiled=True)  11.1 us
    unnamed x149, local copies, waits for them, and re-layouts  10.9 us
    all_to_all x2, starting transfers between devices, temporal_cross(): lax.all_to_all(banded, ('section', 'seq'), split_axis=1, concat_axis=2, t...  10.4 us
    all_to_all x2, waiting for transfers between devices, temporal_cross(): lax.all_to_all(grouped, 'seq', split_axis=2, concat_axis=1, tiled=True)  9.95 us
    ppermute x1, starting transfers between devices, on_device(): sent_second_grad = lax.ppermute(second_grad, 'section', perm=[(0, 1)])  6.02 us
    dot_general x3, matrix products, spatial_forward(): pre = jnp.dot(normed, w_in, preferred_element_type=jnp.float32)  4.76 us
  transfers between devices with their start and end apart: 11, of which 6 were waited for; matrix products, arithmetic and copies ran while one was open for 21% of the time, Pallas kernels for 0%

profile of v21, /device:TPU:0, one launch (start us, length us, event | category | flops | bytes accessed | tf_op | source)
XLA Modules:
  0.0 144.4 jit_solution(8826544664782749934)
XLA Ops:
  8.2 1.9 %fusion.50 = bf16[2,1,512,384]{3,2,0,1:T(8,128)(2,1)} fusion(bf16[2,512,768]{2,1,0:T(8,128)(2,1)S(1)} %bitcast.211, bf16[1,768,384]{2,1,0:T(8,128)(2,1)S(1)} %copy-done.4, bf16[2,1,512,384]{3,2,1,0:T(8,128)(2,1)S(1)} %copy-done.5), kind=kOutput, calls=%fused_computation.86 | convolution fusion | flops 605159424 | bytes 3735552 | tf_op jit(solution)/shard_map/dot_general | solution.py:39
  12.3 7.5 %all-to-all-start = ((bf16[2,1,16,32,384]{4,3,0,1,2:T(8,128)(2,1)}), bf16[2,1,16,32,384]{4,3,0,1,2:T(8,128)(2,1)S(1)}, u32[]{:S(2)}, u32[]{:S(2)}) async-start(bf16[2,1,16,32,384]{4,3,0,1,2:T(8,128)(2,1)} %copy.22), calls=%async_computation | async-start | bytes 1572864 | tf_op jit(solution)/shard_map/all_to_all | solution.py:111
  20.4 1.7 %collective-permute-start.3 = (bf16[384,384]{1,0:T(8,128)(2,1)S(1)}, bf16[384,384]{1,0:T(8,128)(2,1)}, u32[]{:S(2)}, u32[]{:S(2)}) collective-permute-start(bf16[384,384]{1,0:T(8,128)(2,1)S(1)} %constant_dynamic-slice_fusion), channel_id=1, source_target_pairs={{0,16},{16,0},{1,17},{17,1},{2,18},{18,2},{3,19},{19,3},{4,20},{20... | collective-permute-start | bytes 884744 | tf_op jit(solution)/shard_map/ppermute | solution.py:141
  24.4 6.3 %collective-permute-done.3 = bf16[384,384]{1,0:T(8,128)(2,1)} collective-permute-done((bf16[384,384]{1,0:T(8,128)(2,1)S(1)}, bf16[384,384]{1,0:T(8,128)(2,1)}, u32[]{:S(2)}, u32[]{:S(2)}) %collective-permute-start.3) | collective-permute-done | bytes 294944 | tf_op jit(solution)/shard_map/ppermute | solution.py:141
  31.2 5.3 %collective-permute-done.1 = bf16[192,768]{1,0:T(8,128)(2,1)} collective-permute-done((bf16[192,768]{1,0:T(8,128)(2,1)}, bf16[192,768]{1,0:T(8,128)(2,1)}, u32[]{:S(2)}, u32[]{:S(2)}) %collective-permute-start.1) | collective-permute-done | bytes 294944 | tf_op jit(solution)/shard_map/ppermute | solution.py:141
  36.6 2.1 %fusion.69 = bf16[768,384]{1,0:T(8,128)(2,1)} fusion(bf16[384,384]{1,0:T(8,128)(2,1)S(1)} %collective-permute-done.4, bf16[384,384]{1,0:T(8,128)(2,1)} %collective-permute-done.3, pred[]{:T(512)S(6)} %eq.10, pred[]{:T(512)S(6)} %eq.9, bf16[1,768,384]{2,1,0:T(8,128)(2,1)S(1)} %copy-done.4), kind=kLoop, calls=%fused_computation.150 | loop fusion | flops 2949120 | bytes 1769474 | tf_op jit(solution)/shard_map/jit(_where)/select_n | solution.py:157
  38.7 2.1 %fusion.68 = bf16[384,768]{1,0:T(8,128)(2,1)} fusion(bf16[192,768]{1,0:T(8,128)(2,1)S(1)} %collective-permute-done.2, bf16[192,768]{1,0:T(8,128)(2,1)} %collective-permute-done.1, pred[]{:T(512)S(6)} %eq.10, pred[]{:T(512)S(6)} %eq.9, bf16[1,384,768]{2,1,0:T(8,128)(2,1)S(1)} %copy-done.7), kind=kLoop, calls=%fused_computation.148 | loop fusion | flops 2949120 | bytes 1769474 | tf_op jit(solution)/shard_map/jit(_where)/select_n | solution.py:157
  41.1 1.8 %fusion.17 = bf16[2,16,32,384]{3,2,1,0:T(8,128)(2,1)} fusion(f32[2,16,32,384]{3,2,1,0:T(8,128)S(1)} %convert_element_type.380, f32[384]{0:T(512)S(1)} %get-tuple-element.62, f32[384]{0:T(512)S(1)} %get-tuple-element.63, f32[384]{0:T(512)S(1)} %get-tuple-element.64, f32[384]{0:T(512)S(1)} %get-tuple-element.65, f32[384]{0:T(512)S(1)} %get-tuple-element.66, ...), kind=kLoop, calls=%fused_computation.49 | loop fusion | flops 7471104 | bytes 2373120 | tf_op jit(solution)/shard_map/convert_element_type | solution.py:76
  42.9 5.5 %all-to-all-start.1 = ((bf16[1,32,1,32,384]{4,3,2,0,1:T(8,128)(2,1)}), bf16[1,32,1,32,384]{4,3,2,0,1:T(8,128)(2,1)S(1)}, u32[]{:S(2)}, u32[]{:S(2)}) async-start(bf16[1,32,1,32,384]{4,3,2,0,1:T(8,128)(2,1)} %bitcast.15), calls=%async_computation.1 | async-start | bytes 1572864 | tf_op jit(solution)/shard_map/all_to_all | solution.py:116
  55.1 14.7 %all-to-all-done.1 = bf16[1,32,1,32,384]{4,3,2,0,1:T(8,128)(2,1)S(1)} async-done(((bf16[1,32,1,32,384]{4,3,2,0,1:T(8,128)(2,1)}), bf16[1,32,1,32,384]{4,3,2,0,1:T(8,128)(2,1)S(1)}, u32[]{:S(2)}, u32[]{:S(2)}) %all-to-all-start.1) | async-done | bytes 786464 | tf_op jit(solution)/shard_map/all_to_all | solution.py:116
  72.5 1.4 rsqrt.46
  82.7 3.6 %all-to-all-start.2 = ((bf16[2,1,16,32,384]{4,3,1,0,2:T(8,128)(2,1)}), bf16[2,1,16,32,384]{4,3,1,0,2:T(8,128)(2,1)S(1)}, u32[]{:S(2)}, u32[]{:S(2)}) async-start(bf16[2,1,16,32,384]{4,3,1,0,2:T(8,128)(2,1)} %copy.25), calls=%async_computation.2 | async-start | bytes 1572864 | tf_op jit(solution)/shard_map/all_to_all | solution.py:111
  87.6 1.9 %multiply_reduce_fusion = (f32[2,32,16]{2,1,0:T(8,128)S(1)}, f32[2,1,32,16,384]{4,3,2,0,1:T(8,128)}) fusion(f32[2,384]{1,0:T(2,128)S(1)} %get-tuple-element.122, f32[2,384]{1,0:T(2,128)S(1)} %get-tuple-element.123, f32[2,1,32,16,384]{4,3,2,0,1:T(8,128)S(1)} %get-tuple-element.92, f32[384]{0:T(512)S(1)} %copy-done.20, f32[2,1,32,16,384]{4,3,2,0,1:T(8,128)S(1)} %convert.11, ...), kind=kLoop, calls=%fused_computation.95 | loop fusion | flops 4324352 | bytes 6306304 | tf_op jit(solution)/shard_map/reduce_sum | solution.py:35
  90.3 1.8 %multiply_convert_fusion.2 = (bf16[2,1,512,384]{3,2,0,1:T(8,128)(2,1)S(1)}, f32[2,1,512,384]{3,2,0,1:T(8,128)S(1)}) fusion(f32[2,512]{1,0:T(2,128)} %rsqrt.49, f32[384]{0:T(512)S(1)} %reduce.18, f32[2,384]{1,0:T(2,128)S(1)} %get-tuple-element.122, f32[2,384]{1,0:T(2,128)S(1)} %get-tuple-element.123, f32[2,1,32,16,384]{4,3,2,0,1:T(8,128)} %get-tuple-element.84), kind=kLoop, calls=%fused_computation.94 | loop fusion | flops 1966080 | bytes 3943936 | tf_op jit(solution)/shard_map/convert_element_type | solution.py:36
  92.1 2.9 %add_multiply_fusion = f32[1024,768]{1,0:T(8,128)} fusion(bf16[1024,384]{1,0:T(8,128)(2,1)S(1)} %bitcast.193, bf16[1,384,768]{2,1,0:T(8,128)(2,1)S(1)} %copy-done.8), kind=kOutput, calls=%fused_computation.17 | convolution fusion | flops 609484800 | bytes 4521984 | tf_op jit(solution)/shard_map/dot_general | solution.py:37
  95.0 9.9 %all-to-all-done.2 = bf16[2,1,16,32,384]{4,3,1,0,2:T(8,128)(2,1)S(1)} async-done(((bf16[2,1,16,32,384]{4,3,1,0,2:T(8,128)(2,1)}), bf16[2,1,16,32,384]{4,3,1,0,2:T(8,128)(2,1)S(1)}, u32[]{:S(2)}, u32[]{:S(2)}) %all-to-all-start.2) | async-done | bytes 786464 | tf_op jit(solution)/shard_map/all_to_all | solution.py:111
  105.8 2.3 %fusion.35 = bf16[2,16,32,384]{3,2,1,0:T(8,128)(2,1)} fusion(f32[2,16,32,384]{3,2,1,0:T(8,128)S(1)} %convert_element_type.402, f32[2,384]{1,0:T(2,128)S(1)} %bitcast.210, f32[2,384]{1,0:T(2,128)S(1)} %bitcast.203, f32[2,384]{1,0:T(2,128)S(1)} %bitcast.204, f32[2,384]{1,0:T(2,128)S(1)} %bitcast.205, f32[2,384]{1,0:T(2,128)S(1)} %bitcast.206, ...), kind=kLoop, calls=%fused_computation.67 | loop fusion | flops 7471104 | bytes 2386944 | tf_op jit(solution)/shard_map/convert_element_type | solution.py:76
  108.2 4.9 %all-to-all-start.3 = ((bf16[1,32,1,32,384]{4,3,2,0,1:T(8,128)(2,1)}), bf16[1,32,1,32,384]{4,3,2,0,1:T(8,128)(2,1)S(1)}, u32[]{:S(2)}, u32[]{:S(2)}) async-start(bf16[1,32,1,32,384]{4,3,2,0,1:T(8,128)(2,1)} %bitcast.182), calls=%async_computation.3 | async-start | bytes 1572864 | tf_op jit(solution)/shard_map/all_to_all | solution.py:116
  113.1 1.4 collective-permute-start.5
  114.5 1.9 %fusion.65 = bf16[1,1,512,384]{3,2,1,0:T(8,128)(2,1)} fusion(f32[1,1,512,384]{3,2,1,0:T(8,128)} %bitcast.173, f32[1,1,32,16,384]{4,3,2,1,0:T(8,128)S(1)} %fusion.71), kind=kLoop, calls=%fused_computation.130 | loop fusion | flops 393216 | bytes 1966080 | tf_op jit(solution)/shard_map/convert_element_type | solution.py:65
  116.4 6.0 %collective-permute-start.6 = (bf16[1,1,512,384]{3,2,1,0:T(8,128)(2,1)}, bf16[1,1,512,384]{3,2,1,0:T(8,128)(2,1)}, u32[]{:S(2)}, u32[]{:S(2)}) collective-permute-start(bf16[1,1,512,384]{3,2,1,0:T(8,128)(2,1)} %fusion.65), channel_id=1, source_target_pairs={{0,16},{1,17},{2,18},{3,19},{4,20},{5,21},{6,22},{7,23},{8,24},{9,... | collective-permute-start | bytes 1179656 | tf_op jit(solution)/shard_map/ppermute | solution.py:183
  123.9 10.7 %all-to-all-done.3 = bf16[1,32,1,32,384]{4,3,2,0,1:T(8,128)(2,1)S(1)} async-done(((bf16[1,32,1,32,384]{4,3,2,0,1:T(8,128)(2,1)}), bf16[1,32,1,32,384]{4,3,2,0,1:T(8,128)(2,1)S(1)}, u32[]{:S(2)}, u32[]{:S(2)}) %all-to-all-start.3) | async-done | bytes 786464 | tf_op jit(solution)/shard_map/all_to_all | solution.py:116
  134.6 3.1 %multiply_convert_fusion = bf16[1024,768]{1,0:T(8,128)(2,1)S(1)} fusion(f32[1024,768]{1,0:T(8,128)} %add_multiply_fusion, bf16[1024,384]{1,0:T(8,128)(2,1)S(1)} %bitcast.171, bf16[1,768,384]{2,1,0:T(8,128)(2,1)} %param.14), kind=kOutput, calls=%fused_computation.16 | convolution fusion | flops 607125504 | bytes 6094848 | tf_op jit(solution)/shard_map/dot_general | solution.py:54
  141.8 2.6 %fusion.63 = (bf16[1,2,1,512,384]{4,3,2,1,0:T(8,128)(2,1)}, bf16[1,2,1,512,384]{4,3,2,1,0:T(8,128)(2,1)}) fusion(bf16[1,2,1,512,384]{4,3,2,1,0:T(8,128)(2,1)S(1)} %bitcast.187, bf16[1,2,1,512,384]{4,3,2,1,0:T(8,128)(2,1)S(1)} %bitcast.172, bf16[1,1,1,512,384]{4,3,2,1,0:T(8,128)(2,1)S(1)} %bitcast.191, bf16[1,1,1,512,384]{4,3,2,1,0:T(8,128)(2,1)} %bitcast.48, ...), kind=kLoop, calls=%fused_computation.124 | loop fusion | flops 3145728 | bytes 4718593 | tf_op jit(solution)/shard_map/jit(_where)/select_n | solution.py:186
  (223 shorter events, 39.2 us)
Async XLA Ops:
  2.3 2.6 %copy-start.25 = (f32[384]{0:T(512)}, f32[384]{0:T(512)S(1)}, u32[]{:S(2)}) copy-start(f32[384]{0:T(512)S(1)} %get-tuple-element.71) | copy-start | bytes 4612
  2.3 2.6 %copy-start.28 = (f32[384]{0:T(512)}, f32[384]{0:T(512)S(1)}, u32[]{:S(2)}) copy-start(f32[384]{0:T(512)S(1)} %get-tuple-element.72) | copy-start | bytes 4612
  2.3 2.6 %copy-start.30 = (f32[384]{0:T(512)}, f32[384]{0:T(512)S(1)}, u32[]{:S(2)}) copy-start(f32[384]{0:T(512)S(1)} %get-tuple-element.75) | copy-start | bytes 4612
  2.3 2.6 %copy-start.32 = (f32[384]{0:T(512)}, f32[384]{0:T(512)S(1)}, u32[]{:S(2)}) copy-start(f32[384]{0:T(512)S(1)} %get-tuple-element.76) | copy-start | bytes 4612
  2.3 2.6 %copy-start.34 = (f32[384]{0:T(512)}, f32[384]{0:T(512)S(1)}, u32[]{:S(2)}) copy-start(f32[384]{0:T(512)S(1)} %get-tuple-element.77) | copy-start | bytes 4612
  2.3 2.6 %copy-start.36 = (f32[384]{0:T(512)}, f32[384]{0:T(512)S(1)}, u32[]{:S(2)}) copy-start(f32[384]{0:T(512)S(1)} %get-tuple-element.78) | copy-start | bytes 4612
  2.3 2.6 %copy-start.16 = (f32[384]{0:T(512)}, f32[384]{0:T(512)S(1)}, u32[]{:S(2)}) copy-start(f32[384]{0:T(512)S(1)} %get-tuple-element.70) | copy-start | bytes 4612
  2.3 2.6 %copy-start.19 = (f32[384]{0:T(512)}, f32[384]{0:T(512)S(1)}, u32[]{:S(2)}) copy-start(f32[384]{0:T(512)S(1)} %get-tuple-element.73) | copy-start | bytes 4612
  11.3 8.6 %copy-start.13 = (f32[1,2,2,384]{3,2,1,0:T(2,128)S(1)}, f32[1,2,2,384]{3,2,1,0:T(2,128)}, u32[]{:S(2)}) copy-start(f32[1,2,2,384]{3,2,1,0:T(2,128)} %param.11) | copy-start | bytes 18436
  12.3 12.0 %copy-start.12 = (f32[1,9,384]{2,0,1:T(1,128)S(1)}, f32[1,9,384]{2,0,1:T(1,128)}, u32[]{:S(2)}) copy-start(f32[1,9,384]{2,0,1:T(1,128)} %param.10) | copy-start | bytes 41476
  12.3 28.5 %all-to-all-start = ((bf16[2,1,16,32,384]{4,3,0,1,2:T(8,128)(2,1)}), bf16[2,1,16,32,384]{4,3,0,1,2:T(8,128)(2,1)S(1)}, u32[]{:S(2)}, u32[]{:S(2)}) async-start(bf16[2,1,16,32,384]{4,3,0,1,2:T(8,128)(2,1)} %copy.22), calls=%async_computation | async-start | bytes 1572864 | tf_op jit(solution)/shard_map/all_to_all | solution.py:111
  19.9 4.3 %collective-permute-start = (f32[23,384]{1,0:T(8,128)S(1)}, f32[23,384]{1,0:T(8,128)S(1)}, u32[]{:S(2)}, u32[]{:S(2)}) collective-permute-start(f32[23,384]{1,0:T(8,128)S(1)} %pad_maximum_fusion.1), channel_id=1, source_target_pairs={{0,16},{16,0},{1,17},{17,1},{2,18},{18,2},{3,19},{19,3},{4,20},{20... | collective-permute-start | bytes 105992 | tf_op jit(solution)/shard_map/ppermute | solution.py:146
  20.4 10.3 %collective-permute-start.3 = (bf16[384,384]{1,0:T(8,128)(2,1)S(1)}, bf16[384,384]{1,0:T(8,128)(2,1)}, u32[]{:S(2)}, u32[]{:S(2)}) collective-permute-start(bf16[384,384]{1,0:T(8,128)(2,1)S(1)} %constant_dynamic-slice_fusion), channel_id=1, source_target_pairs={{0,16},{16,0},{1,17},{17,1},{2,18},{18,2},{3,19},{19,3},{4,20},{20... | collective-permute-start | bytes 884744 | tf_op jit(solution)/shard_map/ppermute | solution.py:141
  22.8 13.7 %collective-permute-start.1 = (bf16[192,768]{1,0:T(8,128)(2,1)}, bf16[192,768]{1,0:T(8,128)(2,1)}, u32[]{:S(2)}, u32[]{:S(2)}) collective-permute-start(bf16[192,768]{1,0:T(8,128)(2,1)} %constant_dynamic-slice_fusion.1), channel_id=1, source_target_pairs={{0,16},{16,0},{1,17},{17,1},{2,18},{18,2},{3,19},{19,3},{4,20},{20... | collective-permute-start | bytes 884744 | tf_op jit(solution)/shard_map/ppermute | solution.py:141
  30.7 5.9 %collective-permute-start.4 = (bf16[384,384]{1,0:T(8,128)(2,1)}, bf16[384,384]{1,0:T(8,128)(2,1)S(1)}, u32[]{:S(2)}, u32[]{:S(2)}) collective-permute-start(bf16[384,384]{1,0:T(8,128)(2,1)} %collective-permute-done.3), channel_id=1, source_target_pairs={{0,1},{1,0},{2,3},{3,2},{4,5},{5,4},{6,7},{7,6},{8,9},{9,8},{10,11... | collective-permute-start | bytes 884744 | tf_op jit(solution)/shard_map/ppermute | solution.py:142
  36.5 2.2 %collective-permute-start.2 = (bf16[192,768]{1,0:T(8,128)(2,1)}, bf16[192,768]{1,0:T(8,128)(2,1)S(1)}, u32[]{:S(2)}, u32[]{:S(2)}) collective-permute-start(bf16[192,768]{1,0:T(8,128)(2,1)} %collective-permute-done.1), channel_id=1, source_target_pairs={{0,1},{1,0},{2,3},{3,2},{4,5},{5,4},{6,7},{7,6},{8,9},{9,8},{10,11... | collective-permute-start | bytes 884744 | tf_op jit(solution)/shard_map/ppermute | solution.py:142
  42.9 26.8 %all-to-all-start.1 = ((bf16[1,32,1,32,384]{4,3,2,0,1:T(8,128)(2,1)}), bf16[1,32,1,32,384]{4,3,2,0,1:T(8,128)(2,1)S(1)}, u32[]{:S(2)}, u32[]{:S(2)}) async-start(bf16[1,32,1,32,384]{4,3,2,0,1:T(8,128)(2,1)} %bitcast.15), calls=%async_computation.1 | async-start | bytes 1572864 | tf_op jit(solution)/shard_map/all_to_all | solution.py:116
  81.7 4.6 %copy-start.26 = (f32[384]{0:T(512)S(1)}, f32[384]{0:T(512)}, u32[]{:S(2)}) copy-start(f32[384]{0:T(512)} %copy-done.25) | copy-start | bytes 4612
  82.7 22.3 %all-to-all-start.2 = ((bf16[2,1,16,32,384]{4,3,1,0,2:T(8,128)(2,1)}), bf16[2,1,16,32,384]{4,3,1,0,2:T(8,128)(2,1)S(1)}, u32[]{:S(2)}, u32[]{:S(2)}) async-start(bf16[2,1,16,32,384]{4,3,1,0,2:T(8,128)(2,1)} %copy.25), calls=%async_computation.2 | async-start | bytes 1572864 | tf_op jit(solution)/shard_map/all_to_all | solution.py:111
  108.2 26.4 %all-to-all-start.3 = ((bf16[1,32,1,32,384]{4,3,2,0,1:T(8,128)(2,1)}), bf16[1,32,1,32,384]{4,3,2,0,1:T(8,128)(2,1)S(1)}, u32[]{:S(2)}, u32[]{:S(2)}) async-start(bf16[1,32,1,32,384]{4,3,2,0,1:T(8,128)(2,1)} %bitcast.182), calls=%async_computation.3 | async-start | bytes 1572864 | tf_op jit(solution)/shard_map/all_to_all | solution.py:116
  113.0 9.4 %copy-start = (f32[1,16,1,32,384]{4,3,2,0,1:T(8,128)S(1)}, f32[1,16,1,32,384]{4,3,2,0,1:T(8,128)}, u32[]{:S(2)}) copy-start(f32[1,16,1,32,384]{4,3,2,0,1:T(8,128)} %get-tuple-element.97) | copy-start | bytes 2359300
  113.1 28.3 %collective-permute-start.5 = (bf16[1,1,512,384]{3,2,1,0:T(8,128)(2,1)S(1)}, bf16[1,1,512,384]{3,2,1,0:T(8,128)(2,1)}, u32[]{:S(2)}, u32[]{:S(2)}) collective-permute-start(bf16[1,1,512,384]{3,2,1,0:T(8,128)(2,1)S(1)} %bitcast.189), channel_id=1, source_target_pairs={{16,0},{17,1},{18,2},{19,3},{20,4},{21,5},{22,6},{23,7},{24,8},{25... | collective-permute-start | bytes 1179656 | tf_op jit(solution)/shard_map/ppermute | solution.py:184
  116.4 25.0 %collective-permute-start.6 = (bf16[1,1,512,384]{3,2,1,0:T(8,128)(2,1)}, bf16[1,1,512,384]{3,2,1,0:T(8,128)(2,1)}, u32[]{:S(2)}, u32[]{:S(2)}) collective-permute-start(bf16[1,1,512,384]{3,2,1,0:T(8,128)(2,1)} %fusion.65), channel_id=1, source_target_pairs={{0,16},{1,17},{2,18},{3,19},{4,20},{5,21},{6,22},{7,23},{8,24},{9,... | collective-permute-start | bytes 1179656 | tf_op jit(solution)/shard_map/ppermute | solution.py:183
  134.6 3.1 %copy-start.9 = (bf16[1,384,768]{2,1,0:T(8,128)(2,1)S(1)}, bf16[1,384,768]{2,1,0:T(8,128)(2,1)}, u32[]{:S(2)}) copy-start(bf16[1,384,768]{2,1,0:T(8,128)(2,1)} %param.13) | copy-start | bytes 1769476
  (56 other events, 49.7 us)
